TPU v7x, 32 devices: a whole 2x2x4 slice. The times are simulated.
32 devices in a mesh: blk: 16 (over z, y, x), band: 2 (over core).
Axes of the slice: x: 2, y: 2, z: 4, core: 2. Of those that a mesh axis runs over, the one named last changes fastest.
Arguments:
- traces: bfloat16 [1024, 2, 8192], P('blk', None, 'band'), may hold values from -80 to 80
- sources: bfloat16 [32, 2, 8192], P('blk', None, 'band'), may hold values from -80 to 80
- owner: int32 [1024, 1], P('blk'), may hold values from 0 to 15; in each aligned block of 64 rows (0 to 63, 64 to 127, ...) at most 8 rows name the same one
Outputs:
- gathers: float32 [32, 4, 128, 256], P('blk', None, 'band')
Inputs may be any that keep to these rules, and one draw needn't show every extreme that they name: Among the 64 stations of one device's rows, at most 8 name the same owner block, and some owner block is named by exactly 8 of them in every draw.
All inputs are finite; a program needn't handle non-finite values.
Results may differ from a plain program's by a relative error of at most 0.017.
Values may be sent and summed in bfloat16 or wider, within the bound.
No kernel may reach another device: no remote copies, remote signals or barrier semaphores. Data moves between devices by JAX's collectives and lax.ppermute only.
A program may use at most 128 MiB of HBM per device.

v0:
```python
import math

import jax
import jax.numpy as jnp
from jax import lax
from jax.sharding import PartitionSpec as P

BINS = 8192
LAGS = 2048
DEC = 8


EPS = 1e-06


def from_behind(block, axis, distance):
    devices = range(lax.axis_size(axis))
    route = [((i - distance) % len(devices), i) for i in devices]
    return lax.ppermute(block, axis, route)


def per_device(traces, sources, owner):
    blocks = lax.axis_size("blk")
    band_count = lax.axis_size("band")
    station_count = traces.shape[0]
    source_count = sources.shape[0]
    group_bins = traces.shape[2]
    capacity = max(2, 2 * station_count // blocks)
    slot_total = blocks * capacity
    slot_share = slot_total // band_count
    lags_out = LAGS // DEC
    cycle_steps = blocks // 4
    trace_float = traces.astype(jnp.float32)
    source_float = sources.astype(jnp.float32)
    trace_power, source_power = lax.psum(
        (
            jnp.sum(trace_float * trace_float, axis=(1, 2)),
            jnp.sum(source_float * source_float, axis=(1, 2)),
        ),
        "band",
    )
    white_traces = (
        (trace_float * lax.rsqrt(trace_power / (2 * BINS) + EPS)[:, None, None])
        .astype(jnp.bfloat16)
        .reshape(station_count, 2 * group_bins)
    )
    white_sources = (
        (source_float * lax.rsqrt(source_power / (2 * BINS) + EPS)[:, None, None])
        .astype(jnp.bfloat16)
        .reshape(source_count, 2 * group_bins)
    )
    owners = owner[:, 0]
    owner_hits = (owners[:, None] == jnp.arange(blocks, dtype=jnp.int32)[None, :]).astype(jnp.int32)
    earlier = jnp.cumsum(owner_hits, axis=0) - owner_hits
    arrival = jnp.sum(owner_hits * earlier, axis=1)
    slot_index = owners * capacity + arrival
    placing = (jnp.arange(slot_total, dtype=jnp.int32)[:, None] == slot_index[None, :]).astype(
        jnp.bfloat16
    )
    outgoing = jnp.dot(placing, white_traces, preferred_element_type=jnp.float32).astype(
        jnp.bfloat16
    )
    outgoing = outgoing.reshape(blocks, capacity, 2 * group_bins)
    resident = lax.all_to_all(outgoing, "blk", split_axis=0, concat_axis=0, tiled=True).reshape(
        slot_total, 2 * group_bins
    )
    bin_index = lax.axis_index("band") * group_bins + jnp.arange(group_bins, dtype=jnp.int32)
    lag_value = (jnp.arange(lags_out, dtype=jnp.int32) - lags_out // 2) * DEC
    phase_angle = jnp.mod(bin_index[:, None] * lag_value[None, :], BINS).astype(jnp.float32) * (
        2.0 * math.pi / BINS
    )
    cosine_table = jnp.cos(phase_angle)[:, None, :]
    sine_table = jnp.sin(phase_angle)[:, None, :]
    norm_scale = BINS ** (-0.5)

    def correlate(receivers, kernel):
        return lax.psum_scatter(
            jnp.dot(receivers, kernel, preferred_element_type=jnp.float32).astype(jnp.bfloat16),
            "band",
            scatter_dimension=0,
            tiled=True,
        ).astype(jnp.float32)

    source_values = white_sources.astype(jnp.float32)
    real_part = source_values[:, :group_bins].T[:, :, None]
    imag_part = source_values[:, group_bins:].T[:, :, None]
    kernel_real = real_part * cosine_table + imag_part * sine_table
    kernel_imag = imag_part * cosine_table - real_part * sine_table
    joined = jnp.concatenate([kernel_real, kernel_imag], axis=0) * norm_scale
    kernel = joined.reshape(2 * group_bins, source_count * lags_out).astype(jnp.bfloat16)

    def advance(visiting, unused):
        partial_value = correlate(visiting, kernel)
        return (from_behind(visiting, "blk", 1), partial_value)

    visiting, partials = lax.scan(advance, resident, None, length=cycle_steps - 1)
    partials = jnp.concatenate([partials, correlate(visiting, kernel)[None]], axis=0)
    partials = partials.reshape(cycle_steps, slot_share, source_count, lags_out)
    return jnp.transpose(partials, (2, 0, 1, 3))


def solution(mesh):
    placed = (P("blk", None, "band"), P("blk", None, "band"), P("blk", None))
    return jax.shard_map(
        per_device,
        mesh=mesh,
        in_specs=placed,
        out_specs=P("blk", None, "band", None),
        check_vma=False,
    )
```

profile of v0, /device:TPU:0, one launch (start us, length us, event | category | flops | bytes accessed | tf_op | source)
XLA Modules:
  0.0 258.5 jit_solution(10477725890457019970)
XLA Ops:
  7.4 2.8 %fusion.5 = f32[64]{0:T(128)S(1)} fusion(bf16[64,2,4096]{2,1,0:T(2,128)(2,1)} %param.5), kind=kLoop, calls=%fused_computation.18 | loop fusion | flops 1572800 | bytes 1048832 | tf_op jit(solution)/shard_map/reduce_sum | solution.py:37
  10.2 0.9 fusion.9
  13.4 2.6 all-reduce
  16.0 2.5 fusion.6
  19.1 2.0 fusion.1
  21.1 8.3 %all-to-all-start = ((bf16[16,8,8192]{2,1,0:T(8,128)(2,1)}), bf16[16,8,8192]{2,1,0:T(8,128)(2,1)}, u32[]{:S(2)}, u32[]{:S(2)}) async-start(bf16[16,8,8192]{2,1,0:T(8,128)(2,1)} %fusion.1), calls=%async_computation.1 | async-start | bytes 4194304 | tf_op jit(solution)/shard_map/all_to_all | solution.py:64
  29.6 2.0 copy.7
  31.6 2.0 copy.8
  33.6 18.4 %fusion.8 = (f32[4096,256]{1,0:T(8,128)S(1)}, f32[4096,256]{1,0:T(8,128)}) fusion(s32[256]{0:T(256)S(1)} %add_multiply_fusion, s32[4096]{0:T(1024)S(1)} %iota_add_fusion), kind=kLoop, calls=%fused_computation.21 | loop fusion | flops 14680064 | bytes 8406016 | tf_op jit(solution)/shard_map/cos | solution.py:72
  52.0 14.1 %multiply_add_fusion = (f32[4096,2,256]{2,1,0:T(2,128)S(1)}, f32[4096,2,256]{2,1,0:T(2,128)S(1)}) fusion(f32[4096,256]{1,0:T(8,128)} %get-tuple-element.45, f32[4096,2]{1,0:T(8,128)} %copy.8, f32[4096,256]{1,0:T(8,128)S(1)} %get-tuple-element.44, f32[4096,2]{1,0:T(8,128)} %copy.7), kind=kLoop, calls=%fused_computation.7 | loop fusion | flops 12582912 | bytes 25231360 | tf_op jit(solution)/shard_map/add | solution.py:87
  66.1 4.2 %copy.12 = f32[512,8,2,256]{3,1,2,0:T(8,128)} copy(f32[512,8,2,256]{3,2,1,0:T(2,128)S(1)} %bitcast.35) | data formatting | bytes 16777216
  70.3 5.2 %copy.13 = f32[512,8,2,256]{3,1,2,0:T(8,128)} copy(f32[512,8,2,256]{3,2,1,0:T(2,128)S(1)} %bitcast.34) | data formatting | bytes 16777216
  75.5 1.3 slice-done.1
  76.8 7.6 %fusion = bf16[8192,512]{1,0:T(8,128)(2,1)} fusion(f32[4096,512]{1,0:T(8,128)} %bitcast.39, f32[4096,512]{1,0:T(8,128)S(1)} %bitcast.38), kind=kLoop, calls=%fused_computation.3 | loop fusion | flops 12582912 | bytes 25165824 | tf_op jit(solution)/shard_map/convert_element_type | solution.py:90
  84.4 155.5 %while.12 = (s32[]{:T(128)}, bf16[128,8192]{1,0:T(8,128)(2,1)}, f32[3,64,512]{2,1,0:T(8,128)S(1)}, bf16[8192,512]{1,0:T(8,128)(2,1)}, s32[]{:T(128)}) while((s32[]{:T(128)}, bf16[128,8192]{1,0:T(8,128)(2,1)}, f32[3,64,512]{2,1,0:T(8,128)S(1)}, bf16[8192,512]{1,0:T(8,128)(2,1)}, s32[]{:T(128)}) %tuple.21), condition=%wide.region_8.9_spmd, body=%wide.region_6.8_spmd.sunk | while | flops 1073840128 | bytes 23986328 | solution.py:96
  84.4 1.6 copy.19
  86.0 1.9 collective-permute-start
  87.9 5.3 %convolution_convert_fusion.4 = bf16[128,512]{1,0:T(8,128)(2,1)} fusion(bf16[128,8192]{1,0:T(8,128)(2,1)S(1)} %copy.19, bf16[8192,512]{1,0:T(8,128)(2,1)} %get-tuple-element.84), kind=kOutput, calls=%fused_computation.clone.1 | convolution fusion | flops 1073807360 | bytes 10616832 | tf_op jit(solution)/shard_map/while/body/eval_jaxpr/dot_general | solution.py:78
  93.2 7.6 %reduce-scatter.5.cloned.1.call-done = bf16[64,512]{1,0:T(8,128)(2,1)} async-done(((bf16[128,512]{1,0:T(8,128)(2,1)}), bf16[64,512]{1,0:T(8,128)(2,1)}) %reduce-scatter.5.cloned.1.call-update) | async-done | bytes 65552 | tf_op jit(solution)/shard_map/while/body/eval_jaxpr/reduce_scatter | solution.py:77
  101.7 35.5 %collective-permute-done = bf16[128,8192]{1,0:T(8,128)(2,1)} collective-permute-done((bf16[128,8192]{1,0:T(8,128)(2,1)S(1)}, bf16[128,8192]{1,0:T(8,128)(2,1)}, u32[]{:S(2)}, u32[]{:S(2)}) %collective-permute-start) | collective-permute-done | bytes 2097184 | tf_op jit(solution)/shard_map/while/body/eval_jaxpr/ppermute | solution.py:19
  137.1 1.6 copy.19
  138.7 5.3 %convolution_convert_fusion.4 = bf16[128,512]{1,0:T(8,128)(2,1)} fusion(bf16[128,8192]{1,0:T(8,128)(2,1)S(1)} %copy.19, bf16[8192,512]{1,0:T(8,128)(2,1)} %get-tuple-element.84), kind=kOutput, calls=%fused_computation.clone.1 | convolution fusion | flops 1073807360 | bytes 10616832 | tf_op jit(solution)/shard_map/while/body/eval_jaxpr/dot_general | solution.py:78
  144.1 9.1 %reduce-scatter.5.cloned.1.call-done = bf16[64,512]{1,0:T(8,128)(2,1)} async-done(((bf16[128,512]{1,0:T(8,128)(2,1)}), bf16[64,512]{1,0:T(8,128)(2,1)}) %reduce-scatter.5.cloned.1.call-update) | async-done | bytes 65552 | tf_op jit(solution)/shard_map/while/body/eval_jaxpr/reduce_scatter | solution.py:77
  153.1 0.8 convert_dynamic-update-slice_fusion.2
  154.0 35.0 %collective-permute-done = bf16[128,8192]{1,0:T(8,128)(2,1)} collective-permute-done((bf16[128,8192]{1,0:T(8,128)(2,1)S(1)}, bf16[128,8192]{1,0:T(8,128)(2,1)}, u32[]{:S(2)}, u32[]{:S(2)}) %collective-permute-start) | collective-permute-done | bytes 2097184 | tf_op jit(solution)/shard_map/while/body/eval_jaxpr/ppermute | solution.py:19
  189.0 1.6 copy.19
  190.6 5.3 %convolution_convert_fusion.4 = bf16[128,512]{1,0:T(8,128)(2,1)} fusion(bf16[128,8192]{1,0:T(8,128)(2,1)S(1)} %copy.19, bf16[8192,512]{1,0:T(8,128)(2,1)} %get-tuple-element.84), kind=kOutput, calls=%fused_computation.clone.1 | convolution fusion | flops 1073807360 | bytes 10616832 | tf_op jit(solution)/shard_map/while/body/eval_jaxpr/dot_general | solution.py:78
  195.9 9.0 %reduce-scatter.5.cloned.1.call-done = bf16[64,512]{1,0:T(8,128)(2,1)} async-done(((bf16[128,512]{1,0:T(8,128)(2,1)}), bf16[64,512]{1,0:T(8,128)(2,1)}) %reduce-scatter.5.cloned.1.call-update) | async-done | bytes 65552 | tf_op jit(solution)/shard_map/while/body/eval_jaxpr/reduce_scatter | solution.py:77
  205.8 34.1 %collective-permute-done = bf16[128,8192]{1,0:T(8,128)(2,1)} collective-permute-done((bf16[128,8192]{1,0:T(8,128)(2,1)S(1)}, bf16[128,8192]{1,0:T(8,128)(2,1)}, u32[]{:S(2)}, u32[]{:S(2)}) %collective-permute-start) | collective-permute-done | bytes 2097184 | tf_op jit(solution)/shard_map/while/body/eval_jaxpr/ppermute | solution.py:19
  239.9 5.9 %convolution_convert_fusion.2 = bf16[128,512]{1,0:T(8,128)(2,1)} fusion(bf16[128,8192]{1,0:T(8,128)(2,1)} %get-tuple-element.29, bf16[8192,512]{1,0:T(8,128)(2,1)} %get-tuple-element.88), kind=kOutput, calls=%fused_computation.22 | convolution fusion | flops 1073807360 | bytes 10616832 | tf_op jit(solution)/shard_map/dot_general | solution.py:78
  246.2 3.2 %reduce-scatter.3.cloned.1.call-done = bf16[64,512]{1,0:T(8,128)(2,1)} async-done(((bf16[128,512]{1,0:T(8,128)(2,1)}), bf16[64,512]{1,0:T(8,128)(2,1)}) %reduce-scatter.3.cloned.1.call-update) | async-done | bytes 65552 | tf_op jit(solution)/shard_map/reduce_scatter | solution.py:77
  249.3 0.9 reshape.120
  (35 shorter events, 6.2 us)
Async XLA Ops:
  19.1 10.3 %copy-start = (bf16[2,2,4096]{2,1,0:T(2,128)(2,1)S(1)}, bf16[2,2,4096]{2,1,0:T(2,128)(2,1)}, u32[]{:S(2)}) copy-start(bf16[2,2,4096]{2,1,0:T(2,128)(2,1)} %param.6) | copy-start | bytes 98308
  21.1 63.3 %all-to-all-start = ((bf16[16,8,8192]{2,1,0:T(8,128)(2,1)}), bf16[16,8,8192]{2,1,0:T(8,128)(2,1)}, u32[]{:S(2)}, u32[]{:S(2)}) async-start(bf16[16,8,8192]{2,1,0:T(8,128)(2,1)} %fusion.1), calls=%async_computation.1 | async-start | bytes 4194304 | tf_op jit(solution)/shard_map/all_to_all | solution.py:64
  70.3 5.2 %slice-start = ((s8[8388608]{0:T(1024)(128)(4,1)}), s8[4194304]{0:T(1024)(128)(4,1)S(1)}, s32[]{:S(2)}) async-start(s8[8388608]{0:T(1024)(128)(4,1)} %bitcast.36), calls=%async_computation.5 | async-start | bytes 8388608
  70.3 6.5 %slice-start.1 = ((s8[8388608]{0:T(1024)(128)(4,1)}), s8[4194304]{0:T(1024)(128)(4,1)S(1)}, s32[]{:S(2)}) async-start(s8[8388608]{0:T(1024)(128)(4,1)} %bitcast.36), calls=%async_computation.6 | async-start | bytes 8388608
  84.4 16.4 %reduce-scatter.5.cloned.1.call-start = ((), (), s32[]{:S(2)}) async-start(), calls=%async_computation.4 | async-start | bytes 196608 | tf_op jit(solution)/shard_map/while/body/eval_jaxpr/reduce_scatter | solution.py:77
  86.0 51.1 %collective-permute-start = (bf16[128,8192]{1,0:T(8,128)(2,1)S(1)}, bf16[128,8192]{1,0:T(8,128)(2,1)}, u32[]{:S(2)}, u32[]{:S(2)}) collective-permute-start(bf16[128,8192]{1,0:T(8,128)(2,1)S(1)} %copy.19), channel_id=1, source_target_pairs={{30,0},{0,2},{2,4},{4,6},{6,8},{8,10},{10,12},{12,14},{14,16},{16,... | collective-permute-start | bytes 6291464 | tf_op jit(solution)/shard_map/while/body/eval_jaxpr/ppermute | solution.py:19
  137.1 16.0 %reduce-scatter.5.cloned.1.call-start = ((), (), s32[]{:S(2)}) async-start(), calls=%async_computation.4 | async-start | bytes 196608 | tf_op jit(solution)/shard_map/while/body/eval_jaxpr/reduce_scatter | solution.py:77
  138.7 50.3 %collective-permute-start = (bf16[128,8192]{1,0:T(8,128)(2,1)S(1)}, bf16[128,8192]{1,0:T(8,128)(2,1)}, u32[]{:S(2)}, u32[]{:S(2)}) collective-permute-start(bf16[128,8192]{1,0:T(8,128)(2,1)S(1)} %copy.19), channel_id=1, source_target_pairs={{30,0},{0,2},{2,4},{4,6},{6,8},{8,10},{10,12},{12,14},{14,16},{16,... | collective-permute-start | bytes 6291464 | tf_op jit(solution)/shard_map/while/body/eval_jaxpr/ppermute | solution.py:19
  189.0 16.0 %reduce-scatter.5.cloned.1.call-start = ((), (), s32[]{:S(2)}) async-start(), calls=%async_computation.4 | async-start | bytes 196608 | tf_op jit(solution)/shard_map/while/body/eval_jaxpr/reduce_scatter | solution.py:77
  190.6 49.3 %collective-permute-start = (bf16[128,8192]{1,0:T(8,128)(2,1)S(1)}, bf16[128,8192]{1,0:T(8,128)(2,1)}, u32[]{:S(2)}, u32[]{:S(2)}) collective-permute-start(bf16[128,8192]{1,0:T(8,128)(2,1)S(1)} %copy.19), channel_id=1, source_target_pairs={{30,0},{0,2},{2,4},{4,6},{6,8},{8,10},{10,12},{12,14},{14,16},{16,... | collective-permute-start | bytes 6291464 | tf_op jit(solution)/shard_map/while/body/eval_jaxpr/ppermute | solution.py:19
  239.9 9.4 %reduce-scatter.3.cloned.1.call-start = ((), (), s32[]{:S(2)}) async-start(), calls=%async_computation.3 | async-start | bytes 196608 | tf_op jit(solution)/shard_map/reduce_scatter | solution.py:77
Sparse Core Ops, SparseCore 0:
  93.3 7.4 reduce-scatter.4
  144.2 8.8 reduce-scatter.4
  196.0 8.8 reduce-scatter.4
Sparse Core Ops, SparseCore 1:
  246.0 3.3 reduce-scatter.2
where the time goes:
time: 259 us; the launch traced here: 258 us
  waiting for transfers between devices  134 us (52%)
  other arithmetic  51.6 us (20%)
  matrix products  23.8 us (9%)
  local copies, waits for them, and re-layouts  22.1 us (9%)
  between operations  14.6 us (6%)
  starting transfers between devices  10.1 us (4%)
    ppermute x3, waiting for transfers between devices, from_behind(): return lax.ppermute(block, axis, route)  105 us
    reduce_scatter x4, waiting for transfers between devices, correlate(): lax.psum_scatter(jnp.dot(receivers, kernel, preferred_element_type=jnp.fl...  28.9 us
    dot_general x4, matrix products, correlate(): jnp.dot(receivers, kernel, preferred_element_type=jnp.float32)  21.8 us
    cos x1, other arithmetic, per_device(): cosine_table = jnp.cos(phase_angle)[:, None, :]  18.4 us
    add x1, other arithmetic, per_device(): kernel_real = real_part * cosine_table + imag_part * sine_table  14.1 us
    unnamed x10, local copies, waits for them, and re-layouts  11.3 us
    all_to_all x1, starting transfers between devices, per_device(): lax.all_to_all(outgoing, 'blk', split_axis=0, concat_axis=0, tiled=True)  8.26 us
    convert_element_type x1, other arithmetic, per_device(): joined.reshape(2 * group_bins, source_count * lags_out).astype(jnp.bfloat16)  7.63 us
  transfers between devices with their start and end apart: 8, of which 7 were waited for; matrix products, arithmetic and copies ran while one was open for 28% of the time, Pallas kernels for 0%

commit v1 on v0

v1 whole, which is shorter than its diff:
```python
import math

import jax
import jax.numpy as jnp
from jax import lax
from jax.sharding import PartitionSpec as P

BINS = 8192
LAGS = 2048
DEC = 8
PERIOD = BINS // DEC


EPS = 1e-06


def per_device(traces, sources, owner):
    blocks = lax.axis_size("blk")
    station_count = traces.shape[0]
    source_count = sources.shape[0]
    group_bins = traces.shape[2]
    folds = group_bins // PERIOD
    capacity = max(2, 2 * station_count // blocks)
    lags_out = LAGS // DEC
    offsets = blocks // 4

    all_sources = lax.all_gather(sources, "blk", axis=0, tiled=True)

    trace_float = traces.astype(jnp.float32)
    all_source_float = all_sources.astype(jnp.float32)
    trace_power, source_power = lax.psum(
        (
            jnp.sum(trace_float * trace_float, axis=(1, 2)),
            jnp.sum(all_source_float * all_source_float, axis=(1, 2)),
        ),
        "band",
    )
    white_traces = (
        (trace_float * lax.rsqrt(trace_power / (2 * BINS) + EPS)[:, None, None])
        .astype(jnp.bfloat16)
        .reshape(station_count, 2 * group_bins)
    )
    white_sources = (
        (all_source_float * lax.rsqrt(source_power / (2 * BINS) + EPS)[:, None, None])
        .astype(jnp.bfloat16)
        .astype(jnp.float32)
        .reshape(blocks, source_count, 2, folds, PERIOD)
    )

    owners = owner[:, 0]
    owner_hits = (owners[:, None] == jnp.arange(blocks, dtype=jnp.int32)[None, :]).astype(jnp.int32)
    earlier = jnp.cumsum(owner_hits, axis=0) - owner_hits
    arrival = jnp.sum(owner_hits * earlier, axis=1)
    slot_index = owners * capacity + arrival
    placing = (
        jnp.arange(blocks * capacity, dtype=jnp.int32)[:, None] == slot_index[None, :]
    ).astype(jnp.bfloat16)
    placed = jnp.dot(placing, white_traces, preferred_element_type=jnp.float32)
    placed = placed.reshape(blocks, capacity, 2, folds, PERIOD)

    bin_index = jnp.arange(PERIOD, dtype=jnp.int32)
    lag_value = (jnp.arange(lags_out, dtype=jnp.int32) - lags_out // 2) * DEC
    phase_angle = jnp.mod(bin_index[:, None] * lag_value[None, :], BINS).astype(jnp.float32) * (
        2.0 * math.pi / BINS
    )
    table = jnp.concatenate([jnp.cos(phase_angle), jnp.sin(phase_angle)], axis=0).astype(
        jnp.bfloat16
    )
    norm_scale = BINS ** (-0.5)

    real_s = white_sources[:, None, :, 0]
    imag_s = white_sources[:, None, :, 1]
    cross = []
    for offset in range(offsets):
        visiting = jnp.roll(placed, offset, axis=0)
        real_t = visiting[:, :, None, 0]
        imag_t = visiting[:, :, None, 1]
        even = jnp.sum(real_t * real_s + imag_t * imag_s, axis=3)
        odd = jnp.sum(real_t * imag_s - imag_t * real_s, axis=3)
        cross.append(jnp.concatenate([even, odd], axis=-1))
    cross = jnp.stack(cross, axis=1).astype(jnp.bfloat16)
    rows = blocks * offsets * capacity * source_count
    partial = jnp.dot(
        cross.reshape(rows, 2 * PERIOD), table, preferred_element_type=jnp.float32
    )
    partial = (partial * norm_scale).astype(jnp.bfloat16)
    partial = partial.reshape(blocks, offsets, capacity, source_count, lags_out)
    arrived = lax.all_to_all(partial, "blk", split_axis=0, concat_axis=0, tiled=True)
    summed = lax.psum_scatter(
        arrived.astype(jnp.float32), "band", scatter_dimension=0, tiled=True
    )
    half = summed.shape[0]
    return jnp.transpose(summed, (3, 1, 0, 2, 4)).reshape(
        source_count, offsets, half * capacity, lags_out
    )


def solution(mesh):
    placed = (P("blk", None, "band"), P("blk", None, "band"), P("blk", None))
    return jax.shard_map(
        per_device,
        mesh=mesh,
        in_specs=placed,
        out_specs=P("blk", None, "band", None),
        check_vma=False,
    )
```

time: 259 us -> 151 us (0.58)
  waiting for transfers between devices: 134 us -> 7.22 us
  blocking collectives: 2.56 us -> 66.2 us
  other arithmetic: 51.6 us -> 24.5 us
  matrix products: 23.8 us -> 4.13 us
  local copies, waits for them, and re-layouts: 22.1 us -> 35.1 us
  starting transfers between devices: 10.1 us -> 0.01 us
    ppermute x3 -> x0, waiting for transfers between devices: 105 us -> none  [from_behind(): return lax.ppermute(block, axis, route)]
    all_gather x0 -> x1, blocking collectives: none -> 45.7 us  [per_device(): all_sources = lax.all_gather(sources, 'blk', axis=0, tiled=True)]
    reduce_scatter x4 -> x1, waiting for transfers between devices: 28.9 us -> 7.2 us  [per_device(): lax.psum_scatter(arrived.astype(jnp.float32), 'band', scatter_dimension=0...]
    dot_general x5 -> x2, matrix products: 23.8 us -> 4.13 us  [the longest x1 3.44 us: per_device(): jnp.dot(cross.reshape(rows, 2 * PERIOD), table, preferred_element_type=jn...]
    cos x1 -> x0, other arithmetic: 18.4 us -> none  [per_device(): cosine_table = jnp.cos(phase_angle)[:, None, :]]
    all_to_all x0 -> x1, blocking collectives: none -> 18.1 us  [per_device(): lax.all_to_all(partial, 'blk', split_axis=0, concat_axis=0, tiled=True)]
    add x2 -> x0, other arithmetic: 14.1 us -> none  [the longest x1 14.1 us: per_device(): kernel_real = real_part * cosine_table + imag_part * sine_table]
    all_to_all x1 -> x0, starting transfers between devices: 8.26 us -> none  [per_device(): lax.all_to_all(outgoing, 'blk', split_axis=0, concat_axis=0, tiled=True)]
  transfers between devices with their start and end apart: 8 -> 1, of which waited for: 7 -> 1; matrix products, arithmetic and copies ran while one was open for 28% -> 0% of each run, Pallas kernels for 0% -> 0%
where the time goes in v1:
time: 151 us
  blocking collectives  66.2 us (44%)
  local copies, waits for them, and re-layouts  35.1 us (23%)
  other arithmetic  24.5 us (16%)
  between operations  13.6 us (9%)
  waiting for transfers between devices  7.22 us (5%)
  matrix products  4.13 us (3%)
    all_gather x1, blocking collectives, per_device(): all_sources = lax.all_gather(sources, 'blk', axis=0, tiled=True)  45.7 us
    all_to_all x1, blocking collectives, per_device(): lax.all_to_all(partial, 'blk', split_axis=0, concat_axis=0, tiled=True)  18.1 us
    reduce_sum x1, other arithmetic, per_device(): even = jnp.sum(real_t * real_s + imag_t * imag_s, axis=3)  7.3 us
    reduce_scatter x1, waiting for transfers between devices, per_device(): lax.psum_scatter(arrived.astype(jnp.float32), 'band', scatter_dimension=0...  7.2 us
    convert_element_type x1, local copies, waits for them, and re-layouts, per_device(): cross = jnp.stack(cross, axis=1).astype(jnp.bfloat16)  7.2 us
    slice x6, local copies, waits for them, and re-layouts, per_device(): visiting = jnp.roll(placed, offset, axis=0)  6.99 us
    another operation x1, local copies, waits for them, and re-layouts, per_device(): cross = jnp.stack(cross, axis=1).astype(jnp.bfloat16)  6.3 us
    unnamed x19, local copies, waits for them, and re-layouts  5.42 us
  transfers between devices with their start and end apart: 1, of which 1 were waited for; matrix products, arithmetic and copies ran while one was open for 0% of the time, Pallas kernels for 0%

profile of v1, /device:TPU:0, one launch (start us, length us, event | category | flops | bytes accessed | tf_op | source)
XLA Modules:
  0.0 150.7 jit_solution(14130566093052021480)
XLA Ops:
  6.5 45.7 %all_gather.3 = bf16[32,2,4096]{2,1,0:T(2,128)(2,1)S(1)} all-gather(bf16[2,2,4096]{2,1,0:T(2,128)(2,1)} %param.4), channel_id=1, replica_groups=mesh['blk'=16,'band'=2] {'blk'}, dimensions={0}, use_global_device_ids=true | all-gather | bytes 557056 | tf_op jit(solution)/shard_map/all_gather | solution.py:27
  52.2 0.8 copy-done.4
  53.0 0.8 fusion.12
  53.8 2.8 %fusion = f32[64]{0:T(128)S(1)} fusion(bf16[64,2,4096]{2,1,0:T(2,128)(2,1)} %param.3), kind=kLoop, calls=%fused_computation.17 | loop fusion | flops 1572800 | bytes 1048832 | tf_op jit(solution)/shard_map/reduce_sum | solution.py:33
  56.6 2.5 %all-reduce = (f32[32]{0:T(128)S(1)}, f32[64]{0:T(128)S(1)}) all-reduce(f32[32]{0:T(128)S(1)} %fusion.12, f32[64]{0:T(128)S(1)} %fusion), channel_id=1, replica_groups=mesh['blk'=16,'band'=2] {'band'}, use_global_device_ids=true, to_apply=%region_5.6 | all-reduce | flops 96 | bytes 768 | tf_op jit(solution)/shard_map/psum | solution.py:31
  59.1 2.5 %fusion.1 = bf16[64,2,4096]{2,1,0:T(2,128)(2,1)S(1)} fusion(bf16[64,2,4096]{2,1,0:T(2,128)(2,1)} %param.3, f32[64]{0:T(128)S(1)} %add_rsqrt_fusion.1), kind=kLoop, calls=%fused_computation.18 | loop fusion | flops 1572864 | bytes 2097408 | tf_op jit(solution)/shard_map/convert_element_type | solution.py:40
  61.6 0.6 copy.44
  62.6 0.7 fusion.24
  63.5 0.9 slice.106
  64.5 2.1 %slice.103 = f32[112,8192]{1,0:T(8,128)} slice(f32[128,8192]{1,0:T(8,128)S(1)} %fusion.24), slice={[0:112], [0:8192]} | slice | bytes 7340032 | tf_op jit(solution)/shard_map/jit(_roll_static)/slice | solution.py:75
  66.6 0.8 slice.102
  67.4 2.1 %slice.99 = f32[120,8192]{1,0:T(8,128)} slice(f32[128,8192]{1,0:T(8,128)S(1)} %fusion.24), slice={[0:120], [0:8192]} | slice | bytes 7864320 | tf_op jit(solution)/shard_map/jit(_roll_static)/slice | solution.py:75
  69.6 0.7 slice.98
  70.3 2.4 %slice_bitcast_fusion.1 = (f32[16,8,4,1024]{3,1,2,0:T(8,128)}, f32[16,8,4,1024]{3,1,2,0:T(8,128)}) fusion(f32[16,8,2,4,1024]{4,1,3,2,0:T(8,128)S(1)} %bitcast.46), kind=kLoop, calls=%fused_computation.32 | loop fusion | bytes 8388608 | tf_op jit(solution)/shard_map/mul | solution.py:78
  72.7 1.5 %fusion.23 = f32[32,2,4096]{2,1,0:T(2,128)} fusion(f32[32]{0:T(128)S(1)} %add_rsqrt_fusion, bf16[32,2,4096]{2,1,0:T(2,128)(2,1)S(1)} %copy-done.5), kind=kLoop, calls=%fused_computation.57 | loop fusion | flops 1048576 | bytes 1572992 | tf_op jit(solution)/shard_map/reshape | solution.py:47
  74.2 3.3 %reshape.51 = f32[16,2,2,4,1024]{4,3,2,1,0:T(4,128)} reshape(f32[32,2,4096]{2,1,0:T(2,128)} %fusion.23) | data formatting | bytes 2097152 | tf_op jit(solution)/shard_map/reshape | solution.py:47
  77.6 1.3 slice_bitcast_fusion.3
  78.9 1.6 %fusion.3 = (f32[16,8,4,1024]{3,1,2,0:T(8,128)S(1)}, f32[16,8,4,1024]{3,1,2,0:T(8,128)S(1)}) fusion(f32[3,8,2,4,1024]{4,1,3,2,0:T(8,128)} %bitcast.52, f32[13,8,2,4,1024]{4,1,3,2,0:T(8,128)S(1)} %bitcast.49), kind=kLoop, calls=%fused_computation.20 | loop fusion | flops 1048576 | bytes 8388608 | tf_op jit(solution)/shard_map/mul | solution.py:78
  80.5 0.6 copy-done.1
  81.8 1.6 %copy-done = f32[120,8192]{1,0:T(8,128)S(1)} copy-done((f32[120,8192]{1,0:T(8,128)S(1)}, f32[120,8192]{1,0:T(8,128)}, u32[]{:S(2)}) %copy-start) | copy-done | bytes 3932184
  83.9 1.1 copy-done.2
  85.0 0.6 copy-done.3
  85.6 7.3 %add_reduce_fusion.3 = (bf16[16,8,2,1024]{3,1,2,0:T(8,128)(2,1)S(1)}, bf16[16,8,2,1024]{3,1,2,0:T(8,128)(2,1)S(1)}, bf16[16,8,2,1024]{3,1,2,0:T(8,128)(2,1)S(1)}...) fusion(f32[16,2,4,1024]{3,2,1,0:T(4,128)S(1)} %get-tuple-elemen, ...), kind=kLoop, calls=%fused_computation.14 | loop fusion | flops 31457280 | bytes 22020096 | tf_op jit(solution)/shard_map/reduce_sum | solution.py:78
  93.3 0.6 pad_maximum_fusion
  93.9 6.3 %copy.41 = bf16[16,4,8,2,2048]{4,3,2,1,0:T(2,128)(2,1)} copy(bf16[16,4,8,2,2048]{4,2,3,0,1:T(8,128)(2,1)S(1)} %pad_maximum_fusion) | data formatting | bytes 8388608 | tf_op jit(solution)/shard_map/stack | solution.py:81
  100.2 7.2 %convert_element_type.39 = bf16[1024,2048]{1,0:T(8,128)(2,1)} reshape(bf16[16,4,8,2,2048]{4,3,2,1,0:T(2,128)(2,1)} %copy.41) | data formatting | bytes 8388608 | tf_op jit(solution)/shard_map/convert_element_type | solution.py:81
  107.4 4.4 %cosine_convert_fusion = (bf16[1024,256]{1,0:T(8,128)(2,1)S(1)}, bf16[1024,256]{1,0:T(8,128)(2,1)S(1)}) fusion(s32[256]{0:T(256)S(1)} %add_multiply_fusion), kind=kLoop, calls=%fused_computation.53 | loop fusion | flops 4194304 | bytes 1049600 | tf_op jit(solution)/shard_map/convert.1
  111.8 3.4 %fusion.11 = bf16[1024,256]{1,0:T(8,128)(2,1)S(1)} fusion(bf16[1024,2048]{1,0:T(8,128)(2,1)} %convert_element_type.39, bf16[1024,256]{1,0:T(8,128)(2,1)S(1)} %get-tuple-element.32, bf16[1024,256]{1,0:T(8,128)(2,1)S(1)} %get-tuple-element.31), kind=kOutput, calls=%fused_computation.39 | convolution fusion | flops 1076363264 | bytes 5767168 | tf_op jit(solution)/shard_map/dot_general | solution.py:83
  115.5 18.1 %all_to_all.5 = bf16[16,4,8,2,256]{4,2,3,1,0:T(8,128)(2,1)S(1)} all-to-all(bf16[16,4,8,2,256]{4,2,3,1,0:T(8,128)(2,1)S(1)} %copy.42), channel_id=1, replica_groups=mesh['blk'=16,'band'=2] {'blk'}, dimensions={0} | all-to-all | bytes 1048576 | tf_op jit(solution)/shard_map/all_to_all | solution.py:88
  133.6 1.1 convert_element_type.42
  134.8 7.2 %reduce-scatter.2.cloned.1.call-done = f32[8,4,8,2,256]{4,2,3,1,0:T(8,128)} async-done(((f32[16,4,8,2,256]{4,2,3,1,0:T(8,128)}), f32[8,4,8,2,256]{4,2,3,1,0:T(8,128)}) %reduce-scatter.2.cloned.1.call-update) | async-done | bytes 524304 | tf_op jit(solution)/shard_map/reduce_scatter | solution.py:89
  142.0 1.9 %copy.46 = f32[8,4,8,2,256]{4,2,0,1,3:T(8,128)} copy(f32[8,4,8,2,256]{4,2,3,1,0:T(8,128)} %reduce-scatter.2.cloned.1.call-done) | data formatting | bytes 1048576 | tf_op jit(solution)/shard_map/reduce_scatter | solution.py:89
  (29 shorter events, 2.5 us)
Async XLA Ops:
  6.5 55.7 %copy-start.8 = (s32[64,1]{0,1:T(1,128)S(1)}, s32[64,1]{0,1:T(1,128)}, u32[]{:S(2)}) copy-start(s32[64,1]{0,1:T(1,128)} %param.5) | copy-start | bytes 772
  6.5 135.4 %reduce-scatter.2.cloned.1.call-start = ((), (), s32[]{:S(2)}) async-start(), calls=%async_computation.2 | async-start | bytes 1572864 | tf_op jit(solution)/shard_map/reduce_scatter | solution.py:89
  52.2 0.8 copy-start.4
  70.3 2.4 %copy-start.5 = (bf16[32,2,4096]{2,1,0:T(2,128)(2,1)S(1)}, bf16[32,2,4096]{2,1,0:T(2,128)(2,1)}, u32[]{:S(2)}) copy-start(bf16[32,2,4096]{2,1,0:T(2,128)(2,1)} %copy-done.4) | copy-start | bytes 1572868
  78.9 2.3 %copy-start.1 = (f32[112,8192]{1,0:T(8,128)S(1)}, f32[112,8192]{1,0:T(8,128)}, u32[]{:S(2)}) copy-start(f32[112,8192]{1,0:T(8,128)} %slice.103) | copy-start | bytes 11010052
  78.9 2.4 %copy-start.6 = (f32[16,8192]{1,0:T(8,128)S(1)}, f32[16,8192]{1,0:T(8,128)}, u32[]{:S(2)}) copy-start(f32[16,8192]{1,0:T(8,128)} %slice.102) | copy-start | bytes 1572868
  81.3 2.1 %copy-start = (f32[120,8192]{1,0:T(8,128)S(1)}, f32[120,8192]{1,0:T(8,128)}, u32[]{:S(2)}) copy-start(f32[120,8192]{1,0:T(8,128)} %slice.99) | copy-start | bytes 11796484
  81.3 2.1 %copy-start.7 = (f32[8,8192]{1,0:T(8,128)S(1)}, f32[8,8192]{1,0:T(8,128)}, u32[]{:S(2)}) copy-start(f32[8,8192]{1,0:T(8,128)} %slice.98) | copy-start | bytes 786436
  83.4 1.6 %copy-start.2 = (f32[16,8,4,1024]{3,1,2,0:T(8,128)S(1)}, f32[16,8,4,1024]{3,1,2,0:T(8,128)}, u32[]{:S(2)}) copy-start(f32[16,8,4,1024]{3,1,2,0:T(8,128)} %get-tuple-element.27) | copy-start | bytes 6291460
  83.4 2.2 %copy-start.3 = (f32[16,8,4,1024]{3,1,2,0:T(8,128)S(1)}, f32[16,8,4,1024]{3,1,2,0:T(8,128)}, u32[]{:S(2)}) copy-start(f32[16,8,4,1024]{3,1,2,0:T(8,128)} %get-tuple-element.28) | copy-start | bytes 6291460
Sparse Core Ops, SparseCore 0:
  134.9 7.0 reduce-scatter.1

commit v2 on v1

v2 whole, which is shorter than its diff:
```python
import math

import jax
import jax.numpy as jnp
from jax import lax
from jax.sharding import PartitionSpec as P

BINS = 8192
LAGS = 2048
DEC = 8
PERIOD = BINS // DEC


EPS = 1e-06


def shifted(block, distance):
    count = lax.axis_size("blk")
    route = [(i, (i + distance) % count) for i in range(count)]
    return lax.ppermute(block, "blk", route)


def per_device(traces, sources, owner):
    blocks = lax.axis_size("blk")
    station_count = traces.shape[0]
    source_count = sources.shape[0]
    group_bins = traces.shape[2]
    folds = group_bins // PERIOD
    capacity = max(2, 2 * station_count // blocks)
    lags_out = LAGS // DEC
    offsets = blocks // 4
    me = lax.axis_index("blk")
    band = lax.axis_index("band")

    trace_float = traces.astype(jnp.float32)
    source_float = sources.astype(jnp.float32)
    trace_power, source_power = lax.psum(
        (
            jnp.sum(trace_float * trace_float, axis=(1, 2)),
            jnp.sum(source_float * source_float, axis=(1, 2)),
        ),
        "band",
    )
    white_sources = (
        source_float * lax.rsqrt(source_power / (2 * BINS) + EPS)[:, None, None]
    ).astype(jnp.bfloat16)
    visiting = jnp.stack(
        [white_sources] + [shifted(white_sources, j) for j in range(1, blocks)], axis=0
    )
    white_traces = (
        (trace_float * lax.rsqrt(trace_power / (2 * BINS) + EPS)[:, None, None])
        .astype(jnp.bfloat16)
        .reshape(station_count, 2 * group_bins)
    )

    owners = owner[:, 0]
    owner_hits = (owners[:, None] == jnp.arange(blocks, dtype=jnp.int32)[None, :]).astype(jnp.int32)
    earlier = jnp.cumsum(owner_hits, axis=0) - owner_hits
    arrival = jnp.sum(owner_hits * earlier, axis=1)
    slot_index = jnp.mod(me - owners, blocks) * capacity + arrival
    placing = (
        jnp.arange(blocks * capacity, dtype=jnp.int32)[:, None] == slot_index[None, :]
    ).astype(jnp.bfloat16)
    placed = jnp.dot(placing, white_traces, preferred_element_type=jnp.float32).astype(
        jnp.bfloat16
    )
    placed = placed.reshape(blocks, capacity, 2, folds, PERIOD)

    bin_index = jnp.arange(PERIOD, dtype=jnp.int32)
    lag_value = (jnp.arange(lags_out, dtype=jnp.int32) - lags_out // 2) * DEC
    phase_angle = jnp.mod(bin_index[:, None] * lag_value[None, :], BINS).astype(jnp.float32) * (
        2.0 * math.pi / BINS
    )
    table = jnp.concatenate([jnp.cos(phase_angle), jnp.sin(phase_angle)], axis=0).astype(
        jnp.bfloat16
    )
    norm_scale = BINS ** (-0.5)

    source_values = visiting.astype(jnp.float32).reshape(blocks, source_count, 2, folds, PERIOD)
    real_s = source_values[:, None, :, 0]
    imag_s = source_values[:, None, :, 1]
    cross = []
    for offset in range(offsets):
        owned = jnp.roll(placed, -offset, axis=0).astype(jnp.float32)
        real_t = owned[:, :, None, 0]
        imag_t = owned[:, :, None, 1]
        even = jnp.sum(real_t * real_s + imag_t * imag_s, axis=3)
        odd = jnp.sum(real_t * imag_s - imag_t * real_s, axis=3)
        cross.append(jnp.concatenate([even, odd], axis=-1))
    cross = jnp.stack(cross, axis=1).astype(jnp.bfloat16)
    rows = blocks * offsets * capacity * source_count
    partial = jnp.dot(
        cross.reshape(rows, 2 * PERIOD), table, preferred_element_type=jnp.float32
    )
    partial = (partial * norm_scale).astype(jnp.bfloat16)
    partial = partial.reshape(blocks, offsets, capacity, source_count, lags_out)
    returned = jnp.stack(
        [partial[0]] + [shifted(partial[j], blocks - j) for j in range(1, blocks)], axis=0
    )
    doubled = jnp.concatenate([returned, returned], axis=0)
    half = blocks // 2
    start = jnp.mod(-me, blocks)
    mine = lax.dynamic_slice_in_dim(doubled, start + band * half, half, axis=0)
    other = lax.dynamic_slice_in_dim(doubled, start + (1 - band) * half, half, axis=0)
    other = lax.ppermute(other, "band", [(0, 1), (1, 0)])
    summed = mine.astype(jnp.float32) + other.astype(jnp.float32)
    return jnp.transpose(summed, (3, 1, 0, 2, 4)).reshape(
        source_count, offsets, half * capacity, lags_out
    )


def solution(mesh):
    placed = (P("blk", None, "band"), P("blk", None, "band"), P("blk", None))
    return jax.shard_map(
        per_device,
        mesh=mesh,
        in_specs=placed,
        out_specs=P("blk", None, "band", None),
        check_vma=False,
    )
```

time: 151 us -> 131 us (0.87)
  blocking collectives: 66.2 us -> 2.56 us
  starting transfers between devices: 0.01 us -> 57.6 us
  between operations: 13.6 us -> 0.8 us
  local copies, waits for them, and re-layouts: 35.1 us -> 29 us
  waiting for transfers between devices: 7.22 us -> 10.1 us
  other arithmetic: 24.5 us -> 26.1 us
    ppermute x0 -> x31, starting transfers between devices: none -> 57.6 us  [the longest x30 57.5 us: shifted(): return lax.ppermute(block, 'blk', route)]
    all_gather x1 -> x0, blocking collectives: 45.7 us -> none  [per_device(): all_sources = lax.all_gather(sources, 'blk', axis=0, tiled=True)]
    all_to_all x1 -> x0, blocking collectives: 18.1 us -> none  [per_device(): lax.all_to_all(partial, 'blk', split_axis=0, concat_axis=0, tiled=True)]
    ppermute x0 -> x31, waiting for transfers between devices: none -> 10.1 us  [the longest x30 8.63 us: shifted(): return lax.ppermute(block, 'blk', route)]
    reduce_scatter x1 -> x0, waiting for transfers between devices: 7.2 us -> none  [per_device(): lax.psum_scatter(arrived.astype(jnp.float32), 'band', scatter_dimension=0...]
    slice x6 -> x12, local copies, waits for them, and re-layouts: 6.99 us -> 0.23 us  [the longest x10 0.17 us: per_device(): owned = jnp.roll(placed, -offset, axis=0).astype(jnp.float32)]
    mul x2 -> x5, local copies, waits for them, and re-layouts: 3.67 us -> 8.87 us  [per_device(): even = jnp.sum(real_t * real_s + imag_t * imag_s, axis=3)]
    reshape x3 -> x0, local copies, waits for them, and re-layouts: 3.64 us -> none  [the longest x1 3.35 us: per_device(): white_sources = (all_source_float * lax.rsqrt(source_power / (2 * BINS) +...]
  transfers between devices with their start and end apart: 1 -> 31, of which waited for: 1 -> 5; matrix products, arithmetic and copies ran while one was open for 0% -> 17% of each run, Pallas kernels for 0% -> 0%
where the time goes in v2:
time: 131 us; the launch traced here: 130 us
  starting transfers between devices  57.6 us (44%)
  local copies, waits for them, and re-layouts  29 us (22%)
  other arithmetic  26.1 us (20%)
  waiting for transfers between devices  10.1 us (8%)
  matrix products  4.13 us (3%)
  blocking collectives  2.56 us (2%)
    ppermute x30, starting transfers between devices, shifted(): return lax.ppermute(block, 'blk', route)  57.5 us
    reduce_sum x1, other arithmetic, per_device(): even = jnp.sum(real_t * real_s + imag_t * imag_s, axis=3)  9.43 us
    mul x5, local copies, waits for them, and re-layouts, per_device(): even = jnp.sum(real_t * real_s + imag_t * imag_s, axis=3)  8.87 us
    ppermute x30, waiting for transfers between devices, shifted(): return lax.ppermute(block, 'blk', route)  8.63 us
    convert_element_type x1, local copies, waits for them, and re-layouts, per_device(): cross = jnp.stack(cross, axis=1).astype(jnp.bfloat16)  7.32 us
    another operation x1, local copies, waits for them, and re-layouts, per_device(): cross = jnp.stack(cross, axis=1).astype(jnp.bfloat16)  6.34 us
    another operation x1, other arithmetic  5.24 us
    unnamed x57, local copies, waits for them, and re-layouts  4.49 us
  transfers between devices with their start and end apart: 31, of which 5 were waited for; matrix products, arithmetic and copies ran while one was open for 17% of the time, Pallas kernels for 0%

profile of v2, /device:TPU:0, one launch (start us, length us, event | category | flops | bytes accessed | tf_op | source)
XLA Modules:
  0.0 130.4 jit_solution(12075547671070883140)
XLA Ops:
  0.0 2.8 %fusion = f32[64]{0:T(128)S(1)} fusion(bf16[64,2,4096]{2,1,0:T(2,128)(2,1)} %param.3), kind=kLoop, calls=%fused_computation.12 | loop fusion | flops 1572800 | bytes 1048832 | tf_op jit(solution)/shard_map/reduce_sum | solution.py:39
  3.7 2.6 %all-reduce = (f32[2]{0:T(128)S(1)}, f32[64]{0:T(128)S(1)}) all-reduce(f32[2]{0:T(128)S(1)} %fusion.12, f32[64]{0:T(128)S(1)} %fusion), channel_id=1, replica_groups=mesh['blk'=16,'band'=2] {'band'}, use_global_device_ids=true, to_apply=%region_5.6 | all-reduce | flops 66 | bytes 528 | tf_op jit(solution)/shard_map/psum | solution.py:37
  7.1 2.9 %collective-permute-start = (bf16[2,2,4096]{2,1,0:T(2,128)(2,1)S(1)}, bf16[2,2,4096]{2,1,0:T(2,128)(2,1)S(1)}, u32[]{:S(2)}, u32[]{:S(2)}) collective-permute-start(bf16[2,2,4096]{2,1,0:T(2,128)(2,1)S(1)} %fusion.13), channel_id=1, source_target_pairs={{0,2},{2,4},{4,6},{6,8},{8,10},{10,12},{12,14},{14,16},{16,18},{18... | collective-permute-start | bytes 98312 | tf_op jit(solution)/shard_map/ppermute | solution.py:20
  11.5 2.4 %collective-permute-start.2 = (bf16[2,2,4096]{2,1,0:T(2,128)(2,1)S(1)}, bf16[2,2,4096]{2,1,0:T(2,128)(2,1)S(1)}, u32[]{:S(2)}, u32[]{:S(2)}) collective-permute-start(bf16[2,2,4096]{2,1,0:T(2,128)(2,1)S(1)} %fusion.13), channel_id=1, source_target_pairs={{0,6},{2,8},{4,10},{6,12},{8,14},{10,16},{12,18},{14,20},{16,22},{... | collective-permute-start | bytes 98312 | tf_op jit(solution)/shard_map/ppermute | solution.py:20
  14.0 1.6 %collective-permute-start.3 = (bf16[2,2,4096]{2,1,0:T(2,128)(2,1)S(1)}, bf16[2,2,4096]{2,1,0:T(2,128)(2,1)S(1)}, u32[]{:S(2)}, u32[]{:S(2)}) collective-permute-start(bf16[2,2,4096]{2,1,0:T(2,128)(2,1)S(1)} %fusion.13), channel_id=1, source_target_pairs={{0,8},{2,10},{4,12},{6,14},{8,16},{10,18},{12,20},{14,22},{16,24},... | collective-permute-start | bytes 98312 | tf_op jit(solution)/shard_map/ppermute | solution.py:20
  15.5 1.6 %collective-permute-start.4 = (bf16[2,2,4096]{2,1,0:T(2,128)(2,1)S(1)}, bf16[2,2,4096]{2,1,0:T(2,128)(2,1)S(1)}, u32[]{:S(2)}, u32[]{:S(2)}) collective-permute-start(bf16[2,2,4096]{2,1,0:T(2,128)(2,1)S(1)} %fusion.13), channel_id=1, source_target_pairs={{0,10},{2,12},{4,14},{6,16},{8,18},{10,20},{12,22},{14,24},{16,26}... | collective-permute-start | bytes 98312 | tf_op jit(solution)/shard_map/ppermute | solution.py:20
  18.9 2.6 %fusion.1 = bf16[64,2,4096]{2,1,0:T(2,128)(2,1)S(1)} fusion(bf16[64,2,4096]{2,1,0:T(2,128)(2,1)} %param.3, f32[64]{0:T(128)S(1)} %add_rsqrt_fusion.1), kind=kLoop, calls=%fused_computation.13 | loop fusion | flops 1572864 | bytes 2097408 | tf_op jit(solution)/shard_map/convert_element_type | solution.py:52
  24.4 1.8 %slice_bitcast_fusion.1 = (f32[16,8,4,1024]{3,1,2,0:T(8,128)S(1)}, f32[16,8,4,1024]{3,1,2,0:T(8,128)}) fusion(f32[16,8,2,4,1024]{4,1,3,2,0:T(8,128)S(1)} %maximum_convert_fusion.2), kind=kLoop, calls=%fused_computation.15 | loop fusion | bytes 8388608 | tf_op jit(solution)/shard_map/mul | solution.py:87
  26.5 2.3 %slice_bitcast_fusion.3 = (f32[16,8,4,1024]{3,1,2,0:T(8,128)}, f32[16,8,4,1024]{3,1,2,0:T(8,128)}) fusion(f32[16,8,2,4,1024]{4,1,3,2,0:T(8,128)S(1)} %maximum_convert_fusion.1), kind=kLoop, calls=%fused_computation.17 | loop fusion | bytes 8388608 | tf_op jit(solution)/shard_map/mul | solution.py:87
  29.1 2.3 %slice_bitcast_fusion.5 = (f32[16,8,4,1024]{3,1,2,0:T(8,128)}, f32[16,8,4,1024]{3,1,2,0:T(8,128)}) fusion(f32[16,8,2,4,1024]{4,1,3,2,0:T(8,128)S(1)} %maximum_convert_fusion), kind=kLoop, calls=%fused_computation.19 | loop fusion | bytes 8388608 | tf_op jit(solution)/shard_map/mul | solution.py:87
  31.9 2.4 %slice_bitcast_fusion.7 = (f32[16,8,4,1024]{3,1,2,0:T(8,128)}, f32[16,8,4,1024]{3,1,2,0:T(8,128)}) fusion(f32[16,8,2,4,1024]{4,1,3,2,0:T(8,128)S(1)} %convert.49), kind=kLoop, calls=%fused_computation.21 | loop fusion | bytes 8388608 | tf_op jit(solution)/shard_map/mul | solution.py:87
  34.3 5.2 %cosine_convert_fusion = (bf16[1024,256]{1,0:T(8,128)(2,1)S(1)}, bf16[1024,256]{1,0:T(8,128)(2,1)}) fusion(s32[256]{0:T(256)S(1)} %add_multiply_fusion), kind=kLoop, calls=%fused_computation.41 | loop fusion | flops 4194304 | bytes 1049600 | tf_op jit(solution)/shard_map/convert.1
  40.9 4.4 %collective-permute-start.6 = (bf16[2,2,4096]{2,1,0:T(2,128)(2,1)S(1)}, bf16[2,2,4096]{2,1,0:T(2,128)(2,1)S(1)}, u32[]{:S(2)}, u32[]{:S(2)}) collective-permute-start(bf16[2,2,4096]{2,1,0:T(2,128)(2,1)S(1)} %fusion.13), channel_id=1, source_target_pairs={{0,14},{2,16},{4,18},{6,20},{8,22},{10,24},{12,26},{14,28},{16,30}... | collective-permute-start | bytes 98312 | tf_op jit(solution)/shard_map/ppermute | solution.py:20
  45.8 1.8 %collective-permute-start.8 = (bf16[2,2,4096]{2,1,0:T(2,128)(2,1)S(1)}, bf16[2,2,4096]{2,1,0:T(2,128)(2,1)S(1)}, u32[]{:S(2)}, u32[]{:S(2)}) collective-permute-start(bf16[2,2,4096]{2,1,0:T(2,128)(2,1)S(1)} %fusion.13), channel_id=1, source_target_pairs={{0,18},{2,20},{4,22},{6,24},{8,26},{10,28},{12,30},{14,0},{16,2},{... | collective-permute-start | bytes 98312 | tf_op jit(solution)/shard_map/ppermute | solution.py:20
  49.1 4.1 %collective-permute-start.10 = (bf16[2,2,4096]{2,1,0:T(2,128)(2,1)S(1)}, bf16[2,2,4096]{2,1,0:T(2,128)(2,1)S(1)}, u32[]{:S(2)}, u32[]{:S(2)}) collective-permute-start(bf16[2,2,4096]{2,1,0:T(2,128)(2,1)S(1)} %fusion.13), channel_id=1, source_target_pairs={{0,22},{2,24},{4,26},{6,28},{8,30},{10,0},{12,2},{14,4},{16,6},{18... | collective-permute-start | bytes 98312 | tf_op jit(solution)/shard_map/ppermute | solution.py:20
  53.2 1.9 %collective-permute-start.11 = (bf16[2,2,4096]{2,1,0:T(2,128)(2,1)S(1)}, bf16[2,2,4096]{2,1,0:T(2,128)(2,1)S(1)}, u32[]{:S(2)}, u32[]{:S(2)}) collective-permute-start(bf16[2,2,4096]{2,1,0:T(2,128)(2,1)S(1)} %fusion.13), channel_id=1, source_target_pairs={{0,24},{2,26},{4,28},{6,30},{8,0},{10,2},{12,4},{14,6},{16,8},{18,... | collective-permute-start | bytes 98312 | tf_op jit(solution)/shard_map/ppermute | solution.py:20
  56.8 3.9 %collective-permute-start.14 = (bf16[2,2,4096]{2,1,0:T(2,128)(2,1)S(1)}, bf16[2,2,4096]{2,1,0:T(2,128)(2,1)S(1)}, u32[]{:S(2)}, u32[]{:S(2)}) collective-permute-start(bf16[2,2,4096]{2,1,0:T(2,128)(2,1)S(1)} %fusion.13), channel_id=1, source_target_pairs={{0,30},{2,0},{4,2},{6,4},{8,6},{10,8},{12,10},{14,12},{16,14},{18,... | collective-permute-start | bytes 98312 | tf_op jit(solution)/shard_map/ppermute | solution.py:20
  63.9 9.4 %add_reduce_fusion.3 = (bf16[16,8,2,1024]{3,1,2,0:T(8,128)(2,1)S(1)}, bf16[16,8,2,1024]{3,1,2,0:T(8,128)(2,1)S(1)}, bf16[16,8,2,1024]{3,1,2,0:T(8,128)(2,1)S(1)}...) fusion(f32[16,2,4,1024]{3,2,1,0:T(4,128)S(1)} %get-tuple-elemen, ...), kind=kLoop, calls=%fused_computation.9 | loop fusion | flops 31457280 | bytes 22020096 | tf_op jit(solution)/shard_map/reduce_sum | solution.py:87
  74.3 6.3 %copy.22 = bf16[16,4,8,2,2048]{4,3,2,1,0:T(2,128)(2,1)} copy(bf16[16,4,8,2,2048]{4,2,3,0,1:T(8,128)(2,1)S(1)} %pad_maximum_fusion) | data formatting | bytes 8388608 | tf_op jit(solution)/shard_map/stack | solution.py:90
  80.7 7.3 %convert_element_type.70 = bf16[1024,2048]{1,0:T(8,128)(2,1)} reshape(bf16[16,4,8,2,2048]{4,3,2,1,0:T(2,128)(2,1)} %copy.22) | data formatting | bytes 8388608 | tf_op jit(solution)/shard_map/convert_element_type | solution.py:90
  88.0 3.4 %fusion.2 = bf16[1024,256]{1,0:T(8,128)(2,1)S(1)} fusion(bf16[1024,2048]{1,0:T(8,128)(2,1)} %convert_element_type.70, bf16[1024,256]{1,0:T(8,128)(2,1)S(1)} %copy-done.3, bf16[1024,256]{1,0:T(8,128)(2,1)S(1)} %get-tuple-element.47), kind=kOutput, calls=%fused_computation.29 | convolution fusion | flops 1076363264 | bytes 5767168 | tf_op jit(solution)/shard_map/dot_general | solution.py:92
  91.5 6.0 %collective-permute-start.15 = (bf16[4,8,2,256]{3,2,1,0:T(2,128)(2,1)S(1)}, bf16[4,8,2,256]{3,2,1,0:T(2,128)(2,1)S(1)}, u32[]{:S(2)}, u32[]{:S(2)}) collective-permute-start(bf16[4,8,2,256]{3,2,1,0:T(2,128)(2,1)S(1)} %squeeze.49), channel_id=1, source_target_pairs={{0,30},{2,0},{4,2},{6,4},{8,6},{10,8},{12,10},{14,12},{16,14},{18,... | collective-permute-start | bytes 98312 | tf_op jit(solution)/shard_map/ppermute | solution.py:20
  98.4 2.7 %collective-permute-start.19 = (bf16[4,8,2,256]{3,2,1,0:T(2,128)(2,1)S(1)}, bf16[4,8,2,256]{3,2,1,0:T(2,128)(2,1)S(1)}, u32[]{:S(2)}, u32[]{:S(2)}) collective-permute-start(bf16[4,8,2,256]{3,2,1,0:T(2,128)(2,1)S(1)} %squeeze.53), channel_id=1, source_target_pairs={{0,22},{2,24},{4,26},{6,28},{8,30},{10,0},{12,2},{14,4},{16,6},{18... | collective-permute-start | bytes 98312 | tf_op jit(solution)/shard_map/ppermute | solution.py:20
  101.3 3.6 %collective-permute-start.20 = (bf16[4,8,2,256]{3,2,1,0:T(2,128)(2,1)S(1)}, bf16[4,8,2,256]{3,2,1,0:T(2,128)(2,1)S(1)}, u32[]{:S(2)}, u32[]{:S(2)}) collective-permute-start(bf16[4,8,2,256]{3,2,1,0:T(2,128)(2,1)S(1)} %squeeze.54), channel_id=1, source_target_pairs={{0,20},{2,22},{4,24},{6,26},{8,28},{10,30},{12,0},{14,2},{16,4},{1... | collective-permute-start | bytes 98312 | tf_op jit(solution)/shard_map/ppermute | solution.py:20
  105.1 2.1 %collective-permute-start.22 = (bf16[4,8,2,256]{3,2,1,0:T(2,128)(2,1)S(1)}, bf16[4,8,2,256]{3,2,1,0:T(2,128)(2,1)S(1)}, u32[]{:S(2)}, u32[]{:S(2)}) collective-permute-start(bf16[4,8,2,256]{3,2,1,0:T(2,128)(2,1)S(1)} %squeeze.56), channel_id=1, source_target_pairs={{0,16},{2,18},{4,20},{6,22},{8,24},{10,26},{12,28},{14,30},{16,0},... | collective-permute-start | bytes 98312 | tf_op jit(solution)/shard_map/ppermute | solution.py:20
  107.2 3.1 %collective-permute-start.23 = (bf16[4,8,2,256]{3,2,1,0:T(2,128)(2,1)S(1)}, bf16[4,8,2,256]{3,2,1,0:T(2,128)(2,1)S(1)}, u32[]{:S(2)}, u32[]{:S(2)}) collective-permute-start(bf16[4,8,2,256]{3,2,1,0:T(2,128)(2,1)S(1)} %squeeze.57), channel_id=1, source_target_pairs={{0,14},{2,16},{4,18},{6,20},{8,22},{10,24},{12,26},{14,28},{16,30}... | collective-permute-start | bytes 98312 | tf_op jit(solution)/shard_map/ppermute | solution.py:20
  110.3 1.8 %collective-permute-start.24 = (bf16[4,8,2,256]{3,2,1,0:T(2,128)(2,1)S(1)}, bf16[4,8,2,256]{3,2,1,0:T(2,128)(2,1)S(1)}, u32[]{:S(2)}, u32[]{:S(2)}) collective-permute-start(bf16[4,8,2,256]{3,2,1,0:T(2,128)(2,1)S(1)} %squeeze.58), channel_id=1, source_target_pairs={{0,12},{2,14},{4,16},{6,18},{8,20},{10,22},{12,24},{14,26},{16,28}... | collective-permute-start | bytes 98312 | tf_op jit(solution)/shard_map/ppermute | solution.py:20
  112.8 1.9 %collective-permute-start.26 = (bf16[4,8,2,256]{3,2,1,0:T(2,128)(2,1)S(1)}, bf16[4,8,2,256]{3,2,1,0:T(2,128)(2,1)S(1)}, u32[]{:S(2)}, u32[]{:S(2)}) collective-permute-start(bf16[4,8,2,256]{3,2,1,0:T(2,128)(2,1)S(1)} %squeeze.60), channel_id=1, source_target_pairs={{0,8},{2,10},{4,12},{6,14},{8,16},{10,18},{12,20},{14,22},{16,24},... | collective-permute-start | bytes 98312 | tf_op jit(solution)/shard_map/ppermute | solution.py:20
  114.7 3.3 %collective-permute-start.27 = (bf16[4,8,2,256]{3,2,1,0:T(2,128)(2,1)S(1)}, bf16[4,8,2,256]{3,2,1,0:T(2,128)(2,1)S(1)}, u32[]{:S(2)}, u32[]{:S(2)}) collective-permute-start(bf16[4,8,2,256]{3,2,1,0:T(2,128)(2,1)S(1)} %squeeze.61), channel_id=1, source_target_pairs={{0,6},{2,8},{4,10},{6,12},{8,14},{10,16},{12,18},{14,20},{16,22},{... | collective-permute-start | bytes 98312 | tf_op jit(solution)/shard_map/ppermute | solution.py:20
  119.4 3.6 %collective-permute-done.27 = bf16[4,8,2,256]{3,2,1,0:T(2,128)(2,1)S(1)} collective-permute-done((bf16[4,8,2,256]{3,2,1,0:T(2,128)(2,1)S(1)}, bf16[4,8,2,256]{3,2,1,0:T(2,128)(2,1)S(1)}, u32[]{:S(2)}, u32[]{:S(2)}) %collective-permute-start.27) | collective-permute-done | bytes 32800 | tf_op jit(solution)/shard_map/ppermute | solution.py:20
  123.1 1.6 %collective-permute-done.28 = bf16[4,8,2,256]{3,2,1,0:T(2,128)(2,1)S(1)} collective-permute-done((bf16[4,8,2,256]{3,2,1,0:T(2,128)(2,1)S(1)}, bf16[4,8,2,256]{3,2,1,0:T(2,128)(2,1)S(1)}, u32[]{:S(2)}, u32[]{:S(2)}) %collective-permute-start.28) | collective-permute-done | bytes 32800 | tf_op jit(solution)/shard_map/ppermute | solution.py:20
  124.7 2.1 %collective-permute-done.29 = bf16[4,8,2,256]{3,2,1,0:T(2,128)(2,1)S(1)} collective-permute-done((bf16[4,8,2,256]{3,2,1,0:T(2,128)(2,1)S(1)}, bf16[4,8,2,256]{3,2,1,0:T(2,128)(2,1)S(1)}, u32[]{:S(2)}, u32[]{:S(2)}) %collective-permute-start.29) | collective-permute-done | bytes 32800 | tf_op jit(solution)/shard_map/ppermute | solution.py:20
  (166 shorter events, 24.9 us)
Async XLA Ops:
  7.1 32.5 %collective-permute-start = (bf16[2,2,4096]{2,1,0:T(2,128)(2,1)S(1)}, bf16[2,2,4096]{2,1,0:T(2,128)(2,1)S(1)}, u32[]{:S(2)}, u32[]{:S(2)}) collective-permute-start(bf16[2,2,4096]{2,1,0:T(2,128)(2,1)S(1)} %fusion.13), channel_id=1, source_target_pairs={{0,2},{2,4},{4,6},{6,8},{8,10},{10,12},{12,14},{14,16},{16,18},{18... | collective-permute-start | bytes 98312 | tf_op jit(solution)/shard_map/ppermute | solution.py:20
  10.0 30.9 %collective-permute-start.1 = (bf16[2,2,4096]{2,1,0:T(2,128)(2,1)S(1)}, bf16[2,2,4096]{2,1,0:T(2,128)(2,1)S(1)}, u32[]{:S(2)}, u32[]{:S(2)}) collective-permute-start(bf16[2,2,4096]{2,1,0:T(2,128)(2,1)S(1)} %fusion.13), channel_id=1, source_target_pairs={{0,4},{2,6},{4,8},{6,10},{8,12},{10,14},{12,16},{14,18},{16,20},{1... | collective-permute-start | bytes 98312 | tf_op jit(solution)/shard_map/ppermute | solution.py:20
  11.5 33.8 %collective-permute-start.2 = (bf16[2,2,4096]{2,1,0:T(2,128)(2,1)S(1)}, bf16[2,2,4096]{2,1,0:T(2,128)(2,1)S(1)}, u32[]{:S(2)}, u32[]{:S(2)}) collective-permute-start(bf16[2,2,4096]{2,1,0:T(2,128)(2,1)S(1)} %fusion.13), channel_id=1, source_target_pairs={{0,6},{2,8},{4,10},{6,12},{8,14},{10,16},{12,18},{14,20},{16,22},{... | collective-permute-start | bytes 98312 | tf_op jit(solution)/shard_map/ppermute | solution.py:20
  14.0 31.8 %collective-permute-start.3 = (bf16[2,2,4096]{2,1,0:T(2,128)(2,1)S(1)}, bf16[2,2,4096]{2,1,0:T(2,128)(2,1)S(1)}, u32[]{:S(2)}, u32[]{:S(2)}) collective-permute-start(bf16[2,2,4096]{2,1,0:T(2,128)(2,1)S(1)} %fusion.13), channel_id=1, source_target_pairs={{0,8},{2,10},{4,12},{6,14},{8,16},{10,18},{12,20},{14,22},{16,24},... | collective-permute-start | bytes 98312 | tf_op jit(solution)/shard_map/ppermute | solution.py:20
  15.5 32.1 %collective-permute-start.4 = (bf16[2,2,4096]{2,1,0:T(2,128)(2,1)S(1)}, bf16[2,2,4096]{2,1,0:T(2,128)(2,1)S(1)}, u32[]{:S(2)}, u32[]{:S(2)}) collective-permute-start(bf16[2,2,4096]{2,1,0:T(2,128)(2,1)S(1)} %fusion.13), channel_id=1, source_target_pairs={{0,10},{2,12},{4,14},{6,16},{8,18},{10,20},{12,22},{14,24},{16,26}... | collective-permute-start | bytes 98312 | tf_op jit(solution)/shard_map/ppermute | solution.py:20
  39.6 9.5 %collective-permute-start.5 = (bf16[2,2,4096]{2,1,0:T(2,128)(2,1)S(1)}, bf16[2,2,4096]{2,1,0:T(2,128)(2,1)S(1)}, u32[]{:S(2)}, u32[]{:S(2)}) collective-permute-start(bf16[2,2,4096]{2,1,0:T(2,128)(2,1)S(1)} %fusion.13), channel_id=1, source_target_pairs={{0,12},{2,14},{4,16},{6,18},{8,20},{10,22},{12,24},{14,26},{16,28}... | collective-permute-start | bytes 98312 | tf_op jit(solution)/shard_map/ppermute | solution.py:20
  40.9 12.3 %collective-permute-start.6 = (bf16[2,2,4096]{2,1,0:T(2,128)(2,1)S(1)}, bf16[2,2,4096]{2,1,0:T(2,128)(2,1)S(1)}, u32[]{:S(2)}, u32[]{:S(2)}) collective-permute-start(bf16[2,2,4096]{2,1,0:T(2,128)(2,1)S(1)} %fusion.13), channel_id=1, source_target_pairs={{0,14},{2,16},{4,18},{6,20},{8,22},{10,24},{12,26},{14,28},{16,30}... | collective-permute-start | bytes 98312 | tf_op jit(solution)/shard_map/ppermute | solution.py:20
  45.4 9.8 %collective-permute-start.7 = (bf16[2,2,4096]{2,1,0:T(2,128)(2,1)S(1)}, bf16[2,2,4096]{2,1,0:T(2,128)(2,1)S(1)}, u32[]{:S(2)}, u32[]{:S(2)}) collective-permute-start(bf16[2,2,4096]{2,1,0:T(2,128)(2,1)S(1)} %fusion.13), channel_id=1, source_target_pairs={{0,16},{2,18},{4,20},{6,22},{8,24},{10,26},{12,28},{14,30},{16,0},... | collective-permute-start | bytes 98312 | tf_op jit(solution)/shard_map/ppermute | solution.py:20
  45.8 9.4 %collective-permute-start.8 = (bf16[2,2,4096]{2,1,0:T(2,128)(2,1)S(1)}, bf16[2,2,4096]{2,1,0:T(2,128)(2,1)S(1)}, u32[]{:S(2)}, u32[]{:S(2)}) collective-permute-start(bf16[2,2,4096]{2,1,0:T(2,128)(2,1)S(1)} %fusion.13), channel_id=1, source_target_pairs={{0,18},{2,20},{4,22},{6,24},{8,26},{10,28},{12,30},{14,0},{16,2},{... | collective-permute-start | bytes 98312 | tf_op jit(solution)/shard_map/ppermute | solution.py:20
  47.7 9.1 %collective-permute-start.9 = (bf16[2,2,4096]{2,1,0:T(2,128)(2,1)S(1)}, bf16[2,2,4096]{2,1,0:T(2,128)(2,1)S(1)}, u32[]{:S(2)}, u32[]{:S(2)}) collective-permute-start(bf16[2,2,4096]{2,1,0:T(2,128)(2,1)S(1)} %fusion.13), channel_id=1, source_target_pairs={{0,20},{2,22},{4,24},{6,26},{8,28},{10,30},{12,0},{14,2},{16,4},{1... | collective-permute-start | bytes 98312 | tf_op jit(solution)/shard_map/ppermute | solution.py:20
  49.1 11.7 %collective-permute-start.10 = (bf16[2,2,4096]{2,1,0:T(2,128)(2,1)S(1)}, bf16[2,2,4096]{2,1,0:T(2,128)(2,1)S(1)}, u32[]{:S(2)}, u32[]{:S(2)}) collective-permute-start(bf16[2,2,4096]{2,1,0:T(2,128)(2,1)S(1)} %fusion.13), channel_id=1, source_target_pairs={{0,22},{2,24},{4,26},{6,28},{8,30},{10,0},{12,2},{14,4},{16,6},{18... | collective-permute-start | bytes 98312 | tf_op jit(solution)/shard_map/ppermute | solution.py:20
  53.2 7.6 %collective-permute-start.11 = (bf16[2,2,4096]{2,1,0:T(2,128)(2,1)S(1)}, bf16[2,2,4096]{2,1,0:T(2,128)(2,1)S(1)}, u32[]{:S(2)}, u32[]{:S(2)}) collective-permute-start(bf16[2,2,4096]{2,1,0:T(2,128)(2,1)S(1)} %fusion.13), channel_id=1, source_target_pairs={{0,24},{2,26},{4,28},{6,30},{8,0},{10,2},{12,4},{14,6},{16,8},{18,... | collective-permute-start | bytes 98312 | tf_op jit(solution)/shard_map/ppermute | solution.py:20
  55.1 5.8 %collective-permute-start.12 = (bf16[2,2,4096]{2,1,0:T(2,128)(2,1)S(1)}, bf16[2,2,4096]{2,1,0:T(2,128)(2,1)S(1)}, u32[]{:S(2)}, u32[]{:S(2)}) collective-permute-start(bf16[2,2,4096]{2,1,0:T(2,128)(2,1)S(1)} %fusion.13), channel_id=1, source_target_pairs={{0,26},{2,28},{4,30},{6,0},{8,2},{10,4},{12,6},{14,8},{16,10},{18,... | collective-permute-start | bytes 98312 | tf_op jit(solution)/shard_map/ppermute | solution.py:20
  55.3 5.7 %collective-permute-start.13 = (bf16[2,2,4096]{2,1,0:T(2,128)(2,1)S(1)}, bf16[2,2,4096]{2,1,0:T(2,128)(2,1)S(1)}, u32[]{:S(2)}, u32[]{:S(2)}) collective-permute-start(bf16[2,2,4096]{2,1,0:T(2,128)(2,1)S(1)} %fusion.13), channel_id=1, source_target_pairs={{0,28},{2,30},{4,0},{6,2},{8,4},{10,6},{12,8},{14,10},{16,12},{18,... | collective-permute-start | bytes 98312 | tf_op jit(solution)/shard_map/ppermute | solution.py:20
  56.8 5.5 %collective-permute-start.14 = (bf16[2,2,4096]{2,1,0:T(2,128)(2,1)S(1)}, bf16[2,2,4096]{2,1,0:T(2,128)(2,1)S(1)}, u32[]{:S(2)}, u32[]{:S(2)}) collective-permute-start(bf16[2,2,4096]{2,1,0:T(2,128)(2,1)S(1)} %fusion.13), channel_id=1, source_target_pairs={{0,30},{2,0},{4,2},{6,4},{8,6},{10,8},{12,10},{14,12},{16,14},{18,... | collective-permute-start | bytes 98312 | tf_op jit(solution)/shard_map/ppermute | solution.py:20
  80.7 7.3 %copy-start.3 = (bf16[1024,256]{1,0:T(8,128)(2,1)S(1)}, bf16[1024,256]{1,0:T(8,128)(2,1)}, u32[]{:S(2)}) copy-start(bf16[1024,256]{1,0:T(8,128)(2,1)} %get-tuple-element.48) | copy-start | bytes 1572868
  91.5 9.7 %collective-permute-start.15 = (bf16[4,8,2,256]{3,2,1,0:T(2,128)(2,1)S(1)}, bf16[4,8,2,256]{3,2,1,0:T(2,128)(2,1)S(1)}, u32[]{:S(2)}, u32[]{:S(2)}) collective-permute-start(bf16[4,8,2,256]{3,2,1,0:T(2,128)(2,1)S(1)} %squeeze.49), channel_id=1, source_target_pairs={{0,30},{2,0},{4,2},{6,4},{8,6},{10,8},{12,10},{14,12},{16,14},{18,... | collective-permute-start | bytes 98312 | tf_op jit(solution)/shard_map/ppermute | solution.py:20
  97.6 7.4 %collective-permute-start.16 = (bf16[4,8,2,256]{3,2,1,0:T(2,128)(2,1)S(1)}, bf16[4,8,2,256]{3,2,1,0:T(2,128)(2,1)S(1)}, u32[]{:S(2)}, u32[]{:S(2)}) collective-permute-start(bf16[4,8,2,256]{3,2,1,0:T(2,128)(2,1)S(1)} %squeeze.50), channel_id=1, source_target_pairs={{0,28},{2,30},{4,0},{6,2},{8,4},{10,6},{12,8},{14,10},{16,12},{18,... | collective-permute-start | bytes 98312 | tf_op jit(solution)/shard_map/ppermute | solution.py:20
  97.7 7.4 %collective-permute-start.17 = (bf16[4,8,2,256]{3,2,1,0:T(2,128)(2,1)S(1)}, bf16[4,8,2,256]{3,2,1,0:T(2,128)(2,1)S(1)}, u32[]{:S(2)}, u32[]{:S(2)}) collective-permute-start(bf16[4,8,2,256]{3,2,1,0:T(2,128)(2,1)S(1)} %squeeze.51), channel_id=1, source_target_pairs={{0,26},{2,28},{4,30},{6,0},{8,2},{10,4},{12,6},{14,8},{16,10},{18,... | collective-permute-start | bytes 98312 | tf_op jit(solution)/shard_map/ppermute | solution.py:20
  97.7 9.4 %collective-permute-start.18 = (bf16[4,8,2,256]{3,2,1,0:T(2,128)(2,1)S(1)}, bf16[4,8,2,256]{3,2,1,0:T(2,128)(2,1)S(1)}, u32[]{:S(2)}, u32[]{:S(2)}) collective-permute-start(bf16[4,8,2,256]{3,2,1,0:T(2,128)(2,1)S(1)} %squeeze.52), channel_id=1, source_target_pairs={{0,24},{2,26},{4,28},{6,30},{8,0},{10,2},{12,4},{14,6},{16,8},{18,... | collective-permute-start | bytes 98312 | tf_op jit(solution)/shard_map/ppermute | solution.py:20
  98.4 11.9 %collective-permute-start.19 = (bf16[4,8,2,256]{3,2,1,0:T(2,128)(2,1)S(1)}, bf16[4,8,2,256]{3,2,1,0:T(2,128)(2,1)S(1)}, u32[]{:S(2)}, u32[]{:S(2)}) collective-permute-start(bf16[4,8,2,256]{3,2,1,0:T(2,128)(2,1)S(1)} %squeeze.53), channel_id=1, source_target_pairs={{0,22},{2,24},{4,26},{6,28},{8,30},{10,0},{12,2},{14,4},{16,6},{18... | collective-permute-start | bytes 98312 | tf_op jit(solution)/shard_map/ppermute | solution.py:20
  101.3 10.8 %collective-permute-start.20 = (bf16[4,8,2,256]{3,2,1,0:T(2,128)(2,1)S(1)}, bf16[4,8,2,256]{3,2,1,0:T(2,128)(2,1)S(1)}, u32[]{:S(2)}, u32[]{:S(2)}) collective-permute-start(bf16[4,8,2,256]{3,2,1,0:T(2,128)(2,1)S(1)} %squeeze.54), channel_id=1, source_target_pairs={{0,20},{2,22},{4,24},{6,26},{8,28},{10,30},{12,0},{14,2},{16,4},{1... | collective-permute-start | bytes 98312 | tf_op jit(solution)/shard_map/ppermute | solution.py:20
  105.0 7.8 %collective-permute-start.21 = (bf16[4,8,2,256]{3,2,1,0:T(2,128)(2,1)S(1)}, bf16[4,8,2,256]{3,2,1,0:T(2,128)(2,1)S(1)}, u32[]{:S(2)}, u32[]{:S(2)}) collective-permute-start(bf16[4,8,2,256]{3,2,1,0:T(2,128)(2,1)S(1)} %squeeze.55), channel_id=1, source_target_pairs={{0,18},{2,20},{4,22},{6,24},{8,26},{10,28},{12,30},{14,0},{16,2},{... | collective-permute-start | bytes 98312 | tf_op jit(solution)/shard_map/ppermute | solution.py:20
  105.1 9.6 %collective-permute-start.22 = (bf16[4,8,2,256]{3,2,1,0:T(2,128)(2,1)S(1)}, bf16[4,8,2,256]{3,2,1,0:T(2,128)(2,1)S(1)}, u32[]{:S(2)}, u32[]{:S(2)}) collective-permute-start(bf16[4,8,2,256]{3,2,1,0:T(2,128)(2,1)S(1)} %squeeze.56), channel_id=1, source_target_pairs={{0,16},{2,18},{4,20},{6,22},{8,24},{10,26},{12,28},{14,30},{16,0},... | collective-permute-start | bytes 98312 | tf_op jit(solution)/shard_map/ppermute | solution.py:20
  107.2 10.8 %collective-permute-start.23 = (bf16[4,8,2,256]{3,2,1,0:T(2,128)(2,1)S(1)}, bf16[4,8,2,256]{3,2,1,0:T(2,128)(2,1)S(1)}, u32[]{:S(2)}, u32[]{:S(2)}) collective-permute-start(bf16[4,8,2,256]{3,2,1,0:T(2,128)(2,1)S(1)} %squeeze.57), channel_id=1, source_target_pairs={{0,14},{2,16},{4,18},{6,20},{8,22},{10,24},{12,26},{14,28},{16,30}... | collective-permute-start | bytes 98312 | tf_op jit(solution)/shard_map/ppermute | solution.py:20
  110.3 8.9 %collective-permute-start.24 = (bf16[4,8,2,256]{3,2,1,0:T(2,128)(2,1)S(1)}, bf16[4,8,2,256]{3,2,1,0:T(2,128)(2,1)S(1)}, u32[]{:S(2)}, u32[]{:S(2)}) collective-permute-start(bf16[4,8,2,256]{3,2,1,0:T(2,128)(2,1)S(1)} %squeeze.58), channel_id=1, source_target_pairs={{0,12},{2,14},{4,16},{6,18},{8,20},{10,22},{12,24},{14,26},{16,28}... | collective-permute-start | bytes 98312 | tf_op jit(solution)/shard_map/ppermute | solution.py:20
  112.1 7.2 %collective-permute-start.25 = (bf16[4,8,2,256]{3,2,1,0:T(2,128)(2,1)S(1)}, bf16[4,8,2,256]{3,2,1,0:T(2,128)(2,1)S(1)}, u32[]{:S(2)}, u32[]{:S(2)}) collective-permute-start(bf16[4,8,2,256]{3,2,1,0:T(2,128)(2,1)S(1)} %squeeze.59), channel_id=1, source_target_pairs={{0,10},{2,12},{4,14},{6,16},{8,18},{10,20},{12,22},{14,24},{16,26}... | collective-permute-start | bytes 98312 | tf_op jit(solution)/shard_map/ppermute | solution.py:20
  112.8 6.6 %collective-permute-start.26 = (bf16[4,8,2,256]{3,2,1,0:T(2,128)(2,1)S(1)}, bf16[4,8,2,256]{3,2,1,0:T(2,128)(2,1)S(1)}, u32[]{:S(2)}, u32[]{:S(2)}) collective-permute-start(bf16[4,8,2,256]{3,2,1,0:T(2,128)(2,1)S(1)} %squeeze.60), channel_id=1, source_target_pairs={{0,8},{2,10},{4,12},{6,14},{8,16},{10,18},{12,20},{14,22},{16,24},... | collective-permute-start | bytes 98312 | tf_op jit(solution)/shard_map/ppermute | solution.py:20
  114.7 8.4 %collective-permute-start.27 = (bf16[4,8,2,256]{3,2,1,0:T(2,128)(2,1)S(1)}, bf16[4,8,2,256]{3,2,1,0:T(2,128)(2,1)S(1)}, u32[]{:S(2)}, u32[]{:S(2)}) collective-permute-start(bf16[4,8,2,256]{3,2,1,0:T(2,128)(2,1)S(1)} %squeeze.61), channel_id=1, source_target_pairs={{0,6},{2,8},{4,10},{6,12},{8,14},{10,16},{12,18},{14,20},{16,22},{... | collective-permute-start | bytes 98312 | tf_op jit(solution)/shard_map/ppermute | solution.py:20
  118.0 6.7 %collective-permute-start.28 = (bf16[4,8,2,256]{3,2,1,0:T(2,128)(2,1)S(1)}, bf16[4,8,2,256]{3,2,1,0:T(2,128)(2,1)S(1)}, u32[]{:S(2)}, u32[]{:S(2)}) collective-permute-start(bf16[4,8,2,256]{3,2,1,0:T(2,128)(2,1)S(1)} %squeeze.62), channel_id=1, source_target_pairs={{0,4},{2,6},{4,8},{6,10},{8,12},{10,14},{12,16},{14,18},{16,20},{1... | collective-permute-start | bytes 98312 | tf_op jit(solution)/shard_map/ppermute | solution.py:20
  119.2 7.6 %collective-permute-start.29 = (bf16[4,8,2,256]{3,2,1,0:T(2,128)(2,1)S(1)}, bf16[4,8,2,256]{3,2,1,0:T(2,128)(2,1)S(1)}, u32[]{:S(2)}, u32[]{:S(2)}) collective-permute-start(bf16[4,8,2,256]{3,2,1,0:T(2,128)(2,1)S(1)} %squeeze.63), channel_id=1, source_target_pairs={{0,2},{2,4},{4,6},{6,8},{8,10},{10,12},{12,14},{14,16},{16,18},{18... | collective-permute-start | bytes 98312 | tf_op jit(solution)/shard_map/ppermute | solution.py:20
  127.6 1.6 %collective-permute-start.30 = (bf16[8,4,8,2,256]{4,3,2,1,0:T(2,128)(2,1)S(1)}, bf16[8,4,8,2,256]{4,3,2,1,0:T(2,128)(2,1)S(1)}, u32[]{:S(2)}, u32[]{:S(2)}) collective-permute-start(bf16[8,4,8,2,256]{4,3,2,1,0:T(2,128)(2,1)S(1)} %constant_dynamic-slice_fusion), channel_id=1, source_target_pairs={{0,1},{1,0},{2,3},{3,2},{4,5},{5,4},{6,7},{7,6},{8,9},{9,8},{10,11... | collective-permute-start | bytes 786440 | tf_op jit(solution)/shard_map/ppermute | solution.py:105
  (8 other events, 16.7 us)

commit v3 on v1

v3 whole, which is shorter than its diff:
```python
import functools
import math

import jax
import jax.numpy as jnp
from jax import lax
from jax.experimental import pallas as pl
from jax.experimental.pallas import tpu as pltpu
from jax.sharding import PartitionSpec as P

BINS = 8192
LAGS = 2048
DEC = 8
PERIOD = BINS // DEC


EPS = 1e-06


def correlate_kernel(blocks, offsets, capacity, norm_scale, placed_ref, source_ref, table_ref, out_ref, cross_ref):
    block = pl.program_id(0)
    folds = placed_ref.shape[2] // PERIOD
    for offset in range(offsets):
        owned = placed_ref[lax.rem(block - offset + blocks, blocks)]
        real_t = owned[:capacity]
        imag_t = owned[capacity:]
        for source in range(2):
            real_s = source_ref[0, 2 * source : 2 * source + 1]
            imag_s = source_ref[0, 2 * source + 1 : 2 * source + 2]
            even = real_t * real_s + imag_t * imag_s
            odd = real_t * imag_s - imag_t * real_s
            even_fold = even[:, :PERIOD]
            odd_fold = odd[:, :PERIOD]
            for fold in range(1, folds):
                even_fold = even_fold + even[:, fold * PERIOD : (fold + 1) * PERIOD]
                odd_fold = odd_fold + odd[:, fold * PERIOD : (fold + 1) * PERIOD]
            row = (source * offsets + offset) * capacity
            cross_ref[row : row + capacity, :PERIOD] = even_fold
            cross_ref[row : row + capacity, PERIOD:] = odd_fold
    product = jnp.dot(
        cross_ref[...].astype(jnp.bfloat16), table_ref[...], preferred_element_type=jnp.float32
    )
    out_ref[0] = (product * norm_scale).astype(out_ref.dtype)


def correlate(placed, white_sources, table, offsets, capacity):
    blocks, _, group_bins = placed.shape
    rows = 2 * offsets * capacity
    lags_out = table.shape[1]
    body = functools.partial(correlate_kernel, blocks, offsets, capacity, BINS ** (-0.5))
    return pl.pallas_call(
        body,
        grid=(blocks,),
        in_specs=[
            pl.BlockSpec(placed.shape, lambda a: (0, 0, 0)),
            pl.BlockSpec((1,) + white_sources.shape[1:], lambda a: (a, 0, 0)),
            pl.BlockSpec(table.shape, lambda a: (0, 0)),
        ],
        out_specs=pl.BlockSpec((1, rows, lags_out), lambda a: (a, 0, 0)),
        out_shape=jax.ShapeDtypeStruct((blocks, rows, lags_out), jnp.bfloat16),
        scratch_shapes=[pltpu.VMEM((rows, 2 * PERIOD), jnp.float32)],
        cost_estimate=pl.CostEstimate(
            flops=blocks * rows * 2 * PERIOD * lags_out * 2 + blocks * offsets * 16 * capacity * group_bins,
            bytes_accessed=placed.size * 4 + white_sources.size * 4 + table.size * 2 + blocks * rows * lags_out * 2,
            transcendentals=0,
        ),
    )(placed, white_sources, table)


def per_device(traces, sources, owner):
    blocks = lax.axis_size("blk")
    band_count = lax.axis_size("band")
    station_count = traces.shape[0]
    source_count = sources.shape[0]
    group_bins = traces.shape[2]
    capacity = max(2, 2 * station_count // blocks)
    lags_out = LAGS // DEC
    offsets = blocks // 4
    band = lax.axis_index("band")

    every_source = lax.all_gather(sources, ("blk", "band"), axis=0, tiled=True)
    every_source = every_source.reshape(blocks, band_count, source_count, 2, group_bins)
    every_source = every_source.astype(jnp.float32)

    trace_float = traces.astype(jnp.float32)
    trace_power = lax.psum(jnp.sum(trace_float * trace_float, axis=(1, 2)), "band")
    white_traces = (
        (trace_float * lax.rsqrt(trace_power / (2 * BINS) + EPS)[:, None, None])
        .astype(jnp.bfloat16)
        .reshape(station_count, 2 * group_bins)
    )

    owners = owner[:, 0]
    owner_hits = (owners[:, None] == jnp.arange(blocks, dtype=jnp.int32)[None, :]).astype(jnp.int32)
    earlier = jnp.cumsum(owner_hits, axis=0) - owner_hits
    arrival = jnp.sum(owner_hits * earlier, axis=1)
    slot_index = owners * capacity + arrival
    placing = (
        jnp.arange(blocks * capacity, dtype=jnp.int32)[:, None] == slot_index[None, :]
    ).astype(jnp.bfloat16)
    placed = jnp.dot(placing, white_traces, preferred_element_type=jnp.float32)
    placed = placed.reshape(blocks, capacity, 2, group_bins).transpose(0, 2, 1, 3)
    placed = placed.reshape(blocks, 2 * capacity, group_bins)

    bin_index = jnp.arange(PERIOD, dtype=jnp.int32)
    lag_value = (jnp.arange(lags_out, dtype=jnp.int32) - lags_out // 2) * DEC
    phase_angle = jnp.mod(bin_index[:, None] * lag_value[None, :], BINS).astype(jnp.float32) * (
        2.0 * math.pi / BINS
    )
    table = jnp.concatenate([jnp.cos(phase_angle), jnp.sin(phase_angle)], axis=0).astype(
        jnp.bfloat16
    )

    source_power = jnp.sum(every_source * every_source, axis=(1, 3, 4))
    own_band = lax.dynamic_index_in_dim(every_source, band, axis=1, keepdims=False)
    white_sources = (
        (own_band * lax.rsqrt(source_power / (2 * BINS) + EPS)[:, :, None, None])
        .astype(jnp.bfloat16)
        .astype(jnp.float32)
        .reshape(blocks, source_count * 2, group_bins)
    )

    partial = correlate(placed, white_sources, table, offsets, capacity)
    arrived = lax.all_to_all(partial, "blk", split_axis=0, concat_axis=0, tiled=True)
    half = blocks // 2
    mine = lax.dynamic_slice_in_dim(arrived, band * half, half, axis=0)
    other = lax.dynamic_slice_in_dim(arrived, (1 - band) * half, half, axis=0)
    other = lax.ppermute(other, "band", [(0, 1), (1, 0)])
    summed = mine.astype(jnp.float32) + other.astype(jnp.float32)
    summed = summed.reshape(half, source_count, offsets, capacity, lags_out)
    return jnp.transpose(summed, (1, 2, 0, 3, 4)).reshape(
        source_count, offsets, half * capacity, lags_out
    )


def solution(mesh):
    placed = (P("blk", None, "band"), P("blk", None, "band"), P("blk", None))
    return jax.shard_map(
        per_device,
        mesh=mesh,
        in_specs=placed,
        out_specs=P("blk", None, "band", None),
        check_vma=False,
    )
```

time: 151 us -> 117 us (0.77)
  blocking collectives: 66.2 us -> 2.57 us
  waiting for transfers between devices: 7.22 us -> 57.7 us
  local copies, waits for them, and re-layouts: 35.1 us -> 2.34 us
  Pallas kernels: 0 us -> 13.2 us
  other arithmetic: 24.5 us -> 18.2 us
  starting transfers between devices: 0.01 us -> 4.65 us
    all_gather x1 -> x0, blocking collectives: 45.7 us -> none  [per_device(): all_sources = lax.all_gather(sources, 'blk', axis=0, tiled=True)]
    all_gather x0 -> x1, waiting for transfers between devices: none -> 40 us  [per_device(): every_source = lax.all_gather(sources, ('blk', 'band'), axis=0, tiled=True)]
    all_to_all x1 -> x0, blocking collectives: 18.1 us -> none  [per_device(): lax.all_to_all(partial, 'blk', split_axis=0, concat_axis=0, tiled=True)]
    all_to_all x0 -> x1, waiting for transfers between devices: none -> 15.5 us  [per_device(): lax.all_to_all(partial, 'blk', split_axis=0, concat_axis=0, tiled=True)]
    pallas_call x0 -> x1, Pallas kernels: none -> 13.2 us  [correlate(): pl.pallas_call(body, grid=(blocks,), in_specs=[pl.BlockSpec(placed.shape,...]
    reduce_scatter x1 -> x0, waiting for transfers between devices: 7.2 us -> none  [per_device(): lax.psum_scatter(arrived.astype(jnp.float32), 'band', scatter_dimension=0...]
    convert_element_type x1 -> x0, local copies, waits for them, and re-layouts: 7.2 us -> none  [per_device(): cross = jnp.stack(cross, axis=1).astype(jnp.bfloat16)]
    slice x6 -> x0, local copies, waits for them, and re-layouts: 6.99 us -> none  [per_device(): visiting = jnp.roll(placed, offset, axis=0)]
  transfers between devices with their start and end apart: 1 -> 3, of which waited for: 1 -> 3; matrix products, arithmetic and copies ran while one was open for 0% -> 14% of each run, Pallas kernels for 0% -> 0%
where the time goes in v3:
time: 117 us; the launch traced here: 116 us
  waiting for transfers between devices  57.7 us (49%)
  other arithmetic  18.2 us (16%)
  between operations  13.5 us (12%)
  Pallas kernels  13.2 us (11%)
  starting transfers between devices  4.65 us (4%)
  matrix products  3.56 us (3%)
  blocking collectives  2.57 us (2%)
  local copies, waits for them, and re-layouts  2.34 us (2%)
    all_gather x1, waiting for transfers between devices, per_device(): every_source = lax.all_gather(sources, ('blk', 'band'), axis=0, tiled=True)  40 us
    all_to_all x1, waiting for transfers between devices, per_device(): lax.all_to_all(partial, 'blk', split_axis=0, concat_axis=0, tiled=True)  15.5 us
    pallas_call x1, Pallas kernels, correlate(): pl.pallas_call(body, grid=(blocks,), in_specs=[pl.BlockSpec(placed.shape,...  13.2 us
    all_to_all x1, starting transfers between devices, per_device(): lax.all_to_all(partial, 'blk', split_axis=0, concat_axis=0, tiled=True)  4.58 us
    another operation x1, other arithmetic  4.39 us
    dot_general x1, matrix products, per_device(): placed = jnp.dot(placing, white_traces, preferred_element_type=jnp.float32)  3.56 us
    reduce_sum x1, other arithmetic, per_device(): jnp.sum(trace_float * trace_float, axis=(1, 2))  2.82 us
    psum x1, blocking collectives, per_device(): lax.psum(jnp.sum(trace_float * trace_float, axis=(1, 2)), 'band')  2.57 us
  transfers between devices with their start and end apart: 3, of which 3 were waited for; matrix products, arithmetic and copies ran while one was open for 14% of the time, Pallas kernels for 0%

profile of v3, /device:TPU:0, one launch (start us, length us, event | category | flops | bytes accessed | tf_op | source)
XLA Modules:
  0.0 115.9 jit_solution(1554770205477075937)
XLA Ops:
  6.5 0.0 all-gather.2.cloned.1.call-start
  6.5 0.7 all-gather.2.cloned.1.call-update
  7.3 0.7 fusion.13
  8.0 0.1 reduce_window_sum.11
  8.1 0.8 select_reduce_fusion
  9.0 2.8 %fusion = f32[64]{0:T(128)S(1)} fusion(bf16[64,2,4096]{2,1,0:T(2,128)(2,1)} %param.3), kind=kLoop, calls=%fused_computation.3 | loop fusion | flops 1572800 | bytes 1048832 | tf_op jit(solution)/shard_map/reduce_sum | solution.py:86
  11.8 2.6 %psum.7 = f32[64]{0:T(128)S(1)} all-reduce(f32[64]{0:T(128)S(1)} %fusion), channel_id=1, replica_groups=mesh['blk'=16,'band'=2] {'band'}, use_global_device_ids=true, to_apply=%region_3.4 | all-reduce | flops 64 | bytes 512 | tf_op jit(solution)/shard_map/psum | solution.py:86
  14.4 0.7 multiply_add_fusion.1
  15.0 2.5 %fusion.1 = bf16[64,2,4096]{2,1,0:T(2,128)(2,1)S(1)} fusion(bf16[64,2,4096]{2,1,0:T(2,128)(2,1)} %param.3, f32[64]{0:T(128)S(1)} %add_rsqrt_fusion.1), kind=kLoop, calls=%fused_computation.4 | loop fusion | flops 1572864 | bytes 2097408 | tf_op jit(solution)/shard_map/convert_element_type | solution.py:89
  17.6 3.6 %convolution_bitcast_fusion.placed_ref = f32[16,16,4096]{2,1,0:T(8,128)} fusion(s32[64]{0:T(128)S(1)} %multiply_add_fusion.1, s32[16,8]{1,0:T(8,128)S(1)} %multiply_add_fusion, bf16[8,8,2,4096]{3,2,1,0:T(2,128)(2,1)S(1)} %bitcast.39), kind=kOutput, calls=%fused_computation | convolution fusion | flops 134225920 | bytes 5243648 | tf_op jit(solution)/shard_map/dot_general | solution.py:101
  21.1 4.4 %cosine_convert_fusion = (bf16[1024,256]{1,0:T(8,128)(2,1)S(1)}, bf16[1024,256]{1,0:T(8,128)(2,1)S(1)}) fusion(s32[256]{0:T(256)S(1)} %add_multiply_fusion), kind=kLoop, calls=%fused_computation.16 | loop fusion | flops 4194304 | bytes 1049600 | tf_op jit(solution)/shard_map/convert.1
  25.5 1.0 pad_maximum_fusion.table_ref
  26.6 40.0 %all-gather.2.cloned.1.call-done = bf16[64,2,4096]{2,1,0:T(2,128)(2,1)} async-done(((bf16[2,2,4096]{2,1,0:T(2,128)(2,1)}), bf16[64,2,4096]{2,1,0:T(2,128)(2,1)}) %all-gather.2.cloned.1.call-update) | async-done | bytes 1048592 | tf_op jit(solution)/shard_map/all_gather | solution.py:81
  66.6 2.1 %convert.11 = f32[16,2,2,2,4096]{4,3,2,1,0:T(2,128)S(1)} convert(bf16[16,2,2,2,4096]{4,3,2,1,0:T(2,128)(2,1)} %bitcast.38) | non-fusion elementwise | flops 524288 | bytes 3145728 | tf_op jit(solution)/shard_map/convert_element_type | solution.py:83
  68.7 0.0 copy-start
  68.7 0.1 dynamic-slice_bitcast_fusion
  68.8 0.9 squeeze.8
  69.7 0.2 copy-done
  69.9 1.6 %multiply_reduce_fusion = f32[64]{0:T(128)S(1)} fusion(bf16[64,2,4096]{2,1,0:T(2,128)(2,1)S(1)} %copy-done), kind=kLoop, calls=%fused_computation.5 | loop fusion | flops 1572800 | bytes 1048832 | tf_op jit(solution)/shard_map/reduce_sum | solution.py:114
  71.5 0.1 reduce_sum.37
  71.7 0.1 copy.18
  71.8 0.1 copy.19
  71.9 1.3 %fusion.9.source_ref = f32[16,4,4096]{2,1,0:T(4,128)} fusion(f32[16,4,4096]{2,1,0:T(4,128)S(1)} %squeeze.8, f32[16,4]{1,0:T(8,128)S(1)} %copy.19), kind=kLoop, calls=%fused_computation.22 | loop fusion | flops 786432 | bytes 2097408 | tf_op jit(solution)/shard_map/convert_element_type | solution.py:119
  73.2 13.2 %shard_map.37 = bf16[16,64,256]{2,1,0:T(8,128)(2,1)} custom-call(f32[16,16,4096]{2,1,0:T(8,128)} %convolution_bitcast_fusion.placed_ref, f32[16,4,4096]{2,1,0:T(4,128)} %fusion.9.source_ref, bf16[2048,256]{1,0:T(8,128)(2,1)} %pad_maximum_fusion.table_ref), custom_call_target="tpu_custom_call" | custom-call | flops 1107296256 | bytes 6815744 | tf_op jit(solution)/shard_map/pallas_call | solution.py:51
  86.4 4.6 %all-to-all-start = ((bf16[16,64,256]{2,1,0:T(8,128)(2,1)}), bf16[16,64,256]{2,1,0:T(8,128)(2,1)S(1)}, u32[]{:S(2)}, u32[]{:S(2)}) async-start(bf16[16,64,256]{2,1,0:T(8,128)(2,1)} %shard_map.37), calls=%async_computation | async-start | bytes 1048576 | tf_op jit(solution)/shard_map/all_to_all | solution.py:124
  91.0 15.5 %all-to-all-done = bf16[16,64,256]{2,1,0:T(8,128)(2,1)S(1)} async-done(((bf16[16,64,256]{2,1,0:T(8,128)(2,1)}), bf16[16,64,256]{2,1,0:T(8,128)(2,1)S(1)}, u32[]{:S(2)}, u32[]{:S(2)}) %all-to-all-start) | async-done | bytes 524320 | tf_op jit(solution)/shard_map/all_to_all | solution.py:124
  106.5 0.1 collective-permute-start
  106.6 1.5 %collective-permute-done = bf16[8,64,256]{2,1,0:T(8,128)(2,1)S(1)} collective-permute-done((bf16[8,64,256]{2,1,0:T(8,128)(2,1)S(1)}, bf16[8,64,256]{2,1,0:T(8,128)(2,1)S(1)}, u32[]{:S(2)}, u32[]{:S(2)}) %collective-permute-start) | collective-permute-done | bytes 262176 | tf_op jit(solution)/shard_map/ppermute | solution.py:128
  108.1 0.1 convert_add_fusion
  108.2 0.8 copy.33
  (7 shorter events, 0.1 us)
Async XLA Ops:
  6.5 60.1 %all-gather.2.cloned.1.call-start = ((), (), s32[]{:S(2)}) async-start(), calls=%async_computation.1 | async-start | bytes 1081344 | tf_op jit(solution)/shard_map/all_gather | solution.py:81
  68.7 1.2 %copy-start = (bf16[64,2,4096]{2,1,0:T(2,128)(2,1)S(1)}, bf16[64,2,4096]{2,1,0:T(2,128)(2,1)}, u32[]{:S(2)}) copy-start(bf16[64,2,4096]{2,1,0:T(2,128)(2,1)} %all-gather.2.cloned.1.call-done) | copy-start | bytes 3145732
  86.4 20.1 %all-to-all-start = ((bf16[16,64,256]{2,1,0:T(8,128)(2,1)}), bf16[16,64,256]{2,1,0:T(8,128)(2,1)S(1)}, u32[]{:S(2)}, u32[]{:S(2)}) async-start(bf16[16,64,256]{2,1,0:T(8,128)(2,1)} %shard_map.37), calls=%async_computation | async-start | bytes 1048576 | tf_op jit(solution)/shard_map/all_to_all | solution.py:124
  106.5 1.6 %collective-permute-start = (bf16[8,64,256]{2,1,0:T(8,128)(2,1)S(1)}, bf16[8,64,256]{2,1,0:T(8,128)(2,1)S(1)}, u32[]{:S(2)}, u32[]{:S(2)}) collective-permute-start(bf16[8,64,256]{2,1,0:T(8,128)(2,1)S(1)} %constant_dynamic-slice_fusion), channel_id=1, source_target_pairs={{0,1},{1,0},{2,3},{3,2},{4,5},{5,4},{6,7},{7,6},{8,9},{9,8},{10,11... | collective-permute-start | bytes 786440 | tf_op jit(solution)/shard_map/ppermute | solution.py:128
Sparse Core Ops, SparseCore 0:
  10.2 56.3 all-gather.1

commit v4 on v3

--- a/solution.py
+++ b/solution.py
@@ -78,12 +78,26 @@
     offsets = blocks // 4
     band = lax.axis_index("band")
 
-    every_source = lax.all_gather(sources, ("blk", "band"), axis=0, tiled=True)
-    every_source = every_source.reshape(blocks, band_count, source_count, 2, group_bins)
-    every_source = every_source.astype(jnp.float32)
-
     trace_float = traces.astype(jnp.float32)
-    trace_power = lax.psum(jnp.sum(trace_float * trace_float, axis=(1, 2)), "band")
+    source_float = sources.astype(jnp.float32)
+    trace_power, source_power = lax.psum(
+        (
+            jnp.sum(trace_float * trace_float, axis=(1, 2)),
+            jnp.sum(source_float * source_float, axis=(1, 2)),
+        ),
+        "band",
+    )
+    white_sources = (
+        source_float * lax.rsqrt(source_power / (2 * BINS) + EPS)[:, None, None]
+    ).astype(jnp.bfloat16)
+    me = lax.axis_index("blk")
+    held = white_sources[None]
+    step = 1
+    while step < blocks:
+        got = lax.ppermute(held, "blk", [(i, i ^ step) for i in range(blocks)])
+        upper = jnp.bitwise_and(me // step, 1) == 1
+        held = jnp.where(upper, jnp.concatenate([got, held]), jnp.concatenate([held, got]))
+        step *= 2
     white_traces = (
         (trace_float * lax.rsqrt(trace_power / (2 * BINS) + EPS)[:, None, None])
         .astype(jnp.bfloat16)
@@ -111,14 +125,7 @@
         jnp.bfloat16
     )
 
-    source_power = jnp.sum(every_source * every_source, axis=(1, 3, 4))
-    own_band = lax.dynamic_index_in_dim(every_source, band, axis=1, keepdims=False)
-    white_sources = (
-        (own_band * lax.rsqrt(source_power / (2 * BINS) + EPS)[:, :, None, None])
-        .astype(jnp.bfloat16)
-        .astype(jnp.float32)
-        .reshape(blocks, source_count * 2, group_bins)
-    )
+    white_sources = held.astype(jnp.float32).reshape(blocks, source_count * 2, group_bins)
 
     partial = correlate(placed, white_sources, table, offsets, capacity)
     arrived = lax.all_to_all(partial, "blk", split_axis=0, concat_axis=0, tiled=True)

time: 117 us -> 86.7 us (0.74)
  waiting for transfers between devices: 57.7 us -> 31.4 us
  between operations: 13.5 us -> 0.15 us
  starting transfers between devices: 4.65 us -> 14.7 us
  local copies, waits for them, and re-layouts: 2.34 us -> 1.07 us
    all_gather x1 -> x0, waiting for transfers between devices: 40 us -> none  [per_device(): every_source = lax.all_gather(sources, ('blk', 'band'), axis=0, tiled=True)]
    ppermute x0 -> x4, waiting for transfers between devices: none -> 15.2 us  [per_device(): got = lax.ppermute(held, 'blk', [(i, i ^ step) for i in range(blocks)])]
    ppermute x0 -> x4, starting transfers between devices: none -> 8.77 us  [per_device(): got = lax.ppermute(held, 'blk', [(i, i ^ step) for i in range(blocks)])]
    select_n x0 -> x6, other arithmetic: none -> 1.48 us  [per_device(): jnp.where(upper, jnp.concatenate([got, held]), jnp.concatenate([held, got]))]
    all_to_all x1, starting transfers between devices: 4.58 us -> 5.83 us  [per_device(): lax.all_to_all(partial, 'blk', split_axis=0, concat_axis=0, tiled=True)]
  transfers between devices with their start and end apart: 3 -> 6, of which waited for: 3 -> 5; matrix products, arithmetic and copies ran while one was open for 14% -> 18% of each run, Pallas kernels for 0% -> 0%
where the time goes in v4:
time: 86.7 us; the launch traced here: 85.5 us
  waiting for transfers between devices  31.4 us (36%)
  other arithmetic  18.9 us (22%)
  starting transfers between devices  14.7 us (17%)
  Pallas kernels  13.2 us (15%)
  matrix products  3.56 us (4%)
  blocking collectives  2.56 us (3%)
  local copies, waits for them, and re-layouts  1.07 us (1%)
    ppermute x4, waiting for transfers between devices, per_device(): got = lax.ppermute(held, 'blk', [(i, i ^ step) for i in range(blocks)])  15.2 us
    all_to_all x1, waiting for transfers between devices, per_device(): lax.all_to_all(partial, 'blk', split_axis=0, concat_axis=0, tiled=True)  14.7 us
    pallas_call x1, Pallas kernels, correlate(): pl.pallas_call(body, grid=(blocks,), in_specs=[pl.BlockSpec(placed.shape,...  13.2 us
    ppermute x4, starting transfers between devices, per_device(): got = lax.ppermute(held, 'blk', [(i, i ^ step) for i in range(blocks)])  8.77 us
    all_to_all x1, starting transfers between devices, per_device(): lax.all_to_all(partial, 'blk', split_axis=0, concat_axis=0, tiled=True)  5.83 us
    another operation x1, other arithmetic  4.41 us
    dot_general x1, matrix products, per_device(): placed = jnp.dot(placing, white_traces, preferred_element_type=jnp.float32)  3.56 us
    reduce_sum x1, other arithmetic, per_device(): jnp.sum(trace_float * trace_float, axis=(1, 2))  2.81 us
  transfers between devices with their start and end apart: 6, of which 5 were waited for; matrix products, arithmetic and copies ran while one was open for 18% of the time, Pallas kernels for 0%

profile of v4, /device:TPU:0, one launch (start us, length us, event | category | flops | bytes accessed | tf_op | source)
XLA Modules:
  0.0 85.5 jit_solution(11246321333841312938)
XLA Ops:
  0.0 2.8 %fusion = f32[64]{0:T(128)S(1)} fusion(bf16[64,2,4096]{2,1,0:T(2,128)(2,1)} %param.3), kind=kLoop, calls=%fused_computation.3 | loop fusion | flops 1572800 | bytes 1048832 | tf_op jit(solution)/shard_map/reduce_sum | solution.py:85
  2.8 0.9 %fusion.10 = f32[2]{0:T(128)S(1)} fusion(bf16[2,2,4096]{2,1,0:T(2,128)(2,1)} %param.4), kind=kLoop, calls=%fused_computation.30 | loop fusion | flops 49150 | bytes 32776 | tf_op jit(solution)/shard_map/reduce_sum | solution.py:86
  3.7 2.6 %all-reduce = (f32[64]{0:T(128)S(1)}, f32[2]{0:T(128)S(1)}) all-reduce(f32[64]{0:T(128)S(1)} %fusion, f32[2]{0:T(128)S(1)} %fusion.10), channel_id=1, replica_groups=mesh['blk'=16,'band'=2] {'band'}, use_global_device_ids=true, to_apply=%region_3.0 | all-reduce | flops 66 | bytes 528 | tf_op jit(solution)/shard_map/psum | solution.py:83
  6.3 0.9 fusion.17
  7.1 2.9 %collective-permute-start = (bf16[1,2,2,4096]{3,2,1,0:T(2,128)(2,1)S(1)}, bf16[1,2,2,4096]{3,2,1,0:T(2,128)(2,1)S(1)}, u32[]{:S(2)}, u32[]{:S(2)}) collective-permute-start(bf16[1,2,2,4096]{3,2,1,0:T(2,128)(2,1)S(1)} %fusion.17), channel_id=1, source_target_pairs={{0,2},{2,0},{4,6},{6,4},{8,10},{10,8},{12,14},{14,12},{16,18},{18,... | collective-permute-start | bytes 98312 | tf_op jit(solution)/shard_map/ppermute | solution.py:97
  10.0 0.8 fusion.11
  10.9 0.7 fusion.15
  11.6 0.1 reduce_window_sum.11
  11.7 0.8 select_reduce_fusion
  12.6 0.7 multiply_add_fusion.1
  13.2 2.5 %fusion.1 = bf16[64,2,4096]{2,1,0:T(2,128)(2,1)S(1)} fusion(bf16[64,2,4096]{2,1,0:T(2,128)(2,1)} %param.3, f32[64]{0:T(128)S(1)} %add_rsqrt_fusion.1), kind=kLoop, calls=%fused_computation.4 | loop fusion | flops 1572864 | bytes 2097408 | tf_op jit(solution)/shard_map/convert_element_type | solution.py:103
  15.8 4.4 %cosine_convert_fusion = (bf16[1024,256]{1,0:T(8,128)(2,1)S(1)}, bf16[1024,256]{1,0:T(8,128)(2,1)S(1)}) fusion(s32[256]{0:T(256)S(1)} %add_multiply_fusion), kind=kLoop, calls=%fused_computation.15 | loop fusion | flops 4194304 | bytes 1049600 | tf_op jit(solution)/shard_map/convert
  20.2 1.1 %pad_maximum_fusion.table_ref = bf16[2048,256]{1,0:T(8,128)(2,1)} fusion(bf16[1024,256]{1,0:T(8,128)(2,1)S(1)} %get-tuple-element.8, bf16[1024,256]{1,0:T(8,128)(2,1)S(1)} %get-tuple-element.7), kind=kLoop, calls=%fused_computation.13 | loop fusion | flops 2097152 | bytes 2097152 | tf_op jit(solution)/shard_map/concatenate | solution.py:124
  21.3 3.6 %convolution_bitcast_fusion.placed_ref = f32[16,16,4096]{2,1,0:T(8,128)} fusion(s32[64]{0:T(128)S(1)} %multiply_add_fusion.1, s32[16,8]{1,0:T(8,128)S(1)} %multiply_add_fusion, bf16[8,8,2,4096]{3,2,1,0:T(2,128)(2,1)S(1)} %bitcast.33), kind=kOutput, calls=%fused_computation | convolution fusion | flops 134225920 | bytes 5243648 | tf_op jit(solution)/shard_map/dot_general | solution.py:115
  24.9 0.1 broadcast_select_fusion.2
  25.0 1.6 %collective-permute-start.1 = (bf16[2,2,2,4096]{3,2,1,0:T(2,128)(2,1)S(1)}, bf16[2,2,2,4096]{3,2,1,0:T(2,128)(2,1)S(1)}, u32[]{:S(2)}, u32[]{:S(2)}) collective-permute-start(bf16[2,2,2,4096]{3,2,1,0:T(2,128)(2,1)S(1)} %broadcast_select_fusion.2), channel_id=1, source_target_pairs={{0,4},{2,6},{4,0},{6,2},{8,12},{10,14},{12,8},{14,10},{16,20},{18,... | collective-permute-start | bytes 196616 | tf_op jit(solution)/shard_map/ppermute | solution.py:97
  26.7 2.7 %collective-permute-done.1 = bf16[2,2,2,4096]{3,2,1,0:T(2,128)(2,1)S(1)} collective-permute-done((bf16[2,2,2,4096]{3,2,1,0:T(2,128)(2,1)S(1)}, bf16[2,2,2,4096]{3,2,1,0:T(2,128)(2,1)S(1)}, u32[]{:S(2)}, u32[]{:S(2)}) %collective-permute-start.1) | collective-permute-done | bytes 65568 | tf_op jit(solution)/shard_map/ppermute | solution.py:97
  29.3 0.3 broadcast_select_fusion.1
  29.6 1.6 %collective-permute-start.2 = (bf16[4,2,2,4096]{3,2,1,0:T(2,128)(2,1)S(1)}, bf16[4,2,2,4096]{3,2,1,0:T(2,128)(2,1)S(1)}, u32[]{:S(2)}, u32[]{:S(2)}) collective-permute-start(bf16[4,2,2,4096]{3,2,1,0:T(2,128)(2,1)S(1)} %broadcast_select_fusion.1), channel_id=1, source_target_pairs={{0,8},{2,10},{4,12},{6,14},{8,0},{10,2},{12,4},{14,6},{16,24},{18,... | collective-permute-start | bytes 393224 | tf_op jit(solution)/shard_map/ppermute | solution.py:97
  31.3 0.2 maximum_select_fusion.2
  31.5 3.2 %collective-permute-done.2 = bf16[4,2,2,4096]{3,2,1,0:T(2,128)(2,1)S(1)} collective-permute-done((bf16[4,2,2,4096]{3,2,1,0:T(2,128)(2,1)S(1)}, bf16[4,2,2,4096]{3,2,1,0:T(2,128)(2,1)S(1)}, u32[]{:S(2)}, u32[]{:S(2)}) %collective-permute-start.2) | collective-permute-done | bytes 131104 | tf_op jit(solution)/shard_map/ppermute | solution.py:97
  34.7 0.6 broadcast_select_fusion
  35.2 2.7 %collective-permute-start.3 = (bf16[8,2,2,4096]{3,2,1,0:T(2,128)(2,1)S(1)}, bf16[8,2,2,4096]{3,2,1,0:T(2,128)(2,1)S(1)}, u32[]{:S(2)}, u32[]{:S(2)}) collective-permute-start(bf16[8,2,2,4096]{3,2,1,0:T(2,128)(2,1)S(1)} %broadcast_select_fusion), channel_id=1, source_target_pairs={{0,16},{2,18},{4,20},{6,22},{8,24},{10,26},{12,28},{14,30},{16,0},... | collective-permute-start | bytes 786440 | tf_op jit(solution)/shard_map/ppermute | solution.py:97
  38.0 0.3 maximum_select_fusion.1
  38.3 9.4 %collective-permute-done.3 = bf16[8,2,2,4096]{3,2,1,0:T(2,128)(2,1)S(1)} collective-permute-done((bf16[8,2,2,4096]{3,2,1,0:T(2,128)(2,1)S(1)}, bf16[8,2,2,4096]{3,2,1,0:T(2,128)(2,1)S(1)}, u32[]{:S(2)}, u32[]{:S(2)}) %collective-permute-start.3) | collective-permute-done | bytes 262176 | tf_op jit(solution)/shard_map/ppermute | solution.py:97
  47.6 0.1 concatenate.64
  47.7 1.5 %fusion.9.source_ref = f32[16,4,4096]{2,1,0:T(4,128)} fusion(bf16[8,4,4096]{2,1,0:T(4,128)(2,1)S(1)} %maximum_select_fusion.1, bf16[8,4,4096]{2,1,0:T(4,128)(2,1)S(1)} %concatenate.64, pred[]{:T(512)S(6)} %eq.60), kind=kLoop, calls=%fused_computation.20 | loop fusion | flops 1048576 | bytes 1572865 | tf_op jit(solution)/shard_map/convert_element_type | solution.py:128
  49.3 13.2 %shard_map.37 = bf16[16,64,256]{2,1,0:T(8,128)(2,1)} custom-call(f32[16,16,4096]{2,1,0:T(8,128)} %convolution_bitcast_fusion.placed_ref, f32[16,4,4096]{2,1,0:T(4,128)} %fusion.9.source_ref, bf16[2048,256]{1,0:T(8,128)(2,1)} %pad_maximum_fusion.table_ref), custom_call_target="tpu_custom_call" | custom-call | flops 1107296256 | bytes 6815744 | tf_op jit(solution)/shard_map/pallas_call | solution.py:51
  62.5 5.8 %all-to-all-start = ((bf16[16,64,256]{2,1,0:T(8,128)(2,1)}), bf16[16,64,256]{2,1,0:T(8,128)(2,1)S(1)}, u32[]{:S(2)}, u32[]{:S(2)}) async-start(bf16[16,64,256]{2,1,0:T(8,128)(2,1)} %shard_map.37), calls=%async_computation | async-start | bytes 1048576 | tf_op jit(solution)/shard_map/all_to_all | solution.py:131
  68.3 14.7 %all-to-all-done = bf16[16,64,256]{2,1,0:T(8,128)(2,1)S(1)} async-done(((bf16[16,64,256]{2,1,0:T(8,128)(2,1)}), bf16[16,64,256]{2,1,0:T(8,128)(2,1)S(1)}, u32[]{:S(2)}, u32[]{:S(2)}) %all-to-all-start) | async-done | bytes 524320 | tf_op jit(solution)/shard_map/all_to_all | solution.py:131
  83.1 1.5 %collective-permute-done.4 = bf16[8,64,256]{2,1,0:T(8,128)(2,1)S(1)} collective-permute-done((bf16[8,64,256]{2,1,0:T(8,128)(2,1)S(1)}, bf16[8,64,256]{2,1,0:T(8,128)(2,1)S(1)}, u32[]{:S(2)}, u32[]{:S(2)}) %collective-permute-start.4) | collective-permute-done | bytes 262176 | tf_op jit(solution)/shard_map/ppermute | solution.py:135
  84.7 0.8 copy.18
  (13 shorter events, 0.3 us)
Async XLA Ops:
  7.1 17.8 %collective-permute-start = (bf16[1,2,2,4096]{3,2,1,0:T(2,128)(2,1)S(1)}, bf16[1,2,2,4096]{3,2,1,0:T(2,128)(2,1)S(1)}, u32[]{:S(2)}, u32[]{:S(2)}) collective-permute-start(bf16[1,2,2,4096]{3,2,1,0:T(2,128)(2,1)S(1)} %fusion.17), channel_id=1, source_target_pairs={{0,2},{2,0},{4,6},{6,4},{8,10},{10,8},{12,14},{14,12},{16,18},{18,... | collective-permute-start | bytes 98312 | tf_op jit(solution)/shard_map/ppermute | solution.py:97
  25.0 4.3 %collective-permute-start.1 = (bf16[2,2,2,4096]{3,2,1,0:T(2,128)(2,1)S(1)}, bf16[2,2,2,4096]{3,2,1,0:T(2,128)(2,1)S(1)}, u32[]{:S(2)}, u32[]{:S(2)}) collective-permute-start(bf16[2,2,2,4096]{3,2,1,0:T(2,128)(2,1)S(1)} %broadcast_select_fusion.2), channel_id=1, source_target_pairs={{0,4},{2,6},{4,0},{6,2},{8,12},{10,14},{12,8},{14,10},{16,20},{18,... | collective-permute-start | bytes 196616 | tf_op jit(solution)/shard_map/ppermute | solution.py:97
  29.6 5.0 %collective-permute-start.2 = (bf16[4,2,2,4096]{3,2,1,0:T(2,128)(2,1)S(1)}, bf16[4,2,2,4096]{3,2,1,0:T(2,128)(2,1)S(1)}, u32[]{:S(2)}, u32[]{:S(2)}) collective-permute-start(bf16[4,2,2,4096]{3,2,1,0:T(2,128)(2,1)S(1)} %broadcast_select_fusion.1), channel_id=1, source_target_pairs={{0,8},{2,10},{4,12},{6,14},{8,0},{10,2},{12,4},{14,6},{16,24},{18,... | collective-permute-start | bytes 393224 | tf_op jit(solution)/shard_map/ppermute | solution.py:97
  35.2 12.4 %collective-permute-start.3 = (bf16[8,2,2,4096]{3,2,1,0:T(2,128)(2,1)S(1)}, bf16[8,2,2,4096]{3,2,1,0:T(2,128)(2,1)S(1)}, u32[]{:S(2)}, u32[]{:S(2)}) collective-permute-start(bf16[8,2,2,4096]{3,2,1,0:T(2,128)(2,1)S(1)} %broadcast_select_fusion), channel_id=1, source_target_pairs={{0,16},{2,18},{4,20},{6,22},{8,24},{10,26},{12,28},{14,30},{16,0},... | collective-permute-start | bytes 786440 | tf_op jit(solution)/shard_map/ppermute | solution.py:97
  62.5 20.5 %all-to-all-start = ((bf16[16,64,256]{2,1,0:T(8,128)(2,1)}), bf16[16,64,256]{2,1,0:T(8,128)(2,1)S(1)}, u32[]{:S(2)}, u32[]{:S(2)}) async-start(bf16[16,64,256]{2,1,0:T(8,128)(2,1)} %shard_map.37), calls=%async_computation | async-start | bytes 1048576 | tf_op jit(solution)/shard_map/all_to_all | solution.py:131
  83.0 1.6 %collective-permute-start.4 = (bf16[8,64,256]{2,1,0:T(8,128)(2,1)S(1)}, bf16[8,64,256]{2,1,0:T(8,128)(2,1)S(1)}, u32[]{:S(2)}, u32[]{:S(2)}) collective-permute-start(bf16[8,64,256]{2,1,0:T(8,128)(2,1)S(1)} %constant_dynamic-slice_fusion), channel_id=1, source_target_pairs={{0,1},{1,0},{2,3},{3,2},{4,5},{5,4},{6,7},{7,6},{8,9},{9,8},{10,11... | collective-permute-start | bytes 786440 | tf_op jit(solution)/shard_map/ppermute | solution.py:135

commit v5 on v4

v5 whole, which is shorter than its diff:
```python
import functools
import math

import jax
import ml_dtypes
import numpy as np
import jax.numpy as jnp
from jax import lax
from jax.experimental import pallas as pl
from jax.experimental.pallas import tpu as pltpu
from jax.sharding import PartitionSpec as P

BINS = 8192
LAGS = 2048
DEC = 8
PERIOD = BINS // DEC


EPS = 1e-06


def correlate_kernel(blocks, offsets, capacity, group, norm_scale, placed_ref, source_ref, table_ref, out_ref, cross_ref):
    first = pl.program_id(0) * group
    folds = placed_ref.shape[2] // PERIOD
    rows = 2 * offsets * capacity
    for member in range(group):
        block = first + member
        for offset in range(offsets):
            owned = placed_ref[lax.rem(block - offset + blocks, blocks)].astype(jnp.float32)
            real_t = owned[:capacity]
            imag_t = owned[capacity:]
            for source in range(2):
                real_s = source_ref[member, 2 * source : 2 * source + 1].astype(jnp.float32)
                imag_s = source_ref[member, 2 * source + 1 : 2 * source + 2].astype(jnp.float32)
                even = real_t * real_s + imag_t * imag_s
                odd = real_t * imag_s - imag_t * real_s
                even_fold = even[:, :PERIOD]
                odd_fold = odd[:, :PERIOD]
                for fold in range(1, folds):
                    even_fold = even_fold + even[:, fold * PERIOD : (fold + 1) * PERIOD]
                    odd_fold = odd_fold + odd[:, fold * PERIOD : (fold + 1) * PERIOD]
                row = member * rows + (source * offsets + offset) * capacity
                cross_ref[row : row + capacity, :PERIOD] = even_fold
                cross_ref[row : row + capacity, PERIOD:] = odd_fold
    product = jnp.dot(
        cross_ref[...].astype(jnp.bfloat16), table_ref[...], preferred_element_type=jnp.float32
    )
    product = (product * norm_scale).astype(out_ref.dtype)
    for member in range(group):
        out_ref[member] = product[member * rows : (member + 1) * rows]


def correlate(placed, white_sources, table, offsets, capacity):
    blocks, _, group_bins = placed.shape
    rows = 2 * offsets * capacity
    lags_out = table.shape[1]
    group = 4
    body = functools.partial(correlate_kernel, blocks, offsets, capacity, group, BINS ** (-0.5))
    return pl.pallas_call(
        body,
        grid=(blocks // group,),
        in_specs=[
            pl.BlockSpec(placed.shape, lambda a: (0, 0, 0)),
            pl.BlockSpec((group,) + white_sources.shape[1:], lambda a: (a, 0, 0)),
            pl.BlockSpec(table.shape, lambda a: (0, 0)),
        ],
        out_specs=pl.BlockSpec((group, rows, lags_out), lambda a: (a, 0, 0)),
        out_shape=jax.ShapeDtypeStruct((blocks, rows, lags_out), jnp.bfloat16),
        scratch_shapes=[pltpu.VMEM((group * rows, 2 * PERIOD), jnp.float32)],
        cost_estimate=pl.CostEstimate(
            flops=blocks * rows * 2 * PERIOD * lags_out * 2 + blocks * offsets * 16 * capacity * group_bins,
            bytes_accessed=placed.size * 2 + white_sources.size * 2 + table.size * 2 + blocks * rows * lags_out * 2,
            transcendentals=0,
        ),
    )(placed, white_sources, table)


def twiddle_table(lags_out):
    bin_index = np.arange(PERIOD, dtype=np.int64)
    lag_value = (np.arange(lags_out, dtype=np.int64) - lags_out // 2) * DEC
    phase = np.mod(bin_index[:, None] * lag_value[None, :], BINS).astype(np.float32)
    phase = (phase * np.float32(2.0 * math.pi / BINS)).astype(np.float64)
    table = np.concatenate([np.cos(phase), np.sin(phase)], axis=0)
    return table.astype(ml_dtypes.bfloat16)


def per_device(traces, sources, owner):
    blocks = lax.axis_size("blk")
    band_count = lax.axis_size("band")
    station_count = traces.shape[0]
    source_count = sources.shape[0]
    group_bins = traces.shape[2]
    capacity = max(2, 2 * station_count // blocks)
    lags_out = LAGS // DEC
    offsets = blocks // 4
    band = lax.axis_index("band")

    trace_float = traces.astype(jnp.float32)
    source_float = sources.astype(jnp.float32)
    trace_power, source_power = lax.psum(
        (
            jnp.sum(trace_float * trace_float, axis=(1, 2)),
            jnp.sum(source_float * source_float, axis=(1, 2)),
        ),
        "band",
    )
    white_sources = (
        source_float * lax.rsqrt(source_power / (2 * BINS) + EPS)[:, None, None]
    ).astype(jnp.bfloat16)
    me = lax.axis_index("blk")
    held = white_sources[None]
    bits = blocks.bit_length() - 1
    for bit in reversed(range(bits)):
        step = 1 << bit
        got = lax.ppermute(held, "blk", [(i, i ^ step) for i in range(blocks)])
        upper = jnp.bitwise_and(me // step, 1) == 1
        held = jnp.where(upper, jnp.concatenate([got, held]), jnp.concatenate([held, got]))
    held = held.reshape((2,) * bits + held.shape[1:])
    held = held.transpose(tuple(reversed(range(bits))) + tuple(range(bits, held.ndim)))
    white_traces = (
        (trace_float * lax.rsqrt(trace_power / (2 * BINS) + EPS)[:, None, None])
        .astype(jnp.bfloat16)
        .reshape(station_count, 2 * group_bins)
    )

    owners = owner[:, 0]
    owner_hits = (owners[:, None] == jnp.arange(blocks, dtype=jnp.int32)[None, :]).astype(jnp.int32)
    earlier = jnp.cumsum(owner_hits, axis=0) - owner_hits
    arrival = jnp.sum(owner_hits * earlier, axis=1)
    slot_index = owners * capacity + arrival
    placing = (
        jnp.arange(blocks * capacity, dtype=jnp.int32)[:, None] == slot_index[None, :]
    ).astype(jnp.bfloat16)
    placed = jnp.dot(placing, white_traces, preferred_element_type=jnp.float32).astype(jnp.bfloat16)
    placed = placed.reshape(blocks, capacity, 2, group_bins).transpose(0, 2, 1, 3)
    placed = placed.reshape(blocks, 2 * capacity, group_bins)

    table = jnp.asarray(twiddle_table(lags_out))

    white_sources = held.reshape(blocks, source_count * 2, group_bins)

    partial = correlate(placed, white_sources, table, offsets, capacity)
    arrived = lax.all_to_all(partial, "blk", split_axis=0, concat_axis=0, tiled=True)
    half = blocks // 2
    mine = lax.dynamic_slice_in_dim(arrived, band * half, half, axis=0)
    other = lax.dynamic_slice_in_dim(arrived, (1 - band) * half, half, axis=0)
    other = lax.ppermute(other, "band", [(0, 1), (1, 0)])
    summed = mine.astype(jnp.float32) + other.astype(jnp.float32)
    summed = summed.reshape(half, source_count, offsets, capacity, lags_out)
    return jnp.transpose(summed, (1, 2, 0, 3, 4)).reshape(
        source_count, offsets, half * capacity, lags_out
    )


def solution(mesh):
    placed = (P("blk", None, "band"), P("blk", None, "band"), P("blk", None))
    return jax.shard_map(
        per_device,
        mesh=mesh,
        in_specs=placed,
        out_specs=P("blk", None, "band", None),
        check_vma=False,
    )
```

time: 86.7 us -> 62.2 us (0.72)
  waiting for transfers between devices: 31.4 us -> 21.1 us
  other arithmetic: 18.9 us -> 9.77 us
  Pallas kernels: 13.2 us -> 8.64 us
  local copies, waits for them, and re-layouts: 1.07 us -> 2.86 us
  matrix products: 3.56 us -> 2.04 us
    ppermute x4, waiting for transfers between devices: 15.2 us -> 8.8 us  [per_device(): got = lax.ppermute(held, 'blk', [(i, i ^ step) for i in range(blocks)])]
    pallas_call x1, Pallas kernels: 13.2 us -> 8.64 us  [correlate(): pl.pallas_call(body, grid=(blocks // group,), in_specs=[pl.BlockSpec(plac...]
    another operation x1 -> x0, other arithmetic: 4.41 us -> none
    all_to_all x1, waiting for transfers between devices: 14.7 us -> 10.8 us  [per_device(): lax.all_to_all(partial, 'blk', split_axis=0, concat_axis=0, tiled=True)]
    convert_element_type x2 -> x0, other arithmetic: 2.37 us -> none  [the longest x1 1.53 us: per_device(): held.astype(jnp.float32).reshape(blocks, source_count * 2, group_bins)]
    dot_general x1, matrix products: 3.56 us -> 2.04 us  [per_device(): jnp.dot(placing, white_traces, preferred_element_type=jnp.float32)]
    concatenate x1 -> x0, other arithmetic: 1.09 us -> none  [per_device(): jnp.concatenate([jnp.cos(phase_angle), jnp.sin(phase_angle)], axis=0)]
    reshape x0 -> x1, local copies, waits for them, and re-layouts: none -> 0.99 us  [per_device(): white_sources = held.reshape(blocks, source_count * 2, group_bins)]
  transfers between devices with their start and end apart: 6 -> 6, of which waited for: 5 -> 5; matrix products, arithmetic and copies ran while one was open for 18% -> 9% of each run, Pallas kernels for 0% -> 0%
where the time goes in v5:
time: 62.2 us; the launch traced here: 61.8 us
  waiting for transfers between devices  21.1 us (34%)
  starting transfers between devices  14.7 us (24%)
  other arithmetic  9.77 us (16%)
  Pallas kernels  8.64 us (14%)
  local copies, waits for them, and re-layouts  2.86 us (5%)
  blocking collectives  2.56 us (4%)
  matrix products  2.04 us (3%)
    all_to_all x1, waiting for transfers between devices, per_device(): lax.all_to_all(partial, 'blk', split_axis=0, concat_axis=0, tiled=True)  10.8 us
    ppermute x4, waiting for transfers between devices, per_device(): got = lax.ppermute(held, 'blk', [(i, i ^ step) for i in range(blocks)])  8.8 us
    ppermute x4, starting transfers between devices, per_device(): got = lax.ppermute(held, 'blk', [(i, i ^ step) for i in range(blocks)])  8.77 us
    pallas_call x1, Pallas kernels, correlate(): pl.pallas_call(body, grid=(blocks // group,), in_specs=[pl.BlockSpec(plac...  8.64 us
    all_to_all x1, starting transfers between devices, per_device(): lax.all_to_all(partial, 'blk', split_axis=0, concat_axis=0, tiled=True)  5.84 us
    reduce_sum x1, other arithmetic, per_device(): jnp.sum(trace_float * trace_float, axis=(1, 2))  2.82 us
    convert_element_type x1, other arithmetic, per_device(): white_traces = (trace_float * lax.rsqrt(trace_power / (2 * BINS) + EPS)[:...  2.66 us
    psum x1, blocking collectives, per_device(): lax.psum((jnp.sum(trace_float * trace_float, axis=(1, 2)), jnp.sum(source...  2.56 us
  transfers between devices with their start and end apart: 6, of which 5 were waited for; matrix products, arithmetic and copies ran while one was open for 9% of the time, Pallas kernels for 0%

profile of v5, /device:TPU:0, one launch (start us, length us, event | category | flops | bytes accessed | tf_op | source)
XLA Modules:
  0.0 61.8 jit_solution(18250337233710339058)
XLA Ops:
  0.0 2.8 %fusion = f32[64]{0:T(128)S(1)} fusion(bf16[64,2,4096]{2,1,0:T(2,128)(2,1)} %param.4), kind=kLoop, calls=%fused_computation.3 | loop fusion | flops 1572800 | bytes 1048832 | tf_op jit(solution)/shard_map/reduce_sum | solution.py:102
  2.8 0.9 %fusion.2 = f32[2]{0:T(128)S(1)} fusion(bf16[2,2,4096]{2,1,0:T(2,128)(2,1)} %param.5), kind=kLoop, calls=%fused_computation.14 | loop fusion | flops 49150 | bytes 32776 | tf_op jit(solution)/shard_map/reduce_sum | solution.py:103
  3.7 2.6 %all-reduce = (f32[64]{0:T(128)S(1)}, f32[2]{0:T(128)S(1)}) all-reduce(f32[64]{0:T(128)S(1)} %fusion, f32[2]{0:T(128)S(1)} %fusion.2), channel_id=1, replica_groups=mesh['blk'=16,'band'=2] {'band'}, use_global_device_ids=true, to_apply=%region_3.0 | all-reduce | flops 66 | bytes 528 | tf_op jit(solution)/shard_map/psum | solution.py:100
  6.3 0.9 %fusion.6 = bf16[1,2,2,4096]{3,2,1,0:T(2,128)(2,1)S(1)} fusion(f32[2]{0:T(128)S(1)} %add_rsqrt_fusion, bf16[2,2,4096]{2,1,0:T(2,128)(2,1)} %param.5), kind=kLoop, calls=%fused_computation.21 | loop fusion | flops 49152 | bytes 65544 | tf_op jit(solution)/shard_map/broadcast_in_dim | solution.py:111
  7.1 4.0 %collective-permute-start = (bf16[1,2,2,4096]{3,2,1,0:T(2,128)(2,1)S(1)}, bf16[1,2,2,4096]{3,2,1,0:T(2,128)(2,1)S(1)}, u32[]{:S(2)}, u32[]{:S(2)}) collective-permute-start(bf16[1,2,2,4096]{3,2,1,0:T(2,128)(2,1)S(1)} %fusion.6), channel_id=1, source_target_pairs={{0,16},{2,18},{4,20},{6,22},{8,24},{10,26},{12,28},{14,30},{16,0},... | collective-permute-start | bytes 98312 | tf_op jit(solution)/shard_map/ppermute | solution.py:115
  11.1 2.7 %fusion.1 = bf16[64,2,4096]{2,1,0:T(2,128)(2,1)S(1)} fusion(bf16[64,2,4096]{2,1,0:T(2,128)(2,1)} %param.4, f32[64]{0:T(128)S(1)} %add_rsqrt_fusion.1), kind=kLoop, calls=%fused_computation.4 | loop fusion | flops 1572864 | bytes 2097408 | tf_op jit(solution)/shard_map/convert_element_type | solution.py:122
  13.8 0.0 copy-done
  13.8 0.1 fusion.5
  13.9 0.6 copy.7
  14.5 0.1 reduce_window_sum.11
  14.6 0.0 collective-permute-done
  14.6 0.1 broadcast_select_fusion.3
  14.7 1.6 %collective-permute-start.1 = (bf16[2,2,2,4096]{3,2,1,0:T(2,128)(2,1)S(1)}, bf16[2,2,2,4096]{3,2,1,0:T(2,128)(2,1)S(1)}, u32[]{:S(2)}, u32[]{:S(2)}) collective-permute-start(bf16[2,2,2,4096]{3,2,1,0:T(2,128)(2,1)S(1)} %broadcast_select_fusion.3), channel_id=1, source_target_pairs={{0,8},{2,10},{4,12},{6,14},{8,0},{10,2},{12,4},{14,6},{16,24},{18,... | collective-permute-start | bytes 196616 | tf_op jit(solution)/shard_map/ppermute | solution.py:115
  16.4 0.2 select_reduce_fusion
  16.5 2.5 %collective-permute-done.1 = bf16[2,2,2,4096]{3,2,1,0:T(2,128)(2,1)S(1)} collective-permute-done((bf16[2,2,2,4096]{3,2,1,0:T(2,128)(2,1)S(1)}, bf16[2,2,2,4096]{3,2,1,0:T(2,128)(2,1)S(1)}, u32[]{:S(2)}, u32[]{:S(2)}) %collective-permute-start.1) | collective-permute-done | bytes 65568 | tf_op jit(solution)/shard_map/ppermute | solution.py:115
  19.0 0.3 broadcast_select_fusion.2
  19.3 1.6 %collective-permute-start.2 = (bf16[4,2,2,4096]{3,2,1,0:T(2,128)(2,1)S(1)}, bf16[4,2,2,4096]{3,2,1,0:T(2,128)(2,1)S(1)}, u32[]{:S(2)}, u32[]{:S(2)}) collective-permute-start(bf16[4,2,2,4096]{3,2,1,0:T(2,128)(2,1)S(1)} %broadcast_select_fusion.2), channel_id=1, source_target_pairs={{0,4},{2,6},{4,0},{6,2},{8,12},{10,14},{12,8},{14,10},{16,20},{18,... | collective-permute-start | bytes 393224 | tf_op jit(solution)/shard_map/ppermute | solution.py:115
  20.9 3.4 %collective-permute-done.2 = bf16[4,2,2,4096]{3,2,1,0:T(2,128)(2,1)S(1)} collective-permute-done((bf16[4,2,2,4096]{3,2,1,0:T(2,128)(2,1)S(1)}, bf16[4,2,2,4096]{3,2,1,0:T(2,128)(2,1)S(1)}, u32[]{:S(2)}, u32[]{:S(2)}) %collective-permute-start.2) | collective-permute-done | bytes 131104 | tf_op jit(solution)/shard_map/ppermute | solution.py:115
  24.4 0.6 broadcast_select_fusion.1
  25.0 1.6 %collective-permute-start.3 = (bf16[8,2,2,4096]{3,2,1,0:T(2,128)(2,1)S(1)}, bf16[8,2,2,4096]{3,2,1,0:T(2,128)(2,1)S(1)}, u32[]{:S(2)}, u32[]{:S(2)}) collective-permute-start(bf16[8,2,2,4096]{3,2,1,0:T(2,128)(2,1)S(1)} %broadcast_select_fusion.1), channel_id=1, source_target_pairs={{0,2},{2,0},{4,6},{6,4},{8,10},{10,8},{12,14},{14,12},{16,18},{18,... | collective-permute-start | bytes 786440 | tf_op jit(solution)/shard_map/ppermute | solution.py:115
  26.5 2.0 %convolution_convert_fusion = bf16[128,8192]{1,0:T(8,128)(2,1)} fusion(bf16[64,8192]{1,0:T(8,128)(2,1)S(1)} %bitcast.24, s32[64]{0:T(128)S(1)} %multiply_add_fusion), kind=kOutput, calls=%fused_computation | convolution fusion | flops 135274496 | bytes 3145984 | tf_op jit(solution)/shard_map/dot_general | solution.py:134
  28.6 2.8 %collective-permute-done.3 = bf16[8,2,2,4096]{3,2,1,0:T(2,128)(2,1)S(1)} collective-permute-done((bf16[8,2,2,4096]{3,2,1,0:T(2,128)(2,1)S(1)}, bf16[8,2,2,4096]{3,2,1,0:T(2,128)(2,1)S(1)}, u32[]{:S(2)}, u32[]{:S(2)}) %collective-permute-start.3) | collective-permute-done | bytes 262176 | tf_op jit(solution)/shard_map/ppermute | solution.py:115
  31.4 1.2 %broadcast_select_fusion = bf16[16,2,2,4096]{3,2,1,0:T(2,128)(2,1)S(1)} fusion(pred[]{:T(512)S(6)} %eq.44, bf16[8,2,2,4096]{3,2,1,0:T(2,128)(2,1)S(1)} %broadcast_select_fusion.1, bf16[8,2,2,4096]{3,2,1,0:T(2,128)(2,1)S(1)} %collective-permute-done.3), kind=kLoop, calls=%fused_computation.5 | loop fusion | flops 786432 | bytes 1048577 | tf_op jit(solution)/shard_map/jit(_where)/select_n | solution.py:117
  32.6 0.4 copy.11
  33.0 1.0 %reshape.36.source_ref = bf16[16,4,4096]{2,1,0:T(4,128)(2,1)} reshape(bf16[2,2,2,2,2,2,4096]{6,5,4,3,2,1,0:T(2,128)(2,1)S(1)} %bitcast.27) | data formatting | bytes 1048576 | tf_op jit(solution)/shard_map/reshape | solution.py:140
  34.0 8.6 %shard_map.46 = bf16[16,64,256]{2,1,0:T(8,128)(2,1)} custom-call(bf16[16,16,4096]{2,1,0:T(8,128)(2,1)} %bitcast.22, bf16[16,4,4096]{2,1,0:T(4,128)(2,1)} %reshape.36.source_ref, bf16[2048,256]{1,0:T(8,128)(2,1)} %constant.73.clone.table_ref), custom_call_target="tpu_custom_call" | custom-call | flops 1107296256 | bytes 4194304 | tf_op jit(solution)/shard_map/pallas_call | solution.py:59
  42.6 5.8 %all-to-all-start = ((bf16[16,64,256]{2,1,0:T(8,128)(2,1)}), bf16[16,64,256]{2,1,0:T(8,128)(2,1)S(1)}, u32[]{:S(2)}, u32[]{:S(2)}) async-start(bf16[16,64,256]{2,1,0:T(8,128)(2,1)} %shard_map.46), calls=%async_computation | async-start | bytes 1048576 | tf_op jit(solution)/shard_map/all_to_all | solution.py:143
  48.5 10.8 %all-to-all-done = bf16[16,64,256]{2,1,0:T(8,128)(2,1)S(1)} async-done(((bf16[16,64,256]{2,1,0:T(8,128)(2,1)}), bf16[16,64,256]{2,1,0:T(8,128)(2,1)S(1)}, u32[]{:S(2)}, u32[]{:S(2)}) %all-to-all-start) | async-done | bytes 524320 | tf_op jit(solution)/shard_map/all_to_all | solution.py:143
  59.3 0.1 collective-permute-start.4
  59.4 1.5 %collective-permute-done.4 = bf16[8,64,256]{2,1,0:T(8,128)(2,1)S(1)} collective-permute-done((bf16[8,64,256]{2,1,0:T(8,128)(2,1)S(1)}, bf16[8,64,256]{2,1,0:T(8,128)(2,1)S(1)}, u32[]{:S(2)}, u32[]{:S(2)}) %collective-permute-start.4) | collective-permute-done | bytes 262176 | tf_op jit(solution)/shard_map/ppermute | solution.py:147
  60.9 0.1 convert_add_fusion
  60.9 0.8 %copy.10 = f32[2,4,8,8,256]{4,3,2,1,0:T(8,128)} copy(f32[2,4,8,8,256]{4,3,1,0,2:T(8,128)S(1)} %bitcast.26) | data formatting | bytes 1048576 | tf_op jit(solution)/shard_map/transpose | solution.py:150
  (5 shorter events, 0.0 us)
Async XLA Ops:
  0.0 13.8 %copy-start = (s32[64,1]{0,1:T(1,128)S(1)}, s32[64,1]{0,1:T(1,128)}, u32[]{:S(2)}) copy-start(s32[64,1]{0,1:T(1,128)} %param.6) | copy-start | bytes 772
  7.1 7.5 %collective-permute-start = (bf16[1,2,2,4096]{3,2,1,0:T(2,128)(2,1)S(1)}, bf16[1,2,2,4096]{3,2,1,0:T(2,128)(2,1)S(1)}, u32[]{:S(2)}, u32[]{:S(2)}) collective-permute-start(bf16[1,2,2,4096]{3,2,1,0:T(2,128)(2,1)S(1)} %fusion.6), channel_id=1, source_target_pairs={{0,16},{2,18},{4,20},{6,22},{8,24},{10,26},{12,28},{14,30},{16,0},... | collective-permute-start | bytes 98312 | tf_op jit(solution)/shard_map/ppermute | solution.py:115
  14.7 4.3 %collective-permute-start.1 = (bf16[2,2,2,4096]{3,2,1,0:T(2,128)(2,1)S(1)}, bf16[2,2,2,4096]{3,2,1,0:T(2,128)(2,1)S(1)}, u32[]{:S(2)}, u32[]{:S(2)}) collective-permute-start(bf16[2,2,2,4096]{3,2,1,0:T(2,128)(2,1)S(1)} %broadcast_select_fusion.3), channel_id=1, source_target_pairs={{0,8},{2,10},{4,12},{6,14},{8,0},{10,2},{12,4},{14,6},{16,24},{18,... | collective-permute-start | bytes 196616 | tf_op jit(solution)/shard_map/ppermute | solution.py:115
  19.3 5.0 %collective-permute-start.2 = (bf16[4,2,2,4096]{3,2,1,0:T(2,128)(2,1)S(1)}, bf16[4,2,2,4096]{3,2,1,0:T(2,128)(2,1)S(1)}, u32[]{:S(2)}, u32[]{:S(2)}) collective-permute-start(bf16[4,2,2,4096]{3,2,1,0:T(2,128)(2,1)S(1)} %broadcast_select_fusion.2), channel_id=1, source_target_pairs={{0,4},{2,6},{4,0},{6,2},{8,12},{10,14},{12,8},{14,10},{16,20},{18,... | collective-permute-start | bytes 393224 | tf_op jit(solution)/shard_map/ppermute | solution.py:115
  25.0 6.4 %collective-permute-start.3 = (bf16[8,2,2,4096]{3,2,1,0:T(2,128)(2,1)S(1)}, bf16[8,2,2,4096]{3,2,1,0:T(2,128)(2,1)S(1)}, u32[]{:S(2)}, u32[]{:S(2)}) collective-permute-start(bf16[8,2,2,4096]{3,2,1,0:T(2,128)(2,1)S(1)} %broadcast_select_fusion.1), channel_id=1, source_target_pairs={{0,2},{2,0},{4,6},{6,4},{8,10},{10,8},{12,14},{14,12},{16,18},{18,... | collective-permute-start | bytes 786440 | tf_op jit(solution)/shard_map/ppermute | solution.py:115
  42.6 16.6 %all-to-all-start = ((bf16[16,64,256]{2,1,0:T(8,128)(2,1)}), bf16[16,64,256]{2,1,0:T(8,128)(2,1)S(1)}, u32[]{:S(2)}, u32[]{:S(2)}) async-start(bf16[16,64,256]{2,1,0:T(8,128)(2,1)} %shard_map.46), calls=%async_computation | async-start | bytes 1048576 | tf_op jit(solution)/shard_map/all_to_all | solution.py:143
  59.3 1.6 %collective-permute-start.4 = (bf16[8,64,256]{2,1,0:T(8,128)(2,1)S(1)}, bf16[8,64,256]{2,1,0:T(8,128)(2,1)S(1)}, u32[]{:S(2)}, u32[]{:S(2)}) collective-permute-start(bf16[8,64,256]{2,1,0:T(8,128)(2,1)S(1)} %constant_dynamic-slice_fusion), channel_id=1, source_target_pairs={{0,1},{1,0},{2,3},{3,2},{4,5},{5,4},{6,7},{7,6},{8,9},{9,8},{10,11... | collective-permute-start | bytes 786440 | tf_op jit(solution)/shard_map/ppermute | solution.py:147

commit v6 on v5

--- a/solution.py
+++ b/solution.py
@@ -19,19 +19,21 @@
 EPS = 1e-06
 
 
-def correlate_kernel(blocks, offsets, capacity, group, norm_scale, placed_ref, source_ref, table_ref, out_ref, cross_ref):
+def correlate_kernel(blocks, offsets, capacity, group, norm_scale, ids_ref, placed_ref, source_ref, table_ref, out_ref, cross_ref):
     first = pl.program_id(0) * group
     folds = placed_ref.shape[2] // PERIOD
     rows = 2 * offsets * capacity
     for member in range(group):
-        block = first + member
-        for offset in range(offsets):
-            owned = placed_ref[lax.rem(block - offset + blocks, blocks)].astype(jnp.float32)
-            real_t = owned[:capacity]
-            imag_t = owned[capacity:]
-            for source in range(2):
-                real_s = source_ref[member, 2 * source : 2 * source + 1].astype(jnp.float32)
-                imag_s = source_ref[member, 2 * source + 1 : 2 * source + 2].astype(jnp.float32)
+        block = ids_ref[first + member]
+        for source in range(2):
+            real_s = source_ref[member, 2 * source : 2 * source + 1].astype(jnp.float32)
+            imag_s = source_ref[member, 2 * source + 1 : 2 * source + 2].astype(jnp.float32)
+            real_s = jnp.broadcast_to(real_s, (capacity, real_s.shape[1]))
+            imag_s = jnp.broadcast_to(imag_s, (capacity, imag_s.shape[1]))
+            for offset in range(offsets):
+                owned = placed_ref[lax.rem(block - offset + blocks, blocks)].astype(jnp.float32)
+                real_t = owned[:capacity]
+                imag_t = owned[capacity:]
                 even = real_t * real_s + imag_t * imag_s
                 odd = real_t * imag_s - imag_t * real_s
                 even_fold = even[:, :PERIOD]
@@ -50,29 +52,33 @@
         out_ref[member] = product[member * rows : (member + 1) * rows]
 
 
-def correlate(placed, white_sources, table, offsets, capacity):
+def correlate(ids, placed, white_sources, table, offsets, capacity):
     blocks, _, group_bins = placed.shape
+    count = white_sources.shape[0]
     rows = 2 * offsets * capacity
     lags_out = table.shape[1]
-    group = 4
+    group = min(4, count)
     body = functools.partial(correlate_kernel, blocks, offsets, capacity, group, BINS ** (-0.5))
     return pl.pallas_call(
         body,
-        grid=(blocks // group,),
-        in_specs=[
-            pl.BlockSpec(placed.shape, lambda a: (0, 0, 0)),
-            pl.BlockSpec((group,) + white_sources.shape[1:], lambda a: (a, 0, 0)),
-            pl.BlockSpec(table.shape, lambda a: (0, 0)),
-        ],
-        out_specs=pl.BlockSpec((group, rows, lags_out), lambda a: (a, 0, 0)),
-        out_shape=jax.ShapeDtypeStruct((blocks, rows, lags_out), jnp.bfloat16),
-        scratch_shapes=[pltpu.VMEM((group * rows, 2 * PERIOD), jnp.float32)],
+        grid_spec=pltpu.PrefetchScalarGridSpec(
+            num_scalar_prefetch=1,
+            grid=(count // group,),
+            in_specs=[
+                pl.BlockSpec(placed.shape, lambda a, ids: (0, 0, 0)),
+                pl.BlockSpec((group,) + white_sources.shape[1:], lambda a, ids: (a, 0, 0)),
+                pl.BlockSpec(table.shape, lambda a, ids: (0, 0)),
+            ],
+            out_specs=pl.BlockSpec((group, rows, lags_out), lambda a, ids: (a, 0, 0)),
+            scratch_shapes=[pltpu.VMEM((group * rows, 2 * PERIOD), jnp.float32)],
+        ),
+        out_shape=jax.ShapeDtypeStruct((count, rows, lags_out), jnp.bfloat16),
         cost_estimate=pl.CostEstimate(
-            flops=blocks * rows * 2 * PERIOD * lags_out * 2 + blocks * offsets * 16 * capacity * group_bins,
-            bytes_accessed=placed.size * 2 + white_sources.size * 2 + table.size * 2 + blocks * rows * lags_out * 2,
+            flops=count * rows * 2 * PERIOD * lags_out * 2 + count * offsets * 16 * capacity * group_bins,
+            bytes_accessed=placed.size * 2 + white_sources.size * 2 + table.size * 2 + count * rows * lags_out * 2,
             transcendentals=0,
         ),
-    )(placed, white_sources, table)
+    )(ids, placed, white_sources, table)
 
 
 def twiddle_table(lags_out):
@@ -95,28 +101,13 @@
     offsets = blocks // 4
     band = lax.axis_index("band")
 
-    trace_float = traces.astype(jnp.float32)
     source_float = sources.astype(jnp.float32)
-    trace_power, source_power = lax.psum(
-        (
-            jnp.sum(trace_float * trace_float, axis=(1, 2)),
-            jnp.sum(source_float * source_float, axis=(1, 2)),
-        ),
-        "band",
-    )
+    source_power = lax.psum(jnp.sum(source_float * source_float, axis=(1, 2)), "band")
     white_sources = (
         source_float * lax.rsqrt(source_power / (2 * BINS) + EPS)[:, None, None]
-    ).astype(jnp.bfloat16)
-    me = lax.axis_index("blk")
-    held = white_sources[None]
-    bits = blocks.bit_length() - 1
-    for bit in reversed(range(bits)):
-        step = 1 << bit
-        got = lax.ppermute(held, "blk", [(i, i ^ step) for i in range(blocks)])
-        upper = jnp.bitwise_and(me // step, 1) == 1
-        held = jnp.where(upper, jnp.concatenate([got, held]), jnp.concatenate([held, got]))
-    held = held.reshape((2,) * bits + held.shape[1:])
-    held = held.transpose(tuple(reversed(range(bits))) + tuple(range(bits, held.ndim)))
+    ).astype(jnp.bfloat16).reshape(1, source_count * 2, group_bins)
+    trace_float = traces.astype(jnp.float32)
+    trace_power = lax.psum(jnp.sum(trace_float * trace_float, axis=(1, 2)), "band")
     white_traces = (
         (trace_float * lax.rsqrt(trace_power / (2 * BINS) + EPS)[:, None, None])
         .astype(jnp.bfloat16)
@@ -137,9 +128,26 @@
 
     table = jnp.asarray(twiddle_table(lags_out))
 
-    white_sources = held.reshape(blocks, source_count * 2, group_bins)
-
-    partial = correlate(placed, white_sources, table, offsets, capacity)
+    me = lax.axis_index("blk")
+    held = white_sources
+    held_ids = me[None].astype(jnp.int32)
+    results = correlate(held_ids, placed, held, table, offsets, capacity)
+    bits = blocks.bit_length() - 1
+    for bit in reversed(range(bits)):
+        step = 1 << bit
+        got = lax.ppermute(held, "blk", [(i, i ^ step) for i in range(blocks)])
+        got_ids = jnp.bitwise_xor(held_ids, step)
+        got_results = correlate(got_ids, placed, got, table, offsets, capacity)
+        upper = jnp.bitwise_and(me // step, 1) == 1
+        if bit > 0:
+            held = jnp.where(upper, jnp.concatenate([got, held]), jnp.concatenate([held, got]))
+            held_ids = jnp.where(upper, jnp.concatenate([got_ids, held_ids]), jnp.concatenate([held_ids, got_ids]))
+        results = jnp.where(
+            upper, jnp.concatenate([got_results, results]), jnp.concatenate([results, got_results])
+        )
+    partial = results.reshape((2,) * bits + results.shape[1:])
+    partial = partial.transpose(tuple(reversed(range(bits))) + tuple(range(bits, partial.ndim)))
+    partial = partial.reshape(results.shape)
     arrived = lax.all_to_all(partial, "blk", split_axis=0, concat_axis=0, tiled=True)
     half = blocks // 2
     mine = lax.dynamic_slice_in_dim(arrived, band * half, half, axis=0)

time: 62.2 us -> 72.6 us (1.17)
  Pallas kernels: 8.64 us -> 21.1 us
  waiting for transfers between devices: 21.1 us -> 17.9 us
  other arithmetic: 9.77 us -> 12.7 us
  starting transfers between devices: 14.7 us -> 12.4 us
    pallas_call x1 -> x5, Pallas kernels: 8.64 us -> 21.1 us  [correlate(): pl.pallas_call(body, grid_spec=pltpu.PrefetchScalarGridSpec(num_scalar_pr...]
    ppermute x4, waiting for transfers between devices: 8.8 us -> 2.62 us  [per_device(): got = lax.ppermute(held, 'blk', [(i, i ^ step) for i in range(blocks)])]
    select_n x0 -> x4, other arithmetic: none -> 3.92 us  [per_device(): jnp.where(upper, jnp.concatenate([got_results, results]), jnp.concatenate...]
    all_to_all x1, waiting for transfers between devices: 10.8 us -> 13.7 us  [per_device(): lax.all_to_all(partial, 'blk', split_axis=0, concat_axis=0, tiled=True)]
    all_to_all x1, starting transfers between devices: 5.84 us -> 3.57 us  [per_device(): lax.all_to_all(partial, 'blk', split_axis=0, concat_axis=0, tiled=True)]
    select_n x4 -> x3, other arithmetic: 2.12 us -> 0.5 us  [per_device(): jnp.where(upper, jnp.concatenate([got, held]), jnp.concatenate([held, got]))]
    reshape x1, local copies, waits for them, and re-layouts: 0.99 us -> 0.02 us  [per_device(): white_sources = (source_float * lax.rsqrt(source_power / (2 * BINS) + EPS...]
    broadcast_in_dim x1 -> x0, other arithmetic: 0.85 us -> none  [per_device(): held = white_sources[None]]
  transfers between devices with their start and end apart: 6 -> 6, of which waited for: 5 -> 3; matrix products, arithmetic and copies ran while one was open for 9% -> 13% of each run, Pallas kernels for 0% -> 21%
where the time goes in v6:
time: 72.6 us; the launch traced here: 71.9 us
  Pallas kernels  21.1 us (29%)
  waiting for transfers between devices  17.9 us (25%)
  other arithmetic  12.7 us (17%)
  starting transfers between devices  12.4 us (17%)
  local copies, waits for them, and re-layouts  3.02 us (4%)
  blocking collectives  2.56 us (4%)
  matrix products  2.02 us (3%)
    pallas_call x5, Pallas kernels, correlate(): pl.pallas_call(body, grid_spec=pltpu.PrefetchScalarGridSpec(num_scalar_pr...  21.1 us
    all_to_all x1, waiting for transfers between devices, per_device(): lax.all_to_all(partial, 'blk', split_axis=0, concat_axis=0, tiled=True)  13.7 us
    ppermute x4, starting transfers between devices, per_device(): got = lax.ppermute(held, 'blk', [(i, i ^ step) for i in range(blocks)])  8.76 us
    select_n x4, other arithmetic, per_device(): jnp.where(upper, jnp.concatenate([got_results, results]), jnp.concatenate...  3.92 us
    all_to_all x1, starting transfers between devices, per_device(): lax.all_to_all(partial, 'blk', split_axis=0, concat_axis=0, tiled=True)  3.57 us
    reduce_sum x1, other arithmetic, per_device(): jnp.sum(trace_float * trace_float, axis=(1, 2))  2.81 us
    ppermute x4, waiting for transfers between devices, per_device(): got = lax.ppermute(held, 'blk', [(i, i ^ step) for i in range(blocks)])  2.62 us
    psum x1, blocking collectives, per_device(): lax.psum(jnp.sum(trace_float * trace_float, axis=(1, 2)), 'band')  2.56 us
  transfers between devices with their start and end apart: 6, of which 3 were waited for; matrix products, arithmetic and copies ran while one was open for 13% of the time, Pallas kernels for 21%

profile of v6, /device:TPU:0, one launch (start us, length us, event | category | flops | bytes accessed | tf_op | source)
XLA Modules:
  0.0 71.9 jit_solution(18051044710385504776)
XLA Ops:
  0.0 2.8 %fusion = f32[64]{0:T(128)S(1)} fusion(bf16[64,2,4096]{2,1,0:T(2,128)(2,1)} %param.4), kind=kLoop, calls=%fused_computation.3 | loop fusion | flops 1572800 | bytes 1048832 | tf_op jit(solution)/shard_map/reduce_sum | solution.py:110
  2.8 0.9 %fusion.2 = f32[2]{0:T(128)S(1)} fusion(bf16[2,2,4096]{2,1,0:T(2,128)(2,1)} %param.5), kind=kLoop, calls=%fused_computation.14 | loop fusion | flops 49150 | bytes 32776 | tf_op jit(solution)/shard_map/reduce_sum | solution.py:105
  3.7 2.6 %all-reduce = (f32[64]{0:T(128)S(1)}, f32[2]{0:T(128)S(1)}) all-reduce(f32[64]{0:T(128)S(1)} %fusion, f32[2]{0:T(128)S(1)} %fusion.2), channel_id=1, replica_groups=mesh['blk'=16,'band'=2] {'band'}, use_global_device_ids=true, to_apply=%region_3.0 | all-reduce | flops 66 | bytes 528 | tf_op jit(solution)/shard_map/psum | solution.py:110
  6.3 0.9 %fusion.3 = bf16[2,2,4096]{2,1,0:T(2,128)(2,1)S(1)} fusion(bf16[2,2,4096]{2,1,0:T(2,128)(2,1)} %param.5, f32[2]{0:T(128)S(1)} %add_rsqrt_fusion), kind=kLoop, calls=%fused_computation.15 | loop fusion | flops 49152 | bytes 65544 | tf_op jit(solution)/shard_map/convert_element_type | solution.py:108
  7.2 4.0 %collective-permute-start = (bf16[1,4,4096]{2,1,0:T(4,128)(2,1)S(1)}, bf16[1,4,4096]{2,1,0:T(4,128)(2,1)S(1)}, u32[]{:S(2)}, u32[]{:S(2)}) collective-permute-start(bf16[1,4,4096]{2,1,0:T(4,128)(2,1)S(1)} %reshape.39.source_ref), channel_id=1, source_target_pairs={{0,16},{2,18},{4,20},{6,22},{8,24},{10,26},{12,28},{14,30},{16,0},... | collective-permute-start | bytes 98312 | tf_op jit(solution)/shard_map/ppermute | solution.py:138
  11.2 2.6 %fusion.1 = bf16[64,2,4096]{2,1,0:T(2,128)(2,1)S(1)} fusion(bf16[64,2,4096]{2,1,0:T(2,128)(2,1)} %param.4, f32[64]{0:T(128)S(1)} %add_rsqrt_fusion.1), kind=kLoop, calls=%fused_computation.4 | loop fusion | flops 1572864 | bytes 2097408 | tf_op jit(solution)/shard_map/convert_element_type | solution.py:113
  13.7 0.6 copy.8
  14.4 0.1 reduce_window_sum.11
  14.5 0.2 select_reduce_fusion
  14.7 2.0 %convolution_convert_fusion = bf16[128,8192]{1,0:T(8,128)(2,1)} fusion(bf16[64,8192]{1,0:T(8,128)(2,1)S(1)} %bitcast.27, s32[64]{0:T(128)S(1)} %multiply_add_fusion), kind=kOutput, calls=%fused_computation | convolution fusion | flops 135274496 | bytes 3145984 | tf_op jit(solution)/shard_map/dot_general | solution.py:125
  16.9 1.6 %collective-permute-start.1 = (bf16[2,4,4096]{2,1,0:T(4,128)(2,1)S(1)}, bf16[2,4,4096]{2,1,0:T(4,128)(2,1)S(1)}, u32[]{:S(2)}, u32[]{:S(2)}) collective-permute-start(bf16[2,4,4096]{2,1,0:T(4,128)(2,1)S(1)} %maximum_select_fusion.5), channel_id=1, source_target_pairs={{0,8},{2,10},{4,12},{6,14},{8,0},{10,2},{12,4},{14,6},{16,24},{18,... | collective-permute-start | bytes 196616 | tf_op jit(solution)/shard_map/ppermute | solution.py:138
  18.6 2.6 %collective-permute-done.1.source_ref = bf16[2,4,4096]{2,1,0:T(4,128)(2,1)S(1)} collective-permute-done((bf16[2,4,4096]{2,1,0:T(4,128)(2,1)S(1)}, bf16[2,4,4096]{2,1,0:T(4,128)(2,1)S(1)}, u32[]{:S(2)}, u32[]{:S(2)}) %collective-permute-start.1) | collective-permute-done | bytes 65568 | tf_op jit(solution)/shard_map/ppermute | solution.py:138
  21.2 0.1 maximum_select_fusion.3
  21.4 1.6 %collective-permute-start.2 = (bf16[4,4,4096]{2,1,0:T(4,128)(2,1)S(1)}, bf16[4,4,4096]{2,1,0:T(4,128)(2,1)S(1)}, u32[]{:S(2)}, u32[]{:S(2)}) collective-permute-start(bf16[4,4,4096]{2,1,0:T(4,128)(2,1)S(1)} %maximum_select_fusion.3), channel_id=1, source_target_pairs={{0,4},{2,6},{4,0},{6,2},{8,12},{10,14},{12,8},{14,10},{16,20},{18,... | collective-permute-start | bytes 393224 | tf_op jit(solution)/shard_map/ppermute | solution.py:138
  23.0 0.6 fusion.6.ids_ref
  23.5 3.0 %shard_map.50 = bf16[1,64,256]{2,1,0:T(8,128)(2,1)} custom-call(s32[1]{0:T(128)} %bitcast.ids_ref, bf16[16,16,4096]{2,1,0:T(8,128)(2,1)} %bitcast.21, bf16[1,4,4096]{2,1,0:T(4,128)(2,1)} %copy-done.1, bf16[2048,256]{1,0:T(8,128)(2,1)} %constant.79.clone.table_ref), custom_call_target="tpu_custom_call" | custom-call | flops 69206016 | bytes 3211264 | tf_op jit(solution)/shard_map/pallas_call | solution.py:62
  26.5 3.0 %shard_map.49 = bf16[1,64,256]{2,1,0:T(8,128)(2,1)} custom-call(s32[1]{0:T(128)S(6)} %xor.12.ids_ref, bf16[16,16,4096]{2,1,0:T(8,128)(2,1)} %bitcast.22, bf16[1,4,4096]{2,1,0:T(4,128)(2,1)} %copy-done.4, bf16[2048,256]{1,0:T(8,128)(2,1)} %constant.79.clone.table_ref), custom_call_target="tpu_custom_call" | custom-call | flops 69206016 | bytes 3211264 | tf_op jit(solution)/shard_map/pallas_call | solution.py:62
  29.6 0.8 %maximum_select_fusion.6 = bf16[2,64,256]{2,1,0:T(8,128)(2,1)S(1)} fusion(bf16[1,64,256]{2,1,0:T(8,128)(2,1)S(1)} %copy-done.5, bf16[1,64,256]{2,1,0:T(8,128)(2,1)} %shard_map.49, pred[]{:T(512)S(6)} %eq.41), kind=kLoop, calls=%fused_computation.17 | loop fusion | flops 98304 | bytes 131073 | tf_op jit(solution)/shard_map/jit(_where)/select_n | solution.py:145
  30.4 0.3 maximum_select_fusion.1
  30.7 1.6 %collective-permute-start.3 = (bf16[8,4,4096]{2,1,0:T(4,128)(2,1)S(1)}, bf16[8,4,4096]{2,1,0:T(4,128)(2,1)S(1)}, u32[]{:S(2)}, u32[]{:S(2)}) collective-permute-start(bf16[8,4,4096]{2,1,0:T(4,128)(2,1)S(1)} %maximum_select_fusion.1), channel_id=1, source_target_pairs={{0,2},{2,0},{4,6},{6,4},{8,10},{10,8},{12,14},{14,12},{16,18},{18,... | collective-permute-start | bytes 786440 | tf_op jit(solution)/shard_map/ppermute | solution.py:138
  32.3 4.0 %shard_map.48 = bf16[2,64,256]{2,1,0:T(8,128)(2,1)} custom-call(s32[2]{0:T(128)} %copy-done.7, bf16[16,16,4096]{2,1,0:T(8,128)(2,1)} %bitcast.23, bf16[2,4,4096]{2,1,0:T(4,128)(2,1)} %copy-done.2, bf16[2048,256]{1,0:T(8,128)(2,1)} %constant.79.clone.table_ref), custom_call_target="tpu_custom_call" | custom-call | flops 138412032 | bytes 3276800 | tf_op jit(solution)/shard_map/pallas_call | solution.py:62
  36.3 0.9 %maximum_select_fusion.4 = bf16[4,64,256]{2,1,0:T(8,128)(2,1)S(1)} fusion(bf16[2,64,256]{2,1,0:T(8,128)(2,1)S(1)} %maximum_select_fusion.6, bf16[2,64,256]{2,1,0:T(8,128)(2,1)} %shard_map.48, pred[]{:T(512)S(6)} %eq.40), kind=kLoop, calls=%fused_computation.11 | loop fusion | flops 196608 | bytes 262145 | tf_op jit(solution)/shard_map/jit(_where)/select_n | solution.py:145
  37.2 4.8 %shard_map.47 = bf16[4,64,256]{2,1,0:T(8,128)(2,1)} custom-call(s32[4]{0:T(128)} %copy-done.6, bf16[16,16,4096]{2,1,0:T(8,128)(2,1)} %bitcast.24, bf16[4,4,4096]{2,1,0:T(4,128)(2,1)} %copy-done, bf16[2048,256]{1,0:T(8,128)(2,1)} %constant.79.clone.table_ref), custom_call_target="tpu_custom_call" | custom-call | flops 276824064 | bytes 3407872 | tf_op jit(solution)/shard_map/pallas_call | solution.py:62
  42.0 1.0 %maximum_select_fusion.2 = bf16[8,64,256]{2,1,0:T(8,128)(2,1)S(1)} fusion(bf16[4,64,256]{2,1,0:T(8,128)(2,1)S(1)} %maximum_select_fusion.4, bf16[4,64,256]{2,1,0:T(8,128)(2,1)} %shard_map.47, pred[]{:T(512)S(6)} %eq.39), kind=kLoop, calls=%fused_computation.9 | loop fusion | flops 393216 | bytes 524289 | tf_op jit(solution)/shard_map/jit(_where)/select_n | solution.py:145
  43.1 0.7 copy-done.3
  43.8 6.3 %shard_map.46 = bf16[8,64,256]{2,1,0:T(8,128)(2,1)} custom-call(s32[8]{0:T(128)} %fusion.6.ids_ref, bf16[16,16,4096]{2,1,0:T(8,128)(2,1)} %bitcast.25, bf16[8,4,4096]{2,1,0:T(4,128)(2,1)} %copy-done.3, bf16[2048,256]{1,0:T(8,128)(2,1)} %constant.79.clone.table_ref), custom_call_target="tpu_custom_call" | custom-call | flops 553648128 | bytes 3670016 | tf_op jit(solution)/shard_map/pallas_call | solution.py:62
  50.1 1.1 %maximum_select_fusion = bf16[16,64,256]{2,1,0:T(8,128)(2,1)S(1)} fusion(bf16[8,64,256]{2,1,0:T(8,128)(2,1)S(1)} %maximum_select_fusion.2, bf16[8,64,256]{2,1,0:T(8,128)(2,1)} %shard_map.46, pred[]{:T(512)S(6)} %eq.38), kind=kLoop, calls=%fused_computation.5 | loop fusion | flops 786432 | bytes 1048577 | tf_op jit(solution)/shard_map/jit(_where)/select_n | solution.py:145
  51.2 0.8 %copy.6 = bf16[2,2,2,2,64,256]{5,4,0,1,2,3:T(8,128)(2,1)} copy(bf16[2,2,2,2,64,256]{5,4,3,2,1,0:T(8,128)(2,1)S(1)} %bitcast.28) | data formatting | bytes 1048576 | tf_op jit(solution)/shard_map/jit(_where)/select_n | solution.py:145
  52.0 3.6 %all-to-all-start = ((bf16[16,64,256]{2,1,0:T(8,128)(2,1)}), bf16[16,64,256]{2,1,0:T(8,128)(2,1)S(1)}, u32[]{:S(2)}, u32[]{:S(2)}) async-start(bf16[16,64,256]{2,1,0:T(8,128)(2,1)} %bitcast.9), calls=%async_computation | async-start | bytes 1048576 | tf_op jit(solution)/shard_map/all_to_all | solution.py:151
  55.6 13.7 %all-to-all-done = bf16[16,64,256]{2,1,0:T(8,128)(2,1)S(1)} async-done(((bf16[16,64,256]{2,1,0:T(8,128)(2,1)}), bf16[16,64,256]{2,1,0:T(8,128)(2,1)S(1)}, u32[]{:S(2)}, u32[]{:S(2)}) %all-to-all-start) | async-done | bytes 524320 | tf_op jit(solution)/shard_map/all_to_all | solution.py:151
  69.5 1.5 %collective-permute-done.4 = bf16[8,64,256]{2,1,0:T(8,128)(2,1)S(1)} collective-permute-done((bf16[8,64,256]{2,1,0:T(8,128)(2,1)S(1)}, bf16[8,64,256]{2,1,0:T(8,128)(2,1)S(1)}, u32[]{:S(2)}, u32[]{:S(2)}) %collective-permute-start.4) | collective-permute-done | bytes 262176 | tf_op jit(solution)/shard_map/ppermute | solution.py:155
  71.1 0.8 %copy.10 = f32[2,4,8,8,256]{4,3,2,1,0:T(8,128)} copy(f32[2,4,8,8,256]{4,3,1,0,2:T(8,128)S(1)} %bitcast.29) | data formatting | bytes 1048576 | tf_op jit(solution)/shard_map/transpose | solution.py:158
  (31 shorter events, 0.5 us)
Async XLA Ops:
  7.2 9.7 %copy-start.1 = (bf16[1,4,4096]{2,1,0:T(4,128)(2,1)}, bf16[1,4,4096]{2,1,0:T(4,128)(2,1)S(1)}, u32[]{:S(2)}) copy-start(bf16[1,4,4096]{2,1,0:T(4,128)(2,1)S(1)} %reshape.39.source_ref) | copy-start | bytes 98308
  7.2 9.6 %collective-permute-start = (bf16[1,4,4096]{2,1,0:T(4,128)(2,1)S(1)}, bf16[1,4,4096]{2,1,0:T(4,128)(2,1)S(1)}, u32[]{:S(2)}, u32[]{:S(2)}) collective-permute-start(bf16[1,4,4096]{2,1,0:T(4,128)(2,1)S(1)} %reshape.39.source_ref), channel_id=1, source_target_pairs={{0,16},{2,18},{4,20},{6,22},{8,24},{10,26},{12,28},{14,30},{16,0},... | collective-permute-start | bytes 98312 | tf_op jit(solution)/shard_map/ppermute | solution.py:138
  11.2 3.2 %copy-start.8 = (s32[64,1]{0,1:T(1,128)S(1)}, s32[64,1]{0,1:T(1,128)}, u32[]{:S(2)}) copy-start(s32[64,1]{0,1:T(1,128)} %param.6) | copy-start | bytes 772
  16.8 12.7 %copy-start.7 = (s32[2]{0:T(128)}, s32[2]{0:T(128)S(1)}, u32[]{:S(2)}) copy-start(s32[2]{0:T(128)S(1)} %get-tuple-element.9.ids_ref) | copy-start | bytes 28
  16.8 9.7 %copy-start.4 = (bf16[1,4,4096]{2,1,0:T(4,128)(2,1)}, bf16[1,4,4096]{2,1,0:T(4,128)(2,1)S(1)}, u32[]{:S(2)}) copy-start(bf16[1,4,4096]{2,1,0:T(4,128)(2,1)S(1)} %collective-permute-done.source_ref) | copy-start | bytes 98308
  16.9 4.3 %collective-permute-start.1 = (bf16[2,4,4096]{2,1,0:T(4,128)(2,1)S(1)}, bf16[2,4,4096]{2,1,0:T(4,128)(2,1)S(1)}, u32[]{:S(2)}, u32[]{:S(2)}) collective-permute-start(bf16[2,4,4096]{2,1,0:T(4,128)(2,1)S(1)} %maximum_select_fusion.5), channel_id=1, source_target_pairs={{0,8},{2,10},{4,12},{6,14},{8,0},{10,2},{12,4},{14,6},{16,24},{18,... | collective-permute-start | bytes 196616 | tf_op jit(solution)/shard_map/ppermute | solution.py:138
  18.6 10.9 %copy-start.6 = (s32[4]{0:T(128)}, s32[4]{0:T(128)S(1)}, u32[]{:S(2)}) copy-start(s32[4]{0:T(128)S(1)} %get-tuple-element.7.ids_ref) | copy-start | bytes 52
  21.2 8.3 %copy-start.2 = (bf16[2,4,4096]{2,1,0:T(4,128)(2,1)}, bf16[2,4,4096]{2,1,0:T(4,128)(2,1)S(1)}, u32[]{:S(2)}) copy-start(bf16[2,4,4096]{2,1,0:T(4,128)(2,1)S(1)} %collective-permute-done.1.source_ref) | copy-start | bytes 196612
  21.4 9.0 %collective-permute-start.2 = (bf16[4,4,4096]{2,1,0:T(4,128)(2,1)S(1)}, bf16[4,4,4096]{2,1,0:T(4,128)(2,1)S(1)}, u32[]{:S(2)}, u32[]{:S(2)}) collective-permute-start(bf16[4,4,4096]{2,1,0:T(4,128)(2,1)S(1)} %maximum_select_fusion.3), channel_id=1, source_target_pairs={{0,4},{2,6},{4,0},{6,2},{8,12},{10,14},{12,8},{14,10},{16,20},{18,... | collective-permute-start | bytes 393224 | tf_op jit(solution)/shard_map/ppermute | solution.py:138
  26.5 3.0 %copy-start.5 = (bf16[1,64,256]{2,1,0:T(8,128)(2,1)S(1)}, bf16[1,64,256]{2,1,0:T(8,128)(2,1)}, u32[]{:S(2)}) copy-start(bf16[1,64,256]{2,1,0:T(8,128)(2,1)} %shard_map.50) | copy-start | bytes 98308
  30.4 6.8 %copy-start = (bf16[4,4,4096]{2,1,0:T(4,128)(2,1)}, bf16[4,4,4096]{2,1,0:T(4,128)(2,1)S(1)}, u32[]{:S(2)}) copy-start(bf16[4,4,4096]{2,1,0:T(4,128)(2,1)S(1)} %collective-permute-done.2.source_ref) | copy-start | bytes 393220
  30.7 12.3 %collective-permute-start.3 = (bf16[8,4,4096]{2,1,0:T(4,128)(2,1)S(1)}, bf16[8,4,4096]{2,1,0:T(4,128)(2,1)S(1)}, u32[]{:S(2)}, u32[]{:S(2)}) collective-permute-start(bf16[8,4,4096]{2,1,0:T(4,128)(2,1)S(1)} %maximum_select_fusion.1), channel_id=1, source_target_pairs={{0,2},{2,0},{4,6},{6,4},{8,10},{10,8},{12,14},{14,12},{16,18},{18,... | collective-permute-start | bytes 786440 | tf_op jit(solution)/shard_map/ppermute | solution.py:138
  43.0 0.7 copy-start.3
  52.0 17.3 %all-to-all-start = ((bf16[16,64,256]{2,1,0:T(8,128)(2,1)}), bf16[16,64,256]{2,1,0:T(8,128)(2,1)S(1)}, u32[]{:S(2)}, u32[]{:S(2)}) async-start(bf16[16,64,256]{2,1,0:T(8,128)(2,1)} %bitcast.9), calls=%async_computation | async-start | bytes 1048576 | tf_op jit(solution)/shard_map/all_to_all | solution.py:151
  69.4 1.6 %collective-permute-start.4 = (bf16[8,64,256]{2,1,0:T(8,128)(2,1)S(1)}, bf16[8,64,256]{2,1,0:T(8,128)(2,1)S(1)}, u32[]{:S(2)}, u32[]{:S(2)}) collective-permute-start(bf16[8,64,256]{2,1,0:T(8,128)(2,1)S(1)} %constant_dynamic-slice_fusion), channel_id=1, source_target_pairs={{0,1},{1,0},{2,3},{3,2},{4,5},{5,4},{6,7},{7,6},{8,9},{9,8},{10,11... | collective-permute-start | bytes 786440 | tf_op jit(solution)/shard_map/ppermute | solution.py:155

commit v7 on v5

--- a/solution.py
+++ b/solution.py
@@ -95,15 +95,11 @@
     offsets = blocks // 4
     band = lax.axis_index("band")
 
+    source_float = sources.astype(jnp.float32)
+    source_sums = jnp.sum(source_float * source_float, axis=(1, 2))
+    source_power = source_sums + lax.ppermute(source_sums, "band", [(0, 1), (1, 0)])
     trace_float = traces.astype(jnp.float32)
-    source_float = sources.astype(jnp.float32)
-    trace_power, source_power = lax.psum(
-        (
-            jnp.sum(trace_float * trace_float, axis=(1, 2)),
-            jnp.sum(source_float * source_float, axis=(1, 2)),
-        ),
-        "band",
-    )
+    trace_power = lax.psum(jnp.sum(trace_float * trace_float, axis=(1, 2)), "band")
     white_sources = (
         source_float * lax.rsqrt(source_power / (2 * BINS) + EPS)[:, None, None]
     ).astype(jnp.bfloat16)

time: 62.2 us -> 65.3 us (1.050)
  starting transfers between devices: 14.7 us -> 17.6 us
  waiting for transfers between devices: 21.1 us -> 22.1 us
  other arithmetic: 9.77 us -> 9.07 us
    all_to_all x1, starting transfers between devices: 5.84 us -> 7.5 us  [per_device(): lax.all_to_all(partial, 'blk', split_axis=0, concat_axis=0, tiled=True)]
    all_to_all x1, waiting for transfers between devices: 10.8 us -> 11.7 us  [per_device(): lax.all_to_all(partial, 'blk', split_axis=0, concat_axis=0, tiled=True)]
    ppermute x4, starting transfers between devices: 8.77 us -> 9.58 us  [per_device(): got = lax.ppermute(held, 'blk', [(i, i ^ step) for i in range(blocks)])]
    broadcast_in_dim x1, other arithmetic: 0.85 us -> 0.09 us  [per_device(): held = white_sources[None]]
  transfers between devices with their start and end apart: 6 -> 7, of which waited for: 5 -> 6; matrix products, arithmetic and copies ran while one was open for 9% -> 13% of each run, Pallas kernels for 0% -> 0%
where the time goes in v7:
time: 65.3 us; the launch traced here: 64.9 us
  waiting for transfers between devices  22.1 us (34%)
  starting transfers between devices  17.6 us (27%)
  other arithmetic  9.07 us (14%)
  Pallas kernels  8.64 us (13%)
  local copies, waits for them, and re-layouts  2.86 us (4%)
  blocking collectives  2.45 us (4%)
  matrix products  2.04 us (3%)
    all_to_all x1, waiting for transfers between devices, per_device(): lax.all_to_all(partial, 'blk', split_axis=0, concat_axis=0, tiled=True)  11.7 us
    ppermute x4, starting transfers between devices, per_device(): got = lax.ppermute(held, 'blk', [(i, i ^ step) for i in range(blocks)])  9.58 us
    ppermute x4, waiting for transfers between devices, per_device(): got = lax.ppermute(held, 'blk', [(i, i ^ step) for i in range(blocks)])  8.93 us
    pallas_call x1, Pallas kernels, correlate(): pl.pallas_call(body, grid=(blocks // group,), in_specs=[pl.BlockSpec(plac...  8.64 us
    all_to_all x1, starting transfers between devices, per_device(): lax.all_to_all(partial, 'blk', split_axis=0, concat_axis=0, tiled=True)  7.5 us
    reduce_sum x1, other arithmetic, per_device(): jnp.sum(trace_float * trace_float, axis=(1, 2))  2.81 us
    convert_element_type x1, other arithmetic, per_device(): white_traces = (trace_float * lax.rsqrt(trace_power / (2 * BINS) + EPS)[:...  2.66 us
    psum x1, blocking collectives, per_device(): lax.psum(jnp.sum(trace_float * trace_float, axis=(1, 2)), 'band')  2.45 us
  transfers between devices with their start and end apart: 7, of which 6 were waited for; matrix products, arithmetic and copies ran while one was open for 13% of the time, Pallas kernels for 0%

profile of v7, /device:TPU:0, one launch (start us, length us, event | category | flops | bytes accessed | tf_op | source)
XLA Modules:
  0.0 64.9 jit_solution(7426862014136230949)
XLA Ops:
  0.0 1.0 %fusion.2 = f32[2]{0:T(128)S(1)} fusion(bf16[2,2,4096]{2,1,0:T(2,128)(2,1)} %param.5), kind=kLoop, calls=%fused_computation.14 | loop fusion | flops 49150 | bytes 32776 | tf_op jit(solution)/shard_map/reduce_sum | solution.py:99
  1.0 0.5 collective-permute-start
  1.4 2.8 %fusion = f32[64]{0:T(128)S(1)} fusion(bf16[64,2,4096]{2,1,0:T(2,128)(2,1)} %param.4), kind=kLoop, calls=%fused_computation.3 | loop fusion | flops 1572800 | bytes 1048832 | tf_op jit(solution)/shard_map/reduce_sum | solution.py:102
  4.2 2.5 %psum.7 = f32[64]{0:T(128)S(1)} all-reduce(f32[64]{0:T(128)S(1)} %fusion), channel_id=1, replica_groups=mesh['blk'=16,'band'=2] {'band'}, use_global_device_ids=true, to_apply=%region_3.4 | all-reduce | flops 64 | bytes 512 | tf_op jit(solution)/shard_map/psum | solution.py:102
  6.7 2.7 %fusion.1 = bf16[64,2,4096]{2,1,0:T(2,128)(2,1)S(1)} fusion(bf16[64,2,4096]{2,1,0:T(2,128)(2,1)} %param.4, f32[64]{0:T(128)S(1)} %add_rsqrt_fusion.1), kind=kLoop, calls=%fused_computation.4 | loop fusion | flops 1572864 | bytes 2097408 | tf_op jit(solution)/shard_map/convert_element_type | solution.py:118
  9.4 0.1 fusion.6
  9.5 3.8 %collective-permute-start.1 = (bf16[1,2,2,4096]{3,2,1,0:T(2,128)(2,1)S(1)}, bf16[1,2,2,4096]{3,2,1,0:T(2,128)(2,1)S(1)}, u32[]{:S(2)}, u32[]{:S(2)}) collective-permute-start(bf16[1,2,2,4096]{3,2,1,0:T(2,128)(2,1)S(1)} %fusion.6), channel_id=1, source_target_pairs={{0,16},{2,18},{4,20},{6,22},{8,24},{10,26},{12,28},{14,30},{16,0},... | collective-permute-start | bytes 98312 | tf_op jit(solution)/shard_map/ppermute | solution.py:111
  13.3 0.1 fusion.5
  13.4 0.6 copy.7
  14.0 0.1 reduce_window_sum.11
  14.1 1.1 %collective-permute-done.1 = bf16[1,2,2,4096]{3,2,1,0:T(2,128)(2,1)S(1)} collective-permute-done((bf16[1,2,2,4096]{3,2,1,0:T(2,128)(2,1)S(1)}, bf16[1,2,2,4096]{3,2,1,0:T(2,128)(2,1)S(1)}, u32[]{:S(2)}, u32[]{:S(2)}) %collective-permute-start.1) | collective-permute-done | bytes 32800 | tf_op jit(solution)/shard_map/ppermute | solution.py:111
  15.2 0.1 broadcast_select_fusion.3
  15.3 2.0 %collective-permute-start.2 = (bf16[2,2,2,4096]{3,2,1,0:T(2,128)(2,1)S(1)}, bf16[2,2,2,4096]{3,2,1,0:T(2,128)(2,1)S(1)}, u32[]{:S(2)}, u32[]{:S(2)}) collective-permute-start(bf16[2,2,2,4096]{3,2,1,0:T(2,128)(2,1)S(1)} %broadcast_select_fusion.3), channel_id=1, source_target_pairs={{0,8},{2,10},{4,12},{6,14},{8,0},{10,2},{12,4},{14,6},{16,24},{18,... | collective-permute-start | bytes 196616 | tf_op jit(solution)/shard_map/ppermute | solution.py:111
  17.3 0.2 select_reduce_fusion
  17.5 2.2 %collective-permute-done.2 = bf16[2,2,2,4096]{3,2,1,0:T(2,128)(2,1)S(1)} collective-permute-done((bf16[2,2,2,4096]{3,2,1,0:T(2,128)(2,1)S(1)}, bf16[2,2,2,4096]{3,2,1,0:T(2,128)(2,1)S(1)}, u32[]{:S(2)}, u32[]{:S(2)}) %collective-permute-start.2) | collective-permute-done | bytes 65568 | tf_op jit(solution)/shard_map/ppermute | solution.py:111
  19.6 0.3 broadcast_select_fusion.2
  19.9 1.9 %collective-permute-start.3 = (bf16[4,2,2,4096]{3,2,1,0:T(2,128)(2,1)S(1)}, bf16[4,2,2,4096]{3,2,1,0:T(2,128)(2,1)S(1)}, u32[]{:S(2)}, u32[]{:S(2)}) collective-permute-start(bf16[4,2,2,4096]{3,2,1,0:T(2,128)(2,1)S(1)} %broadcast_select_fusion.2), channel_id=1, source_target_pairs={{0,4},{2,6},{4,0},{6,2},{8,12},{10,14},{12,8},{14,10},{16,20},{18,... | collective-permute-start | bytes 393224 | tf_op jit(solution)/shard_map/ppermute | solution.py:111
  21.9 3.1 %collective-permute-done.3 = bf16[4,2,2,4096]{3,2,1,0:T(2,128)(2,1)S(1)} collective-permute-done((bf16[4,2,2,4096]{3,2,1,0:T(2,128)(2,1)S(1)}, bf16[4,2,2,4096]{3,2,1,0:T(2,128)(2,1)S(1)}, u32[]{:S(2)}, u32[]{:S(2)}) %collective-permute-start.3) | collective-permute-done | bytes 131104 | tf_op jit(solution)/shard_map/ppermute | solution.py:111
  25.0 0.6 broadcast_select_fusion.1
  25.6 1.9 %collective-permute-start.4 = (bf16[8,2,2,4096]{3,2,1,0:T(2,128)(2,1)S(1)}, bf16[8,2,2,4096]{3,2,1,0:T(2,128)(2,1)S(1)}, u32[]{:S(2)}, u32[]{:S(2)}) collective-permute-start(bf16[8,2,2,4096]{3,2,1,0:T(2,128)(2,1)S(1)} %broadcast_select_fusion.1), channel_id=1, source_target_pairs={{0,2},{2,0},{4,6},{6,4},{8,10},{10,8},{12,14},{14,12},{16,18},{18,... | collective-permute-start | bytes 786440 | tf_op jit(solution)/shard_map/ppermute | solution.py:111
  27.4 2.0 %convolution_convert_fusion = bf16[128,8192]{1,0:T(8,128)(2,1)} fusion(bf16[64,8192]{1,0:T(8,128)(2,1)S(1)} %bitcast.24, s32[64]{0:T(128)S(1)} %multiply_add_fusion), kind=kOutput, calls=%fused_computation | convolution fusion | flops 135274496 | bytes 3145984 | tf_op jit(solution)/shard_map/dot_general | solution.py:130
  29.5 2.5 %collective-permute-done.4 = bf16[8,2,2,4096]{3,2,1,0:T(2,128)(2,1)S(1)} collective-permute-done((bf16[8,2,2,4096]{3,2,1,0:T(2,128)(2,1)S(1)}, bf16[8,2,2,4096]{3,2,1,0:T(2,128)(2,1)S(1)}, u32[]{:S(2)}, u32[]{:S(2)}) %collective-permute-start.4) | collective-permute-done | bytes 262176 | tf_op jit(solution)/shard_map/ppermute | solution.py:111
  32.0 1.2 %broadcast_select_fusion = bf16[16,2,2,4096]{3,2,1,0:T(2,128)(2,1)S(1)} fusion(pred[]{:T(512)S(6)} %eq.44, bf16[8,2,2,4096]{3,2,1,0:T(2,128)(2,1)S(1)} %broadcast_select_fusion.1, bf16[8,2,2,4096]{3,2,1,0:T(2,128)(2,1)S(1)} %collective-permute-done.4), kind=kLoop, calls=%fused_computation.5 | loop fusion | flops 786432 | bytes 1048577 | tf_op jit(solution)/shard_map/jit(_where)/select_n | solution.py:113
  33.1 0.4 copy.11
  33.6 1.0 %reshape.36.source_ref = bf16[16,4,4096]{2,1,0:T(4,128)(2,1)} reshape(bf16[2,2,2,2,2,2,4096]{6,5,4,3,2,1,0:T(2,128)(2,1)S(1)} %bitcast.27) | data formatting | bytes 1048576 | tf_op jit(solution)/shard_map/reshape | solution.py:136
  34.6 8.6 %shard_map.46 = bf16[16,64,256]{2,1,0:T(8,128)(2,1)} custom-call(bf16[16,16,4096]{2,1,0:T(8,128)(2,1)} %bitcast.22, bf16[16,4,4096]{2,1,0:T(4,128)(2,1)} %reshape.36.source_ref, bf16[2048,256]{1,0:T(8,128)(2,1)} %constant.73.clone.table_ref), custom_call_target="tpu_custom_call" | custom-call | flops 1107296256 | bytes 4194304 | tf_op jit(solution)/shard_map/pallas_call | solution.py:59
  43.2 7.5 %all-to-all-start = ((bf16[16,64,256]{2,1,0:T(8,128)(2,1)}), bf16[16,64,256]{2,1,0:T(8,128)(2,1)S(1)}, u32[]{:S(2)}, u32[]{:S(2)}) async-start(bf16[16,64,256]{2,1,0:T(8,128)(2,1)} %shard_map.46), calls=%async_computation | async-start | bytes 1048576 | tf_op jit(solution)/shard_map/all_to_all | solution.py:139
  50.7 11.7 %all-to-all-done = bf16[16,64,256]{2,1,0:T(8,128)(2,1)S(1)} async-done(((bf16[16,64,256]{2,1,0:T(8,128)(2,1)}), bf16[16,64,256]{2,1,0:T(8,128)(2,1)S(1)}, u32[]{:S(2)}, u32[]{:S(2)}) %all-to-all-start) | async-done | bytes 524320 | tf_op jit(solution)/shard_map/all_to_all | solution.py:139
  62.4 0.1 collective-permute-start.5
  62.5 1.5 %collective-permute-done.5 = bf16[8,64,256]{2,1,0:T(8,128)(2,1)S(1)} collective-permute-done((bf16[8,64,256]{2,1,0:T(8,128)(2,1)S(1)}, bf16[8,64,256]{2,1,0:T(8,128)(2,1)S(1)}, u32[]{:S(2)}, u32[]{:S(2)}) %collective-permute-start.5) | collective-permute-done | bytes 262176 | tf_op jit(solution)/shard_map/ppermute | solution.py:143
  64.0 0.1 convert_add_fusion
  64.1 0.8 %copy.10 = f32[2,4,8,8,256]{4,3,2,1,0:T(8,128)} copy(f32[2,4,8,8,256]{4,3,1,0,2:T(8,128)S(1)} %bitcast.26) | data formatting | bytes 1048576 | tf_op jit(solution)/shard_map/transpose | solution.py:146
  (9 shorter events, 0.0 us)
Async XLA Ops:
  0.0 9.4 %copy-start = (bf16[2,2,4096]{2,1,0:T(2,128)(2,1)S(1)}, bf16[2,2,4096]{2,1,0:T(2,128)(2,1)}, u32[]{:S(2)}) copy-start(bf16[2,2,4096]{2,1,0:T(2,128)(2,1)} %param.5) | copy-start | bytes 98308
  0.0 13.3 %copy-start.1 = (s32[64,1]{0,1:T(1,128)S(1)}, s32[64,1]{0,1:T(1,128)}, u32[]{:S(2)}) copy-start(s32[64,1]{0,1:T(1,128)} %param.6) | copy-start | bytes 772
  1.0 8.4 %collective-permute-start = (f32[2]{0:T(128)S(1)}, f32[2]{0:T(128)S(1)}, u32[]{:S(2)}, u32[]{:S(2)}) collective-permute-start(f32[2]{0:T(128)S(1)} %fusion.2), channel_id=1, source_target_pairs={{0,1},{1,0},{2,3},{3,2},{4,5},{5,4},{6,7},{7,6},{8,9},{9,8},{10,11... | collective-permute-start | bytes 32 | tf_op jit(solution)/shard_map/ppermute | solution.py:100
  9.5 5.7 %collective-permute-start.1 = (bf16[1,2,2,4096]{3,2,1,0:T(2,128)(2,1)S(1)}, bf16[1,2,2,4096]{3,2,1,0:T(2,128)(2,1)S(1)}, u32[]{:S(2)}, u32[]{:S(2)}) collective-permute-start(bf16[1,2,2,4096]{3,2,1,0:T(2,128)(2,1)S(1)} %fusion.6), channel_id=1, source_target_pairs={{0,16},{2,18},{4,20},{6,22},{8,24},{10,26},{12,28},{14,30},{16,0},... | collective-permute-start | bytes 98312 | tf_op jit(solution)/shard_map/ppermute | solution.py:111
  15.3 4.3 %collective-permute-start.2 = (bf16[2,2,2,4096]{3,2,1,0:T(2,128)(2,1)S(1)}, bf16[2,2,2,4096]{3,2,1,0:T(2,128)(2,1)S(1)}, u32[]{:S(2)}, u32[]{:S(2)}) collective-permute-start(bf16[2,2,2,4096]{3,2,1,0:T(2,128)(2,1)S(1)} %broadcast_select_fusion.3), channel_id=1, source_target_pairs={{0,8},{2,10},{4,12},{6,14},{8,0},{10,2},{12,4},{14,6},{16,24},{18,... | collective-permute-start | bytes 196616 | tf_op jit(solution)/shard_map/ppermute | solution.py:111
  19.9 5.0 %collective-permute-start.3 = (bf16[4,2,2,4096]{3,2,1,0:T(2,128)(2,1)S(1)}, bf16[4,2,2,4096]{3,2,1,0:T(2,128)(2,1)S(1)}, u32[]{:S(2)}, u32[]{:S(2)}) collective-permute-start(bf16[4,2,2,4096]{3,2,1,0:T(2,128)(2,1)S(1)} %broadcast_select_fusion.2), channel_id=1, source_target_pairs={{0,4},{2,6},{4,0},{6,2},{8,12},{10,14},{12,8},{14,10},{16,20},{18,... | collective-permute-start | bytes 393224 | tf_op jit(solution)/shard_map/ppermute | solution.py:111
  25.6 6.4 %collective-permute-start.4 = (bf16[8,2,2,4096]{3,2,1,0:T(2,128)(2,1)S(1)}, bf16[8,2,2,4096]{3,2,1,0:T(2,128)(2,1)S(1)}, u32[]{:S(2)}, u32[]{:S(2)}) collective-permute-start(bf16[8,2,2,4096]{3,2,1,0:T(2,128)(2,1)S(1)} %broadcast_select_fusion.1), channel_id=1, source_target_pairs={{0,2},{2,0},{4,6},{6,4},{8,10},{10,8},{12,14},{14,12},{16,18},{18,... | collective-permute-start | bytes 786440 | tf_op jit(solution)/shard_map/ppermute | solution.py:111
  43.2 19.2 %all-to-all-start = ((bf16[16,64,256]{2,1,0:T(8,128)(2,1)}), bf16[16,64,256]{2,1,0:T(8,128)(2,1)S(1)}, u32[]{:S(2)}, u32[]{:S(2)}) async-start(bf16[16,64,256]{2,1,0:T(8,128)(2,1)} %shard_map.46), calls=%async_computation | async-start | bytes 1048576 | tf_op jit(solution)/shard_map/all_to_all | solution.py:139
  62.4 1.6 %collective-permute-start.5 = (bf16[8,64,256]{2,1,0:T(8,128)(2,1)S(1)}, bf16[8,64,256]{2,1,0:T(8,128)(2,1)S(1)}, u32[]{:S(2)}, u32[]{:S(2)}) collective-permute-start(bf16[8,64,256]{2,1,0:T(8,128)(2,1)S(1)} %constant_dynamic-slice_fusion), channel_id=1, source_target_pairs={{0,1},{1,0},{2,3},{3,2},{4,5},{5,4},{6,7},{7,6},{8,9},{9,8},{10,11... | collective-permute-start | bytes 786440 | tf_op jit(solution)/shard_map/ppermute | solution.py:143

commit v8 on v5

--- a/solution.py
+++ b/solution.py
@@ -19,29 +19,41 @@
 EPS = 1e-06
 
 
-def correlate_kernel(blocks, offsets, capacity, group, norm_scale, placed_ref, source_ref, table_ref, out_ref, cross_ref):
+def correlate_kernel(blocks, offsets, capacity, group, norm_scale, counts_ref, placed_ref, source_ref, table_ref, out_ref, cross_ref):
     first = pl.program_id(0) * group
     folds = placed_ref.shape[2] // PERIOD
     rows = 2 * offsets * capacity
     for member in range(group):
         block = first + member
         for offset in range(offsets):
-            owned = placed_ref[lax.rem(block - offset + blocks, blocks)].astype(jnp.float32)
-            real_t = owned[:capacity]
-            imag_t = owned[capacity:]
-            for source in range(2):
-                real_s = source_ref[member, 2 * source : 2 * source + 1].astype(jnp.float32)
-                imag_s = source_ref[member, 2 * source + 1 : 2 * source + 2].astype(jnp.float32)
-                even = real_t * real_s + imag_t * imag_s
-                odd = real_t * imag_s - imag_t * real_s
-                even_fold = even[:, :PERIOD]
-                odd_fold = odd[:, :PERIOD]
-                for fold in range(1, folds):
-                    even_fold = even_fold + even[:, fold * PERIOD : (fold + 1) * PERIOD]
-                    odd_fold = odd_fold + odd[:, fold * PERIOD : (fold + 1) * PERIOD]
-                row = member * rows + (source * offsets + offset) * capacity
-                cross_ref[row : row + capacity, :PERIOD] = even_fold
-                cross_ref[row : row + capacity, PERIOD:] = odd_fold
+            owner_block = lax.rem(block - offset + blocks, blocks)
+            occupied = counts_ref[owner_block] > 0
+
+            @pl.when(occupied)
+            def _():
+                owned = placed_ref[owner_block].astype(jnp.float32)
+                real_t = owned[:capacity]
+                imag_t = owned[capacity:]
+                for source in range(2):
+                    real_s = source_ref[member, 2 * source : 2 * source + 1].astype(jnp.float32)
+                    imag_s = source_ref[member, 2 * source + 1 : 2 * source + 2].astype(jnp.float32)
+                    even = real_t * real_s + imag_t * imag_s
+                    odd = real_t * imag_s - imag_t * real_s
+                    even_fold = even[:, :PERIOD]
+                    odd_fold = odd[:, :PERIOD]
+                    for fold in range(1, folds):
+                        even_fold = even_fold + even[:, fold * PERIOD : (fold + 1) * PERIOD]
+                        odd_fold = odd_fold + odd[:, fold * PERIOD : (fold + 1) * PERIOD]
+                    row = member * rows + (source * offsets + offset) * capacity
+                    cross_ref[row : row + capacity, :PERIOD] = even_fold
+                    cross_ref[row : row + capacity, PERIOD:] = odd_fold
+
+            @pl.when(jnp.logical_not(occupied))
+            def _():
+                for source in range(2):
+                    row = member * rows + (source * offsets + offset) * capacity
+                    cross_ref[row : row + capacity, :] = jnp.zeros((capacity, 2 * PERIOD), jnp.float32)
+
     product = jnp.dot(
         cross_ref[...].astype(jnp.bfloat16), table_ref[...], preferred_element_type=jnp.float32
     )
@@ -50,7 +62,7 @@
         out_ref[member] = product[member * rows : (member + 1) * rows]
 
 
-def correlate(placed, white_sources, table, offsets, capacity):
+def correlate(counts, placed, white_sources, table, offsets, capacity):
     blocks, _, group_bins = placed.shape
     rows = 2 * offsets * capacity
     lags_out = table.shape[1]
@@ -58,21 +70,24 @@
     body = functools.partial(correlate_kernel, blocks, offsets, capacity, group, BINS ** (-0.5))
     return pl.pallas_call(
         body,
-        grid=(blocks // group,),
-        in_specs=[
-            pl.BlockSpec(placed.shape, lambda a: (0, 0, 0)),
-            pl.BlockSpec((group,) + white_sources.shape[1:], lambda a: (a, 0, 0)),
-            pl.BlockSpec(table.shape, lambda a: (0, 0)),
-        ],
-        out_specs=pl.BlockSpec((group, rows, lags_out), lambda a: (a, 0, 0)),
+        grid_spec=pltpu.PrefetchScalarGridSpec(
+            num_scalar_prefetch=1,
+            grid=(blocks // group,),
+            in_specs=[
+                pl.BlockSpec(placed.shape, lambda a, counts: (0, 0, 0)),
+                pl.BlockSpec((group,) + white_sources.shape[1:], lambda a, counts: (a, 0, 0)),
+                pl.BlockSpec(table.shape, lambda a, counts: (0, 0)),
+            ],
+            out_specs=pl.BlockSpec((group, rows, lags_out), lambda a, counts: (a, 0, 0)),
+            scratch_shapes=[pltpu.VMEM((group * rows, 2 * PERIOD), jnp.float32)],
+        ),
         out_shape=jax.ShapeDtypeStruct((blocks, rows, lags_out), jnp.bfloat16),
-        scratch_shapes=[pltpu.VMEM((group * rows, 2 * PERIOD), jnp.float32)],
         cost_estimate=pl.CostEstimate(
             flops=blocks * rows * 2 * PERIOD * lags_out * 2 + blocks * offsets * 16 * capacity * group_bins,
             bytes_accessed=placed.size * 2 + white_sources.size * 2 + table.size * 2 + blocks * rows * lags_out * 2,
             transcendentals=0,
         ),
-    )(placed, white_sources, table)
+    )(counts, placed, white_sources, table)
 
 
 def twiddle_table(lags_out):
@@ -139,7 +154,8 @@
 
     white_sources = held.reshape(blocks, source_count * 2, group_bins)
 
-    partial = correlate(placed, white_sources, table, offsets, capacity)
+    counts = jnp.sum(owner_hits, axis=0).astype(jnp.int32)
+    partial = correlate(counts, placed, white_sources, table, offsets, capacity)
     arrived = lax.all_to_all(partial, "blk", split_axis=0, concat_axis=0, tiled=True)
     half = blocks // 2
     mine = lax.dynamic_slice_in_dim(arrived, band * half, half, axis=0)

time: 62.2 us -> 67.1 us (1.079)
  Pallas kernels: 8.64 us -> 13.5 us
    pallas_call x1, Pallas kernels: 8.64 us -> 13.5 us  [correlate(): pl.pallas_call(body, grid_spec=pltpu.PrefetchScalarGridSpec(num_scalar_pr...]
where the time goes in v8:
time: 67.1 us; the launch traced here: 66.6 us
  waiting for transfers between devices  20.7 us (31%)
  starting transfers between devices  14.7 us (22%)
  Pallas kernels  13.5 us (20%)
  other arithmetic  10.2 us (15%)
  local copies, waits for them, and re-layouts  2.86 us (4%)
  blocking collectives  2.56 us (4%)
  matrix products  2.04 us (3%)
    pallas_call x1, Pallas kernels, correlate(): pl.pallas_call(body, grid_spec=pltpu.PrefetchScalarGridSpec(num_scalar_pr...  13.5 us
    all_to_all x1, waiting for transfers between devices, per_device(): lax.all_to_all(partial, 'blk', split_axis=0, concat_axis=0, tiled=True)  10.8 us
    ppermute x4, starting transfers between devices, per_device(): got = lax.ppermute(held, 'blk', [(i, i ^ step) for i in range(blocks)])  8.77 us
    ppermute x4, waiting for transfers between devices, per_device(): got = lax.ppermute(held, 'blk', [(i, i ^ step) for i in range(blocks)])  8.37 us
    all_to_all x1, starting transfers between devices, per_device(): lax.all_to_all(partial, 'blk', split_axis=0, concat_axis=0, tiled=True)  5.83 us
    reduce_sum x1, other arithmetic, per_device(): jnp.sum(trace_float * trace_float, axis=(1, 2))  2.82 us
    convert_element_type x1, other arithmetic, per_device(): white_traces = (trace_float * lax.rsqrt(trace_power / (2 * BINS) + EPS)[:...  2.66 us
    psum x1, blocking collectives, per_device(): lax.psum((jnp.sum(trace_float * trace_float, axis=(1, 2)), jnp.sum(source...  2.56 us
  transfers between devices with their start and end apart: 6, of which 5 were waited for; matrix products, arithmetic and copies ran while one was open for 9% of the time, Pallas kernels for 0%

profile of v8, /device:TPU:0, one launch (start us, length us, event | category | flops | bytes accessed | tf_op | source)
XLA Modules:
  0.0 66.6 jit_solution(15575827659024758285)
XLA Ops:
  0.0 2.8 %fusion = f32[64]{0:T(128)S(1)} fusion(bf16[64,2,4096]{2,1,0:T(2,128)(2,1)} %param.4), kind=kLoop, calls=%fused_computation.3 | loop fusion | flops 1572800 | bytes 1048832 | tf_op jit(solution)/shard_map/reduce_sum | solution.py:117
  2.8 0.9 %fusion.2 = f32[2]{0:T(128)S(1)} fusion(bf16[2,2,4096]{2,1,0:T(2,128)(2,1)} %param.5), kind=kLoop, calls=%fused_computation.14 | loop fusion | flops 49150 | bytes 32776 | tf_op jit(solution)/shard_map/reduce_sum | solution.py:118
  3.7 2.6 %all-reduce = (f32[64]{0:T(128)S(1)}, f32[2]{0:T(128)S(1)}) all-reduce(f32[64]{0:T(128)S(1)} %fusion, f32[2]{0:T(128)S(1)} %fusion.2), channel_id=1, replica_groups=mesh['blk'=16,'band'=2] {'band'}, use_global_device_ids=true, to_apply=%region_4.5 | all-reduce | flops 66 | bytes 528 | tf_op jit(solution)/shard_map/psum | solution.py:115
  6.3 0.9 %fusion.6 = bf16[1,2,2,4096]{3,2,1,0:T(2,128)(2,1)S(1)} fusion(f32[2]{0:T(128)S(1)} %add_rsqrt_fusion, bf16[2,2,4096]{2,1,0:T(2,128)(2,1)} %param.5), kind=kLoop, calls=%fused_computation.21 | loop fusion | flops 49152 | bytes 65544 | tf_op jit(solution)/shard_map/broadcast_in_dim | solution.py:126
  7.1 4.0 %collective-permute-start = (bf16[1,2,2,4096]{3,2,1,0:T(2,128)(2,1)S(1)}, bf16[1,2,2,4096]{3,2,1,0:T(2,128)(2,1)S(1)}, u32[]{:S(2)}, u32[]{:S(2)}) collective-permute-start(bf16[1,2,2,4096]{3,2,1,0:T(2,128)(2,1)S(1)} %fusion.6), channel_id=1, source_target_pairs={{0,16},{2,18},{4,20},{6,22},{8,24},{10,26},{12,28},{14,30},{16,0},... | collective-permute-start | bytes 98312 | tf_op jit(solution)/shard_map/ppermute | solution.py:130
  11.1 2.7 %fusion.1 = bf16[64,2,4096]{2,1,0:T(2,128)(2,1)S(1)} fusion(bf16[64,2,4096]{2,1,0:T(2,128)(2,1)} %param.4, f32[64]{0:T(128)S(1)} %add_rsqrt_fusion.1), kind=kLoop, calls=%fused_computation.4 | loop fusion | flops 1572864 | bytes 2097408 | tf_op jit(solution)/shard_map/convert_element_type | solution.py:137
  13.8 0.0 copy-done
  13.8 0.1 fusion.5
  13.9 0.1 reduce_window_sum.11
  14.0 0.6 copy.7
  14.6 0.0 collective-permute-done
  14.6 0.1 broadcast_select_fusion.3
  14.7 1.6 %collective-permute-start.1 = (bf16[2,2,2,4096]{3,2,1,0:T(2,128)(2,1)S(1)}, bf16[2,2,2,4096]{3,2,1,0:T(2,128)(2,1)S(1)}, u32[]{:S(2)}, u32[]{:S(2)}) collective-permute-start(bf16[2,2,2,4096]{3,2,1,0:T(2,128)(2,1)S(1)} %broadcast_select_fusion.3), channel_id=1, source_target_pairs={{0,8},{2,10},{4,12},{6,14},{8,0},{10,2},{12,4},{14,6},{16,24},{18,... | collective-permute-start | bytes 196616 | tf_op jit(solution)/shard_map/ppermute | solution.py:130
  16.4 0.6 select_reduce_fusion
  17.0 2.1 %collective-permute-done.1 = bf16[2,2,2,4096]{3,2,1,0:T(2,128)(2,1)S(1)} collective-permute-done((bf16[2,2,2,4096]{3,2,1,0:T(2,128)(2,1)S(1)}, bf16[2,2,2,4096]{3,2,1,0:T(2,128)(2,1)S(1)}, u32[]{:S(2)}, u32[]{:S(2)}) %collective-permute-start.1) | collective-permute-done | bytes 65568 | tf_op jit(solution)/shard_map/ppermute | solution.py:130
  19.1 0.3 broadcast_select_fusion.2
  19.4 1.6 %collective-permute-start.2 = (bf16[4,2,2,4096]{3,2,1,0:T(2,128)(2,1)S(1)}, bf16[4,2,2,4096]{3,2,1,0:T(2,128)(2,1)S(1)}, u32[]{:S(2)}, u32[]{:S(2)}) collective-permute-start(bf16[4,2,2,4096]{3,2,1,0:T(2,128)(2,1)S(1)} %broadcast_select_fusion.2), channel_id=1, source_target_pairs={{0,4},{2,6},{4,0},{6,2},{8,12},{10,14},{12,8},{14,10},{16,20},{18,... | collective-permute-start | bytes 393224 | tf_op jit(solution)/shard_map/ppermute | solution.py:130
  20.9 3.4 %collective-permute-done.2 = bf16[4,2,2,4096]{3,2,1,0:T(2,128)(2,1)S(1)} collective-permute-done((bf16[4,2,2,4096]{3,2,1,0:T(2,128)(2,1)S(1)}, bf16[4,2,2,4096]{3,2,1,0:T(2,128)(2,1)S(1)}, u32[]{:S(2)}, u32[]{:S(2)}) %collective-permute-start.2) | collective-permute-done | bytes 131104 | tf_op jit(solution)/shard_map/ppermute | solution.py:130
  24.4 0.6 broadcast_select_fusion.1
  25.0 1.6 %collective-permute-start.3 = (bf16[8,2,2,4096]{3,2,1,0:T(2,128)(2,1)S(1)}, bf16[8,2,2,4096]{3,2,1,0:T(2,128)(2,1)S(1)}, u32[]{:S(2)}, u32[]{:S(2)}) collective-permute-start(bf16[8,2,2,4096]{3,2,1,0:T(2,128)(2,1)S(1)} %broadcast_select_fusion.1), channel_id=1, source_target_pairs={{0,2},{2,0},{4,6},{6,4},{8,10},{10,8},{12,14},{14,12},{16,18},{18,... | collective-permute-start | bytes 786440 | tf_op jit(solution)/shard_map/ppermute | solution.py:130
  26.5 2.0 %convolution_convert_fusion = bf16[128,8192]{1,0:T(8,128)(2,1)} fusion(bf16[64,8192]{1,0:T(8,128)(2,1)S(1)} %bitcast.24, s32[64]{0:T(128)S(1)} %multiply_add_fusion), kind=kOutput, calls=%fused_computation | convolution fusion | flops 135274496 | bytes 3145984 | tf_op jit(solution)/shard_map/dot_general | solution.py:149
  28.6 2.8 %collective-permute-done.3 = bf16[8,2,2,4096]{3,2,1,0:T(2,128)(2,1)S(1)} collective-permute-done((bf16[8,2,2,4096]{3,2,1,0:T(2,128)(2,1)S(1)}, bf16[8,2,2,4096]{3,2,1,0:T(2,128)(2,1)S(1)}, u32[]{:S(2)}, u32[]{:S(2)}) %collective-permute-start.3) | collective-permute-done | bytes 262176 | tf_op jit(solution)/shard_map/ppermute | solution.py:130
  31.4 1.2 %broadcast_select_fusion = bf16[16,2,2,4096]{3,2,1,0:T(2,128)(2,1)S(1)} fusion(pred[]{:T(512)S(6)} %eq.47, bf16[8,2,2,4096]{3,2,1,0:T(2,128)(2,1)S(1)} %broadcast_select_fusion.1, bf16[8,2,2,4096]{3,2,1,0:T(2,128)(2,1)S(1)} %collective-permute-done.3), kind=kLoop, calls=%fused_computation.5 | loop fusion | flops 786432 | bytes 1048577 | tf_op jit(solution)/shard_map/jit(_where)/select_n | solution.py:132
  32.6 0.4 copy.11
  33.0 1.0 %reshape.36.source_ref = bf16[16,4,4096]{2,1,0:T(4,128)(2,1)} reshape(bf16[2,2,2,2,2,2,4096]{6,5,4,3,2,1,0:T(2,128)(2,1)S(1)} %bitcast.27) | data formatting | bytes 1048576 | tf_op jit(solution)/shard_map/reshape | solution.py:155
  34.0 13.5 %shard_map.46 = bf16[16,64,256]{2,1,0:T(8,128)(2,1)} custom-call(s32[16]{0:T(128)} %get-tuple-element.6.counts_ref, bf16[16,16,4096]{2,1,0:T(8,128)(2,1)} %bitcast.22, bf16[16,4,4096]{2,1,0:T(4,128)(2,1)} %reshape.36.source_ref, bf16[2048,256]{1,0:T(8,128)(2,1)} %constant.73.clone.table_ref), custom_call_target="tpu_custom_call" | custom-call | flops 1107296256 | bytes 4194304 | tf_op jit(solution)/shard_map/pallas_call | solution.py:71
  47.5 5.8 %all-to-all-start = ((bf16[16,64,256]{2,1,0:T(8,128)(2,1)}), bf16[16,64,256]{2,1,0:T(8,128)(2,1)S(1)}, u32[]{:S(2)}, u32[]{:S(2)}) async-start(bf16[16,64,256]{2,1,0:T(8,128)(2,1)} %shard_map.46), calls=%async_computation | async-start | bytes 1048576 | tf_op jit(solution)/shard_map/all_to_all | solution.py:159
  53.3 10.8 %all-to-all-done = bf16[16,64,256]{2,1,0:T(8,128)(2,1)S(1)} async-done(((bf16[16,64,256]{2,1,0:T(8,128)(2,1)}), bf16[16,64,256]{2,1,0:T(8,128)(2,1)S(1)}, u32[]{:S(2)}, u32[]{:S(2)}) %all-to-all-start) | async-done | bytes 524320 | tf_op jit(solution)/shard_map/all_to_all | solution.py:159
  64.1 0.1 collective-permute-start.4
  64.2 1.5 %collective-permute-done.4 = bf16[8,64,256]{2,1,0:T(8,128)(2,1)S(1)} collective-permute-done((bf16[8,64,256]{2,1,0:T(8,128)(2,1)S(1)}, bf16[8,64,256]{2,1,0:T(8,128)(2,1)S(1)}, u32[]{:S(2)}, u32[]{:S(2)}) %collective-permute-start.4) | collective-permute-done | bytes 262176 | tf_op jit(solution)/shard_map/ppermute | solution.py:163
  65.7 0.1 convert_add_fusion
  65.8 0.8 %copy.10 = f32[2,4,8,8,256]{4,3,2,1,0:T(8,128)} copy(f32[2,4,8,8,256]{4,3,1,0,2:T(8,128)S(1)} %bitcast.26) | data formatting | bytes 1048576 | tf_op jit(solution)/shard_map/transpose | solution.py:166
  (5 shorter events, 0.0 us)
Async XLA Ops:
  0.0 13.8 %copy-start = (s32[64,1]{0,1:T(1,128)S(1)}, s32[64,1]{0,1:T(1,128)}, u32[]{:S(2)}) copy-start(s32[64,1]{0,1:T(1,128)} %param.6) | copy-start | bytes 772
  7.1 7.5 %collective-permute-start = (bf16[1,2,2,4096]{3,2,1,0:T(2,128)(2,1)S(1)}, bf16[1,2,2,4096]{3,2,1,0:T(2,128)(2,1)S(1)}, u32[]{:S(2)}, u32[]{:S(2)}) collective-permute-start(bf16[1,2,2,4096]{3,2,1,0:T(2,128)(2,1)S(1)} %fusion.6), channel_id=1, source_target_pairs={{0,16},{2,18},{4,20},{6,22},{8,24},{10,26},{12,28},{14,30},{16,0},... | collective-permute-start | bytes 98312 | tf_op jit(solution)/shard_map/ppermute | solution.py:130
  14.7 4.3 %collective-permute-start.1 = (bf16[2,2,2,4096]{3,2,1,0:T(2,128)(2,1)S(1)}, bf16[2,2,2,4096]{3,2,1,0:T(2,128)(2,1)S(1)}, u32[]{:S(2)}, u32[]{:S(2)}) collective-permute-start(bf16[2,2,2,4096]{3,2,1,0:T(2,128)(2,1)S(1)} %broadcast_select_fusion.3), channel_id=1, source_target_pairs={{0,8},{2,10},{4,12},{6,14},{8,0},{10,2},{12,4},{14,6},{16,24},{18,... | collective-permute-start | bytes 196616 | tf_op jit(solution)/shard_map/ppermute | solution.py:130
  19.4 5.0 %collective-permute-start.2 = (bf16[4,2,2,4096]{3,2,1,0:T(2,128)(2,1)S(1)}, bf16[4,2,2,4096]{3,2,1,0:T(2,128)(2,1)S(1)}, u32[]{:S(2)}, u32[]{:S(2)}) collective-permute-start(bf16[4,2,2,4096]{3,2,1,0:T(2,128)(2,1)S(1)} %broadcast_select_fusion.2), channel_id=1, source_target_pairs={{0,4},{2,6},{4,0},{6,2},{8,12},{10,14},{12,8},{14,10},{16,20},{18,... | collective-permute-start | bytes 393224 | tf_op jit(solution)/shard_map/ppermute | solution.py:130
  25.0 6.4 %collective-permute-start.3 = (bf16[8,2,2,4096]{3,2,1,0:T(2,128)(2,1)S(1)}, bf16[8,2,2,4096]{3,2,1,0:T(2,128)(2,1)S(1)}, u32[]{:S(2)}, u32[]{:S(2)}) collective-permute-start(bf16[8,2,2,4096]{3,2,1,0:T(2,128)(2,1)S(1)} %broadcast_select_fusion.1), channel_id=1, source_target_pairs={{0,2},{2,0},{4,6},{6,4},{8,10},{10,8},{12,14},{14,12},{16,18},{18,... | collective-permute-start | bytes 786440 | tf_op jit(solution)/shard_map/ppermute | solution.py:130
  47.5 16.6 %all-to-all-start = ((bf16[16,64,256]{2,1,0:T(8,128)(2,1)}), bf16[16,64,256]{2,1,0:T(8,128)(2,1)S(1)}, u32[]{:S(2)}, u32[]{:S(2)}) async-start(bf16[16,64,256]{2,1,0:T(8,128)(2,1)} %shard_map.46), calls=%async_computation | async-start | bytes 1048576 | tf_op jit(solution)/shard_map/all_to_all | solution.py:159
  64.1 1.6 %collective-permute-start.4 = (bf16[8,64,256]{2,1,0:T(8,128)(2,1)S(1)}, bf16[8,64,256]{2,1,0:T(8,128)(2,1)S(1)}, u32[]{:S(2)}, u32[]{:S(2)}) collective-permute-start(bf16[8,64,256]{2,1,0:T(8,128)(2,1)S(1)} %constant_dynamic-slice_fusion), channel_id=1, source_target_pairs={{0,1},{1,0},{2,3},{3,2},{4,5},{5,4},{6,7},{7,6},{8,9},{9,8},{10,11... | collective-permute-start | bytes 786440 | tf_op jit(solution)/shard_map/ppermute | solution.py:163

commit v9 on v6

--- a/solution.py
+++ b/solution.py
@@ -25,15 +25,13 @@
     rows = 2 * offsets * capacity
     for member in range(group):
         block = ids_ref[first + member]
-        for source in range(2):
-            real_s = source_ref[member, 2 * source : 2 * source + 1].astype(jnp.float32)
-            imag_s = source_ref[member, 2 * source + 1 : 2 * source + 2].astype(jnp.float32)
-            real_s = jnp.broadcast_to(real_s, (capacity, real_s.shape[1]))
-            imag_s = jnp.broadcast_to(imag_s, (capacity, imag_s.shape[1]))
-            for offset in range(offsets):
-                owned = placed_ref[lax.rem(block - offset + blocks, blocks)].astype(jnp.float32)
-                real_t = owned[:capacity]
-                imag_t = owned[capacity:]
+        for offset in range(offsets):
+            owned = placed_ref[lax.rem(block - offset + blocks, blocks)].astype(jnp.float32)
+            real_t = owned[:capacity]
+            imag_t = owned[capacity:]
+            for source in range(2):
+                real_s = source_ref[member, 2 * source : 2 * source + 1].astype(jnp.float32)
+                imag_s = source_ref[member, 2 * source + 1 : 2 * source + 2].astype(jnp.float32)
                 even = real_t * real_s + imag_t * imag_s
                 odd = real_t * imag_s - imag_t * real_s
                 even_fold = even[:, :PERIOD]
@@ -101,13 +99,18 @@
     offsets = blocks // 4
     band = lax.axis_index("band")
 
+    trace_float = traces.astype(jnp.float32)
     source_float = sources.astype(jnp.float32)
-    source_power = lax.psum(jnp.sum(source_float * source_float, axis=(1, 2)), "band")
+    trace_power, source_power = lax.psum(
+        (
+            jnp.sum(trace_float * trace_float, axis=(1, 2)),
+            jnp.sum(source_float * source_float, axis=(1, 2)),
+        ),
+        "band",
+    )
     white_sources = (
         source_float * lax.rsqrt(source_power / (2 * BINS) + EPS)[:, None, None]
     ).astype(jnp.bfloat16).reshape(1, source_count * 2, group_bins)
-    trace_float = traces.astype(jnp.float32)
-    trace_power = lax.psum(jnp.sum(trace_float * trace_float, axis=(1, 2)), "band")
     white_traces = (
         (trace_float * lax.rsqrt(trace_power / (2 * BINS) + EPS)[:, None, None])
         .astype(jnp.bfloat16)
@@ -131,20 +134,21 @@
     me = lax.axis_index("blk")
     held = white_sources
     held_ids = me[None].astype(jnp.int32)
-    results = correlate(held_ids, placed, held, table, offsets, capacity)
     bits = blocks.bit_length() - 1
-    for bit in reversed(range(bits)):
+    for bit in reversed(range(1, bits)):
         step = 1 << bit
         got = lax.ppermute(held, "blk", [(i, i ^ step) for i in range(blocks)])
+        upper = jnp.bitwise_and(me // step, 1) == 1
+        held = jnp.where(upper, jnp.concatenate([got, held]), jnp.concatenate([held, got]))
         got_ids = jnp.bitwise_xor(held_ids, step)
-        got_results = correlate(got_ids, placed, got, table, offsets, capacity)
-        upper = jnp.bitwise_and(me // step, 1) == 1
-        if bit > 0:
-            held = jnp.where(upper, jnp.concatenate([got, held]), jnp.concatenate([held, got]))
-            held_ids = jnp.where(upper, jnp.concatenate([got_ids, held_ids]), jnp.concatenate([held_ids, got_ids]))
-        results = jnp.where(
-            upper, jnp.concatenate([got_results, results]), jnp.concatenate([results, got_results])
-        )
+        held_ids = jnp.where(upper, jnp.concatenate([got_ids, held_ids]), jnp.concatenate([held_ids, got_ids]))
+    got = lax.ppermute(held, "blk", [(i, i ^ 1) for i in range(blocks)])
+    results = correlate(held_ids, placed, held, table, offsets, capacity)
+    got_results = correlate(jnp.bitwise_xor(held_ids, 1), placed, got, table, offsets, capacity)
+    upper = jnp.bitwise_and(me, 1) == 1
+    results = jnp.where(
+        upper, jnp.concatenate([got_results, results]), jnp.concatenate([results, got_results])
+    )
     partial = results.reshape((2,) * bits + results.shape[1:])
     partial = partial.transpose(tuple(reversed(range(bits))) + tuple(range(bits, partial.ndim)))
     partial = partial.reshape(results.shape)

time: 72.6 us -> 63 us (0.87)
  Pallas kernels: 21.1 us -> 12.6 us
  other arithmetic: 12.7 us -> 10.1 us
  starting transfers between devices: 12.4 us -> 14.1 us
    pallas_call x5 -> x2, Pallas kernels: 21.1 us -> 12.6 us  [correlate(): pl.pallas_call(body, grid_spec=pltpu.PrefetchScalarGridSpec(num_scalar_pr...]
    select_n x4 -> x1, other arithmetic: 3.92 us -> 1.11 us  [per_device(): jnp.where(upper, jnp.concatenate([got_results, results]), jnp.concatenate...]
    ppermute x4 -> x3, waiting for transfers between devices: 2.62 us -> 4.73 us  [per_device(): got = lax.ppermute(held, 'blk', [(i, i ^ step) for i in range(blocks)])]
    all_to_all x1, waiting for transfers between devices: 13.7 us -> 11.7 us  [per_device(): lax.all_to_all(partial, 'blk', split_axis=0, concat_axis=0, tiled=True)]
    all_to_all x1, starting transfers between devices: 3.57 us -> 5.3 us  [per_device(): lax.all_to_all(partial, 'blk', split_axis=0, concat_axis=0, tiled=True)]
    ppermute x0 -> x1, starting transfers between devices: none -> 1.56 us  [per_device(): got = lax.ppermute(held, 'blk', [(i, i ^ 1) for i in range(blocks)])]
    ppermute x4 -> x3, starting transfers between devices: 8.76 us -> 7.21 us  [per_device(): got = lax.ppermute(held, 'blk', [(i, i ^ step) for i in range(blocks)])]
  transfers between devices with their start and end apart: 6 -> 6, of which waited for: 3 -> 4; matrix products, arithmetic and copies ran while one was open for 13% -> 10% of each run, Pallas kernels for 21% -> 10%
where the time goes in v9:
time: 63 us; the launch traced here: 62.6 us
  waiting for transfers between devices  18 us (29%)
  starting transfers between devices  14.1 us (22%)
  Pallas kernels  12.6 us (20%)
  other arithmetic  10.1 us (16%)
  local copies, waits for them, and re-layouts  3.02 us (5%)
  blocking collectives  2.56 us (4%)
  matrix products  2.03 us (3%)
    pallas_call x2, Pallas kernels, correlate(): pl.pallas_call(body, grid_spec=pltpu.PrefetchScalarGridSpec(num_scalar_pr...  12.6 us
    all_to_all x1, waiting for transfers between devices, per_device(): lax.all_to_all(partial, 'blk', split_axis=0, concat_axis=0, tiled=True)  11.7 us
    ppermute x3, starting transfers between devices, per_device(): got = lax.ppermute(held, 'blk', [(i, i ^ step) for i in range(blocks)])  7.21 us
    all_to_all x1, starting transfers between devices, per_device(): lax.all_to_all(partial, 'blk', split_axis=0, concat_axis=0, tiled=True)  5.3 us
    ppermute x3, waiting for transfers between devices, per_device(): got = lax.ppermute(held, 'blk', [(i, i ^ step) for i in range(blocks)])  4.73 us
    reduce_sum x1, other arithmetic, per_device(): jnp.sum(trace_float * trace_float, axis=(1, 2))  2.82 us
    convert_element_type x1, other arithmetic, per_device(): white_traces = (trace_float * lax.rsqrt(trace_power / (2 * BINS) + EPS)[:...  2.67 us
    psum x1, blocking collectives, per_device(): lax.psum((jnp.sum(trace_float * trace_float, axis=(1, 2)), jnp.sum(source...  2.56 us
  transfers between devices with their start and end apart: 6, of which 4 were waited for; matrix products, arithmetic and copies ran while one was open for 10% of the time, Pallas kernels for 10%

profile of v9, /device:TPU:0, one launch (start us, length us, event | category | flops | bytes accessed | tf_op | source)
XLA Modules:
  0.0 62.6 jit_solution(8353836838149905541)
XLA Ops:
  0.0 2.8 %fusion = f32[64]{0:T(128)S(1)} fusion(bf16[64,2,4096]{2,1,0:T(2,128)(2,1)} %param.4), kind=kLoop, calls=%fused_computation.3 | loop fusion | flops 1572800 | bytes 1048832 | tf_op jit(solution)/shard_map/reduce_sum | solution.py:106
  2.8 0.9 %fusion.2 = f32[2]{0:T(128)S(1)} fusion(bf16[2,2,4096]{2,1,0:T(2,128)(2,1)} %param.5), kind=kLoop, calls=%fused_computation.12 | loop fusion | flops 49150 | bytes 32776 | tf_op jit(solution)/shard_map/reduce_sum | solution.py:107
  3.7 2.6 %all-reduce = (f32[64]{0:T(128)S(1)}, f32[2]{0:T(128)S(1)}) all-reduce(f32[64]{0:T(128)S(1)} %fusion, f32[2]{0:T(128)S(1)} %fusion.2), channel_id=1, replica_groups=mesh['blk'=16,'band'=2] {'band'}, use_global_device_ids=true, to_apply=%region_3.0 | all-reduce | flops 66 | bytes 528 | tf_op jit(solution)/shard_map/psum | solution.py:104
  6.3 0.9 %fusion.3 = bf16[2,2,4096]{2,1,0:T(2,128)(2,1)S(1)} fusion(bf16[2,2,4096]{2,1,0:T(2,128)(2,1)} %param.5, f32[2]{0:T(128)S(1)} %add_rsqrt_fusion), kind=kLoop, calls=%fused_computation.13 | loop fusion | flops 49152 | bytes 65544 | tf_op jit(solution)/shard_map/convert_element_type | solution.py:113
  7.2 4.0 %collective-permute-start = (bf16[1,4,4096]{2,1,0:T(4,128)(2,1)S(1)}, bf16[1,4,4096]{2,1,0:T(4,128)(2,1)S(1)}, u32[]{:S(2)}, u32[]{:S(2)}) collective-permute-start(bf16[1,4,4096]{2,1,0:T(4,128)(2,1)S(1)} %reshape.39), channel_id=1, source_target_pairs={{0,16},{2,18},{4,20},{6,22},{8,24},{10,26},{12,28},{14,30},{16,0},... | collective-permute-start | bytes 98312 | tf_op jit(solution)/shard_map/ppermute | solution.py:140
  11.2 2.7 %fusion.1 = bf16[64,2,4096]{2,1,0:T(2,128)(2,1)S(1)} fusion(bf16[64,2,4096]{2,1,0:T(2,128)(2,1)} %param.4, f32[64]{0:T(128)S(1)} %add_rsqrt_fusion.1), kind=kLoop, calls=%fused_computation.4 | loop fusion | flops 1572864 | bytes 2097408 | tf_op jit(solution)/shard_map/convert_element_type | solution.py:116
  13.8 0.1 fusion.5
  13.9 0.1 reduce_window_sum.11
  14.0 0.2 select_reduce_fusion
  14.3 1.6 %collective-permute-start.1 = (bf16[2,4,4096]{2,1,0:T(4,128)(2,1)S(1)}, bf16[2,4,4096]{2,1,0:T(4,128)(2,1)S(1)}, u32[]{:S(2)}, u32[]{:S(2)}) collective-permute-start(bf16[2,4,4096]{2,1,0:T(4,128)(2,1)S(1)} %maximum_select_fusion.3), channel_id=1, source_target_pairs={{0,8},{2,10},{4,12},{6,14},{8,0},{10,2},{12,4},{14,6},{16,24},{18,... | collective-permute-start | bytes 196616 | tf_op jit(solution)/shard_map/ppermute | solution.py:140
  16.0 0.1 broadcast_xor_fusion.2
  16.0 2.6 %collective-permute-done.1 = bf16[2,4,4096]{2,1,0:T(4,128)(2,1)S(1)} collective-permute-done((bf16[2,4,4096]{2,1,0:T(4,128)(2,1)S(1)}, bf16[2,4,4096]{2,1,0:T(4,128)(2,1)S(1)}, u32[]{:S(2)}, u32[]{:S(2)}) %collective-permute-start.1) | collective-permute-done | bytes 65568 | tf_op jit(solution)/shard_map/ppermute | solution.py:140
  18.6 0.1 maximum_select_fusion.2
  18.8 1.6 %collective-permute-start.2 = (bf16[4,4,4096]{2,1,0:T(4,128)(2,1)S(1)}, bf16[4,4,4096]{2,1,0:T(4,128)(2,1)S(1)}, u32[]{:S(2)}, u32[]{:S(2)}) collective-permute-start(bf16[4,4,4096]{2,1,0:T(4,128)(2,1)S(1)} %maximum_select_fusion.2), channel_id=1, source_target_pairs={{0,4},{2,6},{4,0},{6,2},{8,12},{10,14},{12,8},{14,10},{16,20},{18,... | collective-permute-start | bytes 393224 | tf_op jit(solution)/shard_map/ppermute | solution.py:140
  20.4 0.1 broadcast_xor_fusion.1
  20.5 0.6 copy.8
  21.0 0.7 %broadcast_xor_fusion = (s32[8]{0:T(128)}, s32[8]{0:T(128)}) fusion(s32[4]{0:T(128)S(1)} %get-tuple-element.9, s32[4]{0:T(128)S(1)} %get-tuple-element.10, pred[]{:T(512)S(6)} %eq.39), kind=kLoop, calls=%fused_computation.27 | loop fusion | flops 32 | bytes 97 | tf_op jit(solution)/shard_map/xor | solution.py:147
  21.7 2.1 %collective-permute-done.2 = bf16[4,4,4096]{2,1,0:T(4,128)(2,1)S(1)} collective-permute-done((bf16[4,4,4096]{2,1,0:T(4,128)(2,1)S(1)}, bf16[4,4,4096]{2,1,0:T(4,128)(2,1)S(1)}, u32[]{:S(2)}, u32[]{:S(2)}) %collective-permute-start.2) | collective-permute-done | bytes 131104 | tf_op jit(solution)/shard_map/ppermute | solution.py:140
  23.8 0.3 maximum_select_fusion.1.source_ref
  24.1 1.6 %collective-permute-start.3 = (bf16[8,4,4096]{2,1,0:T(4,128)(2,1)S(1)}, bf16[8,4,4096]{2,1,0:T(4,128)(2,1)S(1)}, u32[]{:S(2)}, u32[]{:S(2)}) collective-permute-start(bf16[8,4,4096]{2,1,0:T(4,128)(2,1)S(1)} %maximum_select_fusion.1.source_ref), channel_id=1, source_target_pairs={{0,2},{2,0},{4,6},{6,4},{8,10},{10,8},{12,14},{14,12},{16,18},{18,... | collective-permute-start | bytes 786440 | tf_op jit(solution)/shard_map/ppermute | solution.py:145
  25.7 2.0 %convolution_convert_fusion = bf16[128,8192]{1,0:T(8,128)(2,1)} fusion(bf16[64,8192]{1,0:T(8,128)(2,1)S(1)} %bitcast.24, s32[64]{0:T(128)S(1)} %multiply_add_fusion), kind=kOutput, calls=%fused_computation | convolution fusion | flops 135274496 | bytes 3145984 | tf_op jit(solution)/shard_map/dot_general | solution.py:128
  27.7 6.3 %shard_map.47 = bf16[8,64,256]{2,1,0:T(8,128)(2,1)} custom-call(s32[8]{0:T(128)} %get-tuple-element.8.ids_ref, bf16[16,16,4096]{2,1,0:T(8,128)(2,1)} %bitcast.21, bf16[8,4,4096]{2,1,0:T(4,128)(2,1)} %copy-done, bf16[2048,256]{1,0:T(8,128)(2,1)} %constant.71.clone.table_ref), custom_call_target="tpu_custom_call" | custom-call | flops 553648128 | bytes 3670016 | tf_op jit(solution)/shard_map/pallas_call | solution.py:60
  34.0 0.7 %copy-done.2 = bf16[8,4,4096]{2,1,0:T(4,128)(2,1)} copy-done((bf16[8,4,4096]{2,1,0:T(4,128)(2,1)}, bf16[8,4,4096]{2,1,0:T(4,128)(2,1)S(1)}, u32[]{:S(2)}) %copy-start.2) | copy-done | bytes 262168
  34.7 6.3 %shard_map.46 = bf16[8,64,256]{2,1,0:T(8,128)(2,1)} custom-call(s32[8]{0:T(128)} %get-tuple-element.7.ids_ref, bf16[16,16,4096]{2,1,0:T(8,128)(2,1)} %bitcast.22, bf16[8,4,4096]{2,1,0:T(4,128)(2,1)} %copy-done.2, bf16[2048,256]{1,0:T(8,128)(2,1)} %constant.71.clone.table_ref), custom_call_target="tpu_custom_call" | custom-call | flops 553648128 | bytes 3670016 | tf_op jit(solution)/shard_map/pallas_call | solution.py:60
  41.0 1.1 %maximum_select_fusion = bf16[16,64,256]{2,1,0:T(8,128)(2,1)S(1)} fusion(bf16[8,64,256]{2,1,0:T(8,128)(2,1)S(1)} %copy-done.1, bf16[8,64,256]{2,1,0:T(8,128)(2,1)} %shard_map.46, pred[]{:T(512)S(6)} %eq.38), kind=kLoop, calls=%fused_computation.5 | loop fusion | flops 786432 | bytes 1048577 | tf_op jit(solution)/shard_map/jit(_where)/select_n | solution.py:149
  42.1 0.8 %copy.6 = bf16[2,2,2,2,64,256]{5,4,0,1,2,3:T(8,128)(2,1)} copy(bf16[2,2,2,2,64,256]{5,4,3,2,1,0:T(8,128)(2,1)S(1)} %bitcast.25) | data formatting | bytes 1048576 | tf_op jit(solution)/shard_map/jit(_where)/select_n | solution.py:149
  43.0 5.3 %all-to-all-start = ((bf16[16,64,256]{2,1,0:T(8,128)(2,1)}), bf16[16,64,256]{2,1,0:T(8,128)(2,1)S(1)}, u32[]{:S(2)}, u32[]{:S(2)}) async-start(bf16[16,64,256]{2,1,0:T(8,128)(2,1)} %bitcast.9), calls=%async_computation | async-start | bytes 1048576 | tf_op jit(solution)/shard_map/all_to_all | solution.py:155
  48.3 11.7 %all-to-all-done = bf16[16,64,256]{2,1,0:T(8,128)(2,1)S(1)} async-done(((bf16[16,64,256]{2,1,0:T(8,128)(2,1)}), bf16[16,64,256]{2,1,0:T(8,128)(2,1)S(1)}, u32[]{:S(2)}, u32[]{:S(2)}) %all-to-all-start) | async-done | bytes 524320 | tf_op jit(solution)/shard_map/all_to_all | solution.py:155
  60.1 0.1 collective-permute-start.4
  60.1 1.5 %collective-permute-done.4 = bf16[8,64,256]{2,1,0:T(8,128)(2,1)S(1)} collective-permute-done((bf16[8,64,256]{2,1,0:T(8,128)(2,1)S(1)}, bf16[8,64,256]{2,1,0:T(8,128)(2,1)S(1)}, u32[]{:S(2)}, u32[]{:S(2)}) %collective-permute-start.4) | collective-permute-done | bytes 262176 | tf_op jit(solution)/shard_map/ppermute | solution.py:159
  61.7 0.1 convert_add_fusion
  61.7 0.8 %copy.10 = f32[2,4,8,8,256]{4,3,2,1,0:T(8,128)} copy(f32[2,4,8,8,256]{4,3,1,0,2:T(8,128)S(1)} %bitcast.26) | data formatting | bytes 1048576 | tf_op jit(solution)/shard_map/transpose | solution.py:162
  (15 shorter events, 0.1 us)
Async XLA Ops:
  0.0 13.8 %copy-start.3 = (s32[64,1]{0,1:T(1,128)S(1)}, s32[64,1]{0,1:T(1,128)}, u32[]{:S(2)}) copy-start(s32[64,1]{0,1:T(1,128)} %param.6) | copy-start | bytes 772
  7.2 7.1 %collective-permute-start = (bf16[1,4,4096]{2,1,0:T(4,128)(2,1)S(1)}, bf16[1,4,4096]{2,1,0:T(4,128)(2,1)S(1)}, u32[]{:S(2)}, u32[]{:S(2)}) collective-permute-start(bf16[1,4,4096]{2,1,0:T(4,128)(2,1)S(1)} %reshape.39), channel_id=1, source_target_pairs={{0,16},{2,18},{4,20},{6,22},{8,24},{10,26},{12,28},{14,30},{16,0},... | collective-permute-start | bytes 98312 | tf_op jit(solution)/shard_map/ppermute | solution.py:140
  14.3 4.3 %collective-permute-start.1 = (bf16[2,4,4096]{2,1,0:T(4,128)(2,1)S(1)}, bf16[2,4,4096]{2,1,0:T(4,128)(2,1)S(1)}, u32[]{:S(2)}, u32[]{:S(2)}) collective-permute-start(bf16[2,4,4096]{2,1,0:T(4,128)(2,1)S(1)} %maximum_select_fusion.3), channel_id=1, source_target_pairs={{0,8},{2,10},{4,12},{6,14},{8,0},{10,2},{12,4},{14,6},{16,24},{18,... | collective-permute-start | bytes 196616 | tf_op jit(solution)/shard_map/ppermute | solution.py:140
  18.8 5.0 %collective-permute-start.2 = (bf16[4,4,4096]{2,1,0:T(4,128)(2,1)S(1)}, bf16[4,4,4096]{2,1,0:T(4,128)(2,1)S(1)}, u32[]{:S(2)}, u32[]{:S(2)}) collective-permute-start(bf16[4,4,4096]{2,1,0:T(4,128)(2,1)S(1)} %maximum_select_fusion.2), channel_id=1, source_target_pairs={{0,4},{2,6},{4,0},{6,2},{8,12},{10,14},{12,8},{14,10},{16,20},{18,... | collective-permute-start | bytes 393224 | tf_op jit(solution)/shard_map/ppermute | solution.py:140
  24.1 3.6 %copy-start = (bf16[8,4,4096]{2,1,0:T(4,128)(2,1)}, bf16[8,4,4096]{2,1,0:T(4,128)(2,1)S(1)}, u32[]{:S(2)}) copy-start(bf16[8,4,4096]{2,1,0:T(4,128)(2,1)S(1)} %maximum_select_fusion.1.source_ref) | copy-start | bytes 786436
  24.1 9.9 %collective-permute-start.3 = (bf16[8,4,4096]{2,1,0:T(4,128)(2,1)S(1)}, bf16[8,4,4096]{2,1,0:T(4,128)(2,1)S(1)}, u32[]{:S(2)}, u32[]{:S(2)}) collective-permute-start(bf16[8,4,4096]{2,1,0:T(4,128)(2,1)S(1)} %maximum_select_fusion.1.source_ref), channel_id=1, source_target_pairs={{0,2},{2,0},{4,6},{6,4},{8,10},{10,8},{12,14},{14,12},{16,18},{18,... | collective-permute-start | bytes 786440 | tf_op jit(solution)/shard_map/ppermute | solution.py:145
  34.0 7.0 %copy-start.1 = (bf16[8,64,256]{2,1,0:T(8,128)(2,1)S(1)}, bf16[8,64,256]{2,1,0:T(8,128)(2,1)}, u32[]{:S(2)}) copy-start(bf16[8,64,256]{2,1,0:T(8,128)(2,1)} %shard_map.47) | copy-start | bytes 786436
  34.0 0.7 %copy-start.2 = (bf16[8,4,4096]{2,1,0:T(4,128)(2,1)}, bf16[8,4,4096]{2,1,0:T(4,128)(2,1)S(1)}, u32[]{:S(2)}) copy-start(bf16[8,4,4096]{2,1,0:T(4,128)(2,1)S(1)} %collective-permute-done.3.source_ref) | copy-start | bytes 786436
  43.0 17.1 %all-to-all-start = ((bf16[16,64,256]{2,1,0:T(8,128)(2,1)}), bf16[16,64,256]{2,1,0:T(8,128)(2,1)S(1)}, u32[]{:S(2)}, u32[]{:S(2)}) async-start(bf16[16,64,256]{2,1,0:T(8,128)(2,1)} %bitcast.9), calls=%async_computation | async-start | bytes 1048576 | tf_op jit(solution)/shard_map/all_to_all | solution.py:155
  60.1 1.6 %collective-permute-start.4 = (bf16[8,64,256]{2,1,0:T(8,128)(2,1)S(1)}, bf16[8,64,256]{2,1,0:T(8,128)(2,1)S(1)}, u32[]{:S(2)}, u32[]{:S(2)}) collective-permute-start(bf16[8,64,256]{2,1,0:T(8,128)(2,1)S(1)} %constant_dynamic-slice_fusion), channel_id=1, source_target_pairs={{0,1},{1,0},{2,3},{3,2},{4,5},{5,4},{6,7},{7,6},{8,9},{9,8},{10,11... | collective-permute-start | bytes 786440 | tf_op jit(solution)/shard_map/ppermute | solution.py:159

commit v10 on v5

--- a/solution.py
+++ b/solution.py
@@ -110,13 +110,25 @@
     me = lax.axis_index("blk")
     held = white_sources[None]
     bits = blocks.bit_length() - 1
-    for bit in reversed(range(bits)):
-        step = 1 << bit
-        got = lax.ppermute(held, "blk", [(i, i ^ step) for i in range(blocks)])
-        upper = jnp.bitwise_and(me // step, 1) == 1
-        held = jnp.where(upper, jnp.concatenate([got, held]), jnp.concatenate([held, got]))
-    held = held.reshape((2,) * bits + held.shape[1:])
-    held = held.transpose(tuple(reversed(range(bits))) + tuple(range(bits, held.ndim)))
+    shift = bits
+    while shift > 0:
+        width = 2 if shift >= 2 else 1
+        shift -= width
+        radix = 1 << width
+        position = jnp.bitwise_and(me >> shift, radix - 1)
+        widened = jnp.zeros((radix,) + held.shape, held.dtype)
+        for partner in range(radix):
+            if partner == 0:
+                got = held
+            else:
+                route = [(i, i ^ (partner << shift)) for i in range(blocks)]
+                got = lax.ppermute(held, "blk", route)
+            widened = lax.dynamic_update_slice_in_dim(
+                widened, got[None], jnp.bitwise_xor(position, partner), axis=0
+            )
+        held = widened
+    groups = held.ndim - white_sources.ndim
+    held = held.transpose(tuple(reversed(range(groups))) + tuple(range(groups, held.ndim)))
     white_traces = (
         (trace_float * lax.rsqrt(trace_power / (2 * BINS) + EPS)[:, None, None])
         .astype(jnp.bfloat16)

time: 62.2 us -> 59.5 us (0.957)
  other arithmetic: 9.77 us -> 7.57 us
  waiting for transfers between devices: 21.1 us -> 19.9 us
  local copies, waits for them, and re-layouts: 2.86 us -> 3.51 us
    ppermute x4 -> x6, waiting for transfers between devices: 8.8 us -> 5.33 us  [per_device(): got = lax.ppermute(held, 'blk', route)]
    all_to_all x1, waiting for transfers between devices: 10.8 us -> 13.1 us  [per_device(): lax.all_to_all(partial, 'blk', split_axis=0, concat_axis=0, tiled=True)]
    select_n x4 -> x0, other arithmetic: 2.12 us -> none  [per_device(): jnp.where(upper, jnp.concatenate([got, held]), jnp.concatenate([held, got]))]
    dynamic_update_slice x0 -> x1, other arithmetic: none -> 0.88 us  [per_device(): lax.dynamic_update_slice_in_dim(widened, got[None], jnp.bitwise_xor(posit...]
    broadcast_in_dim x1 -> x0, other arithmetic: 0.85 us -> none  [per_device(): held = white_sources[None]]
    ppermute x4 -> x6, starting transfers between devices: 8.77 us -> 9.11 us  [per_device(): got = lax.ppermute(held, 'blk', route)]
  transfers between devices with their start and end apart: 6 -> 8, of which waited for: 5 -> 4; matrix products, arithmetic and copies ran while one was open for 9% -> 11% of each run, Pallas kernels for 0% -> 0%
where the time goes in v10:
time: 59.5 us; the launch traced here: 59.1 us
  waiting for transfers between devices  19.9 us (33%)
  starting transfers between devices  14.7 us (25%)
  Pallas kernels  8.64 us (15%)
  other arithmetic  7.57 us (13%)
  local copies, waits for them, and re-layouts  3.51 us (6%)
  blocking collectives  2.56 us (4%)
  matrix products  2.04 us (3%)
    all_to_all x1, waiting for transfers between devices, per_device(): lax.all_to_all(partial, 'blk', split_axis=0, concat_axis=0, tiled=True)  13.1 us
    ppermute x6, starting transfers between devices, per_device(): got = lax.ppermute(held, 'blk', route)  9.11 us
    pallas_call x1, Pallas kernels, correlate(): pl.pallas_call(body, grid=(blocks // group,), in_specs=[pl.BlockSpec(plac...  8.64 us
    all_to_all x1, starting transfers between devices, per_device(): lax.all_to_all(partial, 'blk', split_axis=0, concat_axis=0, tiled=True)  5.52 us
    ppermute x6, waiting for transfers between devices, per_device(): got = lax.ppermute(held, 'blk', route)  5.33 us
    reduce_sum x1, other arithmetic, per_device(): jnp.sum(trace_float * trace_float, axis=(1, 2))  2.81 us
    psum x1, blocking collectives, per_device(): lax.psum((jnp.sum(trace_float * trace_float, axis=(1, 2)), jnp.sum(source...  2.56 us
    convert_element_type x1, other arithmetic, per_device(): white_traces = (trace_float * lax.rsqrt(trace_power / (2 * BINS) + EPS)[:...  2.56 us
  transfers between devices with their start and end apart: 8, of which 4 were waited for; matrix products, arithmetic and copies ran while one was open for 11% of the time, Pallas kernels for 0%

profile of v10, /device:TPU:0, one launch (start us, length us, event | category | flops | bytes accessed | tf_op | source)
XLA Modules:
  0.0 59.1 jit_solution(2166461119006439143)
XLA Ops:
  0.0 2.8 %fusion = f32[64]{0:T(128)S(1)} fusion(bf16[64,2,4096]{2,1,0:T(2,128)(2,1)} %param.4), kind=kLoop, calls=%fused_computation.3 | loop fusion | flops 1572800 | bytes 1048832 | tf_op jit(solution)/shard_map/reduce_sum | solution.py:102
  2.8 0.9 %fusion.2 = f32[2]{0:T(128)S(1)} fusion(bf16[2,2,4096]{2,1,0:T(2,128)(2,1)} %param.5), kind=kLoop, calls=%fused_computation.13 | loop fusion | flops 49150 | bytes 32776 | tf_op jit(solution)/shard_map/reduce_sum | solution.py:103
  3.7 2.6 %all-reduce = (f32[64]{0:T(128)S(1)}, f32[2]{0:T(128)S(1)}) all-reduce(f32[64]{0:T(128)S(1)} %fusion, f32[2]{0:T(128)S(1)} %fusion.2), channel_id=1, replica_groups=mesh['blk'=16,'band'=2] {'band'}, use_global_device_ids=true, to_apply=%region_3.0 | all-reduce | flops 66 | bytes 528 | tf_op jit(solution)/shard_map/psum | solution.py:100
  6.3 0.1 broadcast_in_dim.36
  6.4 0.9 %bitcast_dynamic-update-slice_fusion.7 = (bf16[4,1,2,2,4096]{4,3,2,0,1:T(2,128)(2,1)S(1)}, bf16[2,2,4096]{2,1,0:T(2,128)(2,1)S(1)}) fusion(bf16[4,1,2,2,4096]{4,3,2,0,1:T(2,128)(2,1)S(1)} %broadcast_in_dim.36, s32[]{:T(128)S(6)} %select_n.30, f32[2]{0:T(128)S(1)} %add_rsqrt_fusion, bf16[2,2,4096]{2,1,0:T(2,128)(2,1)} %param.5), kind=kLoop, calls=%fused_computation.19 | loop fusion | flops 49152 | bytes 98820 | tf_op jit(solution)/shard_map/dynamic_update_slice | solution.py:126
  7.2 3.0 %collective-permute-start = (bf16[1,2,2,4096]{3,2,1,0:T(2,128)(2,1)S(1)}, bf16[1,2,2,4096]{3,2,1,0:T(2,128)(2,1)S(1)}, u32[]{:S(2)}, u32[]{:S(2)}) collective-permute-start(bf16[1,2,2,4096]{3,2,1,0:T(2,128)(2,1)S(1)} %bitcast.53), channel_id=1, source_target_pairs={{0,8},{2,10},{4,12},{6,14},{8,0},{10,2},{12,4},{14,6},{16,24},{18,... | collective-permute-start | bytes 98312 | tf_op jit(solution)/shard_map/ppermute | solution.py:125
  10.2 2.6 %collective-permute-start.1 = (bf16[1,2,2,4096]{3,2,1,0:T(2,128)(2,1)S(1)}, bf16[1,2,2,4096]{3,2,1,0:T(2,128)(2,1)S(1)}, u32[]{:S(2)}, u32[]{:S(2)}) collective-permute-start(bf16[1,2,2,4096]{3,2,1,0:T(2,128)(2,1)S(1)} %bitcast.54), channel_id=1, source_target_pairs={{0,16},{2,18},{4,20},{6,22},{8,24},{10,26},{12,28},{14,30},{16,0},... | collective-permute-start | bytes 98312 | tf_op jit(solution)/shard_map/ppermute | solution.py:125
  12.8 2.6 %fusion.1 = bf16[64,2,4096]{2,1,0:T(2,128)(2,1)S(1)} fusion(bf16[64,2,4096]{2,1,0:T(2,128)(2,1)} %param.4, f32[64]{0:T(128)S(1)} %add_rsqrt_fusion.1), kind=kLoop, calls=%fused_computation.4 | loop fusion | flops 1572864 | bytes 2097408 | tf_op jit(solution)/shard_map/convert_element_type | solution.py:134
  15.4 0.6 copy.13
  16.0 0.1 fusion.5
  16.0 0.1 reduce_window_sum.11
  16.1 0.2 select_reduce_fusion
  16.3 2.0 %convolution_convert_fusion = bf16[128,8192]{1,0:T(8,128)(2,1)} fusion(bf16[64,8192]{1,0:T(8,128)(2,1)S(1)} %bitcast.50, s32[64]{0:T(128)S(1)} %multiply_add_fusion), kind=kOutput, calls=%fused_computation | convolution fusion | flops 135274496 | bytes 3145984 | tf_op jit(solution)/shard_map/dot_general | solution.py:146
  18.5 0.0 collective-permute-done.2
  18.5 1.8 %collective-permute-start.3 = (bf16[4,1,2,2,4096]{4,3,2,0,1:T(2,128)(2,1)S(1)}, bf16[4,1,2,2,4096]{4,3,2,0,1:T(2,128)(2,1)S(1)}, u32[]{:S(2)}, u32[]{:S(2)}) collective-permute-start(bf16[4,1,2,2,4096]{4,3,2,0,1:T(2,128)(2,1)S(1)} %bitcast_dynamic-update-slice_fusion.4), channel_id=1, source_target_pairs={{0,2},{2,0},{4,6},{6,4},{8,10},{10,8},{12,14},{14,12},{16,18},{18,... | collective-permute-start | bytes 393224 | tf_op jit(solution)/shard_map/ppermute | solution.py:125
  20.3 1.5 %collective-permute-start.4 = (bf16[4,1,2,2,4096]{4,3,2,0,1:T(2,128)(2,1)S(1)}, bf16[4,1,2,2,4096]{4,3,2,0,1:T(2,128)(2,1)S(1)}, u32[]{:S(2)}, u32[]{:S(2)}) collective-permute-start(bf16[4,1,2,2,4096]{4,3,2,0,1:T(2,128)(2,1)S(1)} %bitcast_dynamic-update-slice_fusion.4), channel_id=1, source_target_pairs={{0,4},{2,6},{4,0},{6,2},{8,12},{10,14},{12,8},{14,10},{16,20},{18,... | collective-permute-start | bytes 393224 | tf_op jit(solution)/shard_map/ppermute | solution.py:125
  21.8 0.3 collective-permute-start.5
  22.1 0.5 broadcast_in_dim.35
  22.6 0.1 bitcast_dynamic-update-slice_fusion.2
  22.7 1.4 %collective-permute-done.3 = bf16[4,1,2,2,4096]{4,3,2,0,1:T(2,128)(2,1)S(1)} collective-permute-done((bf16[4,1,2,2,4096]{4,3,2,0,1:T(2,128)(2,1)S(1)}, bf16[4,1,2,2,4096]{4,3,2,0,1:T(2,128)(2,1)S(1)}, u32[]{:S(2)}, u32[]{:S(2)}) %collective-permute-start.3) | collective-permute-done | bytes 131104 | tf_op jit(solution)/shard_map/ppermute | solution.py:125
  24.0 0.1 bitcast_dynamic-update-slice_fusion.1
  24.2 3.9 %collective-permute-done.4 = bf16[4,1,2,2,4096]{4,3,2,0,1:T(2,128)(2,1)S(1)} collective-permute-done((bf16[4,1,2,2,4096]{4,3,2,0,1:T(2,128)(2,1)S(1)}, bf16[4,1,2,2,4096]{4,3,2,0,1:T(2,128)(2,1)S(1)}, u32[]{:S(2)}, u32[]{:S(2)}) %collective-permute-start.4) | collective-permute-done | bytes 131104 | tf_op jit(solution)/shard_map/ppermute | solution.py:125
  28.1 0.1 bitcast_dynamic-update-slice_fusion
  28.2 0.1 bitcast_dynamic-update-slice_fusion.3
  28.3 1.0 %reshape.31.source_ref = bf16[16,4,4096]{2,1,0:T(4,128)(2,1)} reshape(bf16[1,4,4,2,2,4096]{5,4,3,2,1,0:T(2,128)(2,1)S(1)} %bitcast.52) | data formatting | bytes 1048576 | tf_op jit(solution)/shard_map/reshape | solution.py:152
  29.3 8.6 %shard_map.46 = bf16[16,64,256]{2,1,0:T(8,128)(2,1)} custom-call(bf16[16,16,4096]{2,1,0:T(8,128)(2,1)} %bitcast.48, bf16[16,4,4096]{2,1,0:T(4,128)(2,1)} %reshape.31.source_ref, bf16[2048,256]{1,0:T(8,128)(2,1)} %constant.42.clone.table_ref), custom_call_target="tpu_custom_call" | custom-call | flops 1107296256 | bytes 4194304 | tf_op jit(solution)/shard_map/pallas_call | solution.py:59
  37.9 5.5 %all-to-all-start = ((bf16[16,64,256]{2,1,0:T(8,128)(2,1)}), bf16[16,64,256]{2,1,0:T(8,128)(2,1)S(1)}, u32[]{:S(2)}, u32[]{:S(2)}) async-start(bf16[16,64,256]{2,1,0:T(8,128)(2,1)} %shard_map.46), calls=%async_computation | async-start | bytes 1048576 | tf_op jit(solution)/shard_map/all_to_all | solution.py:155
  43.5 13.1 %all-to-all-done = bf16[16,64,256]{2,1,0:T(8,128)(2,1)S(1)} async-done(((bf16[16,64,256]{2,1,0:T(8,128)(2,1)}), bf16[16,64,256]{2,1,0:T(8,128)(2,1)S(1)}, u32[]{:S(2)}, u32[]{:S(2)}) %all-to-all-start) | async-done | bytes 524320 | tf_op jit(solution)/shard_map/all_to_all | solution.py:155
  56.6 0.1 collective-permute-start.6
  56.7 1.5 %collective-permute-done.6 = bf16[8,64,256]{2,1,0:T(8,128)(2,1)S(1)} collective-permute-done((bf16[8,64,256]{2,1,0:T(8,128)(2,1)S(1)}, bf16[8,64,256]{2,1,0:T(8,128)(2,1)S(1)}, u32[]{:S(2)}, u32[]{:S(2)}) %collective-permute-start.6) | collective-permute-done | bytes 262176 | tf_op jit(solution)/shard_map/ppermute | solution.py:159
  58.2 0.1 convert_add_fusion
  58.2 0.8 %copy.15 = f32[2,4,8,8,256]{4,3,2,1,0:T(8,128)} copy(f32[2,4,8,8,256]{4,3,1,0,2:T(8,128)S(1)} %bitcast.51) | data formatting | bytes 1048576 | tf_op jit(solution)/shard_map/transpose | solution.py:162
  (13 shorter events, 0.2 us)
Async XLA Ops:
  7.2 11.2 %collective-permute-start = (bf16[1,2,2,4096]{3,2,1,0:T(2,128)(2,1)S(1)}, bf16[1,2,2,4096]{3,2,1,0:T(2,128)(2,1)S(1)}, u32[]{:S(2)}, u32[]{:S(2)}) collective-permute-start(bf16[1,2,2,4096]{3,2,1,0:T(2,128)(2,1)S(1)} %bitcast.53), channel_id=1, source_target_pairs={{0,8},{2,10},{4,12},{6,14},{8,0},{10,2},{12,4},{14,6},{16,24},{18,... | collective-permute-start | bytes 98312 | tf_op jit(solution)/shard_map/ppermute | solution.py:125
  10.2 8.2 %collective-permute-start.1 = (bf16[1,2,2,4096]{3,2,1,0:T(2,128)(2,1)S(1)}, bf16[1,2,2,4096]{3,2,1,0:T(2,128)(2,1)S(1)}, u32[]{:S(2)}, u32[]{:S(2)}) collective-permute-start(bf16[1,2,2,4096]{3,2,1,0:T(2,128)(2,1)S(1)} %bitcast.54), channel_id=1, source_target_pairs={{0,16},{2,18},{4,20},{6,22},{8,24},{10,26},{12,28},{14,30},{16,0},... | collective-permute-start | bytes 98312 | tf_op jit(solution)/shard_map/ppermute | solution.py:125
  12.8 5.7 %collective-permute-start.2 = (bf16[1,2,2,4096]{3,2,1,0:T(2,128)(2,1)S(1)}, bf16[1,2,2,4096]{3,2,1,0:T(2,128)(2,1)S(1)}, u32[]{:S(2)}, u32[]{:S(2)}) collective-permute-start(bf16[1,2,2,4096]{3,2,1,0:T(2,128)(2,1)S(1)} %bitcast.55), channel_id=1, source_target_pairs={{0,24},{2,26},{4,28},{6,30},{8,16},{10,18},{12,20},{14,22},{16,8},... | collective-permute-start | bytes 98312 | tf_op jit(solution)/shard_map/ppermute | solution.py:125
  12.8 3.2 %copy-start = (s32[64,1]{0,1:T(1,128)S(1)}, s32[64,1]{0,1:T(1,128)}, u32[]{:S(2)}) copy-start(s32[64,1]{0,1:T(1,128)} %param.6) | copy-start | bytes 772
  18.5 5.5 %collective-permute-start.3 = (bf16[4,1,2,2,4096]{4,3,2,0,1:T(2,128)(2,1)S(1)}, bf16[4,1,2,2,4096]{4,3,2,0,1:T(2,128)(2,1)S(1)}, u32[]{:S(2)}, u32[]{:S(2)}) collective-permute-start(bf16[4,1,2,2,4096]{4,3,2,0,1:T(2,128)(2,1)S(1)} %bitcast_dynamic-update-slice_fusion.4), channel_id=1, source_target_pairs={{0,2},{2,0},{4,6},{6,4},{8,10},{10,8},{12,14},{14,12},{16,18},{18,... | collective-permute-start | bytes 393224 | tf_op jit(solution)/shard_map/ppermute | solution.py:125
  20.3 7.8 %collective-permute-start.4 = (bf16[4,1,2,2,4096]{4,3,2,0,1:T(2,128)(2,1)S(1)}, bf16[4,1,2,2,4096]{4,3,2,0,1:T(2,128)(2,1)S(1)}, u32[]{:S(2)}, u32[]{:S(2)}) collective-permute-start(bf16[4,1,2,2,4096]{4,3,2,0,1:T(2,128)(2,1)S(1)} %bitcast_dynamic-update-slice_fusion.4), channel_id=1, source_target_pairs={{0,4},{2,6},{4,0},{6,2},{8,12},{10,14},{12,8},{14,10},{16,20},{18,... | collective-permute-start | bytes 393224 | tf_op jit(solution)/shard_map/ppermute | solution.py:125
  21.8 6.4 %collective-permute-start.5 = (bf16[4,1,2,2,4096]{4,3,2,0,1:T(2,128)(2,1)S(1)}, bf16[4,1,2,2,4096]{4,3,2,0,1:T(2,128)(2,1)S(1)}, u32[]{:S(2)}, u32[]{:S(2)}) collective-permute-start(bf16[4,1,2,2,4096]{4,3,2,0,1:T(2,128)(2,1)S(1)} %bitcast_dynamic-update-slice_fusion.4), channel_id=1, source_target_pairs={{0,6},{2,4},{4,2},{6,0},{8,14},{10,12},{12,10},{14,8},{16,22},{18,... | collective-permute-start | bytes 393224 | tf_op jit(solution)/shard_map/ppermute | solution.py:125
  37.9 18.6 %all-to-all-start = ((bf16[16,64,256]{2,1,0:T(8,128)(2,1)}), bf16[16,64,256]{2,1,0:T(8,128)(2,1)S(1)}, u32[]{:S(2)}, u32[]{:S(2)}) async-start(bf16[16,64,256]{2,1,0:T(8,128)(2,1)} %shard_map.46), calls=%async_computation | async-start | bytes 1048576 | tf_op jit(solution)/shard_map/all_to_all | solution.py:155
  56.6 1.6 %collective-permute-start.6 = (bf16[8,64,256]{2,1,0:T(8,128)(2,1)S(1)}, bf16[8,64,256]{2,1,0:T(8,128)(2,1)S(1)}, u32[]{:S(2)}, u32[]{:S(2)}) collective-permute-start(bf16[8,64,256]{2,1,0:T(8,128)(2,1)S(1)} %constant_dynamic-slice_fusion), channel_id=1, source_target_pairs={{0,1},{1,0},{2,3},{3,2},{4,5},{5,4},{6,7},{7,6},{8,9},{9,8},{10,11... | collective-permute-start | bytes 786440 | tf_op jit(solution)/shard_map/ppermute | solution.py:159

commit v11 on v10

--- a/solution.py
+++ b/solution.py
@@ -26,12 +26,12 @@
     for member in range(group):
         block = first + member
         for offset in range(offsets):
-            owned = placed_ref[lax.rem(block - offset + blocks, blocks)].astype(jnp.float32)
+            owned = placed_ref[lax.rem(block - offset + blocks, blocks)]
             real_t = owned[:capacity]
             imag_t = owned[capacity:]
             for source in range(2):
-                real_s = source_ref[member, 2 * source : 2 * source + 1].astype(jnp.float32)
-                imag_s = source_ref[member, 2 * source + 1 : 2 * source + 2].astype(jnp.float32)
+                real_s = source_ref[member, 2 * source : 2 * source + 1]
+                imag_s = source_ref[member, 2 * source + 1 : 2 * source + 2]
                 even = real_t * real_s + imag_t * imag_s
                 odd = real_t * imag_s - imag_t * real_s
                 even_fold = even[:, :PERIOD]
@@ -40,8 +40,8 @@
                     even_fold = even_fold + even[:, fold * PERIOD : (fold + 1) * PERIOD]
                     odd_fold = odd_fold + odd[:, fold * PERIOD : (fold + 1) * PERIOD]
                 row = member * rows + (source * offsets + offset) * capacity
-                cross_ref[row : row + capacity, :PERIOD] = even_fold
-                cross_ref[row : row + capacity, PERIOD:] = odd_fold
+                cross_ref[row : row + capacity, :PERIOD] = even_fold.astype(jnp.float32)
+                cross_ref[row : row + capacity, PERIOD:] = odd_fold.astype(jnp.float32)
     product = jnp.dot(
         cross_ref[...].astype(jnp.bfloat16), table_ref[...], preferred_element_type=jnp.float32
     )

time: 59.5 us -> 57.3 us (0.963)
  Pallas kernels: 8.64 us -> 6.39 us
    pallas_call x1, Pallas kernels: 8.64 us -> 6.39 us  [correlate(): pl.pallas_call(body, grid=(blocks // group,), in_specs=[pl.BlockSpec(plac...]
where the time goes in v11:
time: 57.3 us; the launch traced here: 56.8 us
  waiting for transfers between devices  19.9 us (35%)
  starting transfers between devices  14.7 us (26%)
  other arithmetic  7.57 us (13%)
  Pallas kernels  6.39 us (11%)
  local copies, waits for them, and re-layouts  3.51 us (6%)
  blocking collectives  2.56 us (4%)
  matrix products  2.04 us (4%)
    all_to_all x1, waiting for transfers between devices, per_device(): lax.all_to_all(partial, 'blk', split_axis=0, concat_axis=0, tiled=True)  13.1 us
    ppermute x6, starting transfers between devices, per_device(): got = lax.ppermute(held, 'blk', route)  9.11 us
    pallas_call x1, Pallas kernels, correlate(): pl.pallas_call(body, grid=(blocks // group,), in_specs=[pl.BlockSpec(plac...  6.39 us
    all_to_all x1, starting transfers between devices, per_device(): lax.all_to_all(partial, 'blk', split_axis=0, concat_axis=0, tiled=True)  5.52 us
    ppermute x6, waiting for transfers between devices, per_device(): got = lax.ppermute(held, 'blk', route)  5.33 us
    reduce_sum x1, other arithmetic, per_device(): jnp.sum(trace_float * trace_float, axis=(1, 2))  2.81 us
    psum x1, blocking collectives, per_device(): lax.psum((jnp.sum(trace_float * trace_float, axis=(1, 2)), jnp.sum(source...  2.56 us
    convert_element_type x1, other arithmetic, per_device(): white_traces = (trace_float * lax.rsqrt(trace_power / (2 * BINS) + EPS)[:...  2.56 us
  transfers between devices with their start and end apart: 8, of which 4 were waited for; matrix products, arithmetic and copies ran while one was open for 11% of the time, Pallas kernels for 0%

profile of v11, /device:TPU:0, one launch (start us, length us, event | category | flops | bytes accessed | tf_op | source)
XLA Modules:
  0.0 56.8 jit_solution(3615130312975066234)
XLA Ops:
  0.0 2.8 %fusion = f32[64]{0:T(128)S(1)} fusion(bf16[64,2,4096]{2,1,0:T(2,128)(2,1)} %param.4), kind=kLoop, calls=%fused_computation.3 | loop fusion | flops 1572800 | bytes 1048832 | tf_op jit(solution)/shard_map/reduce_sum | solution.py:102
  2.8 0.9 %fusion.2 = f32[2]{0:T(128)S(1)} fusion(bf16[2,2,4096]{2,1,0:T(2,128)(2,1)} %param.5), kind=kLoop, calls=%fused_computation.13 | loop fusion | flops 49150 | bytes 32776 | tf_op jit(solution)/shard_map/reduce_sum | solution.py:103
  3.7 2.6 %all-reduce = (f32[64]{0:T(128)S(1)}, f32[2]{0:T(128)S(1)}) all-reduce(f32[64]{0:T(128)S(1)} %fusion, f32[2]{0:T(128)S(1)} %fusion.2), channel_id=1, replica_groups=mesh['blk'=16,'band'=2] {'band'}, use_global_device_ids=true, to_apply=%region_3.0 | all-reduce | flops 66 | bytes 528 | tf_op jit(solution)/shard_map/psum | solution.py:100
  6.3 0.1 broadcast_in_dim.36
  6.4 0.9 %bitcast_dynamic-update-slice_fusion.7 = (bf16[4,1,2,2,4096]{4,3,2,0,1:T(2,128)(2,1)S(1)}, bf16[2,2,4096]{2,1,0:T(2,128)(2,1)S(1)}) fusion(bf16[4,1,2,2,4096]{4,3,2,0,1:T(2,128)(2,1)S(1)} %broadcast_in_dim.36, s32[]{:T(128)S(6)} %select_n.30, f32[2]{0:T(128)S(1)} %add_rsqrt_fusion, bf16[2,2,4096]{2,1,0:T(2,128)(2,1)} %param.5), kind=kLoop, calls=%fused_computation.19 | loop fusion | flops 49152 | bytes 98820 | tf_op jit(solution)/shard_map/dynamic_update_slice | solution.py:126
  7.2 3.0 %collective-permute-start = (bf16[1,2,2,4096]{3,2,1,0:T(2,128)(2,1)S(1)}, bf16[1,2,2,4096]{3,2,1,0:T(2,128)(2,1)S(1)}, u32[]{:S(2)}, u32[]{:S(2)}) collective-permute-start(bf16[1,2,2,4096]{3,2,1,0:T(2,128)(2,1)S(1)} %bitcast.53), channel_id=1, source_target_pairs={{0,8},{2,10},{4,12},{6,14},{8,0},{10,2},{12,4},{14,6},{16,24},{18,... | collective-permute-start | bytes 98312 | tf_op jit(solution)/shard_map/ppermute | solution.py:125
  10.2 2.6 %collective-permute-start.1 = (bf16[1,2,2,4096]{3,2,1,0:T(2,128)(2,1)S(1)}, bf16[1,2,2,4096]{3,2,1,0:T(2,128)(2,1)S(1)}, u32[]{:S(2)}, u32[]{:S(2)}) collective-permute-start(bf16[1,2,2,4096]{3,2,1,0:T(2,128)(2,1)S(1)} %bitcast.54), channel_id=1, source_target_pairs={{0,16},{2,18},{4,20},{6,22},{8,24},{10,26},{12,28},{14,30},{16,0},... | collective-permute-start | bytes 98312 | tf_op jit(solution)/shard_map/ppermute | solution.py:125
  12.8 2.6 %fusion.1 = bf16[64,2,4096]{2,1,0:T(2,128)(2,1)S(1)} fusion(bf16[64,2,4096]{2,1,0:T(2,128)(2,1)} %param.4, f32[64]{0:T(128)S(1)} %add_rsqrt_fusion.1), kind=kLoop, calls=%fused_computation.4 | loop fusion | flops 1572864 | bytes 2097408 | tf_op jit(solution)/shard_map/convert_element_type | solution.py:134
  15.4 0.6 %copy.13 = bf16[8,8,2,4096]{3,1,2,0:T(8,128)(2,1)S(1)} copy(bf16[8,8,2,4096]{3,2,1,0:T(2,128)(2,1)S(1)} %bitcast.49) | data formatting | bytes 2097152
  16.0 0.1 fusion.5
  16.0 0.1 reduce_window_sum.11
  16.1 0.2 select_reduce_fusion
  16.3 2.0 %convolution_convert_fusion = bf16[128,8192]{1,0:T(8,128)(2,1)} fusion(bf16[64,8192]{1,0:T(8,128)(2,1)S(1)} %bitcast.50, s32[64]{0:T(128)S(1)} %multiply_add_fusion), kind=kOutput, calls=%fused_computation | convolution fusion | flops 135274496 | bytes 3145984 | tf_op jit(solution)/shard_map/dot_general | solution.py:146
  18.5 0.0 collective-permute-done.2
  18.5 1.8 %collective-permute-start.3 = (bf16[4,1,2,2,4096]{4,3,2,0,1:T(2,128)(2,1)S(1)}, bf16[4,1,2,2,4096]{4,3,2,0,1:T(2,128)(2,1)S(1)}, u32[]{:S(2)}, u32[]{:S(2)}) collective-permute-start(bf16[4,1,2,2,4096]{4,3,2,0,1:T(2,128)(2,1)S(1)} %bitcast_dynamic-update-slice_fusion.4), channel_id=1, source_target_pairs={{0,2},{2,0},{4,6},{6,4},{8,10},{10,8},{12,14},{14,12},{16,18},{18,... | collective-permute-start | bytes 393224 | tf_op jit(solution)/shard_map/ppermute | solution.py:125
  20.3 1.5 %collective-permute-start.4 = (bf16[4,1,2,2,4096]{4,3,2,0,1:T(2,128)(2,1)S(1)}, bf16[4,1,2,2,4096]{4,3,2,0,1:T(2,128)(2,1)S(1)}, u32[]{:S(2)}, u32[]{:S(2)}) collective-permute-start(bf16[4,1,2,2,4096]{4,3,2,0,1:T(2,128)(2,1)S(1)} %bitcast_dynamic-update-slice_fusion.4), channel_id=1, source_target_pairs={{0,4},{2,6},{4,0},{6,2},{8,12},{10,14},{12,8},{14,10},{16,20},{18,... | collective-permute-start | bytes 393224 | tf_op jit(solution)/shard_map/ppermute | solution.py:125
  21.8 0.3 collective-permute-start.5
  22.1 0.5 broadcast_in_dim.35
  22.6 0.1 bitcast_dynamic-update-slice_fusion.2
  22.7 1.4 %collective-permute-done.3 = bf16[4,1,2,2,4096]{4,3,2,0,1:T(2,128)(2,1)S(1)} collective-permute-done((bf16[4,1,2,2,4096]{4,3,2,0,1:T(2,128)(2,1)S(1)}, bf16[4,1,2,2,4096]{4,3,2,0,1:T(2,128)(2,1)S(1)}, u32[]{:S(2)}, u32[]{:S(2)}) %collective-permute-start.3) | collective-permute-done | bytes 131104 | tf_op jit(solution)/shard_map/ppermute | solution.py:125
  24.0 0.1 bitcast_dynamic-update-slice_fusion.1
  24.2 3.9 %collective-permute-done.4 = bf16[4,1,2,2,4096]{4,3,2,0,1:T(2,128)(2,1)S(1)} collective-permute-done((bf16[4,1,2,2,4096]{4,3,2,0,1:T(2,128)(2,1)S(1)}, bf16[4,1,2,2,4096]{4,3,2,0,1:T(2,128)(2,1)S(1)}, u32[]{:S(2)}, u32[]{:S(2)}) %collective-permute-start.4) | collective-permute-done | bytes 131104 | tf_op jit(solution)/shard_map/ppermute | solution.py:125
  28.1 0.1 bitcast_dynamic-update-slice_fusion
  28.2 0.1 bitcast_dynamic-update-slice_fusion.3
  28.3 1.0 %reshape.31.source_ref = bf16[16,4,4096]{2,1,0:T(4,128)(2,1)} reshape(bf16[1,4,4,2,2,4096]{5,4,3,2,1,0:T(2,128)(2,1)S(1)} %bitcast.52) | data formatting | bytes 1048576 | tf_op jit(solution)/shard_map/reshape | solution.py:152
  29.3 6.4 %shard_map.46 = bf16[16,64,256]{2,1,0:T(8,128)(2,1)} custom-call(bf16[16,16,4096]{2,1,0:T(8,128)(2,1)} %bitcast.48, bf16[16,4,4096]{2,1,0:T(4,128)(2,1)} %reshape.31.source_ref, bf16[2048,256]{1,0:T(8,128)(2,1)} %constant.42.clone.table_ref), custom_call_target="tpu_custom_call" | custom-call | flops 1107296256 | bytes 4194304 | tf_op jit(solution)/shard_map/pallas_call | solution.py:59
  35.7 5.5 %all-to-all-start = ((bf16[16,64,256]{2,1,0:T(8,128)(2,1)}), bf16[16,64,256]{2,1,0:T(8,128)(2,1)S(1)}, u32[]{:S(2)}, u32[]{:S(2)}) async-start(bf16[16,64,256]{2,1,0:T(8,128)(2,1)} %shard_map.46), calls=%async_computation | async-start | bytes 1048576 | tf_op jit(solution)/shard_map/all_to_all | solution.py:155
  41.2 13.1 %all-to-all-done = bf16[16,64,256]{2,1,0:T(8,128)(2,1)S(1)} async-done(((bf16[16,64,256]{2,1,0:T(8,128)(2,1)}), bf16[16,64,256]{2,1,0:T(8,128)(2,1)S(1)}, u32[]{:S(2)}, u32[]{:S(2)}) %all-to-all-start) | async-done | bytes 524320 | tf_op jit(solution)/shard_map/all_to_all | solution.py:155
  54.3 0.1 collective-permute-start.6
  54.4 1.5 %collective-permute-done.6 = bf16[8,64,256]{2,1,0:T(8,128)(2,1)S(1)} collective-permute-done((bf16[8,64,256]{2,1,0:T(8,128)(2,1)S(1)}, bf16[8,64,256]{2,1,0:T(8,128)(2,1)S(1)}, u32[]{:S(2)}, u32[]{:S(2)}) %collective-permute-start.6) | collective-permute-done | bytes 262176 | tf_op jit(solution)/shard_map/ppermute | solution.py:159
  55.9 0.1 convert_add_fusion
  56.0 0.8 %copy.15 = f32[2,4,8,8,256]{4,3,2,1,0:T(8,128)} copy(f32[2,4,8,8,256]{4,3,1,0,2:T(8,128)S(1)} %bitcast.51) | data formatting | bytes 1048576 | tf_op jit(solution)/shard_map/transpose | solution.py:162
  (13 shorter events, 0.2 us)
Async XLA Ops:
  7.2 11.2 %collective-permute-start = (bf16[1,2,2,4096]{3,2,1,0:T(2,128)(2,1)S(1)}, bf16[1,2,2,4096]{3,2,1,0:T(2,128)(2,1)S(1)}, u32[]{:S(2)}, u32[]{:S(2)}) collective-permute-start(bf16[1,2,2,4096]{3,2,1,0:T(2,128)(2,1)S(1)} %bitcast.53), channel_id=1, source_target_pairs={{0,8},{2,10},{4,12},{6,14},{8,0},{10,2},{12,4},{14,6},{16,24},{18,... | collective-permute-start | bytes 98312 | tf_op jit(solution)/shard_map/ppermute | solution.py:125
  10.2 8.2 %collective-permute-start.1 = (bf16[1,2,2,4096]{3,2,1,0:T(2,128)(2,1)S(1)}, bf16[1,2,2,4096]{3,2,1,0:T(2,128)(2,1)S(1)}, u32[]{:S(2)}, u32[]{:S(2)}) collective-permute-start(bf16[1,2,2,4096]{3,2,1,0:T(2,128)(2,1)S(1)} %bitcast.54), channel_id=1, source_target_pairs={{0,16},{2,18},{4,20},{6,22},{8,24},{10,26},{12,28},{14,30},{16,0},... | collective-permute-start | bytes 98312 | tf_op jit(solution)/shard_map/ppermute | solution.py:125
  12.8 5.7 %collective-permute-start.2 = (bf16[1,2,2,4096]{3,2,1,0:T(2,128)(2,1)S(1)}, bf16[1,2,2,4096]{3,2,1,0:T(2,128)(2,1)S(1)}, u32[]{:S(2)}, u32[]{:S(2)}) collective-permute-start(bf16[1,2,2,4096]{3,2,1,0:T(2,128)(2,1)S(1)} %bitcast.55), channel_id=1, source_target_pairs={{0,24},{2,26},{4,28},{6,30},{8,16},{10,18},{12,20},{14,22},{16,8},... | collective-permute-start | bytes 98312 | tf_op jit(solution)/shard_map/ppermute | solution.py:125
  12.8 3.2 %copy-start = (s32[64,1]{0,1:T(1,128)S(1)}, s32[64,1]{0,1:T(1,128)}, u32[]{:S(2)}) copy-start(s32[64,1]{0,1:T(1,128)} %param.6) | copy-start | bytes 772
  18.5 5.5 %collective-permute-start.3 = (bf16[4,1,2,2,4096]{4,3,2,0,1:T(2,128)(2,1)S(1)}, bf16[4,1,2,2,4096]{4,3,2,0,1:T(2,128)(2,1)S(1)}, u32[]{:S(2)}, u32[]{:S(2)}) collective-permute-start(bf16[4,1,2,2,4096]{4,3,2,0,1:T(2,128)(2,1)S(1)} %bitcast_dynamic-update-slice_fusion.4), channel_id=1, source_target_pairs={{0,2},{2,0},{4,6},{6,4},{8,10},{10,8},{12,14},{14,12},{16,18},{18,... | collective-permute-start | bytes 393224 | tf_op jit(solution)/shard_map/ppermute | solution.py:125
  20.3 7.8 %collective-permute-start.4 = (bf16[4,1,2,2,4096]{4,3,2,0,1:T(2,128)(2,1)S(1)}, bf16[4,1,2,2,4096]{4,3,2,0,1:T(2,128)(2,1)S(1)}, u32[]{:S(2)}, u32[]{:S(2)}) collective-permute-start(bf16[4,1,2,2,4096]{4,3,2,0,1:T(2,128)(2,1)S(1)} %bitcast_dynamic-update-slice_fusion.4), channel_id=1, source_target_pairs={{0,4},{2,6},{4,0},{6,2},{8,12},{10,14},{12,8},{14,10},{16,20},{18,... | collective-permute-start | bytes 393224 | tf_op jit(solution)/shard_map/ppermute | solution.py:125
  21.8 6.4 %collective-permute-start.5 = (bf16[4,1,2,2,4096]{4,3,2,0,1:T(2,128)(2,1)S(1)}, bf16[4,1,2,2,4096]{4,3,2,0,1:T(2,128)(2,1)S(1)}, u32[]{:S(2)}, u32[]{:S(2)}) collective-permute-start(bf16[4,1,2,2,4096]{4,3,2,0,1:T(2,128)(2,1)S(1)} %bitcast_dynamic-update-slice_fusion.4), channel_id=1, source_target_pairs={{0,6},{2,4},{4,2},{6,0},{8,14},{10,12},{12,10},{14,8},{16,22},{18,... | collective-permute-start | bytes 393224 | tf_op jit(solution)/shard_map/ppermute | solution.py:125
  35.7 18.6 %all-to-all-start = ((bf16[16,64,256]{2,1,0:T(8,128)(2,1)}), bf16[16,64,256]{2,1,0:T(8,128)(2,1)S(1)}, u32[]{:S(2)}, u32[]{:S(2)}) async-start(bf16[16,64,256]{2,1,0:T(8,128)(2,1)} %shard_map.46), calls=%async_computation | async-start | bytes 1048576 | tf_op jit(solution)/shard_map/all_to_all | solution.py:155
  54.3 1.6 %collective-permute-start.6 = (bf16[8,64,256]{2,1,0:T(8,128)(2,1)S(1)}, bf16[8,64,256]{2,1,0:T(8,128)(2,1)S(1)}, u32[]{:S(2)}, u32[]{:S(2)}) collective-permute-start(bf16[8,64,256]{2,1,0:T(8,128)(2,1)S(1)} %constant_dynamic-slice_fusion), channel_id=1, source_target_pairs={{0,1},{1,0},{2,3},{3,2},{4,5},{5,4},{6,7},{7,6},{8,9},{9,8},{10,11... | collective-permute-start | bytes 786440 | tf_op jit(solution)/shard_map/ppermute | solution.py:159

commit v12 on v11

--- a/solution.py
+++ b/solution.py
@@ -129,21 +129,19 @@
         held = widened
     groups = held.ndim - white_sources.ndim
     held = held.transpose(tuple(reversed(range(groups))) + tuple(range(groups, held.ndim)))
-    white_traces = (
-        (trace_float * lax.rsqrt(trace_power / (2 * BINS) + EPS)[:, None, None])
-        .astype(jnp.bfloat16)
-        .reshape(station_count, 2 * group_bins)
-    )
-
     owners = owner[:, 0]
     owner_hits = (owners[:, None] == jnp.arange(blocks, dtype=jnp.int32)[None, :]).astype(jnp.int32)
     earlier = jnp.cumsum(owner_hits, axis=0) - owner_hits
     arrival = jnp.sum(owner_hits * earlier, axis=1)
     slot_index = owners * capacity + arrival
-    placing = (
-        jnp.arange(blocks * capacity, dtype=jnp.int32)[:, None] == slot_index[None, :]
-    ).astype(jnp.bfloat16)
-    placed = jnp.dot(placing, white_traces, preferred_element_type=jnp.float32).astype(jnp.bfloat16)
+    chosen = jnp.arange(blocks * capacity, dtype=jnp.int32)[:, None] == slot_index[None, :]
+    raw_placed = jnp.dot(
+        chosen.astype(jnp.bfloat16), traces.reshape(station_count, 2 * group_bins),
+        preferred_element_type=jnp.float32,
+    )
+    station_scale = lax.rsqrt(trace_power / (2 * BINS) + EPS)
+    slot_scale = jnp.sum(jnp.where(chosen, station_scale[None, :], 0.0), axis=1)
+    placed = (raw_placed * slot_scale[:, None]).astype(jnp.bfloat16)
     placed = placed.reshape(blocks, capacity, 2, group_bins).transpose(0, 2, 1, 3)
     placed = placed.reshape(blocks, 2 * capacity, group_bins)
 

time: 57.3 us -> 56.2 us (0.981)
  other arithmetic: 7.57 us -> 5.13 us
  local copies, waits for them, and re-layouts: 3.51 us -> 4.73 us
    convert_element_type x1 -> x0, other arithmetic: 2.56 us -> none  [per_device(): white_traces = (trace_float * lax.rsqrt(trace_power / (2 * BINS) + EPS)[:...]
    unnamed x3, local copies, waits for them, and re-layouts: 0.59 us -> 1.81 us
  transfers between devices with their start and end apart: 8 -> 8, of which waited for: 4 -> 6; matrix products, arithmetic and copies ran while one was open for 11% -> 10% of each run, Pallas kernels for 0% -> 0%
where the time goes in v12:
time: 56.2 us; the launch traced here: 55.7 us
  waiting for transfers between devices  20.4 us (36%)
  starting transfers between devices  14.3 us (25%)
  Pallas kernels  6.39 us (11%)
  other arithmetic  5.13 us (9%)
  local copies, waits for them, and re-layouts  4.73 us (8%)
  blocking collectives  2.56 us (5%)
  matrix products  2.18 us (4%)
    all_to_all x1, waiting for transfers between devices, per_device(): lax.all_to_all(partial, 'blk', split_axis=0, concat_axis=0, tiled=True)  13.1 us
    ppermute x6, starting transfers between devices, per_device(): got = lax.ppermute(held, 'blk', route)  9.11 us
    pallas_call x1, Pallas kernels, correlate(): pl.pallas_call(body, grid=(blocks // group,), in_specs=[pl.BlockSpec(plac...  6.39 us
    ppermute x6, waiting for transfers between devices, per_device(): got = lax.ppermute(held, 'blk', route)  5.76 us
    all_to_all x1, starting transfers between devices, per_device(): lax.all_to_all(partial, 'blk', split_axis=0, concat_axis=0, tiled=True)  5.1 us
    reduce_sum x1, other arithmetic, per_device(): jnp.sum(trace_float * trace_float, axis=(1, 2))  2.82 us
    psum x1, blocking collectives, per_device(): lax.psum((jnp.sum(trace_float * trace_float, axis=(1, 2)), jnp.sum(source...  2.56 us
    dot_general x1, matrix products, per_device(): jnp.dot(chosen.astype(jnp.bfloat16), traces.reshape(station_count, 2 * gr...  2.18 us
  transfers between devices with their start and end apart: 8, of which 6 were waited for; matrix products, arithmetic and copies ran while one was open for 10% of the time, Pallas kernels for 0%

profile of v12, /device:TPU:0, one launch (start us, length us, event | category | flops | bytes accessed | tf_op | source)
XLA Modules:
  0.0 55.7 jit_solution(1640619162255232324)
XLA Ops:
  0.0 2.8 %multiply_reduce_fusion = f32[64]{0:T(128)S(1)} fusion(bf16[64,2,4096]{2,1,0:T(2,128)(2,1)} %param.4), kind=kLoop, calls=%fused_computation.2 | loop fusion | flops 1572800 | bytes 1048832 | tf_op jit(solution)/shard_map/reduce_sum | solution.py:102
  2.8 0.9 %fusion.1 = f32[2]{0:T(128)S(1)} fusion(bf16[2,2,4096]{2,1,0:T(2,128)(2,1)} %param.5), kind=kLoop, calls=%fused_computation.11 | loop fusion | flops 49150 | bytes 32776 | tf_op jit(solution)/shard_map/reduce_sum | solution.py:103
  3.7 2.6 %all-reduce = (f32[64]{0:T(128)S(1)}, f32[2]{0:T(128)S(1)}) all-reduce(f32[64]{0:T(128)S(1)} %multiply_reduce_fusion, f32[2]{0:T(128)S(1)} %fusion.1), channel_id=1, replica_groups=mesh['blk'=16,'band'=2] {'band'}, use_global_device_ids=true, to_apply=%region_3.0 | all-reduce | flops 66 | bytes 528 | tf_op jit(solution)/shard_map/psum | solution.py:100
  6.3 0.1 broadcast_in_dim.51
  6.4 0.9 %bitcast_dynamic-update-slice_fusion.7 = (bf16[4,1,2,2,4096]{4,3,2,0,1:T(2,128)(2,1)S(1)}, bf16[2,2,4096]{2,1,0:T(2,128)(2,1)S(1)}) fusion(bf16[4,1,2,2,4096]{4,3,2,0,1:T(2,128)(2,1)S(1)} %broadcast_in_dim.51, s32[]{:T(128)S(6)} %select_n.35, f32[2]{0:T(128)S(1)} %add_rsqrt_fusion, bf16[2,2,4096]{2,1,0:T(2,128)(2,1)} %param.5), kind=kLoop, calls=%fused_computation.16 | loop fusion | flops 49152 | bytes 98820 | tf_op jit(solution)/shard_map/dynamic_update_slice | solution.py:126
  7.2 3.0 %collective-permute-start = (bf16[1,2,2,4096]{3,2,1,0:T(2,128)(2,1)S(1)}, bf16[1,2,2,4096]{3,2,1,0:T(2,128)(2,1)S(1)}, u32[]{:S(2)}, u32[]{:S(2)}) collective-permute-start(bf16[1,2,2,4096]{3,2,1,0:T(2,128)(2,1)S(1)} %bitcast.53), channel_id=1, source_target_pairs={{0,8},{2,10},{4,12},{6,14},{8,0},{10,2},{12,4},{14,6},{16,24},{18,... | collective-permute-start | bytes 98312 | tf_op jit(solution)/shard_map/ppermute | solution.py:125
  10.2 2.6 %collective-permute-start.1 = (bf16[1,2,2,4096]{3,2,1,0:T(2,128)(2,1)S(1)}, bf16[1,2,2,4096]{3,2,1,0:T(2,128)(2,1)S(1)}, u32[]{:S(2)}, u32[]{:S(2)}) collective-permute-start(bf16[1,2,2,4096]{3,2,1,0:T(2,128)(2,1)S(1)} %bitcast.54), channel_id=1, source_target_pairs={{0,16},{2,18},{4,20},{6,22},{8,24},{10,26},{12,28},{14,30},{16,0},... | collective-permute-start | bytes 98312 | tf_op jit(solution)/shard_map/ppermute | solution.py:125
  12.8 1.8 %copy.21 = bf16[8,8,2,4096]{3,1,2,0:T(8,128)(2,1)S(1)} copy(bf16[8,8,2,4096]{3,2,1,0:T(2,128)(2,1)} %bitcast.49) | data formatting | bytes 2097152
  14.6 0.1 fusion.3
  14.7 0.1 reduce_window_sum.11
  14.8 0.2 select_reduce_fusion.1
  15.0 0.1 select_reduce_fusion
  15.1 2.2 %fusion = bf16[128,8192]{1,0:T(8,128)(2,1)} fusion(bf16[64,8192]{1,0:T(8,128)(2,1)S(1)} %bitcast.50, f32[128]{0:T(128)S(1)} %select_reduce_fusion, s32[64]{0:T(128)S(1)} %multiply_add_fusion), kind=kOutput, calls=%fused_computation.1 | convolution fusion | flops 136323072 | bytes 3146496 | tf_op jit(solution)/shard_map/dot_general | solution.py:138
  17.4 1.1 %collective-permute-done.2 = bf16[1,2,2,4096]{3,2,1,0:T(2,128)(2,1)S(1)} collective-permute-done((bf16[1,2,2,4096]{3,2,1,0:T(2,128)(2,1)S(1)}, bf16[1,2,2,4096]{3,2,1,0:T(2,128)(2,1)S(1)}, u32[]{:S(2)}, u32[]{:S(2)}) %collective-permute-start.2) | collective-permute-done | bytes 32800 | tf_op jit(solution)/shard_map/ppermute | solution.py:125
  18.6 1.6 %collective-permute-start.3 = (bf16[4,1,2,2,4096]{4,3,2,0,1:T(2,128)(2,1)S(1)}, bf16[4,1,2,2,4096]{4,3,2,0,1:T(2,128)(2,1)S(1)}, u32[]{:S(2)}, u32[]{:S(2)}) collective-permute-start(bf16[4,1,2,2,4096]{4,3,2,0,1:T(2,128)(2,1)S(1)} %bitcast_dynamic-update-slice_fusion.4), channel_id=1, source_target_pairs={{0,2},{2,0},{4,6},{6,4},{8,10},{10,8},{12,14},{14,12},{16,18},{18,... | collective-permute-start | bytes 393224 | tf_op jit(solution)/shard_map/ppermute | solution.py:125
  20.1 1.5 %collective-permute-start.4 = (bf16[4,1,2,2,4096]{4,3,2,0,1:T(2,128)(2,1)S(1)}, bf16[4,1,2,2,4096]{4,3,2,0,1:T(2,128)(2,1)S(1)}, u32[]{:S(2)}, u32[]{:S(2)}) collective-permute-start(bf16[4,1,2,2,4096]{4,3,2,0,1:T(2,128)(2,1)S(1)} %bitcast_dynamic-update-slice_fusion.4), channel_id=1, source_target_pairs={{0,4},{2,6},{4,0},{6,2},{8,12},{10,14},{12,8},{14,10},{16,20},{18,... | collective-permute-start | bytes 393224 | tf_op jit(solution)/shard_map/ppermute | solution.py:125
  21.6 0.5 collective-permute-start.5
  22.1 0.5 broadcast_in_dim.50
  22.6 0.1 bitcast_dynamic-update-slice_fusion.2
  22.7 2.2 %collective-permute-done.3 = bf16[4,1,2,2,4096]{4,3,2,0,1:T(2,128)(2,1)S(1)} collective-permute-done((bf16[4,1,2,2,4096]{4,3,2,0,1:T(2,128)(2,1)S(1)}, bf16[4,1,2,2,4096]{4,3,2,0,1:T(2,128)(2,1)S(1)}, u32[]{:S(2)}, u32[]{:S(2)}) %collective-permute-start.3) | collective-permute-done | bytes 131104 | tf_op jit(solution)/shard_map/ppermute | solution.py:125
  24.9 0.1 bitcast_dynamic-update-slice_fusion.1
  25.0 1.1 %collective-permute-done.4 = bf16[4,1,2,2,4096]{4,3,2,0,1:T(2,128)(2,1)S(1)} collective-permute-done((bf16[4,1,2,2,4096]{4,3,2,0,1:T(2,128)(2,1)S(1)}, bf16[4,1,2,2,4096]{4,3,2,0,1:T(2,128)(2,1)S(1)}, u32[]{:S(2)}, u32[]{:S(2)}) %collective-permute-start.4) | collective-permute-done | bytes 131104 | tf_op jit(solution)/shard_map/ppermute | solution.py:125
  26.1 0.1 bitcast_dynamic-update-slice_fusion
  26.2 1.3 %collective-permute-done.5 = bf16[4,1,2,2,4096]{4,3,2,0,1:T(2,128)(2,1)S(1)} collective-permute-done((bf16[4,1,2,2,4096]{4,3,2,0,1:T(2,128)(2,1)S(1)}, bf16[4,1,2,2,4096]{4,3,2,0,1:T(2,128)(2,1)S(1)}, u32[]{:S(2)}, u32[]{:S(2)}) %collective-permute-start.5) | collective-permute-done | bytes 131104 | tf_op jit(solution)/shard_map/ppermute | solution.py:125
  27.5 0.1 bitcast_dynamic-update-slice_fusion.3
  27.6 1.0 %reshape.32.source_ref = bf16[16,4,4096]{2,1,0:T(4,128)(2,1)} reshape(bf16[1,4,4,2,2,4096]{5,4,3,2,1,0:T(2,128)(2,1)S(1)} %bitcast.52) | data formatting | bytes 1048576 | tf_op jit(solution)/shard_map/reshape | solution.py:150
  28.6 6.4 %shard_map.46 = bf16[16,64,256]{2,1,0:T(8,128)(2,1)} custom-call(bf16[16,16,4096]{2,1,0:T(8,128)(2,1)} %bitcast.48, bf16[16,4,4096]{2,1,0:T(4,128)(2,1)} %reshape.32.source_ref, bf16[2048,256]{1,0:T(8,128)(2,1)} %constant.42.clone.table_ref), custom_call_target="tpu_custom_call" | custom-call | flops 1107296256 | bytes 4194304 | tf_op jit(solution)/shard_map/pallas_call | solution.py:59
  35.0 5.1 %all-to-all-start = ((bf16[16,64,256]{2,1,0:T(8,128)(2,1)}), bf16[16,64,256]{2,1,0:T(8,128)(2,1)S(1)}, u32[]{:S(2)}, u32[]{:S(2)}) async-start(bf16[16,64,256]{2,1,0:T(8,128)(2,1)} %shard_map.46), calls=%async_computation | async-start | bytes 1048576 | tf_op jit(solution)/shard_map/all_to_all | solution.py:153
  40.1 13.1 %all-to-all-done = bf16[16,64,256]{2,1,0:T(8,128)(2,1)S(1)} async-done(((bf16[16,64,256]{2,1,0:T(8,128)(2,1)}), bf16[16,64,256]{2,1,0:T(8,128)(2,1)S(1)}, u32[]{:S(2)}, u32[]{:S(2)}) %all-to-all-start) | async-done | bytes 524320 | tf_op jit(solution)/shard_map/all_to_all | solution.py:153
  53.2 0.1 collective-permute-start.6
  53.3 1.5 %collective-permute-done.6 = bf16[8,64,256]{2,1,0:T(8,128)(2,1)S(1)} collective-permute-done((bf16[8,64,256]{2,1,0:T(8,128)(2,1)S(1)}, bf16[8,64,256]{2,1,0:T(8,128)(2,1)S(1)}, u32[]{:S(2)}, u32[]{:S(2)}) %collective-permute-start.6) | collective-permute-done | bytes 262176 | tf_op jit(solution)/shard_map/ppermute | solution.py:157
  54.9 0.8 %copy.23 = f32[2,4,8,8,256]{4,3,2,1,0:T(8,128)} copy(f32[2,4,8,8,256]{4,3,1,0,2:T(8,128)S(1)} %bitcast.51) | data formatting | bytes 1048576 | tf_op jit(solution)/shard_map/transpose | solution.py:160
  (13 shorter events, 0.2 us)
Async XLA Ops:
  0.0 14.6 %copy-start = (s32[64,1]{0,1:T(1,128)S(1)}, s32[64,1]{0,1:T(1,128)}, u32[]{:S(2)}) copy-start(s32[64,1]{0,1:T(1,128)} %param.6) | copy-start | bytes 772
  7.2 10.0 %collective-permute-start = (bf16[1,2,2,4096]{3,2,1,0:T(2,128)(2,1)S(1)}, bf16[1,2,2,4096]{3,2,1,0:T(2,128)(2,1)S(1)}, u32[]{:S(2)}, u32[]{:S(2)}) collective-permute-start(bf16[1,2,2,4096]{3,2,1,0:T(2,128)(2,1)S(1)} %bitcast.53), channel_id=1, source_target_pairs={{0,8},{2,10},{4,12},{6,14},{8,0},{10,2},{12,4},{14,6},{16,24},{18,... | collective-permute-start | bytes 98312 | tf_op jit(solution)/shard_map/ppermute | solution.py:125
  10.2 7.1 %collective-permute-start.1 = (bf16[1,2,2,4096]{3,2,1,0:T(2,128)(2,1)S(1)}, bf16[1,2,2,4096]{3,2,1,0:T(2,128)(2,1)S(1)}, u32[]{:S(2)}, u32[]{:S(2)}) collective-permute-start(bf16[1,2,2,4096]{3,2,1,0:T(2,128)(2,1)S(1)} %bitcast.54), channel_id=1, source_target_pairs={{0,16},{2,18},{4,20},{6,22},{8,24},{10,26},{12,28},{14,30},{16,0},... | collective-permute-start | bytes 98312 | tf_op jit(solution)/shard_map/ppermute | solution.py:125
  12.8 5.7 %collective-permute-start.2 = (bf16[1,2,2,4096]{3,2,1,0:T(2,128)(2,1)S(1)}, bf16[1,2,2,4096]{3,2,1,0:T(2,128)(2,1)S(1)}, u32[]{:S(2)}, u32[]{:S(2)}) collective-permute-start(bf16[1,2,2,4096]{3,2,1,0:T(2,128)(2,1)S(1)} %bitcast.55), channel_id=1, source_target_pairs={{0,24},{2,26},{4,28},{6,30},{8,16},{10,18},{12,20},{14,22},{16,8},... | collective-permute-start | bytes 98312 | tf_op jit(solution)/shard_map/ppermute | solution.py:125
  18.6 6.3 %collective-permute-start.3 = (bf16[4,1,2,2,4096]{4,3,2,0,1:T(2,128)(2,1)S(1)}, bf16[4,1,2,2,4096]{4,3,2,0,1:T(2,128)(2,1)S(1)}, u32[]{:S(2)}, u32[]{:S(2)}) collective-permute-start(bf16[4,1,2,2,4096]{4,3,2,0,1:T(2,128)(2,1)S(1)} %bitcast_dynamic-update-slice_fusion.4), channel_id=1, source_target_pairs={{0,2},{2,0},{4,6},{6,4},{8,10},{10,8},{12,14},{14,12},{16,18},{18,... | collective-permute-start | bytes 393224 | tf_op jit(solution)/shard_map/ppermute | solution.py:125
  20.1 6.0 %collective-permute-start.4 = (bf16[4,1,2,2,4096]{4,3,2,0,1:T(2,128)(2,1)S(1)}, bf16[4,1,2,2,4096]{4,3,2,0,1:T(2,128)(2,1)S(1)}, u32[]{:S(2)}, u32[]{:S(2)}) collective-permute-start(bf16[4,1,2,2,4096]{4,3,2,0,1:T(2,128)(2,1)S(1)} %bitcast_dynamic-update-slice_fusion.4), channel_id=1, source_target_pairs={{0,4},{2,6},{4,0},{6,2},{8,12},{10,14},{12,8},{14,10},{16,20},{18,... | collective-permute-start | bytes 393224 | tf_op jit(solution)/shard_map/ppermute | solution.py:125
  21.6 5.9 %collective-permute-start.5 = (bf16[4,1,2,2,4096]{4,3,2,0,1:T(2,128)(2,1)S(1)}, bf16[4,1,2,2,4096]{4,3,2,0,1:T(2,128)(2,1)S(1)}, u32[]{:S(2)}, u32[]{:S(2)}) collective-permute-start(bf16[4,1,2,2,4096]{4,3,2,0,1:T(2,128)(2,1)S(1)} %bitcast_dynamic-update-slice_fusion.4), channel_id=1, source_target_pairs={{0,6},{2,4},{4,2},{6,0},{8,14},{10,12},{12,10},{14,8},{16,22},{18,... | collective-permute-start | bytes 393224 | tf_op jit(solution)/shard_map/ppermute | solution.py:125
  35.0 18.2 %all-to-all-start = ((bf16[16,64,256]{2,1,0:T(8,128)(2,1)}), bf16[16,64,256]{2,1,0:T(8,128)(2,1)S(1)}, u32[]{:S(2)}, u32[]{:S(2)}) async-start(bf16[16,64,256]{2,1,0:T(8,128)(2,1)} %shard_map.46), calls=%async_computation | async-start | bytes 1048576 | tf_op jit(solution)/shard_map/all_to_all | solution.py:153
  53.2 1.6 %collective-permute-start.6 = (bf16[8,64,256]{2,1,0:T(8,128)(2,1)S(1)}, bf16[8,64,256]{2,1,0:T(8,128)(2,1)S(1)}, u32[]{:S(2)}, u32[]{:S(2)}) collective-permute-start(bf16[8,64,256]{2,1,0:T(8,128)(2,1)S(1)} %constant_dynamic-slice_fusion), channel_id=1, source_target_pairs={{0,1},{1,0},{2,3},{3,2},{4,5},{5,4},{6,7},{7,6},{8,9},{9,8},{10,11... | collective-permute-start | bytes 786440 | tf_op jit(solution)/shard_map/ppermute | solution.py:157

commit v13 on v12

--- a/solution.py
+++ b/solution.py
@@ -95,18 +95,15 @@
     offsets = blocks // 4
     band = lax.axis_index("band")
 
-    trace_float = traces.astype(jnp.float32)
     source_float = sources.astype(jnp.float32)
-    trace_power, source_power = lax.psum(
-        (
-            jnp.sum(trace_float * trace_float, axis=(1, 2)),
-            jnp.sum(source_float * source_float, axis=(1, 2)),
-        ),
-        "band",
-    )
+    source_sums = jnp.sum(source_float * source_float, axis=(1, 2))
+    source_power = source_sums + lax.ppermute(source_sums, "band", [(0, 1), (1, 0)])
     white_sources = (
         source_float * lax.rsqrt(source_power / (2 * BINS) + EPS)[:, None, None]
     ).astype(jnp.bfloat16)
+    traces, white_sources = lax.optimization_barrier((traces, white_sources))
+    trace_float = traces.astype(jnp.float32)
+    trace_power = lax.psum(jnp.sum(trace_float * trace_float, axis=(1, 2)), "band")
     me = lax.axis_index("blk")
     held = white_sources[None]
     bits = blocks.bit_length() - 1

time: 56.2 us -> 60.3 us (1.073)
  other arithmetic: 5.13 us -> 7.06 us
  waiting for transfers between devices: 20.4 us -> 21.5 us
  starting transfers between devices: 14.3 us -> 15.3 us
    all_to_all x1, waiting for transfers between devices: 13.1 us -> 14.4 us  [per_device(): lax.all_to_all(partial, 'blk', split_axis=0, concat_axis=0, tiled=True)]
    dynamic_update_slice x1 -> x0, other arithmetic: 0.88 us -> none  [per_device(): lax.dynamic_update_slice_in_dim(widened, got[None], jnp.bitwise_xor(posit...]
    convert_element_type x0 -> x1, other arithmetic: none -> 0.85 us  [per_device(): white_sources = (source_float * lax.rsqrt(source_power / (2 * BINS) + EPS...]
    all_to_all x1, starting transfers between devices: 5.1 us -> 5.94 us  [per_device(): lax.all_to_all(partial, 'blk', split_axis=0, concat_axis=0, tiled=True)]
    add x1, other arithmetic: 0.01 us -> 0.67 us  [per_device(): slot_index = owners * capacity + arrival]
    reduce_sum x1, other arithmetic: 0.18 us -> 0.84 us  [per_device(): arrival = jnp.sum(owner_hits * earlier, axis=1)]
    convert_element_type x1, other arithmetic: 0.07 us -> 0.73 us  [per_device(): (owners[:, None] == jnp.arange(blocks, dtype=jnp.int32)[None, :]).astype(...]
    unnamed x3 -> x1, local copies, waits for them, and re-layouts: 1.81 us -> 1.81 us
  transfers between devices with their start and end apart: 8 -> 9, of which waited for: 6 -> 4; matrix products, arithmetic and copies ran while one was open for 10% -> 17% of each run, Pallas kernels for 0% -> 0%
where the time goes in v13:
time: 60.3 us; the launch traced here: 59.8 us
  waiting for transfers between devices  21.5 us (36%)
  starting transfers between devices  15.3 us (25%)
  other arithmetic  7.06 us (12%)
  Pallas kernels  6.39 us (11%)
  local copies, waits for them, and re-layouts  4.78 us (8%)
  blocking collectives  2.47 us (4%)
  matrix products  2.17 us (4%)
    all_to_all x1, waiting for transfers between devices, per_device(): lax.all_to_all(partial, 'blk', split_axis=0, concat_axis=0, tiled=True)  14.4 us
    ppermute x6, starting transfers between devices, per_device(): got = lax.ppermute(held, 'blk', route)  8.82 us
    pallas_call x1, Pallas kernels, correlate(): pl.pallas_call(body, grid=(blocks // group,), in_specs=[pl.BlockSpec(plac...  6.39 us
    all_to_all x1, starting transfers between devices, per_device(): lax.all_to_all(partial, 'blk', split_axis=0, concat_axis=0, tiled=True)  5.94 us
    ppermute x6, waiting for transfers between devices, per_device(): got = lax.ppermute(held, 'blk', route)  5.63 us
    reduce_sum x1, other arithmetic, per_device(): jnp.sum(trace_float * trace_float, axis=(1, 2))  2.81 us
    psum x1, blocking collectives, per_device(): lax.psum(jnp.sum(trace_float * trace_float, axis=(1, 2)), 'band')  2.47 us
    dot_general x1, matrix products, per_device(): jnp.dot(chosen.astype(jnp.bfloat16), traces.reshape(station_count, 2 * gr...  2.17 us
  transfers between devices with their start and end apart: 9, of which 4 were waited for; matrix products, arithmetic and copies ran while one was open for 17% of the time, Pallas kernels for 0%

profile of v13, /device:TPU:0, one launch (start us, length us, event | category | flops | bytes accessed | tf_op | source)
XLA Modules:
  0.0 59.8 jit_solution(5455702279574215341)
XLA Ops:
  0.0 0.9 %fusion.1 = f32[2]{0:T(128)S(1)} fusion(bf16[2,2,4096]{2,1,0:T(2,128)(2,1)} %param.5), kind=kLoop, calls=%fused_computation.11 | loop fusion | flops 49150 | bytes 32776 | tf_op jit(solution)/shard_map/reduce_sum | solution.py:99
  0.9 0.5 collective-permute-start
  1.3 0.7 %fusion.3 = s32[64,16]{1,0:T(8,128)S(1)} fusion(s32[64]{0:T(128)} %bitcast.56), kind=kLoop, calls=%fused_computation.20 | loop fusion | flops 2048 | bytes 4352 | tf_op jit(solution)/shard_map/convert_element_type | solution.py:130
  2.1 0.1 reduce_window_sum.11
  2.2 0.8 %select_reduce_fusion.1 = s32[64]{0:T(128)S(1)} fusion(s32[64,16]{1,0:T(8,128)S(1)} %reduce_window_sum.11, s32[64]{0:T(128)} %bitcast.57), kind=kLoop, calls=%fused_computation.18 | loop fusion | flops 5056 | bytes 4608 | tf_op jit(solution)/shard_map/reduce_sum | solution.py:132
  3.0 0.7 %multiply_add_fusion = s32[64]{0:T(128)S(1)} fusion(s32[64]{0:T(128)S(1)} %select_reduce_fusion.1, s32[64,1]{0,1:T(1,128)} %param.6), kind=kLoop, calls=%fused_computation.26 | loop fusion | flops 128 | bytes 768 | tf_op jit(solution)/shard_map/add | solution.py:133
  3.7 0.9 %fusion.2 = bf16[2,2,4096]{2,1,0:T(2,128)(2,1)S(1)} fusion(bf16[2,2,4096]{2,1,0:T(2,128)(2,1)} %param.5, f32[2]{0:T(128)S(1)} %add_rsqrt_fusion.1), kind=kLoop, calls=%fused_computation.12 | loop fusion | flops 49152 | bytes 65544 | tf_op jit(solution)/shard_map/convert_element_type | solution.py:103
  4.5 2.7 %collective-permute-start.1 = (bf16[1,2,2,4096]{3,2,1,0:T(2,128)(2,1)S(1)}, bf16[1,2,2,4096]{3,2,1,0:T(2,128)(2,1)S(1)}, u32[]{:S(2)}, u32[]{:S(2)}) collective-permute-start(bf16[1,2,2,4096]{3,2,1,0:T(2,128)(2,1)S(1)} %bitcast.53), channel_id=1, source_target_pairs={{0,8},{2,10},{4,12},{6,14},{8,0},{10,2},{12,4},{14,6},{16,24},{18,... | collective-permute-start | bytes 98312 | tf_op jit(solution)/shard_map/ppermute | solution.py:122
  7.2 2.6 %collective-permute-start.2 = (bf16[1,2,2,4096]{3,2,1,0:T(2,128)(2,1)S(1)}, bf16[1,2,2,4096]{3,2,1,0:T(2,128)(2,1)S(1)}, u32[]{:S(2)}, u32[]{:S(2)}) collective-permute-start(bf16[1,2,2,4096]{3,2,1,0:T(2,128)(2,1)S(1)} %bitcast.54), channel_id=1, source_target_pairs={{0,16},{2,18},{4,20},{6,22},{8,24},{10,26},{12,28},{14,30},{16,0},... | collective-permute-start | bytes 98312 | tf_op jit(solution)/shard_map/ppermute | solution.py:122
  9.8 2.8 %multiply_reduce_fusion = f32[64]{0:T(128)S(1)} fusion(bf16[64,2,4096]{2,1,0:T(2,128)(2,1)} %param.4), kind=kLoop, calls=%fused_computation.2 | loop fusion | flops 1572800 | bytes 1048832 | tf_op jit(solution)/shard_map/reduce_sum | solution.py:106
  12.6 1.8 %copy.21 = bf16[8,8,2,4096]{3,1,2,0:T(8,128)(2,1)S(1)} copy(bf16[8,8,2,4096]{3,2,1,0:T(2,128)(2,1)} %bitcast.49) | data formatting | bytes 2097152
  14.4 2.5 %psum.7 = f32[64]{0:T(128)S(1)} all-reduce(f32[64]{0:T(128)S(1)} %multiply_reduce_fusion), channel_id=1, replica_groups=mesh['blk'=16,'band'=2] {'band'}, use_global_device_ids=true, to_apply=%region_4.5 | all-reduce | flops 64 | bytes 512 | tf_op jit(solution)/shard_map/psum | solution.py:106
  16.9 0.1 select_reduce_fusion
  17.0 0.1 broadcast_in_dim.51
  17.1 2.2 %fusion = bf16[128,8192]{1,0:T(8,128)(2,1)} fusion(bf16[64,8192]{1,0:T(8,128)(2,1)S(1)} %bitcast.50, f32[128]{0:T(128)S(1)} %select_reduce_fusion, s32[64]{0:T(128)S(1)} %multiply_add_fusion), kind=kOutput, calls=%fused_computation.1 | convolution fusion | flops 136323072 | bytes 3146496 | tf_op jit(solution)/shard_map/dot_general | solution.py:135
  19.4 1.8 %collective-permute-start.4 = (bf16[4,1,2,2,4096]{4,3,2,0,1:T(2,128)(2,1)S(1)}, bf16[4,1,2,2,4096]{4,3,2,0,1:T(2,128)(2,1)S(1)}, u32[]{:S(2)}, u32[]{:S(2)}) collective-permute-start(bf16[4,1,2,2,4096]{4,3,2,0,1:T(2,128)(2,1)S(1)} %bitcast_dynamic-update-slice_fusion.4), channel_id=1, source_target_pairs={{0,2},{2,0},{4,6},{6,4},{8,10},{10,8},{12,14},{14,12},{16,18},{18,... | collective-permute-start | bytes 393224 | tf_op jit(solution)/shard_map/ppermute | solution.py:122
  21.2 1.5 %collective-permute-start.5 = (bf16[4,1,2,2,4096]{4,3,2,0,1:T(2,128)(2,1)S(1)}, bf16[4,1,2,2,4096]{4,3,2,0,1:T(2,128)(2,1)S(1)}, u32[]{:S(2)}, u32[]{:S(2)}) collective-permute-start(bf16[4,1,2,2,4096]{4,3,2,0,1:T(2,128)(2,1)S(1)} %bitcast_dynamic-update-slice_fusion.4), channel_id=1, source_target_pairs={{0,4},{2,6},{4,0},{6,2},{8,12},{10,14},{12,8},{14,10},{16,20},{18,... | collective-permute-start | bytes 393224 | tf_op jit(solution)/shard_map/ppermute | solution.py:122
  22.7 0.3 collective-permute-start.6
  23.0 0.5 broadcast_in_dim.50
  23.5 0.1 bitcast_dynamic-update-slice_fusion.2
  23.6 1.6 %collective-permute-done.4 = bf16[4,1,2,2,4096]{4,3,2,0,1:T(2,128)(2,1)S(1)} collective-permute-done((bf16[4,1,2,2,4096]{4,3,2,0,1:T(2,128)(2,1)S(1)}, bf16[4,1,2,2,4096]{4,3,2,0,1:T(2,128)(2,1)S(1)}, u32[]{:S(2)}, u32[]{:S(2)}) %collective-permute-start.4) | collective-permute-done | bytes 131104 | tf_op jit(solution)/shard_map/ppermute | solution.py:122
  25.2 0.1 bitcast_dynamic-update-slice_fusion.1
  25.3 4.0 %collective-permute-done.5 = bf16[4,1,2,2,4096]{4,3,2,0,1:T(2,128)(2,1)S(1)} collective-permute-done((bf16[4,1,2,2,4096]{4,3,2,0,1:T(2,128)(2,1)S(1)}, bf16[4,1,2,2,4096]{4,3,2,0,1:T(2,128)(2,1)S(1)}, u32[]{:S(2)}, u32[]{:S(2)}) %collective-permute-start.5) | collective-permute-done | bytes 131104 | tf_op jit(solution)/shard_map/ppermute | solution.py:122
  29.3 0.1 bitcast_dynamic-update-slice_fusion
  29.4 0.1 bitcast_dynamic-update-slice_fusion.3
  29.6 1.0 %reshape.32.source_ref = bf16[16,4,4096]{2,1,0:T(4,128)(2,1)} reshape(bf16[1,4,4,2,2,4096]{5,4,3,2,1,0:T(2,128)(2,1)S(1)} %bitcast.52) | data formatting | bytes 1048576 | tf_op jit(solution)/shard_map/reshape | solution.py:147
  30.5 6.4 %shard_map.46 = bf16[16,64,256]{2,1,0:T(8,128)(2,1)} custom-call(bf16[16,16,4096]{2,1,0:T(8,128)(2,1)} %bitcast.48, bf16[16,4,4096]{2,1,0:T(4,128)(2,1)} %reshape.32.source_ref, bf16[2048,256]{1,0:T(8,128)(2,1)} %constant.42.clone.table_ref), custom_call_target="tpu_custom_call" | custom-call | flops 1107296256 | bytes 4194304 | tf_op jit(solution)/shard_map/pallas_call | solution.py:59
  36.9 5.9 %all-to-all-start = ((bf16[16,64,256]{2,1,0:T(8,128)(2,1)}), bf16[16,64,256]{2,1,0:T(8,128)(2,1)S(1)}, u32[]{:S(2)}, u32[]{:S(2)}) async-start(bf16[16,64,256]{2,1,0:T(8,128)(2,1)} %shard_map.46), calls=%async_computation | async-start | bytes 1048576 | tf_op jit(solution)/shard_map/all_to_all | solution.py:150
  42.9 14.4 %all-to-all-done = bf16[16,64,256]{2,1,0:T(8,128)(2,1)S(1)} async-done(((bf16[16,64,256]{2,1,0:T(8,128)(2,1)}), bf16[16,64,256]{2,1,0:T(8,128)(2,1)S(1)}, u32[]{:S(2)}, u32[]{:S(2)}) %all-to-all-start) | async-done | bytes 524320 | tf_op jit(solution)/shard_map/all_to_all | solution.py:150
  57.3 0.1 collective-permute-start.7
  57.4 1.5 %collective-permute-done.7 = bf16[8,64,256]{2,1,0:T(8,128)(2,1)S(1)} collective-permute-done((bf16[8,64,256]{2,1,0:T(8,128)(2,1)S(1)}, bf16[8,64,256]{2,1,0:T(8,128)(2,1)S(1)}, u32[]{:S(2)}, u32[]{:S(2)}) %collective-permute-start.7) | collective-permute-done | bytes 262176 | tf_op jit(solution)/shard_map/ppermute | solution.py:154
  58.9 0.8 %copy.23 = f32[2,4,8,8,256]{4,3,2,1,0:T(8,128)} copy(f32[2,4,8,8,256]{4,3,1,0,2:T(8,128)S(1)} %bitcast.51) | data formatting | bytes 1048576 | tf_op jit(solution)/shard_map/transpose | solution.py:157
  (14 shorter events, 0.3 us)
Async XLA Ops:
  0.9 2.8 %collective-permute-start = (f32[2]{0:T(128)S(1)}, f32[2]{0:T(128)S(1)}, u32[]{:S(2)}, u32[]{:S(2)}) collective-permute-start(f32[2]{0:T(128)S(1)} %fusion.1), channel_id=1, source_target_pairs={{0,1},{1,0},{2,3},{3,2},{4,5},{5,4},{6,7},{7,6},{8,9},{9,8},{10,11... | collective-permute-start | bytes 32 | tf_op jit(solution)/shard_map/ppermute | solution.py:100
  4.5 14.8 %collective-permute-start.1 = (bf16[1,2,2,4096]{3,2,1,0:T(2,128)(2,1)S(1)}, bf16[1,2,2,4096]{3,2,1,0:T(2,128)(2,1)S(1)}, u32[]{:S(2)}, u32[]{:S(2)}) collective-permute-start(bf16[1,2,2,4096]{3,2,1,0:T(2,128)(2,1)S(1)} %bitcast.53), channel_id=1, source_target_pairs={{0,8},{2,10},{4,12},{6,14},{8,0},{10,2},{12,4},{14,6},{16,24},{18,... | collective-permute-start | bytes 98312 | tf_op jit(solution)/shard_map/ppermute | solution.py:122
  7.2 12.1 %collective-permute-start.2 = (bf16[1,2,2,4096]{3,2,1,0:T(2,128)(2,1)S(1)}, bf16[1,2,2,4096]{3,2,1,0:T(2,128)(2,1)S(1)}, u32[]{:S(2)}, u32[]{:S(2)}) collective-permute-start(bf16[1,2,2,4096]{3,2,1,0:T(2,128)(2,1)S(1)} %bitcast.54), channel_id=1, source_target_pairs={{0,16},{2,18},{4,20},{6,22},{8,24},{10,26},{12,28},{14,30},{16,0},... | collective-permute-start | bytes 98312 | tf_op jit(solution)/shard_map/ppermute | solution.py:122
  9.8 9.6 %collective-permute-start.3 = (bf16[1,2,2,4096]{3,2,1,0:T(2,128)(2,1)S(1)}, bf16[1,2,2,4096]{3,2,1,0:T(2,128)(2,1)S(1)}, u32[]{:S(2)}, u32[]{:S(2)}) collective-permute-start(bf16[1,2,2,4096]{3,2,1,0:T(2,128)(2,1)S(1)} %bitcast.55), channel_id=1, source_target_pairs={{0,24},{2,26},{4,28},{6,30},{8,16},{10,18},{12,20},{14,22},{16,8},... | collective-permute-start | bytes 98312 | tf_op jit(solution)/shard_map/ppermute | solution.py:122
  19.4 5.8 %collective-permute-start.4 = (bf16[4,1,2,2,4096]{4,3,2,0,1:T(2,128)(2,1)S(1)}, bf16[4,1,2,2,4096]{4,3,2,0,1:T(2,128)(2,1)S(1)}, u32[]{:S(2)}, u32[]{:S(2)}) collective-permute-start(bf16[4,1,2,2,4096]{4,3,2,0,1:T(2,128)(2,1)S(1)} %bitcast_dynamic-update-slice_fusion.4), channel_id=1, source_target_pairs={{0,2},{2,0},{4,6},{6,4},{8,10},{10,8},{12,14},{14,12},{16,18},{18,... | collective-permute-start | bytes 393224 | tf_op jit(solution)/shard_map/ppermute | solution.py:122
  21.2 8.1 %collective-permute-start.5 = (bf16[4,1,2,2,4096]{4,3,2,0,1:T(2,128)(2,1)S(1)}, bf16[4,1,2,2,4096]{4,3,2,0,1:T(2,128)(2,1)S(1)}, u32[]{:S(2)}, u32[]{:S(2)}) collective-permute-start(bf16[4,1,2,2,4096]{4,3,2,0,1:T(2,128)(2,1)S(1)} %bitcast_dynamic-update-slice_fusion.4), channel_id=1, source_target_pairs={{0,4},{2,6},{4,0},{6,2},{8,12},{10,14},{12,8},{14,10},{16,20},{18,... | collective-permute-start | bytes 393224 | tf_op jit(solution)/shard_map/ppermute | solution.py:122
  22.7 6.7 %collective-permute-start.6 = (bf16[4,1,2,2,4096]{4,3,2,0,1:T(2,128)(2,1)S(1)}, bf16[4,1,2,2,4096]{4,3,2,0,1:T(2,128)(2,1)S(1)}, u32[]{:S(2)}, u32[]{:S(2)}) collective-permute-start(bf16[4,1,2,2,4096]{4,3,2,0,1:T(2,128)(2,1)S(1)} %bitcast_dynamic-update-slice_fusion.4), channel_id=1, source_target_pairs={{0,6},{2,4},{4,2},{6,0},{8,14},{10,12},{12,10},{14,8},{16,22},{18,... | collective-permute-start | bytes 393224 | tf_op jit(solution)/shard_map/ppermute | solution.py:122
  36.9 20.3 %all-to-all-start = ((bf16[16,64,256]{2,1,0:T(8,128)(2,1)}), bf16[16,64,256]{2,1,0:T(8,128)(2,1)S(1)}, u32[]{:S(2)}, u32[]{:S(2)}) async-start(bf16[16,64,256]{2,1,0:T(8,128)(2,1)} %shard_map.46), calls=%async_computation | async-start | bytes 1048576 | tf_op jit(solution)/shard_map/all_to_all | solution.py:150
  57.3 1.6 %collective-permute-start.7 = (bf16[8,64,256]{2,1,0:T(8,128)(2,1)S(1)}, bf16[8,64,256]{2,1,0:T(8,128)(2,1)S(1)}, u32[]{:S(2)}, u32[]{:S(2)}) collective-permute-start(bf16[8,64,256]{2,1,0:T(8,128)(2,1)S(1)} %constant_dynamic-slice_fusion), channel_id=1, source_target_pairs={{0,1},{1,0},{2,3},{3,2},{4,5},{5,4},{6,7},{7,6},{8,9},{9,8},{10,11... | collective-permute-start | bytes 786440 | tf_op jit(solution)/shard_map/ppermute | solution.py:154

commit v14 on v12

--- a/solution.py
+++ b/solution.py
@@ -150,14 +150,21 @@
     white_sources = held.reshape(blocks, source_count * 2, group_bins)
 
     partial = correlate(placed, white_sources, table, offsets, capacity)
-    arrived = lax.all_to_all(partial, "blk", split_axis=0, concat_axis=0, tiled=True)
+    rows = partial.shape[1] // source_count
+    keep = lax.dynamic_slice_in_dim(partial, band * rows, rows, axis=1)
+    give = lax.dynamic_slice_in_dim(partial, (1 - band) * rows, rows, axis=1)
+    give = lax.ppermute(give, "band", [(0, 1), (1, 0)])
+    summed = (keep.astype(jnp.float32) + give.astype(jnp.float32)).astype(jnp.bfloat16)
+    arrived = lax.all_to_all(summed, "blk", split_axis=0, concat_axis=0, tiled=True)
     half = blocks // 2
-    mine = lax.dynamic_slice_in_dim(arrived, band * half, half, axis=0)
-    other = lax.dynamic_slice_in_dim(arrived, (1 - band) * half, half, axis=0)
-    other = lax.ppermute(other, "band", [(0, 1), (1, 0)])
-    summed = mine.astype(jnp.float32) + other.astype(jnp.float32)
-    summed = summed.reshape(half, source_count, offsets, capacity, lags_out)
-    return jnp.transpose(summed, (1, 2, 0, 3, 4)).reshape(
+    own_half = lax.dynamic_slice_in_dim(arrived, band * half, half, axis=0)
+    other_half = lax.dynamic_slice_in_dim(arrived, (1 - band) * half, half, axis=0)
+    other_source = lax.ppermute(other_half, "band", [(0, 1), (1, 0)])
+    first = jnp.where(band == 0, own_half, other_source)
+    second = jnp.where(band == 0, other_source, own_half)
+    both = jnp.stack([first, second], axis=0).astype(jnp.float32)
+    both = both.reshape(source_count, half, offsets, capacity, lags_out)
+    return jnp.transpose(both, (0, 2, 1, 3, 4)).reshape(
         source_count, offsets, half * capacity, lags_out
     )
 

time: 56.2 us -> 57.4 us (1.021)
  other arithmetic: 5.13 us -> 7.66 us
  waiting for transfers between devices: 20.4 us -> 18.8 us
    all_to_all x1, waiting for transfers between devices: 13.1 us -> 10.2 us  [per_device(): lax.all_to_all(summed, 'blk', split_axis=0, concat_axis=0, tiled=True)]
    convert_element_type x0 -> x1, other arithmetic: none -> 1.73 us  [per_device(): (keep.astype(jnp.float32) + give.astype(jnp.float32)).astype(jnp.bfloat16)]
    ppermute x1 -> x2, waiting for transfers between devices: 1.52 us -> 2.85 us  [the longest x1 1.52 us: per_device(): give = lax.ppermute(give, 'band', [(0, 1), (1, 0)])]
    dynamic_slice x1 -> x2, local copies, waits for them, and re-layouts: 0.02 us -> 0.98 us  [the longest x1 0.97 us: per_device(): give = lax.dynamic_slice_in_dim(partial, (1 - band) * rows, rows, axis=1)]
    transpose x1 -> x0, local copies, waits for them, and re-layouts: 0.84 us -> none  [per_device(): jnp.transpose(summed, (1, 2, 0, 3, 4))]
    reshape x0 -> x1, other arithmetic: none -> 0.84 us  [per_device(): jnp.transpose(both, (0, 2, 1, 3, 4))]
  transfers between devices with their start and end apart: 8 -> 9, of which waited for: 6 -> 7; matrix products, arithmetic and copies ran while one was open for 10% -> 9% of each run, Pallas kernels for 0% -> 0%
where the time goes in v14:
time: 57.4 us; the launch traced here: 56.9 us
  waiting for transfers between devices  18.8 us (33%)
  starting transfers between devices  14.4 us (25%)
  other arithmetic  7.66 us (13%)
  Pallas kernels  6.39 us (11%)
  local copies, waits for them, and re-layouts  4.85 us (8%)
  blocking collectives  2.56 us (4%)
  matrix products  2.18 us (4%)
    all_to_all x1, waiting for transfers between devices, per_device(): lax.all_to_all(summed, 'blk', split_axis=0, concat_axis=0, tiled=True)  10.2 us
    ppermute x6, starting transfers between devices, per_device(): got = lax.ppermute(held, 'blk', route)  9.11 us
    pallas_call x1, Pallas kernels, correlate(): pl.pallas_call(body, grid=(blocks // group,), in_specs=[pl.BlockSpec(plac...  6.39 us
    ppermute x6, waiting for transfers between devices, per_device(): got = lax.ppermute(held, 'blk', route)  5.76 us
    all_to_all x1, starting transfers between devices, per_device(): lax.all_to_all(summed, 'blk', split_axis=0, concat_axis=0, tiled=True)  5.1 us
    reduce_sum x1, other arithmetic, per_device(): jnp.sum(trace_float * trace_float, axis=(1, 2))  2.82 us
    psum x1, blocking collectives, per_device(): lax.psum((jnp.sum(trace_float * trace_float, axis=(1, 2)), jnp.sum(source...  2.56 us
    dot_general x1, matrix products, per_device(): jnp.dot(chosen.astype(jnp.bfloat16), traces.reshape(station_count, 2 * gr...  2.18 us
  transfers between devices with their start and end apart: 9, of which 7 were waited for; matrix products, arithmetic and copies ran while one was open for 9% of the time, Pallas kernels for 0%

profile of v14, /device:TPU:0, one launch (start us, length us, event | category | flops | bytes accessed | tf_op | source)
XLA Modules:
  0.0 56.9 jit_solution(3726742838332985552)
XLA Ops:
  0.0 2.8 %multiply_reduce_fusion = f32[64]{0:T(128)S(1)} fusion(bf16[64,2,4096]{2,1,0:T(2,128)(2,1)} %param.4), kind=kLoop, calls=%fused_computation.2 | loop fusion | flops 1572800 | bytes 1048832 | tf_op jit(solution)/shard_map/reduce_sum | solution.py:102
  2.8 0.9 %fusion.1 = f32[2]{0:T(128)S(1)} fusion(bf16[2,2,4096]{2,1,0:T(2,128)(2,1)} %param.5), kind=kLoop, calls=%fused_computation.14 | loop fusion | flops 49150 | bytes 32776 | tf_op jit(solution)/shard_map/reduce_sum | solution.py:103
  3.7 2.6 %all-reduce = (f32[64]{0:T(128)S(1)}, f32[2]{0:T(128)S(1)}) all-reduce(f32[64]{0:T(128)S(1)} %multiply_reduce_fusion, f32[2]{0:T(128)S(1)} %fusion.1), channel_id=1, replica_groups=mesh['blk'=16,'band'=2] {'band'}, use_global_device_ids=true, to_apply=%region_3.0 | all-reduce | flops 66 | bytes 528 | tf_op jit(solution)/shard_map/psum | solution.py:100
  6.4 0.9 %bitcast_dynamic-update-slice_fusion.7 = (bf16[4,1,2,2,4096]{4,3,2,0,1:T(2,128)(2,1)S(1)}, bf16[2,2,4096]{2,1,0:T(2,128)(2,1)S(1)}) fusion(bf16[4,1,2,2,4096]{4,3,2,0,1:T(2,128)(2,1)S(1)} %broadcast_in_dim.51, s32[]{:T(128)S(6)} %select_n.54, f32[2]{0:T(128)S(1)} %add_rsqrt_fusion, bf16[2,2,4096]{2,1,0:T(2,128)(2,1)} %param.5), kind=kLoop, calls=%fused_computation.19 | loop fusion | flops 49152 | bytes 98820 | tf_op jit(solution)/shard_map/dynamic_update_slice | solution.py:126
  7.2 3.0 %collective-permute-start = (bf16[1,2,2,4096]{3,2,1,0:T(2,128)(2,1)S(1)}, bf16[1,2,2,4096]{3,2,1,0:T(2,128)(2,1)S(1)}, u32[]{:S(2)}, u32[]{:S(2)}) collective-permute-start(bf16[1,2,2,4096]{3,2,1,0:T(2,128)(2,1)S(1)} %bitcast.55), channel_id=1, source_target_pairs={{0,8},{2,10},{4,12},{6,14},{8,0},{10,2},{12,4},{14,6},{16,24},{18,... | collective-permute-start | bytes 98312 | tf_op jit(solution)/shard_map/ppermute | solution.py:125
  10.2 2.6 %collective-permute-start.1 = (bf16[1,2,2,4096]{3,2,1,0:T(2,128)(2,1)S(1)}, bf16[1,2,2,4096]{3,2,1,0:T(2,128)(2,1)S(1)}, u32[]{:S(2)}, u32[]{:S(2)}) collective-permute-start(bf16[1,2,2,4096]{3,2,1,0:T(2,128)(2,1)S(1)} %bitcast.56), channel_id=1, source_target_pairs={{0,16},{2,18},{4,20},{6,22},{8,24},{10,26},{12,28},{14,30},{16,0},... | collective-permute-start | bytes 98312 | tf_op jit(solution)/shard_map/ppermute | solution.py:125
  12.8 1.8 %copy.21 = bf16[8,8,2,4096]{3,1,2,0:T(8,128)(2,1)S(1)} copy(bf16[8,8,2,4096]{3,2,1,0:T(2,128)(2,1)} %bitcast.52) | data formatting | bytes 2097152
  14.7 0.1 reduce_window_sum.11
  14.8 0.2 select_reduce_fusion.1
  15.0 0.1 select_reduce_fusion
  15.1 2.2 %fusion = bf16[128,8192]{1,0:T(8,128)(2,1)} fusion(bf16[64,8192]{1,0:T(8,128)(2,1)S(1)} %bitcast.53, f32[128]{0:T(128)S(1)} %select_reduce_fusion, s32[64]{0:T(128)S(1)} %multiply_add_fusion), kind=kOutput, calls=%fused_computation.1 | convolution fusion | flops 136323072 | bytes 3146496 | tf_op jit(solution)/shard_map/dot_general | solution.py:138
  17.4 1.1 %collective-permute-done.2 = bf16[1,2,2,4096]{3,2,1,0:T(2,128)(2,1)S(1)} collective-permute-done((bf16[1,2,2,4096]{3,2,1,0:T(2,128)(2,1)S(1)}, bf16[1,2,2,4096]{3,2,1,0:T(2,128)(2,1)S(1)}, u32[]{:S(2)}, u32[]{:S(2)}) %collective-permute-start.2) | collective-permute-done | bytes 32800 | tf_op jit(solution)/shard_map/ppermute | solution.py:125
  18.6 1.6 %collective-permute-start.3 = (bf16[4,1,2,2,4096]{4,3,2,0,1:T(2,128)(2,1)S(1)}, bf16[4,1,2,2,4096]{4,3,2,0,1:T(2,128)(2,1)S(1)}, u32[]{:S(2)}, u32[]{:S(2)}) collective-permute-start(bf16[4,1,2,2,4096]{4,3,2,0,1:T(2,128)(2,1)S(1)} %bitcast_dynamic-update-slice_fusion.4), channel_id=1, source_target_pairs={{0,2},{2,0},{4,6},{6,4},{8,10},{10,8},{12,14},{14,12},{16,18},{18,... | collective-permute-start | bytes 393224 | tf_op jit(solution)/shard_map/ppermute | solution.py:125
  20.1 1.5 %collective-permute-start.4 = (bf16[4,1,2,2,4096]{4,3,2,0,1:T(2,128)(2,1)S(1)}, bf16[4,1,2,2,4096]{4,3,2,0,1:T(2,128)(2,1)S(1)}, u32[]{:S(2)}, u32[]{:S(2)}) collective-permute-start(bf16[4,1,2,2,4096]{4,3,2,0,1:T(2,128)(2,1)S(1)} %bitcast_dynamic-update-slice_fusion.4), channel_id=1, source_target_pairs={{0,4},{2,6},{4,0},{6,2},{8,12},{10,14},{12,8},{14,10},{16,20},{18,... | collective-permute-start | bytes 393224 | tf_op jit(solution)/shard_map/ppermute | solution.py:125
  21.6 0.5 collective-permute-start.5
  22.1 0.5 broadcast_in_dim.50
  22.6 0.1 bitcast_dynamic-update-slice_fusion.2
  22.7 2.2 %collective-permute-done.3 = bf16[4,1,2,2,4096]{4,3,2,0,1:T(2,128)(2,1)S(1)} collective-permute-done((bf16[4,1,2,2,4096]{4,3,2,0,1:T(2,128)(2,1)S(1)}, bf16[4,1,2,2,4096]{4,3,2,0,1:T(2,128)(2,1)S(1)}, u32[]{:S(2)}, u32[]{:S(2)}) %collective-permute-start.3) | collective-permute-done | bytes 131104 | tf_op jit(solution)/shard_map/ppermute | solution.py:125
  24.9 0.1 bitcast_dynamic-update-slice_fusion.1
  25.0 1.1 %collective-permute-done.4 = bf16[4,1,2,2,4096]{4,3,2,0,1:T(2,128)(2,1)S(1)} collective-permute-done((bf16[4,1,2,2,4096]{4,3,2,0,1:T(2,128)(2,1)S(1)}, bf16[4,1,2,2,4096]{4,3,2,0,1:T(2,128)(2,1)S(1)}, u32[]{:S(2)}, u32[]{:S(2)}) %collective-permute-start.4) | collective-permute-done | bytes 131104 | tf_op jit(solution)/shard_map/ppermute | solution.py:125
  26.1 0.1 bitcast_dynamic-update-slice_fusion
  26.2 1.3 %collective-permute-done.5 = bf16[4,1,2,2,4096]{4,3,2,0,1:T(2,128)(2,1)S(1)} collective-permute-done((bf16[4,1,2,2,4096]{4,3,2,0,1:T(2,128)(2,1)S(1)}, bf16[4,1,2,2,4096]{4,3,2,0,1:T(2,128)(2,1)S(1)}, u32[]{:S(2)}, u32[]{:S(2)}) %collective-permute-start.5) | collective-permute-done | bytes 131104 | tf_op jit(solution)/shard_map/ppermute | solution.py:125
  27.5 0.1 bitcast_dynamic-update-slice_fusion.3
  27.6 1.0 %reshape.37.source_ref = bf16[16,4,4096]{2,1,0:T(4,128)(2,1)} reshape(bf16[1,4,4,2,2,4096]{5,4,3,2,1,0:T(2,128)(2,1)S(1)} %bitcast.54) | data formatting | bytes 1048576 | tf_op jit(solution)/shard_map/reshape | solution.py:150
  28.6 6.4 %shard_map.46 = bf16[16,64,256]{2,1,0:T(8,128)(2,1)} custom-call(bf16[16,16,4096]{2,1,0:T(8,128)(2,1)} %bitcast.51, bf16[16,4,4096]{2,1,0:T(4,128)(2,1)} %reshape.37.source_ref, bf16[2048,256]{1,0:T(8,128)(2,1)} %constant.46.clone.table_ref), custom_call_target="tpu_custom_call" | custom-call | flops 1107296256 | bytes 4194304 | tf_op jit(solution)/shard_map/pallas_call | solution.py:59
  35.0 1.0 %constant_dynamic-slice_fusion.1 = bf16[16,32,256]{2,1,0:T(8,128)(2,1)S(1)} fusion(bf16[16,64,256]{2,1,0:T(8,128)(2,1)} %shard_map.46, s32[]{:T(128)S(6)} %select_n.63), kind=kLoop, calls=%fused_computation.27 | loop fusion | bytes 524292 | tf_op jit(solution)/shard_map/dynamic_slice | solution.py:155
  36.1 1.5 %collective-permute-done.6 = bf16[16,32,256]{2,1,0:T(8,128)(2,1)S(1)} collective-permute-done((bf16[16,32,256]{2,1,0:T(8,128)(2,1)S(1)}, bf16[16,32,256]{2,1,0:T(8,128)(2,1)S(1)}, u32[]{:S(2)}, u32[]{:S(2)}) %collective-permute-start.6) | collective-permute-done | bytes 262176 | tf_op jit(solution)/shard_map/ppermute | solution.py:156
  37.6 1.7 %add_convert_fusion = bf16[16,32,256]{2,1,0:T(8,128)(2,1)} fusion(bf16[16,32,256]{2,1,0:T(8,128)(2,1)S(1)} %collective-permute-done.6, bf16[16,64,256]{2,1,0:T(8,128)(2,1)} %shard_map.46, s32[]{:T(128)S(6)} %select_n.62), kind=kLoop, calls=%fused_computation.5 | loop fusion | flops 524288 | bytes 786436 | tf_op jit(solution)/shard_map/convert_element_type | solution.py:157
  39.3 5.1 %all-to-all-start = ((bf16[16,32,256]{2,1,0:T(8,128)(2,1)}), bf16[16,32,256]{2,1,0:T(8,128)(2,1)S(1)}, u32[]{:S(2)}, u32[]{:S(2)}) async-start(bf16[16,32,256]{2,1,0:T(8,128)(2,1)} %add_convert_fusion), calls=%async_computation | async-start | bytes 524288 | tf_op jit(solution)/shard_map/all_to_all | solution.py:158
  44.4 10.2 %all-to-all-done = bf16[16,32,256]{2,1,0:T(8,128)(2,1)S(1)} async-done(((bf16[16,32,256]{2,1,0:T(8,128)(2,1)}), bf16[16,32,256]{2,1,0:T(8,128)(2,1)S(1)}, u32[]{:S(2)}, u32[]{:S(2)}) %all-to-all-start) | async-done | bytes 262176 | tf_op jit(solution)/shard_map/all_to_all | solution.py:158
  54.7 1.3 %collective-permute-done.7 = bf16[8,32,256]{2,1,0:T(8,128)(2,1)S(1)} collective-permute-done((bf16[8,32,256]{2,1,0:T(8,128)(2,1)S(1)}, bf16[8,32,256]{2,1,0:T(8,128)(2,1)S(1)}, u32[]{:S(2)}, u32[]{:S(2)}) %collective-permute-start.7) | collective-permute-done | bytes 131104 | tf_op jit(solution)/shard_map/ppermute | solution.py:162
  56.1 0.8 %copy_bitcast_fusion = f32[2,4,64,256]{3,2,1,0:T(8,128)} fusion(bf16[1,8,4,8,256]{4,3,2,1,0:T(8,128)(2,1)S(1)} %get-tuple-element.10, bf16[1,8,4,8,256]{4,3,2,1,0:T(8,128)(2,1)S(1)} %get-tuple-element.9), kind=kLoop, calls=%fused_computation.3 | loop fusion | flops 262144 | bytes 786432 | tf_op jit(solution)/shard_map/reshape | solution.py:167
  (17 shorter events, 0.5 us)
Async XLA Ops:
  0.0 14.6 %copy-start = (s32[64,1]{0,1:T(1,128)S(1)}, s32[64,1]{0,1:T(1,128)}, u32[]{:S(2)}) copy-start(s32[64,1]{0,1:T(1,128)} %param.6) | copy-start | bytes 772
  7.2 10.0 %collective-permute-start = (bf16[1,2,2,4096]{3,2,1,0:T(2,128)(2,1)S(1)}, bf16[1,2,2,4096]{3,2,1,0:T(2,128)(2,1)S(1)}, u32[]{:S(2)}, u32[]{:S(2)}) collective-permute-start(bf16[1,2,2,4096]{3,2,1,0:T(2,128)(2,1)S(1)} %bitcast.55), channel_id=1, source_target_pairs={{0,8},{2,10},{4,12},{6,14},{8,0},{10,2},{12,4},{14,6},{16,24},{18,... | collective-permute-start | bytes 98312 | tf_op jit(solution)/shard_map/ppermute | solution.py:125
  10.2 7.1 %collective-permute-start.1 = (bf16[1,2,2,4096]{3,2,1,0:T(2,128)(2,1)S(1)}, bf16[1,2,2,4096]{3,2,1,0:T(2,128)(2,1)S(1)}, u32[]{:S(2)}, u32[]{:S(2)}) collective-permute-start(bf16[1,2,2,4096]{3,2,1,0:T(2,128)(2,1)S(1)} %bitcast.56), channel_id=1, source_target_pairs={{0,16},{2,18},{4,20},{6,22},{8,24},{10,26},{12,28},{14,30},{16,0},... | collective-permute-start | bytes 98312 | tf_op jit(solution)/shard_map/ppermute | solution.py:125
  12.8 5.7 %collective-permute-start.2 = (bf16[1,2,2,4096]{3,2,1,0:T(2,128)(2,1)S(1)}, bf16[1,2,2,4096]{3,2,1,0:T(2,128)(2,1)S(1)}, u32[]{:S(2)}, u32[]{:S(2)}) collective-permute-start(bf16[1,2,2,4096]{3,2,1,0:T(2,128)(2,1)S(1)} %bitcast.57), channel_id=1, source_target_pairs={{0,24},{2,26},{4,28},{6,30},{8,16},{10,18},{12,20},{14,22},{16,8},... | collective-permute-start | bytes 98312 | tf_op jit(solution)/shard_map/ppermute | solution.py:125
  18.6 6.3 %collective-permute-start.3 = (bf16[4,1,2,2,4096]{4,3,2,0,1:T(2,128)(2,1)S(1)}, bf16[4,1,2,2,4096]{4,3,2,0,1:T(2,128)(2,1)S(1)}, u32[]{:S(2)}, u32[]{:S(2)}) collective-permute-start(bf16[4,1,2,2,4096]{4,3,2,0,1:T(2,128)(2,1)S(1)} %bitcast_dynamic-update-slice_fusion.4), channel_id=1, source_target_pairs={{0,2},{2,0},{4,6},{6,4},{8,10},{10,8},{12,14},{14,12},{16,18},{18,... | collective-permute-start | bytes 393224 | tf_op jit(solution)/shard_map/ppermute | solution.py:125
  20.1 6.0 %collective-permute-start.4 = (bf16[4,1,2,2,4096]{4,3,2,0,1:T(2,128)(2,1)S(1)}, bf16[4,1,2,2,4096]{4,3,2,0,1:T(2,128)(2,1)S(1)}, u32[]{:S(2)}, u32[]{:S(2)}) collective-permute-start(bf16[4,1,2,2,4096]{4,3,2,0,1:T(2,128)(2,1)S(1)} %bitcast_dynamic-update-slice_fusion.4), channel_id=1, source_target_pairs={{0,4},{2,6},{4,0},{6,2},{8,12},{10,14},{12,8},{14,10},{16,20},{18,... | collective-permute-start | bytes 393224 | tf_op jit(solution)/shard_map/ppermute | solution.py:125
  21.6 5.9 %collective-permute-start.5 = (bf16[4,1,2,2,4096]{4,3,2,0,1:T(2,128)(2,1)S(1)}, bf16[4,1,2,2,4096]{4,3,2,0,1:T(2,128)(2,1)S(1)}, u32[]{:S(2)}, u32[]{:S(2)}) collective-permute-start(bf16[4,1,2,2,4096]{4,3,2,0,1:T(2,128)(2,1)S(1)} %bitcast_dynamic-update-slice_fusion.4), channel_id=1, source_target_pairs={{0,6},{2,4},{4,2},{6,0},{8,14},{10,12},{12,10},{14,8},{16,22},{18,... | collective-permute-start | bytes 393224 | tf_op jit(solution)/shard_map/ppermute | solution.py:125
  36.0 1.6 %collective-permute-start.6 = (bf16[16,32,256]{2,1,0:T(8,128)(2,1)S(1)}, bf16[16,32,256]{2,1,0:T(8,128)(2,1)S(1)}, u32[]{:S(2)}, u32[]{:S(2)}) collective-permute-start(bf16[16,32,256]{2,1,0:T(8,128)(2,1)S(1)} %constant_dynamic-slice_fusion.1), channel_id=1, source_target_pairs={{0,1},{1,0},{2,3},{3,2},{4,5},{5,4},{6,7},{7,6},{8,9},{9,8},{10,11... | collective-permute-start | bytes 786440 | tf_op jit(solution)/shard_map/ppermute | solution.py:156
  39.3 15.3 %all-to-all-start = ((bf16[16,32,256]{2,1,0:T(8,128)(2,1)}), bf16[16,32,256]{2,1,0:T(8,128)(2,1)S(1)}, u32[]{:S(2)}, u32[]{:S(2)}) async-start(bf16[16,32,256]{2,1,0:T(8,128)(2,1)} %add_convert_fusion), calls=%async_computation | async-start | bytes 524288 | tf_op jit(solution)/shard_map/all_to_all | solution.py:158
  54.6 1.4 %collective-permute-start.7 = (bf16[8,32,256]{2,1,0:T(8,128)(2,1)S(1)}, bf16[8,32,256]{2,1,0:T(8,128)(2,1)S(1)}, u32[]{:S(2)}, u32[]{:S(2)}) collective-permute-start(bf16[8,32,256]{2,1,0:T(8,128)(2,1)S(1)} %constant_dynamic-slice_fusion), channel_id=1, source_target_pairs={{0,1},{1,0},{2,3},{3,2},{4,5},{5,4},{6,7},{7,6},{8,9},{9,8},{10,11... | collective-permute-start | bytes 393224 | tf_op jit(solution)/shard_map/ppermute | solution.py:162

commit v15 on v12

--- a/solution.py
+++ b/solution.py
@@ -21,14 +21,14 @@
 
 def correlate_kernel(blocks, offsets, capacity, group, norm_scale, placed_ref, source_ref, table_ref, out_ref, cross_ref):
     first = pl.program_id(0) * group
-    folds = placed_ref.shape[2] // PERIOD
+    folds = placed_ref.shape[3] // PERIOD
     rows = 2 * offsets * capacity
     for member in range(group):
         block = first + member
         for offset in range(offsets):
-            owned = placed_ref[lax.rem(block - offset + blocks, blocks)]
-            real_t = owned[:capacity]
-            imag_t = owned[capacity:]
+            owner_block = lax.rem(block - offset + blocks, blocks)
+            real_t = placed_ref[0, owner_block]
+            imag_t = placed_ref[1, owner_block]
             for source in range(2):
                 real_s = source_ref[member, 2 * source : 2 * source + 1]
                 imag_s = source_ref[member, 2 * source + 1 : 2 * source + 2]
@@ -51,7 +51,7 @@
 
 
 def correlate(placed, white_sources, table, offsets, capacity):
-    blocks, _, group_bins = placed.shape
+    _, blocks, _, group_bins = placed.shape
     rows = 2 * offsets * capacity
     lags_out = table.shape[1]
     group = 4
@@ -60,7 +60,7 @@
         body,
         grid=(blocks // group,),
         in_specs=[
-            pl.BlockSpec(placed.shape, lambda a: (0, 0, 0)),
+            pl.BlockSpec(placed.shape, lambda a: (0, 0, 0, 0)),
             pl.BlockSpec((group,) + white_sources.shape[1:], lambda a: (a, 0, 0)),
             pl.BlockSpec(table.shape, lambda a: (0, 0)),
         ],
@@ -135,15 +135,13 @@
     arrival = jnp.sum(owner_hits * earlier, axis=1)
     slot_index = owners * capacity + arrival
     chosen = jnp.arange(blocks * capacity, dtype=jnp.int32)[:, None] == slot_index[None, :]
-    raw_placed = jnp.dot(
-        chosen.astype(jnp.bfloat16), traces.reshape(station_count, 2 * group_bins),
-        preferred_element_type=jnp.float32,
+    raw_placed = jnp.einsum(
+        "si,ipk->psk", chosen.astype(jnp.bfloat16), traces, preferred_element_type=jnp.float32
     )
     station_scale = lax.rsqrt(trace_power / (2 * BINS) + EPS)
     slot_scale = jnp.sum(jnp.where(chosen, station_scale[None, :], 0.0), axis=1)
-    placed = (raw_placed * slot_scale[:, None]).astype(jnp.bfloat16)
-    placed = placed.reshape(blocks, capacity, 2, group_bins).transpose(0, 2, 1, 3)
-    placed = placed.reshape(blocks, 2 * capacity, group_bins)
+    placed = (raw_placed * slot_scale[None, :, None]).astype(jnp.bfloat16)
+    placed = placed.reshape(2, blocks, capacity, group_bins)
 
     table = jnp.asarray(twiddle_table(lags_out))
 

time: 56.2 us -> 57.2 us (1.018)
  other arithmetic: 5.13 us -> 7.18 us
  local copies, waits for them, and re-layouts: 4.73 us -> 2.92 us
  matrix products: 2.18 us -> 3.04 us
    unnamed x3 -> x2, local copies, waits for them, and re-layouts: 1.81 us -> 0.01 us
    dot_general x1, matrix products: 2.18 us -> 3.04 us  [per_device(): jnp.einsum('si,ipk->psk', chosen.astype(jnp.bfloat16), traces, preferred_...]
    add x1, other arithmetic: 0.01 us -> 0.67 us  [per_device(): slot_index = owners * capacity + arrival]
    reduce_sum x1, other arithmetic: 0.18 us -> 0.84 us  [per_device(): arrival = jnp.sum(owner_hits * earlier, axis=1)]
    convert_element_type x1, other arithmetic: 0.07 us -> 0.73 us  [per_device(): (owners[:, None] == jnp.arange(blocks, dtype=jnp.int32)[None, :]).astype(...]
  transfers between devices with their start and end apart: 8 -> 8, of which waited for: 6 -> 5; matrix products, arithmetic and copies ran while one was open for 10% -> 11% of each run, Pallas kernels for 0% -> 0%
where the time goes in v15:
time: 57.2 us; the launch traced here: 56.8 us
  waiting for transfers between devices  19.9 us (35%)
  starting transfers between devices  14.7 us (26%)
  other arithmetic  7.18 us (13%)
  Pallas kernels  6.39 us (11%)
  matrix products  3.04 us (5%)
  local copies, waits for them, and re-layouts  2.92 us (5%)
  blocking collectives  2.57 us (4%)
    all_to_all x1, waiting for transfers between devices, per_device(): lax.all_to_all(partial, 'blk', split_axis=0, concat_axis=0, tiled=True)  13.1 us
    ppermute x6, starting transfers between devices, per_device(): got = lax.ppermute(held, 'blk', route)  9.11 us
    pallas_call x1, Pallas kernels, correlate(): pl.pallas_call(body, grid=(blocks // group,), in_specs=[pl.BlockSpec(plac...  6.39 us
    all_to_all x1, starting transfers between devices, per_device(): lax.all_to_all(partial, 'blk', split_axis=0, concat_axis=0, tiled=True)  5.52 us
    ppermute x6, waiting for transfers between devices, per_device(): got = lax.ppermute(held, 'blk', route)  5.33 us
    dot_general x1, matrix products, per_device(): jnp.einsum('si,ipk->psk', chosen.astype(jnp.bfloat16), traces, preferred_...  3.04 us
    reduce_sum x1, other arithmetic, per_device(): jnp.sum(trace_float * trace_float, axis=(1, 2))  2.81 us
    psum x1, blocking collectives, per_device(): lax.psum((jnp.sum(trace_float * trace_float, axis=(1, 2)), jnp.sum(source...  2.57 us
  transfers between devices with their start and end apart: 8, of which 5 were waited for; matrix products, arithmetic and copies ran while one was open for 11% of the time, Pallas kernels for 0%

profile of v15, /device:TPU:0, one launch (start us, length us, event | category | flops | bytes accessed | tf_op | source)
XLA Modules:
  0.0 56.8 jit_solution(1080383356281169308)
XLA Ops:
  0.0 1.0 %fusion.3 = f32[2]{0:T(128)S(1)} fusion(bf16[2,2,4096]{2,1,0:T(2,128)(2,1)} %param.5), kind=kLoop, calls=%fused_computation.13 | loop fusion | flops 49150 | bytes 32776 | tf_op jit(solution)/shard_map/reduce_sum | solution.py:103
  1.0 2.8 %multiply_reduce_fusion = f32[64]{0:T(128)S(1)} fusion(bf16[64,2,4096]{2,1,0:T(2,128)(2,1)} %param.4), kind=kLoop, calls=%fused_computation.3 | loop fusion | flops 1572800 | bytes 1048832 | tf_op jit(solution)/shard_map/reduce_sum | solution.py:102
  3.8 2.6 %all-reduce = (f32[64]{0:T(128)S(1)}, f32[2]{0:T(128)S(1)}) all-reduce(f32[64]{0:T(128)S(1)} %multiply_reduce_fusion, f32[2]{0:T(128)S(1)} %fusion.3), channel_id=1, replica_groups=mesh['blk'=16,'band'=2] {'band'}, use_global_device_ids=true, to_apply=%region_3.0 | all-reduce | flops 66 | bytes 528 | tf_op jit(solution)/shard_map/psum | solution.py:100
  6.4 0.1 broadcast_in_dim.51
  6.5 0.9 %bitcast_dynamic-update-slice_fusion.7 = (bf16[4,1,2,2,4096]{4,3,2,0,1:T(2,128)(2,1)S(1)}, bf16[2,2,4096]{2,1,0:T(2,128)(2,1)S(1)}) fusion(bf16[4,1,2,2,4096]{4,3,2,0,1:T(2,128)(2,1)S(1)} %broadcast_in_dim.51, s32[]{:T(128)S(6)} %select_n.35, f32[2]{0:T(128)S(1)} %add_rsqrt_fusion, bf16[2,2,4096]{2,1,0:T(2,128)(2,1)} %param.5), kind=kLoop, calls=%fused_computation.18 | loop fusion | flops 49152 | bytes 98820 | tf_op jit(solution)/shard_map/dynamic_update_slice | solution.py:126
  7.3 3.0 %collective-permute-start = (bf16[1,2,2,4096]{3,2,1,0:T(2,128)(2,1)S(1)}, bf16[1,2,2,4096]{3,2,1,0:T(2,128)(2,1)S(1)}, u32[]{:S(2)}, u32[]{:S(2)}) collective-permute-start(bf16[1,2,2,4096]{3,2,1,0:T(2,128)(2,1)S(1)} %bitcast.49), channel_id=1, source_target_pairs={{0,8},{2,10},{4,12},{6,14},{8,0},{10,2},{12,4},{14,6},{16,24},{18,... | collective-permute-start | bytes 98312 | tf_op jit(solution)/shard_map/ppermute | solution.py:125
  10.3 2.6 %collective-permute-start.1 = (bf16[1,2,2,4096]{3,2,1,0:T(2,128)(2,1)S(1)}, bf16[1,2,2,4096]{3,2,1,0:T(2,128)(2,1)S(1)}, u32[]{:S(2)}, u32[]{:S(2)}) collective-permute-start(bf16[1,2,2,4096]{3,2,1,0:T(2,128)(2,1)S(1)} %bitcast.50), channel_id=1, source_target_pairs={{0,16},{2,18},{4,20},{6,22},{8,24},{10,26},{12,28},{14,30},{16,0},... | collective-permute-start | bytes 98312 | tf_op jit(solution)/shard_map/ppermute | solution.py:125
  12.9 0.7 %fusion.5 = s32[64,16]{1,0:T(8,128)S(1)} fusion(s32[64]{0:T(128)} %bitcast.52), kind=kLoop, calls=%fused_computation.22 | loop fusion | flops 2048 | bytes 4352 | tf_op jit(solution)/shard_map/convert_element_type | solution.py:133
  13.6 0.1 reduce_window_sum.11
  13.7 0.8 %select_reduce_fusion.1 = s32[64]{0:T(128)S(1)} fusion(s32[64,16]{1,0:T(8,128)S(1)} %reduce_window_sum.11, s32[64]{0:T(128)} %bitcast.53), kind=kLoop, calls=%fused_computation.20 | loop fusion | flops 5056 | bytes 4608 | tf_op jit(solution)/shard_map/reduce_sum | solution.py:135
  14.6 0.7 %multiply_add_fusion = s32[64]{0:T(128)S(1)} fusion(s32[64]{0:T(128)S(1)} %select_reduce_fusion.1, s32[64,1]{0,1:T(1,128)} %param.6), kind=kLoop, calls=%fused_computation.29 | loop fusion | flops 128 | bytes 768 | tf_op jit(solution)/shard_map/add | solution.py:136
  15.2 0.1 select_reduce_fusion
  15.3 3.0 %fusion.1.placed_ref = bf16[2,16,8,4096]{3,2,1,0:T(8,128)(2,1)} fusion(f32[128]{0:T(128)S(1)} %select_reduce_fusion, bf16[64,2,4096]{2,1,0:T(2,128)(2,1)S(1)} %copy-done, s32[64]{0:T(128)S(1)} %multiply_add_fusion), kind=kOutput, calls=%fused_computation.2 | convolution fusion | flops 136323072 | bytes 3146496 | tf_op jit(solution)/shard_map/si,ipk->psk/dot_general | solution.py:138
  18.5 0.1 collective-permute-done.2
  18.6 1.7 %collective-permute-start.3 = (bf16[4,1,2,2,4096]{4,3,2,0,1:T(2,128)(2,1)S(1)}, bf16[4,1,2,2,4096]{4,3,2,0,1:T(2,128)(2,1)S(1)}, u32[]{:S(2)}, u32[]{:S(2)}) collective-permute-start(bf16[4,1,2,2,4096]{4,3,2,0,1:T(2,128)(2,1)S(1)} %bitcast_dynamic-update-slice_fusion.4), channel_id=1, source_target_pairs={{0,2},{2,0},{4,6},{6,4},{8,10},{10,8},{12,14},{14,12},{16,18},{18,... | collective-permute-start | bytes 393224 | tf_op jit(solution)/shard_map/ppermute | solution.py:125
  20.3 1.5 %collective-permute-start.4 = (bf16[4,1,2,2,4096]{4,3,2,0,1:T(2,128)(2,1)S(1)}, bf16[4,1,2,2,4096]{4,3,2,0,1:T(2,128)(2,1)S(1)}, u32[]{:S(2)}, u32[]{:S(2)}) collective-permute-start(bf16[4,1,2,2,4096]{4,3,2,0,1:T(2,128)(2,1)S(1)} %bitcast_dynamic-update-slice_fusion.4), channel_id=1, source_target_pairs={{0,4},{2,6},{4,0},{6,2},{8,12},{10,14},{12,8},{14,10},{16,20},{18,... | collective-permute-start | bytes 393224 | tf_op jit(solution)/shard_map/ppermute | solution.py:125
  21.8 0.4 collective-permute-start.5
  22.2 0.5 broadcast_in_dim.50
  22.7 0.1 bitcast_dynamic-update-slice_fusion.2
  22.8 1.4 %collective-permute-done.3 = bf16[4,1,2,2,4096]{4,3,2,0,1:T(2,128)(2,1)S(1)} collective-permute-done((bf16[4,1,2,2,4096]{4,3,2,0,1:T(2,128)(2,1)S(1)}, bf16[4,1,2,2,4096]{4,3,2,0,1:T(2,128)(2,1)S(1)}, u32[]{:S(2)}, u32[]{:S(2)}) %collective-permute-start.3) | collective-permute-done | bytes 131104 | tf_op jit(solution)/shard_map/ppermute | solution.py:125
  24.2 0.1 bitcast_dynamic-update-slice_fusion.1
  24.3 3.8 %collective-permute-done.4 = bf16[4,1,2,2,4096]{4,3,2,0,1:T(2,128)(2,1)S(1)} collective-permute-done((bf16[4,1,2,2,4096]{4,3,2,0,1:T(2,128)(2,1)S(1)}, bf16[4,1,2,2,4096]{4,3,2,0,1:T(2,128)(2,1)S(1)}, u32[]{:S(2)}, u32[]{:S(2)}) %collective-permute-start.4) | collective-permute-done | bytes 131104 | tf_op jit(solution)/shard_map/ppermute | solution.py:125
  28.1 0.1 bitcast_dynamic-update-slice_fusion
  28.2 0.1 bitcast_dynamic-update-slice_fusion.3
  28.3 1.0 %reshape.24.source_ref = bf16[16,4,4096]{2,1,0:T(4,128)(2,1)} reshape(bf16[1,4,4,2,2,4096]{5,4,3,2,1,0:T(2,128)(2,1)S(1)} %bitcast.48) | data formatting | bytes 1048576 | tf_op jit(solution)/shard_map/reshape | solution.py:148
  29.3 6.4 %shard_map.46 = bf16[16,64,256]{2,1,0:T(8,128)(2,1)} custom-call(bf16[2,16,8,4096]{3,2,1,0:T(8,128)(2,1)} %fusion.1.placed_ref, bf16[16,4,4096]{2,1,0:T(4,128)(2,1)} %reshape.24.source_ref, bf16[2048,256]{1,0:T(8,128)(2,1)} %constant.42.clone.table_ref), custom_call_target="tpu_custom_call" | custom-call | flops 1107296256 | bytes 4194304 | tf_op jit(solution)/shard_map/pallas_call | solution.py:59
  35.7 5.5 %all-to-all-start = ((bf16[16,64,256]{2,1,0:T(8,128)(2,1)}), bf16[16,64,256]{2,1,0:T(8,128)(2,1)S(1)}, u32[]{:S(2)}, u32[]{:S(2)}) async-start(bf16[16,64,256]{2,1,0:T(8,128)(2,1)} %shard_map.46), calls=%async_computation | async-start | bytes 1048576 | tf_op jit(solution)/shard_map/all_to_all | solution.py:151
  41.2 13.1 %all-to-all-done = bf16[16,64,256]{2,1,0:T(8,128)(2,1)S(1)} async-done(((bf16[16,64,256]{2,1,0:T(8,128)(2,1)}), bf16[16,64,256]{2,1,0:T(8,128)(2,1)S(1)}, u32[]{:S(2)}, u32[]{:S(2)}) %all-to-all-start) | async-done | bytes 524320 | tf_op jit(solution)/shard_map/all_to_all | solution.py:151
  54.3 0.1 collective-permute-start.6
  54.4 1.5 %collective-permute-done.6 = bf16[8,64,256]{2,1,0:T(8,128)(2,1)S(1)} collective-permute-done((bf16[8,64,256]{2,1,0:T(8,128)(2,1)S(1)}, bf16[8,64,256]{2,1,0:T(8,128)(2,1)S(1)}, u32[]{:S(2)}, u32[]{:S(2)}) %collective-permute-start.6) | collective-permute-done | bytes 262176 | tf_op jit(solution)/shard_map/ppermute | solution.py:155
  55.9 0.1 convert_add_fusion
  56.0 0.8 %copy.17 = f32[2,4,8,8,256]{4,3,2,1,0:T(8,128)} copy(f32[2,4,8,8,256]{4,3,1,0,2:T(8,128)S(1)} %bitcast.47) | data formatting | bytes 1048576 | tf_op jit(solution)/shard_map/transpose | solution.py:158
  (12 shorter events, 0.2 us)
Async XLA Ops:
  0.0 15.3 %copy-start = (bf16[64,2,4096]{2,1,0:T(2,128)(2,1)S(1)}, bf16[64,2,4096]{2,1,0:T(2,128)(2,1)}, u32[]{:S(2)}) copy-start(bf16[64,2,4096]{2,1,0:T(2,128)(2,1)} %param.4) | copy-start | bytes 3145732
  7.3 11.1 %collective-permute-start = (bf16[1,2,2,4096]{3,2,1,0:T(2,128)(2,1)S(1)}, bf16[1,2,2,4096]{3,2,1,0:T(2,128)(2,1)S(1)}, u32[]{:S(2)}, u32[]{:S(2)}) collective-permute-start(bf16[1,2,2,4096]{3,2,1,0:T(2,128)(2,1)S(1)} %bitcast.49), channel_id=1, source_target_pairs={{0,8},{2,10},{4,12},{6,14},{8,0},{10,2},{12,4},{14,6},{16,24},{18,... | collective-permute-start | bytes 98312 | tf_op jit(solution)/shard_map/ppermute | solution.py:125
  10.3 8.1 %collective-permute-start.1 = (bf16[1,2,2,4096]{3,2,1,0:T(2,128)(2,1)S(1)}, bf16[1,2,2,4096]{3,2,1,0:T(2,128)(2,1)S(1)}, u32[]{:S(2)}, u32[]{:S(2)}) collective-permute-start(bf16[1,2,2,4096]{3,2,1,0:T(2,128)(2,1)S(1)} %bitcast.50), channel_id=1, source_target_pairs={{0,16},{2,18},{4,20},{6,22},{8,24},{10,26},{12,28},{14,30},{16,0},... | collective-permute-start | bytes 98312 | tf_op jit(solution)/shard_map/ppermute | solution.py:125
  12.9 5.7 %collective-permute-start.2 = (bf16[1,2,2,4096]{3,2,1,0:T(2,128)(2,1)S(1)}, bf16[1,2,2,4096]{3,2,1,0:T(2,128)(2,1)S(1)}, u32[]{:S(2)}, u32[]{:S(2)}) collective-permute-start(bf16[1,2,2,4096]{3,2,1,0:T(2,128)(2,1)S(1)} %bitcast.51), channel_id=1, source_target_pairs={{0,24},{2,26},{4,28},{6,30},{8,16},{10,18},{12,20},{14,22},{16,8},... | collective-permute-start | bytes 98312 | tf_op jit(solution)/shard_map/ppermute | solution.py:125
  18.6 5.5 %collective-permute-start.3 = (bf16[4,1,2,2,4096]{4,3,2,0,1:T(2,128)(2,1)S(1)}, bf16[4,1,2,2,4096]{4,3,2,0,1:T(2,128)(2,1)S(1)}, u32[]{:S(2)}, u32[]{:S(2)}) collective-permute-start(bf16[4,1,2,2,4096]{4,3,2,0,1:T(2,128)(2,1)S(1)} %bitcast_dynamic-update-slice_fusion.4), channel_id=1, source_target_pairs={{0,2},{2,0},{4,6},{6,4},{8,10},{10,8},{12,14},{14,12},{16,18},{18,... | collective-permute-start | bytes 393224 | tf_op jit(solution)/shard_map/ppermute | solution.py:125
  20.3 7.8 %collective-permute-start.4 = (bf16[4,1,2,2,4096]{4,3,2,0,1:T(2,128)(2,1)S(1)}, bf16[4,1,2,2,4096]{4,3,2,0,1:T(2,128)(2,1)S(1)}, u32[]{:S(2)}, u32[]{:S(2)}) collective-permute-start(bf16[4,1,2,2,4096]{4,3,2,0,1:T(2,128)(2,1)S(1)} %bitcast_dynamic-update-slice_fusion.4), channel_id=1, source_target_pairs={{0,4},{2,6},{4,0},{6,2},{8,12},{10,14},{12,8},{14,10},{16,20},{18,... | collective-permute-start | bytes 393224 | tf_op jit(solution)/shard_map/ppermute | solution.py:125
  21.8 6.4 %collective-permute-start.5 = (bf16[4,1,2,2,4096]{4,3,2,0,1:T(2,128)(2,1)S(1)}, bf16[4,1,2,2,4096]{4,3,2,0,1:T(2,128)(2,1)S(1)}, u32[]{:S(2)}, u32[]{:S(2)}) collective-permute-start(bf16[4,1,2,2,4096]{4,3,2,0,1:T(2,128)(2,1)S(1)} %bitcast_dynamic-update-slice_fusion.4), channel_id=1, source_target_pairs={{0,6},{2,4},{4,2},{6,0},{8,14},{10,12},{12,10},{14,8},{16,22},{18,... | collective-permute-start | bytes 393224 | tf_op jit(solution)/shard_map/ppermute | solution.py:125
  35.7 18.6 %all-to-all-start = ((bf16[16,64,256]{2,1,0:T(8,128)(2,1)}), bf16[16,64,256]{2,1,0:T(8,128)(2,1)S(1)}, u32[]{:S(2)}, u32[]{:S(2)}) async-start(bf16[16,64,256]{2,1,0:T(8,128)(2,1)} %shard_map.46), calls=%async_computation | async-start | bytes 1048576 | tf_op jit(solution)/shard_map/all_to_all | solution.py:151
  54.3 1.6 %collective-permute-start.6 = (bf16[8,64,256]{2,1,0:T(8,128)(2,1)S(1)}, bf16[8,64,256]{2,1,0:T(8,128)(2,1)S(1)}, u32[]{:S(2)}, u32[]{:S(2)}) collective-permute-start(bf16[8,64,256]{2,1,0:T(8,128)(2,1)S(1)} %constant_dynamic-slice_fusion), channel_id=1, source_target_pairs={{0,1},{1,0},{2,3},{3,2},{4,5},{5,4},{6,7},{7,6},{8,9},{9,8},{10,11... | collective-permute-start | bytes 786440 | tf_op jit(solution)/shard_map/ppermute | solution.py:155

commit v16 on v15

--- a/solution.py
+++ b/solution.py
@@ -54,7 +54,7 @@
     _, blocks, _, group_bins = placed.shape
     rows = 2 * offsets * capacity
     lags_out = table.shape[1]
-    group = 4
+    group = 8
     body = functools.partial(correlate_kernel, blocks, offsets, capacity, group, BINS ** (-0.5))
     return pl.pallas_call(
         body,

time: 57.2 us -> 56.9 us (level)
  no operation moved by 1% of the time
where the time goes in v16:
time: 56.9 us; the launch traced here: 56.5 us
  waiting for transfers between devices  19.9 us (35%)
  starting transfers between devices  14.7 us (26%)
  other arithmetic  7.18 us (13%)
  Pallas kernels  6.11 us (11%)
  matrix products  3.04 us (5%)
  local copies, waits for them, and re-layouts  2.92 us (5%)
  blocking collectives  2.57 us (5%)
    all_to_all x1, waiting for transfers between devices, per_device(): lax.all_to_all(partial, 'blk', split_axis=0, concat_axis=0, tiled=True)  13.1 us
    ppermute x6, starting transfers between devices, per_device(): got = lax.ppermute(held, 'blk', route)  9.11 us
    pallas_call x1, Pallas kernels, correlate(): pl.pallas_call(body, grid=(blocks // group,), in_specs=[pl.BlockSpec(plac...  6.11 us
    all_to_all x1, starting transfers between devices, per_device(): lax.all_to_all(partial, 'blk', split_axis=0, concat_axis=0, tiled=True)  5.52 us
    ppermute x6, waiting for transfers between devices, per_device(): got = lax.ppermute(held, 'blk', route)  5.33 us
    dot_general x1, matrix products, per_device(): jnp.einsum('si,ipk->psk', chosen.astype(jnp.bfloat16), traces, preferred_...  3.04 us
    reduce_sum x1, other arithmetic, per_device(): jnp.sum(trace_float * trace_float, axis=(1, 2))  2.81 us
    psum x1, blocking collectives, per_device(): lax.psum((jnp.sum(trace_float * trace_float, axis=(1, 2)), jnp.sum(source...  2.57 us
  transfers between devices with their start and end apart: 8, of which 5 were waited for; matrix products, arithmetic and copies ran while one was open for 11% of the time, Pallas kernels for 0%

profile of v16, /device:TPU:0, one launch (start us, length us, event | category | flops | bytes accessed | tf_op | source)
XLA Modules:
  0.0 56.5 jit_solution(10828475509665010619)
XLA Ops:
  0.0 1.0 %fusion.3 = f32[2]{0:T(128)S(1)} fusion(bf16[2,2,4096]{2,1,0:T(2,128)(2,1)} %param.5), kind=kLoop, calls=%fused_computation.13 | loop fusion | flops 49150 | bytes 32776 | tf_op jit(solution)/shard_map/reduce_sum | solution.py:103
  1.0 2.8 %multiply_reduce_fusion = f32[64]{0:T(128)S(1)} fusion(bf16[64,2,4096]{2,1,0:T(2,128)(2,1)} %param.4), kind=kLoop, calls=%fused_computation.3 | loop fusion | flops 1572800 | bytes 1048832 | tf_op jit(solution)/shard_map/reduce_sum | solution.py:102
  3.8 2.6 %all-reduce = (f32[64]{0:T(128)S(1)}, f32[2]{0:T(128)S(1)}) all-reduce(f32[64]{0:T(128)S(1)} %multiply_reduce_fusion, f32[2]{0:T(128)S(1)} %fusion.3), channel_id=1, replica_groups=mesh['blk'=16,'band'=2] {'band'}, use_global_device_ids=true, to_apply=%region_3.0 | all-reduce | flops 66 | bytes 528 | tf_op jit(solution)/shard_map/psum | solution.py:100
  6.4 0.1 broadcast_in_dim.51
  6.5 0.9 %bitcast_dynamic-update-slice_fusion.7 = (bf16[4,1,2,2,4096]{4,3,2,0,1:T(2,128)(2,1)S(1)}, bf16[2,2,4096]{2,1,0:T(2,128)(2,1)S(1)}) fusion(bf16[4,1,2,2,4096]{4,3,2,0,1:T(2,128)(2,1)S(1)} %broadcast_in_dim.51, s32[]{:T(128)S(6)} %select_n.35, f32[2]{0:T(128)S(1)} %add_rsqrt_fusion, bf16[2,2,4096]{2,1,0:T(2,128)(2,1)} %param.5), kind=kLoop, calls=%fused_computation.18 | loop fusion | flops 49152 | bytes 98820 | tf_op jit(solution)/shard_map/dynamic_update_slice | solution.py:126
  7.3 3.0 %collective-permute-start = (bf16[1,2,2,4096]{3,2,1,0:T(2,128)(2,1)S(1)}, bf16[1,2,2,4096]{3,2,1,0:T(2,128)(2,1)S(1)}, u32[]{:S(2)}, u32[]{:S(2)}) collective-permute-start(bf16[1,2,2,4096]{3,2,1,0:T(2,128)(2,1)S(1)} %bitcast.49), channel_id=1, source_target_pairs={{0,8},{2,10},{4,12},{6,14},{8,0},{10,2},{12,4},{14,6},{16,24},{18,... | collective-permute-start | bytes 98312 | tf_op jit(solution)/shard_map/ppermute | solution.py:125
  10.3 2.6 %collective-permute-start.1 = (bf16[1,2,2,4096]{3,2,1,0:T(2,128)(2,1)S(1)}, bf16[1,2,2,4096]{3,2,1,0:T(2,128)(2,1)S(1)}, u32[]{:S(2)}, u32[]{:S(2)}) collective-permute-start(bf16[1,2,2,4096]{3,2,1,0:T(2,128)(2,1)S(1)} %bitcast.50), channel_id=1, source_target_pairs={{0,16},{2,18},{4,20},{6,22},{8,24},{10,26},{12,28},{14,30},{16,0},... | collective-permute-start | bytes 98312 | tf_op jit(solution)/shard_map/ppermute | solution.py:125
  12.9 0.7 %fusion.5 = s32[64,16]{1,0:T(8,128)S(1)} fusion(s32[64]{0:T(128)} %bitcast.52), kind=kLoop, calls=%fused_computation.22 | loop fusion | flops 2048 | bytes 4352 | tf_op jit(solution)/shard_map/convert_element_type | solution.py:133
  13.6 0.1 reduce_window_sum.11
  13.7 0.8 %select_reduce_fusion.1 = s32[64]{0:T(128)S(1)} fusion(s32[64,16]{1,0:T(8,128)S(1)} %reduce_window_sum.11, s32[64]{0:T(128)} %bitcast.53), kind=kLoop, calls=%fused_computation.20 | loop fusion | flops 5056 | bytes 4608 | tf_op jit(solution)/shard_map/reduce_sum | solution.py:135
  14.6 0.7 %multiply_add_fusion = s32[64]{0:T(128)S(1)} fusion(s32[64]{0:T(128)S(1)} %select_reduce_fusion.1, s32[64,1]{0,1:T(1,128)} %param.6), kind=kLoop, calls=%fused_computation.29 | loop fusion | flops 128 | bytes 768 | tf_op jit(solution)/shard_map/add | solution.py:136
  15.2 0.1 select_reduce_fusion
  15.3 3.0 %fusion.1.placed_ref = bf16[2,16,8,4096]{3,2,1,0:T(8,128)(2,1)} fusion(f32[128]{0:T(128)S(1)} %select_reduce_fusion, bf16[64,2,4096]{2,1,0:T(2,128)(2,1)S(1)} %copy-done, s32[64]{0:T(128)S(1)} %multiply_add_fusion), kind=kOutput, calls=%fused_computation.2 | convolution fusion | flops 136323072 | bytes 3146496 | tf_op jit(solution)/shard_map/si,ipk->psk/dot_general | solution.py:138
  18.5 0.1 collective-permute-done.2
  18.6 1.7 %collective-permute-start.3 = (bf16[4,1,2,2,4096]{4,3,2,0,1:T(2,128)(2,1)S(1)}, bf16[4,1,2,2,4096]{4,3,2,0,1:T(2,128)(2,1)S(1)}, u32[]{:S(2)}, u32[]{:S(2)}) collective-permute-start(bf16[4,1,2,2,4096]{4,3,2,0,1:T(2,128)(2,1)S(1)} %bitcast_dynamic-update-slice_fusion.4), channel_id=1, source_target_pairs={{0,2},{2,0},{4,6},{6,4},{8,10},{10,8},{12,14},{14,12},{16,18},{18,... | collective-permute-start | bytes 393224 | tf_op jit(solution)/shard_map/ppermute | solution.py:125
  20.3 1.5 %collective-permute-start.4 = (bf16[4,1,2,2,4096]{4,3,2,0,1:T(2,128)(2,1)S(1)}, bf16[4,1,2,2,4096]{4,3,2,0,1:T(2,128)(2,1)S(1)}, u32[]{:S(2)}, u32[]{:S(2)}) collective-permute-start(bf16[4,1,2,2,4096]{4,3,2,0,1:T(2,128)(2,1)S(1)} %bitcast_dynamic-update-slice_fusion.4), channel_id=1, source_target_pairs={{0,4},{2,6},{4,0},{6,2},{8,12},{10,14},{12,8},{14,10},{16,20},{18,... | collective-permute-start | bytes 393224 | tf_op jit(solution)/shard_map/ppermute | solution.py:125
  21.8 0.4 collective-permute-start.5
  22.2 0.5 broadcast_in_dim.50
  22.7 0.1 bitcast_dynamic-update-slice_fusion.2
  22.8 1.4 %collective-permute-done.3 = bf16[4,1,2,2,4096]{4,3,2,0,1:T(2,128)(2,1)S(1)} collective-permute-done((bf16[4,1,2,2,4096]{4,3,2,0,1:T(2,128)(2,1)S(1)}, bf16[4,1,2,2,4096]{4,3,2,0,1:T(2,128)(2,1)S(1)}, u32[]{:S(2)}, u32[]{:S(2)}) %collective-permute-start.3) | collective-permute-done | bytes 131104 | tf_op jit(solution)/shard_map/ppermute | solution.py:125
  24.2 0.1 bitcast_dynamic-update-slice_fusion.1
  24.3 3.8 %collective-permute-done.4 = bf16[4,1,2,2,4096]{4,3,2,0,1:T(2,128)(2,1)S(1)} collective-permute-done((bf16[4,1,2,2,4096]{4,3,2,0,1:T(2,128)(2,1)S(1)}, bf16[4,1,2,2,4096]{4,3,2,0,1:T(2,128)(2,1)S(1)}, u32[]{:S(2)}, u32[]{:S(2)}) %collective-permute-start.4) | collective-permute-done | bytes 131104 | tf_op jit(solution)/shard_map/ppermute | solution.py:125
  28.1 0.1 bitcast_dynamic-update-slice_fusion
  28.2 0.1 bitcast_dynamic-update-slice_fusion.3
  28.3 1.0 %reshape.24.source_ref = bf16[16,4,4096]{2,1,0:T(4,128)(2,1)} reshape(bf16[1,4,4,2,2,4096]{5,4,3,2,1,0:T(2,128)(2,1)S(1)} %bitcast.48) | data formatting | bytes 1048576 | tf_op jit(solution)/shard_map/reshape | solution.py:148
  29.3 6.1 %shard_map.46 = bf16[16,64,256]{2,1,0:T(8,128)(2,1)} custom-call(bf16[2,16,8,4096]{3,2,1,0:T(8,128)(2,1)} %fusion.1.placed_ref, bf16[16,4,4096]{2,1,0:T(4,128)(2,1)} %reshape.24.source_ref, bf16[2048,256]{1,0:T(8,128)(2,1)} %constant.42.clone.table_ref), custom_call_target="tpu_custom_call" | custom-call | flops 1107296256 | bytes 4194304 | tf_op jit(solution)/shard_map/pallas_call | solution.py:59
  35.4 5.5 %all-to-all-start = ((bf16[16,64,256]{2,1,0:T(8,128)(2,1)}), bf16[16,64,256]{2,1,0:T(8,128)(2,1)S(1)}, u32[]{:S(2)}, u32[]{:S(2)}) async-start(bf16[16,64,256]{2,1,0:T(8,128)(2,1)} %shard_map.46), calls=%async_computation | async-start | bytes 1048576 | tf_op jit(solution)/shard_map/all_to_all | solution.py:151
  40.9 13.1 %all-to-all-done = bf16[16,64,256]{2,1,0:T(8,128)(2,1)S(1)} async-done(((bf16[16,64,256]{2,1,0:T(8,128)(2,1)}), bf16[16,64,256]{2,1,0:T(8,128)(2,1)S(1)}, u32[]{:S(2)}, u32[]{:S(2)}) %all-to-all-start) | async-done | bytes 524320 | tf_op jit(solution)/shard_map/all_to_all | solution.py:151
  54.0 0.1 collective-permute-start.6
  54.1 1.5 %collective-permute-done.6 = bf16[8,64,256]{2,1,0:T(8,128)(2,1)S(1)} collective-permute-done((bf16[8,64,256]{2,1,0:T(8,128)(2,1)S(1)}, bf16[8,64,256]{2,1,0:T(8,128)(2,1)S(1)}, u32[]{:S(2)}, u32[]{:S(2)}) %collective-permute-start.6) | collective-permute-done | bytes 262176 | tf_op jit(solution)/shard_map/ppermute | solution.py:155
  55.6 0.1 convert_add_fusion
  55.7 0.8 %copy.17 = f32[2,4,8,8,256]{4,3,2,1,0:T(8,128)} copy(f32[2,4,8,8,256]{4,3,1,0,2:T(8,128)S(1)} %bitcast.47) | data formatting | bytes 1048576 | tf_op jit(solution)/shard_map/transpose | solution.py:158
  (12 shorter events, 0.2 us)
Async XLA Ops:
  0.0 15.3 %copy-start = (bf16[64,2,4096]{2,1,0:T(2,128)(2,1)S(1)}, bf16[64,2,4096]{2,1,0:T(2,128)(2,1)}, u32[]{:S(2)}) copy-start(bf16[64,2,4096]{2,1,0:T(2,128)(2,1)} %param.4) | copy-start | bytes 3145732
  7.3 11.1 %collective-permute-start = (bf16[1,2,2,4096]{3,2,1,0:T(2,128)(2,1)S(1)}, bf16[1,2,2,4096]{3,2,1,0:T(2,128)(2,1)S(1)}, u32[]{:S(2)}, u32[]{:S(2)}) collective-permute-start(bf16[1,2,2,4096]{3,2,1,0:T(2,128)(2,1)S(1)} %bitcast.49), channel_id=1, source_target_pairs={{0,8},{2,10},{4,12},{6,14},{8,0},{10,2},{12,4},{14,6},{16,24},{18,... | collective-permute-start | bytes 98312 | tf_op jit(solution)/shard_map/ppermute | solution.py:125
  10.3 8.1 %collective-permute-start.1 = (bf16[1,2,2,4096]{3,2,1,0:T(2,128)(2,1)S(1)}, bf16[1,2,2,4096]{3,2,1,0:T(2,128)(2,1)S(1)}, u32[]{:S(2)}, u32[]{:S(2)}) collective-permute-start(bf16[1,2,2,4096]{3,2,1,0:T(2,128)(2,1)S(1)} %bitcast.50), channel_id=1, source_target_pairs={{0,16},{2,18},{4,20},{6,22},{8,24},{10,26},{12,28},{14,30},{16,0},... | collective-permute-start | bytes 98312 | tf_op jit(solution)/shard_map/ppermute | solution.py:125
  12.9 5.7 %collective-permute-start.2 = (bf16[1,2,2,4096]{3,2,1,0:T(2,128)(2,1)S(1)}, bf16[1,2,2,4096]{3,2,1,0:T(2,128)(2,1)S(1)}, u32[]{:S(2)}, u32[]{:S(2)}) collective-permute-start(bf16[1,2,2,4096]{3,2,1,0:T(2,128)(2,1)S(1)} %bitcast.51), channel_id=1, source_target_pairs={{0,24},{2,26},{4,28},{6,30},{8,16},{10,18},{12,20},{14,22},{16,8},... | collective-permute-start | bytes 98312 | tf_op jit(solution)/shard_map/ppermute | solution.py:125
  18.6 5.5 %collective-permute-start.3 = (bf16[4,1,2,2,4096]{4,3,2,0,1:T(2,128)(2,1)S(1)}, bf16[4,1,2,2,4096]{4,3,2,0,1:T(2,128)(2,1)S(1)}, u32[]{:S(2)}, u32[]{:S(2)}) collective-permute-start(bf16[4,1,2,2,4096]{4,3,2,0,1:T(2,128)(2,1)S(1)} %bitcast_dynamic-update-slice_fusion.4), channel_id=1, source_target_pairs={{0,2},{2,0},{4,6},{6,4},{8,10},{10,8},{12,14},{14,12},{16,18},{18,... | collective-permute-start | bytes 393224 | tf_op jit(solution)/shard_map/ppermute | solution.py:125
  20.3 7.8 %collective-permute-start.4 = (bf16[4,1,2,2,4096]{4,3,2,0,1:T(2,128)(2,1)S(1)}, bf16[4,1,2,2,4096]{4,3,2,0,1:T(2,128)(2,1)S(1)}, u32[]{:S(2)}, u32[]{:S(2)}) collective-permute-start(bf16[4,1,2,2,4096]{4,3,2,0,1:T(2,128)(2,1)S(1)} %bitcast_dynamic-update-slice_fusion.4), channel_id=1, source_target_pairs={{0,4},{2,6},{4,0},{6,2},{8,12},{10,14},{12,8},{14,10},{16,20},{18,... | collective-permute-start | bytes 393224 | tf_op jit(solution)/shard_map/ppermute | solution.py:125
  21.8 6.4 %collective-permute-start.5 = (bf16[4,1,2,2,4096]{4,3,2,0,1:T(2,128)(2,1)S(1)}, bf16[4,1,2,2,4096]{4,3,2,0,1:T(2,128)(2,1)S(1)}, u32[]{:S(2)}, u32[]{:S(2)}) collective-permute-start(bf16[4,1,2,2,4096]{4,3,2,0,1:T(2,128)(2,1)S(1)} %bitcast_dynamic-update-slice_fusion.4), channel_id=1, source_target_pairs={{0,6},{2,4},{4,2},{6,0},{8,14},{10,12},{12,10},{14,8},{16,22},{18,... | collective-permute-start | bytes 393224 | tf_op jit(solution)/shard_map/ppermute | solution.py:125
  35.4 18.6 %all-to-all-start = ((bf16[16,64,256]{2,1,0:T(8,128)(2,1)}), bf16[16,64,256]{2,1,0:T(8,128)(2,1)S(1)}, u32[]{:S(2)}, u32[]{:S(2)}) async-start(bf16[16,64,256]{2,1,0:T(8,128)(2,1)} %shard_map.46), calls=%async_computation | async-start | bytes 1048576 | tf_op jit(solution)/shard_map/all_to_all | solution.py:151
  54.0 1.6 %collective-permute-start.6 = (bf16[8,64,256]{2,1,0:T(8,128)(2,1)S(1)}, bf16[8,64,256]{2,1,0:T(8,128)(2,1)S(1)}, u32[]{:S(2)}, u32[]{:S(2)}) collective-permute-start(bf16[8,64,256]{2,1,0:T(8,128)(2,1)S(1)} %constant_dynamic-slice_fusion), channel_id=1, source_target_pairs={{0,1},{1,0},{2,3},{3,2},{4,5},{5,4},{6,7},{7,6},{8,9},{9,8},{10,11... | collective-permute-start | bytes 786440 | tf_op jit(solution)/shard_map/ppermute | solution.py:155

commit v17 on v16

--- a/solution.py
+++ b/solution.py
@@ -148,16 +148,14 @@
     white_sources = held.reshape(blocks, source_count * 2, group_bins)
 
     partial = correlate(placed, white_sources, table, offsets, capacity)
-    arrived = lax.all_to_all(partial, "blk", split_axis=0, concat_axis=0, tiled=True)
-    half = blocks // 2
-    mine = lax.dynamic_slice_in_dim(arrived, band * half, half, axis=0)
-    other = lax.dynamic_slice_in_dim(arrived, (1 - band) * half, half, axis=0)
+    partial = partial.reshape(blocks, source_count, offsets, capacity, lags_out)
+    arrived = lax.all_to_all(partial, "blk", split_axis=0, concat_axis=3, tiled=True)
+    arrived = arrived.reshape(source_count, offsets, blocks * capacity, lags_out)
+    half = blocks * capacity // 2
+    mine = lax.dynamic_slice_in_dim(arrived, band * half, half, axis=2)
+    other = lax.dynamic_slice_in_dim(arrived, (1 - band) * half, half, axis=2)
     other = lax.ppermute(other, "band", [(0, 1), (1, 0)])
-    summed = mine.astype(jnp.float32) + other.astype(jnp.float32)
-    summed = summed.reshape(half, source_count, offsets, capacity, lags_out)
-    return jnp.transpose(summed, (1, 2, 0, 3, 4)).reshape(
-        source_count, offsets, half * capacity, lags_out
-    )
+    return mine.astype(jnp.float32) + other.astype(jnp.float32)
 
 
 def solution(mesh):

time: 56.9 us -> 56.9 us (level)
  other arithmetic: 7.18 us -> 7.97 us
  local copies, waits for them, and re-layouts: 2.92 us -> 2.13 us
    transpose x1 -> x0, local copies, waits for them, and re-layouts: 0.84 us -> none  [per_device(): jnp.transpose(summed, (1, 2, 0, 3, 4))]
    add x1, other arithmetic: 0.06 us -> 0.86 us  [per_device(): return mine.astype(jnp.float32) + other.astype(jnp.float32)]
where the time goes in v17:
time: 56.9 us; the launch traced here: 56.5 us
  waiting for transfers between devices  19.9 us (35%)
  starting transfers between devices  14.7 us (26%)
  other arithmetic  7.97 us (14%)
  Pallas kernels  6.11 us (11%)
  matrix products  3.04 us (5%)
  blocking collectives  2.57 us (5%)
  local copies, waits for them, and re-layouts  2.13 us (4%)
    all_to_all x1, waiting for transfers between devices, per_device(): lax.all_to_all(partial, 'blk', split_axis=0, concat_axis=3, tiled=True)  13.1 us
    ppermute x6, starting transfers between devices, per_device(): got = lax.ppermute(held, 'blk', route)  9.11 us
    pallas_call x1, Pallas kernels, correlate(): pl.pallas_call(body, grid=(blocks // group,), in_specs=[pl.BlockSpec(plac...  6.11 us
    all_to_all x1, starting transfers between devices, per_device(): lax.all_to_all(partial, 'blk', split_axis=0, concat_axis=3, tiled=True)  5.52 us
    ppermute x6, waiting for transfers between devices, per_device(): got = lax.ppermute(held, 'blk', route)  5.33 us
    dot_general x1, matrix products, per_device(): jnp.einsum('si,ipk->psk', chosen.astype(jnp.bfloat16), traces, preferred_...  3.04 us
    reduce_sum x1, other arithmetic, per_device(): jnp.sum(trace_float * trace_float, axis=(1, 2))  2.81 us
    psum x1, blocking collectives, per_device(): lax.psum((jnp.sum(trace_float * trace_float, axis=(1, 2)), jnp.sum(source...  2.57 us
  transfers between devices with their start and end apart: 8, of which 5 were waited for; matrix products, arithmetic and copies ran while one was open for 11% of the time, Pallas kernels for 0%

profile of v17, /device:TPU:0, one launch (start us, length us, event | category | flops | bytes accessed | tf_op | source)
XLA Modules:
  0.0 56.5 jit_solution(1726934807622890747)
XLA Ops:
  0.0 1.0 %fusion.3 = f32[2]{0:T(128)S(1)} fusion(bf16[2,2,4096]{2,1,0:T(2,128)(2,1)} %param.5), kind=kLoop, calls=%fused_computation.13 | loop fusion | flops 49150 | bytes 32776 | tf_op jit(solution)/shard_map/reduce_sum | solution.py:103
  1.0 2.8 %multiply_reduce_fusion = f32[64]{0:T(128)S(1)} fusion(bf16[64,2,4096]{2,1,0:T(2,128)(2,1)} %param.4), kind=kLoop, calls=%fused_computation.3 | loop fusion | flops 1572800 | bytes 1048832 | tf_op jit(solution)/shard_map/reduce_sum | solution.py:102
  3.8 2.6 %all-reduce = (f32[64]{0:T(128)S(1)}, f32[2]{0:T(128)S(1)}) all-reduce(f32[64]{0:T(128)S(1)} %multiply_reduce_fusion, f32[2]{0:T(128)S(1)} %fusion.3), channel_id=1, replica_groups=mesh['blk'=16,'band'=2] {'band'}, use_global_device_ids=true, to_apply=%region_3.0 | all-reduce | flops 66 | bytes 528 | tf_op jit(solution)/shard_map/psum | solution.py:100
  6.4 0.1 broadcast_in_dim.51
  6.5 0.9 %bitcast_dynamic-update-slice_fusion.7 = (bf16[4,1,2,2,4096]{4,3,2,0,1:T(2,128)(2,1)S(1)}, bf16[2,2,4096]{2,1,0:T(2,128)(2,1)S(1)}) fusion(bf16[4,1,2,2,4096]{4,3,2,0,1:T(2,128)(2,1)S(1)} %broadcast_in_dim.51, s32[]{:T(128)S(6)} %select_n.35, f32[2]{0:T(128)S(1)} %add_rsqrt_fusion, bf16[2,2,4096]{2,1,0:T(2,128)(2,1)} %param.5), kind=kLoop, calls=%fused_computation.18 | loop fusion | flops 49152 | bytes 98820 | tf_op jit(solution)/shard_map/dynamic_update_slice | solution.py:126
  7.3 3.0 %collective-permute-start = (bf16[1,2,2,4096]{3,2,1,0:T(2,128)(2,1)S(1)}, bf16[1,2,2,4096]{3,2,1,0:T(2,128)(2,1)S(1)}, u32[]{:S(2)}, u32[]{:S(2)}) collective-permute-start(bf16[1,2,2,4096]{3,2,1,0:T(2,128)(2,1)S(1)} %bitcast.51), channel_id=1, source_target_pairs={{0,8},{2,10},{4,12},{6,14},{8,0},{10,2},{12,4},{14,6},{16,24},{18,... | collective-permute-start | bytes 98312 | tf_op jit(solution)/shard_map/ppermute | solution.py:125
  10.3 2.6 %collective-permute-start.1 = (bf16[1,2,2,4096]{3,2,1,0:T(2,128)(2,1)S(1)}, bf16[1,2,2,4096]{3,2,1,0:T(2,128)(2,1)S(1)}, u32[]{:S(2)}, u32[]{:S(2)}) collective-permute-start(bf16[1,2,2,4096]{3,2,1,0:T(2,128)(2,1)S(1)} %bitcast.52), channel_id=1, source_target_pairs={{0,16},{2,18},{4,20},{6,22},{8,24},{10,26},{12,28},{14,30},{16,0},... | collective-permute-start | bytes 98312 | tf_op jit(solution)/shard_map/ppermute | solution.py:125
  12.9 0.7 %fusion.5 = s32[64,16]{1,0:T(8,128)S(1)} fusion(s32[64]{0:T(128)} %bitcast.54), kind=kLoop, calls=%fused_computation.22 | loop fusion | flops 2048 | bytes 4352 | tf_op jit(solution)/shard_map/convert_element_type | solution.py:133
  13.6 0.1 reduce_window_sum.11
  13.7 0.8 %select_reduce_fusion.1 = s32[64]{0:T(128)S(1)} fusion(s32[64,16]{1,0:T(8,128)S(1)} %reduce_window_sum.11, s32[64]{0:T(128)} %bitcast.55), kind=kLoop, calls=%fused_computation.20 | loop fusion | flops 5056 | bytes 4608 | tf_op jit(solution)/shard_map/reduce_sum | solution.py:135
  14.6 0.7 %multiply_add_fusion = s32[64]{0:T(128)S(1)} fusion(s32[64]{0:T(128)S(1)} %select_reduce_fusion.1, s32[64,1]{0,1:T(1,128)} %param.6), kind=kLoop, calls=%fused_computation.29 | loop fusion | flops 128 | bytes 768 | tf_op jit(solution)/shard_map/add | solution.py:136
  15.2 0.1 select_reduce_fusion
  15.3 3.0 %fusion.1.placed_ref = bf16[2,16,8,4096]{3,2,1,0:T(8,128)(2,1)} fusion(f32[128]{0:T(128)S(1)} %select_reduce_fusion, bf16[64,2,4096]{2,1,0:T(2,128)(2,1)S(1)} %copy-done, s32[64]{0:T(128)S(1)} %multiply_add_fusion), kind=kOutput, calls=%fused_computation.2 | convolution fusion | flops 136323072 | bytes 3146496 | tf_op jit(solution)/shard_map/si,ipk->psk/dot_general | solution.py:138
  18.4 0.0 collective-permute-done
  18.5 0.1 collective-permute-done.2
  18.6 1.7 %collective-permute-start.3 = (bf16[4,1,2,2,4096]{4,3,2,0,1:T(2,128)(2,1)S(1)}, bf16[4,1,2,2,4096]{4,3,2,0,1:T(2,128)(2,1)S(1)}, u32[]{:S(2)}, u32[]{:S(2)}) collective-permute-start(bf16[4,1,2,2,4096]{4,3,2,0,1:T(2,128)(2,1)S(1)} %bitcast_dynamic-update-slice_fusion.4), channel_id=1, source_target_pairs={{0,2},{2,0},{4,6},{6,4},{8,10},{10,8},{12,14},{14,12},{16,18},{18,... | collective-permute-start | bytes 393224 | tf_op jit(solution)/shard_map/ppermute | solution.py:125
  20.3 1.5 %collective-permute-start.4 = (bf16[4,1,2,2,4096]{4,3,2,0,1:T(2,128)(2,1)S(1)}, bf16[4,1,2,2,4096]{4,3,2,0,1:T(2,128)(2,1)S(1)}, u32[]{:S(2)}, u32[]{:S(2)}) collective-permute-start(bf16[4,1,2,2,4096]{4,3,2,0,1:T(2,128)(2,1)S(1)} %bitcast_dynamic-update-slice_fusion.4), channel_id=1, source_target_pairs={{0,4},{2,6},{4,0},{6,2},{8,12},{10,14},{12,8},{14,10},{16,20},{18,... | collective-permute-start | bytes 393224 | tf_op jit(solution)/shard_map/ppermute | solution.py:125
  21.8 0.4 collective-permute-start.5
  22.2 0.5 broadcast_in_dim.50
  22.7 0.1 bitcast_dynamic-update-slice_fusion.2
  22.8 1.4 %collective-permute-done.3 = bf16[4,1,2,2,4096]{4,3,2,0,1:T(2,128)(2,1)S(1)} collective-permute-done((bf16[4,1,2,2,4096]{4,3,2,0,1:T(2,128)(2,1)S(1)}, bf16[4,1,2,2,4096]{4,3,2,0,1:T(2,128)(2,1)S(1)}, u32[]{:S(2)}, u32[]{:S(2)}) %collective-permute-start.3) | collective-permute-done | bytes 131104 | tf_op jit(solution)/shard_map/ppermute | solution.py:125
  24.2 0.1 bitcast_dynamic-update-slice_fusion.1
  24.3 3.8 %collective-permute-done.4 = bf16[4,1,2,2,4096]{4,3,2,0,1:T(2,128)(2,1)S(1)} collective-permute-done((bf16[4,1,2,2,4096]{4,3,2,0,1:T(2,128)(2,1)S(1)}, bf16[4,1,2,2,4096]{4,3,2,0,1:T(2,128)(2,1)S(1)}, u32[]{:S(2)}, u32[]{:S(2)}) %collective-permute-start.4) | collective-permute-done | bytes 131104 | tf_op jit(solution)/shard_map/ppermute | solution.py:125
  28.1 0.1 bitcast_dynamic-update-slice_fusion
  28.2 0.1 bitcast_dynamic-update-slice_fusion.3
  28.3 1.0 %reshape.25.source_ref = bf16[16,4,4096]{2,1,0:T(4,128)(2,1)} reshape(bf16[1,4,4,2,2,4096]{5,4,3,2,1,0:T(2,128)(2,1)S(1)} %bitcast.49) | data formatting | bytes 1048576 | tf_op jit(solution)/shard_map/reshape | solution.py:148
  29.3 6.1 %shard_map.46 = bf16[16,64,256]{2,1,0:T(8,128)(2,1)} custom-call(bf16[2,16,8,4096]{3,2,1,0:T(8,128)(2,1)} %fusion.1.placed_ref, bf16[16,4,4096]{2,1,0:T(4,128)(2,1)} %reshape.25.source_ref, bf16[2048,256]{1,0:T(8,128)(2,1)} %constant.43.clone.table_ref), custom_call_target="tpu_custom_call" | custom-call | flops 1107296256 | bytes 4194304 | tf_op jit(solution)/shard_map/pallas_call | solution.py:59
  35.4 5.5 %all-to-all-start = ((bf16[16,2,4,8,256]{4,3,2,1,0:T(8,128)(2,1)}), bf16[16,2,4,8,256]{4,3,2,1,0:T(8,128)(2,1)S(1)}, u32[]{:S(2)}, u32[]{:S(2)}) async-start(bf16[16,2,4,8,256]{4,3,2,1,0:T(8,128)(2,1)} %bitcast.50), calls=%async_computation | async-start | bytes 1048576 | tf_op jit(solution)/shard_map/all_to_all | solution.py:152
  40.9 13.1 %all-to-all-done = bf16[16,2,4,8,256]{4,3,2,1,0:T(8,128)(2,1)S(1)} async-done(((bf16[16,2,4,8,256]{4,3,2,1,0:T(8,128)(2,1)}), bf16[16,2,4,8,256]{4,3,2,1,0:T(8,128)(2,1)S(1)}, u32[]{:S(2)}, u32[]{:S(2)}) %all-to-all-start) | async-done | bytes 524320 | tf_op jit(solution)/shard_map/all_to_all | solution.py:152
  54.1 0.1 collective-permute-start.6
  54.2 1.5 %collective-permute-done.6 = bf16[2,4,64,256]{3,2,1,0:T(8,128)(2,1)S(1)} collective-permute-done((bf16[2,4,64,256]{3,2,1,0:T(8,128)(2,1)S(1)}, bf16[2,4,64,256]{3,2,1,0:T(8,128)(2,1)S(1)}, u32[]{:S(2)}, u32[]{:S(2)}) %collective-permute-start.6) | collective-permute-done | bytes 262176 | tf_op jit(solution)/shard_map/ppermute | solution.py:157
  55.7 0.9 %convert_add_fusion = f32[2,4,64,256]{3,2,1,0:T(8,128)} fusion(bf16[2,4,64,256]{3,2,1,0:T(8,128)(2,1)S(1)} %collective-permute-done.6, bf16[2,4,128,256]{3,2,1,0:T(8,128)(2,1)S(1)} %copy_bitcast_fusion, s32[]{:T(128)S(6)} %select_n.43), kind=kLoop, calls=%fused_computation.6 | loop fusion | flops 393216 | bytes 1048580 | tf_op jit(solution)/shard_map/add | solution.py:158
  (12 shorter events, 0.2 us)
Async XLA Ops:
  0.0 15.3 %copy-start = (bf16[64,2,4096]{2,1,0:T(2,128)(2,1)S(1)}, bf16[64,2,4096]{2,1,0:T(2,128)(2,1)}, u32[]{:S(2)}) copy-start(bf16[64,2,4096]{2,1,0:T(2,128)(2,1)} %param.4) | copy-start | bytes 3145732
  7.3 11.1 %collective-permute-start = (bf16[1,2,2,4096]{3,2,1,0:T(2,128)(2,1)S(1)}, bf16[1,2,2,4096]{3,2,1,0:T(2,128)(2,1)S(1)}, u32[]{:S(2)}, u32[]{:S(2)}) collective-permute-start(bf16[1,2,2,4096]{3,2,1,0:T(2,128)(2,1)S(1)} %bitcast.51), channel_id=1, source_target_pairs={{0,8},{2,10},{4,12},{6,14},{8,0},{10,2},{12,4},{14,6},{16,24},{18,... | collective-permute-start | bytes 98312 | tf_op jit(solution)/shard_map/ppermute | solution.py:125
  10.3 8.1 %collective-permute-start.1 = (bf16[1,2,2,4096]{3,2,1,0:T(2,128)(2,1)S(1)}, bf16[1,2,2,4096]{3,2,1,0:T(2,128)(2,1)S(1)}, u32[]{:S(2)}, u32[]{:S(2)}) collective-permute-start(bf16[1,2,2,4096]{3,2,1,0:T(2,128)(2,1)S(1)} %bitcast.52), channel_id=1, source_target_pairs={{0,16},{2,18},{4,20},{6,22},{8,24},{10,26},{12,28},{14,30},{16,0},... | collective-permute-start | bytes 98312 | tf_op jit(solution)/shard_map/ppermute | solution.py:125
  12.9 5.7 %collective-permute-start.2 = (bf16[1,2,2,4096]{3,2,1,0:T(2,128)(2,1)S(1)}, bf16[1,2,2,4096]{3,2,1,0:T(2,128)(2,1)S(1)}, u32[]{:S(2)}, u32[]{:S(2)}) collective-permute-start(bf16[1,2,2,4096]{3,2,1,0:T(2,128)(2,1)S(1)} %bitcast.53), channel_id=1, source_target_pairs={{0,24},{2,26},{4,28},{6,30},{8,16},{10,18},{12,20},{14,22},{16,8},... | collective-permute-start | bytes 98312 | tf_op jit(solution)/shard_map/ppermute | solution.py:125
  18.6 5.5 %collective-permute-start.3 = (bf16[4,1,2,2,4096]{4,3,2,0,1:T(2,128)(2,1)S(1)}, bf16[4,1,2,2,4096]{4,3,2,0,1:T(2,128)(2,1)S(1)}, u32[]{:S(2)}, u32[]{:S(2)}) collective-permute-start(bf16[4,1,2,2,4096]{4,3,2,0,1:T(2,128)(2,1)S(1)} %bitcast_dynamic-update-slice_fusion.4), channel_id=1, source_target_pairs={{0,2},{2,0},{4,6},{6,4},{8,10},{10,8},{12,14},{14,12},{16,18},{18,... | collective-permute-start | bytes 393224 | tf_op jit(solution)/shard_map/ppermute | solution.py:125
  20.3 7.8 %collective-permute-start.4 = (bf16[4,1,2,2,4096]{4,3,2,0,1:T(2,128)(2,1)S(1)}, bf16[4,1,2,2,4096]{4,3,2,0,1:T(2,128)(2,1)S(1)}, u32[]{:S(2)}, u32[]{:S(2)}) collective-permute-start(bf16[4,1,2,2,4096]{4,3,2,0,1:T(2,128)(2,1)S(1)} %bitcast_dynamic-update-slice_fusion.4), channel_id=1, source_target_pairs={{0,4},{2,6},{4,0},{6,2},{8,12},{10,14},{12,8},{14,10},{16,20},{18,... | collective-permute-start | bytes 393224 | tf_op jit(solution)/shard_map/ppermute | solution.py:125
  21.8 6.4 %collective-permute-start.5 = (bf16[4,1,2,2,4096]{4,3,2,0,1:T(2,128)(2,1)S(1)}, bf16[4,1,2,2,4096]{4,3,2,0,1:T(2,128)(2,1)S(1)}, u32[]{:S(2)}, u32[]{:S(2)}) collective-permute-start(bf16[4,1,2,2,4096]{4,3,2,0,1:T(2,128)(2,1)S(1)} %bitcast_dynamic-update-slice_fusion.4), channel_id=1, source_target_pairs={{0,6},{2,4},{4,2},{6,0},{8,14},{10,12},{12,10},{14,8},{16,22},{18,... | collective-permute-start | bytes 393224 | tf_op jit(solution)/shard_map/ppermute | solution.py:125
  35.4 18.6 %all-to-all-start = ((bf16[16,2,4,8,256]{4,3,2,1,0:T(8,128)(2,1)}), bf16[16,2,4,8,256]{4,3,2,1,0:T(8,128)(2,1)S(1)}, u32[]{:S(2)}, u32[]{:S(2)}) async-start(bf16[16,2,4,8,256]{4,3,2,1,0:T(8,128)(2,1)} %bitcast.50), calls=%async_computation | async-start | bytes 1048576 | tf_op jit(solution)/shard_map/all_to_all | solution.py:152
  54.1 1.6 %collective-permute-start.6 = (bf16[2,4,64,256]{3,2,1,0:T(8,128)(2,1)S(1)}, bf16[2,4,64,256]{3,2,1,0:T(8,128)(2,1)S(1)}, u32[]{:S(2)}, u32[]{:S(2)}) collective-permute-start(bf16[2,4,64,256]{3,2,1,0:T(8,128)(2,1)S(1)} %constant_dynamic-slice_fusion), channel_id=1, source_target_pairs={{0,1},{1,0},{2,3},{3,2},{4,5},{5,4},{6,7},{7,6},{8,9},{9,8},{10,11... | collective-permute-start | bytes 786440 | tf_op jit(solution)/shard_map/ppermute | solution.py:157

commit v18 on v12

--- a/solution.py
+++ b/solution.py
@@ -54,7 +54,7 @@
     blocks, _, group_bins = placed.shape
     rows = 2 * offsets * capacity
     lags_out = table.shape[1]
-    group = 4
+    group = 8
     body = functools.partial(correlate_kernel, blocks, offsets, capacity, group, BINS ** (-0.5))
     return pl.pallas_call(
         body,

time: 56.2 us -> 55.9 us (level)
  no operation moved by 1% of the time
where the time goes in v18:
time: 55.9 us; the launch traced here: 55.5 us
  waiting for transfers between devices  20.4 us (36%)
  starting transfers between devices  14.3 us (26%)
  Pallas kernels  6.11 us (11%)
  other arithmetic  5.13 us (9%)
  local copies, waits for them, and re-layouts  4.73 us (8%)
  blocking collectives  2.56 us (5%)
  matrix products  2.18 us (4%)
    all_to_all x1, waiting for transfers between devices, per_device(): lax.all_to_all(partial, 'blk', split_axis=0, concat_axis=0, tiled=True)  13.1 us
    ppermute x6, starting transfers between devices, per_device(): got = lax.ppermute(held, 'blk', route)  9.11 us
    pallas_call x1, Pallas kernels, correlate(): pl.pallas_call(body, grid=(blocks // group,), in_specs=[pl.BlockSpec(plac...  6.11 us
    ppermute x6, waiting for transfers between devices, per_device(): got = lax.ppermute(held, 'blk', route)  5.76 us
    all_to_all x1, starting transfers between devices, per_device(): lax.all_to_all(partial, 'blk', split_axis=0, concat_axis=0, tiled=True)  5.1 us
    reduce_sum x1, other arithmetic, per_device(): jnp.sum(trace_float * trace_float, axis=(1, 2))  2.82 us
    psum x1, blocking collectives, per_device(): lax.psum((jnp.sum(trace_float * trace_float, axis=(1, 2)), jnp.sum(source...  2.56 us
    dot_general x1, matrix products, per_device(): jnp.dot(chosen.astype(jnp.bfloat16), traces.reshape(station_count, 2 * gr...  2.18 us
  transfers between devices with their start and end apart: 8, of which 6 were waited for; matrix products, arithmetic and copies ran while one was open for 10% of the time, Pallas kernels for 0%

profile of v18, /device:TPU:0, one launch (start us, length us, event | category | flops | bytes accessed | tf_op | source)
XLA Modules:
  0.0 55.5 jit_solution(2639720969234603746)
XLA Ops:
  0.0 2.8 %multiply_reduce_fusion = f32[64]{0:T(128)S(1)} fusion(bf16[64,2,4096]{2,1,0:T(2,128)(2,1)} %param.4), kind=kLoop, calls=%fused_computation.2 | loop fusion | flops 1572800 | bytes 1048832 | tf_op jit(solution)/shard_map/reduce_sum | solution.py:102
  2.8 0.9 %fusion.1 = f32[2]{0:T(128)S(1)} fusion(bf16[2,2,4096]{2,1,0:T(2,128)(2,1)} %param.5), kind=kLoop, calls=%fused_computation.11 | loop fusion | flops 49150 | bytes 32776 | tf_op jit(solution)/shard_map/reduce_sum | solution.py:103
  3.7 2.6 %all-reduce = (f32[64]{0:T(128)S(1)}, f32[2]{0:T(128)S(1)}) all-reduce(f32[64]{0:T(128)S(1)} %multiply_reduce_fusion, f32[2]{0:T(128)S(1)} %fusion.1), channel_id=1, replica_groups=mesh['blk'=16,'band'=2] {'band'}, use_global_device_ids=true, to_apply=%region_3.0 | all-reduce | flops 66 | bytes 528 | tf_op jit(solution)/shard_map/psum | solution.py:100
  6.3 0.1 broadcast_in_dim.51
  6.4 0.9 %bitcast_dynamic-update-slice_fusion.7 = (bf16[4,1,2,2,4096]{4,3,2,0,1:T(2,128)(2,1)S(1)}, bf16[2,2,4096]{2,1,0:T(2,128)(2,1)S(1)}) fusion(bf16[4,1,2,2,4096]{4,3,2,0,1:T(2,128)(2,1)S(1)} %broadcast_in_dim.51, s32[]{:T(128)S(6)} %select_n.35, f32[2]{0:T(128)S(1)} %add_rsqrt_fusion, bf16[2,2,4096]{2,1,0:T(2,128)(2,1)} %param.5), kind=kLoop, calls=%fused_computation.16 | loop fusion | flops 49152 | bytes 98820 | tf_op jit(solution)/shard_map/dynamic_update_slice | solution.py:126
  7.2 3.0 %collective-permute-start = (bf16[1,2,2,4096]{3,2,1,0:T(2,128)(2,1)S(1)}, bf16[1,2,2,4096]{3,2,1,0:T(2,128)(2,1)S(1)}, u32[]{:S(2)}, u32[]{:S(2)}) collective-permute-start(bf16[1,2,2,4096]{3,2,1,0:T(2,128)(2,1)S(1)} %bitcast.53), channel_id=1, source_target_pairs={{0,8},{2,10},{4,12},{6,14},{8,0},{10,2},{12,4},{14,6},{16,24},{18,... | collective-permute-start | bytes 98312 | tf_op jit(solution)/shard_map/ppermute | solution.py:125
  10.2 2.6 %collective-permute-start.1 = (bf16[1,2,2,4096]{3,2,1,0:T(2,128)(2,1)S(1)}, bf16[1,2,2,4096]{3,2,1,0:T(2,128)(2,1)S(1)}, u32[]{:S(2)}, u32[]{:S(2)}) collective-permute-start(bf16[1,2,2,4096]{3,2,1,0:T(2,128)(2,1)S(1)} %bitcast.54), channel_id=1, source_target_pairs={{0,16},{2,18},{4,20},{6,22},{8,24},{10,26},{12,28},{14,30},{16,0},... | collective-permute-start | bytes 98312 | tf_op jit(solution)/shard_map/ppermute | solution.py:125
  12.8 1.8 %copy.21 = bf16[8,8,2,4096]{3,1,2,0:T(8,128)(2,1)S(1)} copy(bf16[8,8,2,4096]{3,2,1,0:T(2,128)(2,1)} %bitcast.49) | data formatting | bytes 2097152
  14.6 0.1 fusion.3
  14.7 0.1 reduce_window_sum.11
  14.8 0.2 select_reduce_fusion.1
  15.0 0.1 select_reduce_fusion
  15.1 2.2 %fusion = bf16[128,8192]{1,0:T(8,128)(2,1)} fusion(bf16[64,8192]{1,0:T(8,128)(2,1)S(1)} %bitcast.50, f32[128]{0:T(128)S(1)} %select_reduce_fusion, s32[64]{0:T(128)S(1)} %multiply_add_fusion), kind=kOutput, calls=%fused_computation.1 | convolution fusion | flops 136323072 | bytes 3146496 | tf_op jit(solution)/shard_map/dot_general | solution.py:138
  17.4 1.1 %collective-permute-done.2 = bf16[1,2,2,4096]{3,2,1,0:T(2,128)(2,1)S(1)} collective-permute-done((bf16[1,2,2,4096]{3,2,1,0:T(2,128)(2,1)S(1)}, bf16[1,2,2,4096]{3,2,1,0:T(2,128)(2,1)S(1)}, u32[]{:S(2)}, u32[]{:S(2)}) %collective-permute-start.2) | collective-permute-done | bytes 32800 | tf_op jit(solution)/shard_map/ppermute | solution.py:125
  18.6 1.6 %collective-permute-start.3 = (bf16[4,1,2,2,4096]{4,3,2,0,1:T(2,128)(2,1)S(1)}, bf16[4,1,2,2,4096]{4,3,2,0,1:T(2,128)(2,1)S(1)}, u32[]{:S(2)}, u32[]{:S(2)}) collective-permute-start(bf16[4,1,2,2,4096]{4,3,2,0,1:T(2,128)(2,1)S(1)} %bitcast_dynamic-update-slice_fusion.4), channel_id=1, source_target_pairs={{0,2},{2,0},{4,6},{6,4},{8,10},{10,8},{12,14},{14,12},{16,18},{18,... | collective-permute-start | bytes 393224 | tf_op jit(solution)/shard_map/ppermute | solution.py:125
  20.1 1.5 %collective-permute-start.4 = (bf16[4,1,2,2,4096]{4,3,2,0,1:T(2,128)(2,1)S(1)}, bf16[4,1,2,2,4096]{4,3,2,0,1:T(2,128)(2,1)S(1)}, u32[]{:S(2)}, u32[]{:S(2)}) collective-permute-start(bf16[4,1,2,2,4096]{4,3,2,0,1:T(2,128)(2,1)S(1)} %bitcast_dynamic-update-slice_fusion.4), channel_id=1, source_target_pairs={{0,4},{2,6},{4,0},{6,2},{8,12},{10,14},{12,8},{14,10},{16,20},{18,... | collective-permute-start | bytes 393224 | tf_op jit(solution)/shard_map/ppermute | solution.py:125
  21.6 0.5 collective-permute-start.5
  22.1 0.5 broadcast_in_dim.50
  22.6 0.1 bitcast_dynamic-update-slice_fusion.2
  22.7 2.2 %collective-permute-done.3 = bf16[4,1,2,2,4096]{4,3,2,0,1:T(2,128)(2,1)S(1)} collective-permute-done((bf16[4,1,2,2,4096]{4,3,2,0,1:T(2,128)(2,1)S(1)}, bf16[4,1,2,2,4096]{4,3,2,0,1:T(2,128)(2,1)S(1)}, u32[]{:S(2)}, u32[]{:S(2)}) %collective-permute-start.3) | collective-permute-done | bytes 131104 | tf_op jit(solution)/shard_map/ppermute | solution.py:125
  24.9 0.1 bitcast_dynamic-update-slice_fusion.1
  25.0 1.1 %collective-permute-done.4 = bf16[4,1,2,2,4096]{4,3,2,0,1:T(2,128)(2,1)S(1)} collective-permute-done((bf16[4,1,2,2,4096]{4,3,2,0,1:T(2,128)(2,1)S(1)}, bf16[4,1,2,2,4096]{4,3,2,0,1:T(2,128)(2,1)S(1)}, u32[]{:S(2)}, u32[]{:S(2)}) %collective-permute-start.4) | collective-permute-done | bytes 131104 | tf_op jit(solution)/shard_map/ppermute | solution.py:125
  26.1 0.1 bitcast_dynamic-update-slice_fusion
  26.2 1.3 %collective-permute-done.5 = bf16[4,1,2,2,4096]{4,3,2,0,1:T(2,128)(2,1)S(1)} collective-permute-done((bf16[4,1,2,2,4096]{4,3,2,0,1:T(2,128)(2,1)S(1)}, bf16[4,1,2,2,4096]{4,3,2,0,1:T(2,128)(2,1)S(1)}, u32[]{:S(2)}, u32[]{:S(2)}) %collective-permute-start.5) | collective-permute-done | bytes 131104 | tf_op jit(solution)/shard_map/ppermute | solution.py:125
  27.5 0.1 bitcast_dynamic-update-slice_fusion.3
  27.6 1.0 %reshape.32.source_ref = bf16[16,4,4096]{2,1,0:T(4,128)(2,1)} reshape(bf16[1,4,4,2,2,4096]{5,4,3,2,1,0:T(2,128)(2,1)S(1)} %bitcast.52) | data formatting | bytes 1048576 | tf_op jit(solution)/shard_map/reshape | solution.py:150
  28.6 6.1 %shard_map.46 = bf16[16,64,256]{2,1,0:T(8,128)(2,1)} custom-call(bf16[16,16,4096]{2,1,0:T(8,128)(2,1)} %bitcast.48, bf16[16,4,4096]{2,1,0:T(4,128)(2,1)} %reshape.32.source_ref, bf16[2048,256]{1,0:T(8,128)(2,1)} %constant.42.clone.table_ref), custom_call_target="tpu_custom_call" | custom-call | flops 1107296256 | bytes 4194304 | tf_op jit(solution)/shard_map/pallas_call | solution.py:59
  34.7 5.1 %all-to-all-start = ((bf16[16,64,256]{2,1,0:T(8,128)(2,1)}), bf16[16,64,256]{2,1,0:T(8,128)(2,1)S(1)}, u32[]{:S(2)}, u32[]{:S(2)}) async-start(bf16[16,64,256]{2,1,0:T(8,128)(2,1)} %shard_map.46), calls=%async_computation | async-start | bytes 1048576 | tf_op jit(solution)/shard_map/all_to_all | solution.py:153
  39.9 13.1 %all-to-all-done = bf16[16,64,256]{2,1,0:T(8,128)(2,1)S(1)} async-done(((bf16[16,64,256]{2,1,0:T(8,128)(2,1)}), bf16[16,64,256]{2,1,0:T(8,128)(2,1)S(1)}, u32[]{:S(2)}, u32[]{:S(2)}) %all-to-all-start) | async-done | bytes 524320 | tf_op jit(solution)/shard_map/all_to_all | solution.py:153
  52.9 0.1 collective-permute-start.6
  53.0 1.5 %collective-permute-done.6 = bf16[8,64,256]{2,1,0:T(8,128)(2,1)S(1)} collective-permute-done((bf16[8,64,256]{2,1,0:T(8,128)(2,1)S(1)}, bf16[8,64,256]{2,1,0:T(8,128)(2,1)S(1)}, u32[]{:S(2)}, u32[]{:S(2)}) %collective-permute-start.6) | collective-permute-done | bytes 262176 | tf_op jit(solution)/shard_map/ppermute | solution.py:157
  54.6 0.8 %copy.23 = f32[2,4,8,8,256]{4,3,2,1,0:T(8,128)} copy(f32[2,4,8,8,256]{4,3,1,0,2:T(8,128)S(1)} %bitcast.51) | data formatting | bytes 1048576 | tf_op jit(solution)/shard_map/transpose | solution.py:160
  (13 shorter events, 0.2 us)
Async XLA Ops:
  0.0 14.6 %copy-start = (s32[64,1]{0,1:T(1,128)S(1)}, s32[64,1]{0,1:T(1,128)}, u32[]{:S(2)}) copy-start(s32[64,1]{0,1:T(1,128)} %param.6) | copy-start | bytes 772
  7.2 10.0 %collective-permute-start = (bf16[1,2,2,4096]{3,2,1,0:T(2,128)(2,1)S(1)}, bf16[1,2,2,4096]{3,2,1,0:T(2,128)(2,1)S(1)}, u32[]{:S(2)}, u32[]{:S(2)}) collective-permute-start(bf16[1,2,2,4096]{3,2,1,0:T(2,128)(2,1)S(1)} %bitcast.53), channel_id=1, source_target_pairs={{0,8},{2,10},{4,12},{6,14},{8,0},{10,2},{12,4},{14,6},{16,24},{18,... | collective-permute-start | bytes 98312 | tf_op jit(solution)/shard_map/ppermute | solution.py:125
  10.2 7.1 %collective-permute-start.1 = (bf16[1,2,2,4096]{3,2,1,0:T(2,128)(2,1)S(1)}, bf16[1,2,2,4096]{3,2,1,0:T(2,128)(2,1)S(1)}, u32[]{:S(2)}, u32[]{:S(2)}) collective-permute-start(bf16[1,2,2,4096]{3,2,1,0:T(2,128)(2,1)S(1)} %bitcast.54), channel_id=1, source_target_pairs={{0,16},{2,18},{4,20},{6,22},{8,24},{10,26},{12,28},{14,30},{16,0},... | collective-permute-start | bytes 98312 | tf_op jit(solution)/shard_map/ppermute | solution.py:125
  12.8 5.7 %collective-permute-start.2 = (bf16[1,2,2,4096]{3,2,1,0:T(2,128)(2,1)S(1)}, bf16[1,2,2,4096]{3,2,1,0:T(2,128)(2,1)S(1)}, u32[]{:S(2)}, u32[]{:S(2)}) collective-permute-start(bf16[1,2,2,4096]{3,2,1,0:T(2,128)(2,1)S(1)} %bitcast.55), channel_id=1, source_target_pairs={{0,24},{2,26},{4,28},{6,30},{8,16},{10,18},{12,20},{14,22},{16,8},... | collective-permute-start | bytes 98312 | tf_op jit(solution)/shard_map/ppermute | solution.py:125
  18.6 6.3 %collective-permute-start.3 = (bf16[4,1,2,2,4096]{4,3,2,0,1:T(2,128)(2,1)S(1)}, bf16[4,1,2,2,4096]{4,3,2,0,1:T(2,128)(2,1)S(1)}, u32[]{:S(2)}, u32[]{:S(2)}) collective-permute-start(bf16[4,1,2,2,4096]{4,3,2,0,1:T(2,128)(2,1)S(1)} %bitcast_dynamic-update-slice_fusion.4), channel_id=1, source_target_pairs={{0,2},{2,0},{4,6},{6,4},{8,10},{10,8},{12,14},{14,12},{16,18},{18,... | collective-permute-start | bytes 393224 | tf_op jit(solution)/shard_map/ppermute | solution.py:125
  20.1 6.0 %collective-permute-start.4 = (bf16[4,1,2,2,4096]{4,3,2,0,1:T(2,128)(2,1)S(1)}, bf16[4,1,2,2,4096]{4,3,2,0,1:T(2,128)(2,1)S(1)}, u32[]{:S(2)}, u32[]{:S(2)}) collective-permute-start(bf16[4,1,2,2,4096]{4,3,2,0,1:T(2,128)(2,1)S(1)} %bitcast_dynamic-update-slice_fusion.4), channel_id=1, source_target_pairs={{0,4},{2,6},{4,0},{6,2},{8,12},{10,14},{12,8},{14,10},{16,20},{18,... | collective-permute-start | bytes 393224 | tf_op jit(solution)/shard_map/ppermute | solution.py:125
  21.6 5.9 %collective-permute-start.5 = (bf16[4,1,2,2,4096]{4,3,2,0,1:T(2,128)(2,1)S(1)}, bf16[4,1,2,2,4096]{4,3,2,0,1:T(2,128)(2,1)S(1)}, u32[]{:S(2)}, u32[]{:S(2)}) collective-permute-start(bf16[4,1,2,2,4096]{4,3,2,0,1:T(2,128)(2,1)S(1)} %bitcast_dynamic-update-slice_fusion.4), channel_id=1, source_target_pairs={{0,6},{2,4},{4,2},{6,0},{8,14},{10,12},{12,10},{14,8},{16,22},{18,... | collective-permute-start | bytes 393224 | tf_op jit(solution)/shard_map/ppermute | solution.py:125
  34.7 18.2 %all-to-all-start = ((bf16[16,64,256]{2,1,0:T(8,128)(2,1)}), bf16[16,64,256]{2,1,0:T(8,128)(2,1)S(1)}, u32[]{:S(2)}, u32[]{:S(2)}) async-start(bf16[16,64,256]{2,1,0:T(8,128)(2,1)} %shard_map.46), calls=%async_computation | async-start | bytes 1048576 | tf_op jit(solution)/shard_map/all_to_all | solution.py:153
  52.9 1.6 %collective-permute-start.6 = (bf16[8,64,256]{2,1,0:T(8,128)(2,1)S(1)}, bf16[8,64,256]{2,1,0:T(8,128)(2,1)S(1)}, u32[]{:S(2)}, u32[]{:S(2)}) collective-permute-start(bf16[8,64,256]{2,1,0:T(8,128)(2,1)S(1)} %constant_dynamic-slice_fusion), channel_id=1, source_target_pairs={{0,1},{1,0},{2,3},{3,2},{4,5},{5,4},{6,7},{7,6},{8,9},{9,8},{10,11... | collective-permute-start | bytes 786440 | tf_op jit(solution)/shard_map/ppermute | solution.py:157

commit v19 on v18

--- a/solution.py
+++ b/solution.py
@@ -54,7 +54,7 @@
     blocks, _, group_bins = placed.shape
     rows = 2 * offsets * capacity
     lags_out = table.shape[1]
-    group = 8
+    group = 16
     body = functools.partial(correlate_kernel, blocks, offsets, capacity, group, BINS ** (-0.5))
     return pl.pallas_call(
         body,

time: 55.9 us -> 55.9 us (level)
  no operation moved by 1% of the time
where the time goes in v19:
time: 55.9 us; the launch traced here: 55.5 us
  waiting for transfers between devices  20.4 us (36%)
  starting transfers between devices  14.3 us (26%)
  Pallas kernels  6.14 us (11%)
  other arithmetic  5.13 us (9%)
  local copies, waits for them, and re-layouts  4.73 us (8%)
  blocking collectives  2.56 us (5%)
  matrix products  2.18 us (4%)
    all_to_all x1, waiting for transfers between devices, per_device(): lax.all_to_all(partial, 'blk', split_axis=0, concat_axis=0, tiled=True)  13.1 us
    ppermute x6, starting transfers between devices, per_device(): got = lax.ppermute(held, 'blk', route)  9.11 us
    pallas_call x1, Pallas kernels, correlate(): pl.pallas_call(body, grid=(blocks // group,), in_specs=[pl.BlockSpec(plac...  6.14 us
    ppermute x6, waiting for transfers between devices, per_device(): got = lax.ppermute(held, 'blk', route)  5.76 us
    all_to_all x1, starting transfers between devices, per_device(): lax.all_to_all(partial, 'blk', split_axis=0, concat_axis=0, tiled=True)  5.1 us
    reduce_sum x1, other arithmetic, per_device(): jnp.sum(trace_float * trace_float, axis=(1, 2))  2.82 us
    psum x1, blocking collectives, per_device(): lax.psum((jnp.sum(trace_float * trace_float, axis=(1, 2)), jnp.sum(source...  2.56 us
    dot_general x1, matrix products, per_device(): jnp.dot(chosen.astype(jnp.bfloat16), traces.reshape(station_count, 2 * gr...  2.18 us
  transfers between devices with their start and end apart: 8, of which 6 were waited for; matrix products, arithmetic and copies ran while one was open for 10% of the time, Pallas kernels for 0%

profile of v19, /device:TPU:0, one launch (start us, length us, event | category | flops | bytes accessed | tf_op | source)
XLA Modules:
  0.0 55.5 jit_solution(1344166809529455214)
XLA Ops:
  0.0 2.8 %multiply_reduce_fusion = f32[64]{0:T(128)S(1)} fusion(bf16[64,2,4096]{2,1,0:T(2,128)(2,1)} %param.4), kind=kLoop, calls=%fused_computation.2 | loop fusion | flops 1572800 | bytes 1048832 | tf_op jit(solution)/shard_map/reduce_sum | solution.py:102
  2.8 0.9 %fusion.1 = f32[2]{0:T(128)S(1)} fusion(bf16[2,2,4096]{2,1,0:T(2,128)(2,1)} %param.5), kind=kLoop, calls=%fused_computation.11 | loop fusion | flops 49150 | bytes 32776 | tf_op jit(solution)/shard_map/reduce_sum | solution.py:103
  3.7 2.6 %all-reduce = (f32[64]{0:T(128)S(1)}, f32[2]{0:T(128)S(1)}) all-reduce(f32[64]{0:T(128)S(1)} %multiply_reduce_fusion, f32[2]{0:T(128)S(1)} %fusion.1), channel_id=1, replica_groups=mesh['blk'=16,'band'=2] {'band'}, use_global_device_ids=true, to_apply=%region_3.0 | all-reduce | flops 66 | bytes 528 | tf_op jit(solution)/shard_map/psum | solution.py:100
  6.3 0.1 broadcast_in_dim.51
  6.4 0.9 %bitcast_dynamic-update-slice_fusion.7 = (bf16[4,1,2,2,4096]{4,3,2,0,1:T(2,128)(2,1)S(1)}, bf16[2,2,4096]{2,1,0:T(2,128)(2,1)S(1)}) fusion(bf16[4,1,2,2,4096]{4,3,2,0,1:T(2,128)(2,1)S(1)} %broadcast_in_dim.51, s32[]{:T(128)S(6)} %select_n.35, f32[2]{0:T(128)S(1)} %add_rsqrt_fusion, bf16[2,2,4096]{2,1,0:T(2,128)(2,1)} %param.5), kind=kLoop, calls=%fused_computation.16 | loop fusion | flops 49152 | bytes 98820 | tf_op jit(solution)/shard_map/dynamic_update_slice | solution.py:126
  7.2 3.0 %collective-permute-start = (bf16[1,2,2,4096]{3,2,1,0:T(2,128)(2,1)S(1)}, bf16[1,2,2,4096]{3,2,1,0:T(2,128)(2,1)S(1)}, u32[]{:S(2)}, u32[]{:S(2)}) collective-permute-start(bf16[1,2,2,4096]{3,2,1,0:T(2,128)(2,1)S(1)} %bitcast.53), channel_id=1, source_target_pairs={{0,8},{2,10},{4,12},{6,14},{8,0},{10,2},{12,4},{14,6},{16,24},{18,... | collective-permute-start | bytes 98312 | tf_op jit(solution)/shard_map/ppermute | solution.py:125
  10.2 2.6 %collective-permute-start.1 = (bf16[1,2,2,4096]{3,2,1,0:T(2,128)(2,1)S(1)}, bf16[1,2,2,4096]{3,2,1,0:T(2,128)(2,1)S(1)}, u32[]{:S(2)}, u32[]{:S(2)}) collective-permute-start(bf16[1,2,2,4096]{3,2,1,0:T(2,128)(2,1)S(1)} %bitcast.54), channel_id=1, source_target_pairs={{0,16},{2,18},{4,20},{6,22},{8,24},{10,26},{12,28},{14,30},{16,0},... | collective-permute-start | bytes 98312 | tf_op jit(solution)/shard_map/ppermute | solution.py:125
  12.8 1.8 %copy.21 = bf16[8,8,2,4096]{3,1,2,0:T(8,128)(2,1)S(1)} copy(bf16[8,8,2,4096]{3,2,1,0:T(2,128)(2,1)} %bitcast.49) | data formatting | bytes 2097152
  14.6 0.1 fusion.3
  14.7 0.1 reduce_window_sum.11
  14.8 0.2 select_reduce_fusion.1
  15.0 0.1 select_reduce_fusion
  15.1 2.2 %fusion = bf16[128,8192]{1,0:T(8,128)(2,1)} fusion(bf16[64,8192]{1,0:T(8,128)(2,1)S(1)} %bitcast.50, f32[128]{0:T(128)S(1)} %select_reduce_fusion, s32[64]{0:T(128)S(1)} %multiply_add_fusion), kind=kOutput, calls=%fused_computation.1 | convolution fusion | flops 136323072 | bytes 3146496 | tf_op jit(solution)/shard_map/dot_general | solution.py:138
  17.4 1.1 %collective-permute-done.2 = bf16[1,2,2,4096]{3,2,1,0:T(2,128)(2,1)S(1)} collective-permute-done((bf16[1,2,2,4096]{3,2,1,0:T(2,128)(2,1)S(1)}, bf16[1,2,2,4096]{3,2,1,0:T(2,128)(2,1)S(1)}, u32[]{:S(2)}, u32[]{:S(2)}) %collective-permute-start.2) | collective-permute-done | bytes 32800 | tf_op jit(solution)/shard_map/ppermute | solution.py:125
  18.6 1.6 %collective-permute-start.3 = (bf16[4,1,2,2,4096]{4,3,2,0,1:T(2,128)(2,1)S(1)}, bf16[4,1,2,2,4096]{4,3,2,0,1:T(2,128)(2,1)S(1)}, u32[]{:S(2)}, u32[]{:S(2)}) collective-permute-start(bf16[4,1,2,2,4096]{4,3,2,0,1:T(2,128)(2,1)S(1)} %bitcast_dynamic-update-slice_fusion.4), channel_id=1, source_target_pairs={{0,2},{2,0},{4,6},{6,4},{8,10},{10,8},{12,14},{14,12},{16,18},{18,... | collective-permute-start | bytes 393224 | tf_op jit(solution)/shard_map/ppermute | solution.py:125
  20.1 1.5 %collective-permute-start.4 = (bf16[4,1,2,2,4096]{4,3,2,0,1:T(2,128)(2,1)S(1)}, bf16[4,1,2,2,4096]{4,3,2,0,1:T(2,128)(2,1)S(1)}, u32[]{:S(2)}, u32[]{:S(2)}) collective-permute-start(bf16[4,1,2,2,4096]{4,3,2,0,1:T(2,128)(2,1)S(1)} %bitcast_dynamic-update-slice_fusion.4), channel_id=1, source_target_pairs={{0,4},{2,6},{4,0},{6,2},{8,12},{10,14},{12,8},{14,10},{16,20},{18,... | collective-permute-start | bytes 393224 | tf_op jit(solution)/shard_map/ppermute | solution.py:125
  21.6 0.5 collective-permute-start.5
  22.1 0.5 broadcast_in_dim.50
  22.6 0.1 bitcast_dynamic-update-slice_fusion.2
  22.7 2.2 %collective-permute-done.3 = bf16[4,1,2,2,4096]{4,3,2,0,1:T(2,128)(2,1)S(1)} collective-permute-done((bf16[4,1,2,2,4096]{4,3,2,0,1:T(2,128)(2,1)S(1)}, bf16[4,1,2,2,4096]{4,3,2,0,1:T(2,128)(2,1)S(1)}, u32[]{:S(2)}, u32[]{:S(2)}) %collective-permute-start.3) | collective-permute-done | bytes 131104 | tf_op jit(solution)/shard_map/ppermute | solution.py:125
  24.9 0.1 bitcast_dynamic-update-slice_fusion.1
  25.0 1.1 %collective-permute-done.4 = bf16[4,1,2,2,4096]{4,3,2,0,1:T(2,128)(2,1)S(1)} collective-permute-done((bf16[4,1,2,2,4096]{4,3,2,0,1:T(2,128)(2,1)S(1)}, bf16[4,1,2,2,4096]{4,3,2,0,1:T(2,128)(2,1)S(1)}, u32[]{:S(2)}, u32[]{:S(2)}) %collective-permute-start.4) | collective-permute-done | bytes 131104 | tf_op jit(solution)/shard_map/ppermute | solution.py:125
  26.1 0.1 bitcast_dynamic-update-slice_fusion
  26.2 1.3 %collective-permute-done.5 = bf16[4,1,2,2,4096]{4,3,2,0,1:T(2,128)(2,1)S(1)} collective-permute-done((bf16[4,1,2,2,4096]{4,3,2,0,1:T(2,128)(2,1)S(1)}, bf16[4,1,2,2,4096]{4,3,2,0,1:T(2,128)(2,1)S(1)}, u32[]{:S(2)}, u32[]{:S(2)}) %collective-permute-start.5) | collective-permute-done | bytes 131104 | tf_op jit(solution)/shard_map/ppermute | solution.py:125
  27.5 0.1 bitcast_dynamic-update-slice_fusion.3
  27.6 1.0 %reshape.32.source_ref = bf16[16,4,4096]{2,1,0:T(4,128)(2,1)} reshape(bf16[1,4,4,2,2,4096]{5,4,3,2,1,0:T(2,128)(2,1)S(1)} %bitcast.52) | data formatting | bytes 1048576 | tf_op jit(solution)/shard_map/reshape | solution.py:150
  28.6 6.1 %shard_map.46 = bf16[16,64,256]{2,1,0:T(8,128)(2,1)} custom-call(bf16[16,16,4096]{2,1,0:T(8,128)(2,1)} %bitcast.48, bf16[16,4,4096]{2,1,0:T(4,128)(2,1)} %reshape.32.source_ref, bf16[2048,256]{1,0:T(8,128)(2,1)} %constant.42.clone.table_ref), custom_call_target="tpu_custom_call" | custom-call | flops 1107296256 | bytes 4194304 | tf_op jit(solution)/shard_map/pallas_call | solution.py:59
  34.8 5.1 %all-to-all-start = ((bf16[16,64,256]{2,1,0:T(8,128)(2,1)}), bf16[16,64,256]{2,1,0:T(8,128)(2,1)S(1)}, u32[]{:S(2)}, u32[]{:S(2)}) async-start(bf16[16,64,256]{2,1,0:T(8,128)(2,1)} %shard_map.46), calls=%async_computation | async-start | bytes 1048576 | tf_op jit(solution)/shard_map/all_to_all | solution.py:153
  39.9 13.1 %all-to-all-done = bf16[16,64,256]{2,1,0:T(8,128)(2,1)S(1)} async-done(((bf16[16,64,256]{2,1,0:T(8,128)(2,1)}), bf16[16,64,256]{2,1,0:T(8,128)(2,1)S(1)}, u32[]{:S(2)}, u32[]{:S(2)}) %all-to-all-start) | async-done | bytes 524320 | tf_op jit(solution)/shard_map/all_to_all | solution.py:153
  53.0 0.1 collective-permute-start.6
  53.1 1.5 %collective-permute-done.6 = bf16[8,64,256]{2,1,0:T(8,128)(2,1)S(1)} collective-permute-done((bf16[8,64,256]{2,1,0:T(8,128)(2,1)S(1)}, bf16[8,64,256]{2,1,0:T(8,128)(2,1)S(1)}, u32[]{:S(2)}, u32[]{:S(2)}) %collective-permute-start.6) | collective-permute-done | bytes 262176 | tf_op jit(solution)/shard_map/ppermute | solution.py:157
  54.6 0.8 %copy.23 = f32[2,4,8,8,256]{4,3,2,1,0:T(8,128)} copy(f32[2,4,8,8,256]{4,3,1,0,2:T(8,128)S(1)} %bitcast.51) | data formatting | bytes 1048576 | tf_op jit(solution)/shard_map/transpose | solution.py:160
  (13 shorter events, 0.2 us)
Async XLA Ops:
  0.0 14.6 %copy-start = (s32[64,1]{0,1:T(1,128)S(1)}, s32[64,1]{0,1:T(1,128)}, u32[]{:S(2)}) copy-start(s32[64,1]{0,1:T(1,128)} %param.6) | copy-start | bytes 772
  7.2 10.0 %collective-permute-start = (bf16[1,2,2,4096]{3,2,1,0:T(2,128)(2,1)S(1)}, bf16[1,2,2,4096]{3,2,1,0:T(2,128)(2,1)S(1)}, u32[]{:S(2)}, u32[]{:S(2)}) collective-permute-start(bf16[1,2,2,4096]{3,2,1,0:T(2,128)(2,1)S(1)} %bitcast.53), channel_id=1, source_target_pairs={{0,8},{2,10},{4,12},{6,14},{8,0},{10,2},{12,4},{14,6},{16,24},{18,... | collective-permute-start | bytes 98312 | tf_op jit(solution)/shard_map/ppermute | solution.py:125
  10.2 7.1 %collective-permute-start.1 = (bf16[1,2,2,4096]{3,2,1,0:T(2,128)(2,1)S(1)}, bf16[1,2,2,4096]{3,2,1,0:T(2,128)(2,1)S(1)}, u32[]{:S(2)}, u32[]{:S(2)}) collective-permute-start(bf16[1,2,2,4096]{3,2,1,0:T(2,128)(2,1)S(1)} %bitcast.54), channel_id=1, source_target_pairs={{0,16},{2,18},{4,20},{6,22},{8,24},{10,26},{12,28},{14,30},{16,0},... | collective-permute-start | bytes 98312 | tf_op jit(solution)/shard_map/ppermute | solution.py:125
  12.8 5.7 %collective-permute-start.2 = (bf16[1,2,2,4096]{3,2,1,0:T(2,128)(2,1)S(1)}, bf16[1,2,2,4096]{3,2,1,0:T(2,128)(2,1)S(1)}, u32[]{:S(2)}, u32[]{:S(2)}) collective-permute-start(bf16[1,2,2,4096]{3,2,1,0:T(2,128)(2,1)S(1)} %bitcast.55), channel_id=1, source_target_pairs={{0,24},{2,26},{4,28},{6,30},{8,16},{10,18},{12,20},{14,22},{16,8},... | collective-permute-start | bytes 98312 | tf_op jit(solution)/shard_map/ppermute | solution.py:125
  18.6 6.3 %collective-permute-start.3 = (bf16[4,1,2,2,4096]{4,3,2,0,1:T(2,128)(2,1)S(1)}, bf16[4,1,2,2,4096]{4,3,2,0,1:T(2,128)(2,1)S(1)}, u32[]{:S(2)}, u32[]{:S(2)}) collective-permute-start(bf16[4,1,2,2,4096]{4,3,2,0,1:T(2,128)(2,1)S(1)} %bitcast_dynamic-update-slice_fusion.4), channel_id=1, source_target_pairs={{0,2},{2,0},{4,6},{6,4},{8,10},{10,8},{12,14},{14,12},{16,18},{18,... | collective-permute-start | bytes 393224 | tf_op jit(solution)/shard_map/ppermute | solution.py:125
  20.1 6.0 %collective-permute-start.4 = (bf16[4,1,2,2,4096]{4,3,2,0,1:T(2,128)(2,1)S(1)}, bf16[4,1,2,2,4096]{4,3,2,0,1:T(2,128)(2,1)S(1)}, u32[]{:S(2)}, u32[]{:S(2)}) collective-permute-start(bf16[4,1,2,2,4096]{4,3,2,0,1:T(2,128)(2,1)S(1)} %bitcast_dynamic-update-slice_fusion.4), channel_id=1, source_target_pairs={{0,4},{2,6},{4,0},{6,2},{8,12},{10,14},{12,8},{14,10},{16,20},{18,... | collective-permute-start | bytes 393224 | tf_op jit(solution)/shard_map/ppermute | solution.py:125
  21.6 5.9 %collective-permute-start.5 = (bf16[4,1,2,2,4096]{4,3,2,0,1:T(2,128)(2,1)S(1)}, bf16[4,1,2,2,4096]{4,3,2,0,1:T(2,128)(2,1)S(1)}, u32[]{:S(2)}, u32[]{:S(2)}) collective-permute-start(bf16[4,1,2,2,4096]{4,3,2,0,1:T(2,128)(2,1)S(1)} %bitcast_dynamic-update-slice_fusion.4), channel_id=1, source_target_pairs={{0,6},{2,4},{4,2},{6,0},{8,14},{10,12},{12,10},{14,8},{16,22},{18,... | collective-permute-start | bytes 393224 | tf_op jit(solution)/shard_map/ppermute | solution.py:125
  34.8 18.2 %all-to-all-start = ((bf16[16,64,256]{2,1,0:T(8,128)(2,1)}), bf16[16,64,256]{2,1,0:T(8,128)(2,1)S(1)}, u32[]{:S(2)}, u32[]{:S(2)}) async-start(bf16[16,64,256]{2,1,0:T(8,128)(2,1)} %shard_map.46), calls=%async_computation | async-start | bytes 1048576 | tf_op jit(solution)/shard_map/all_to_all | solution.py:153
  53.0 1.6 %collective-permute-start.6 = (bf16[8,64,256]{2,1,0:T(8,128)(2,1)S(1)}, bf16[8,64,256]{2,1,0:T(8,128)(2,1)S(1)}, u32[]{:S(2)}, u32[]{:S(2)}) collective-permute-start(bf16[8,64,256]{2,1,0:T(8,128)(2,1)S(1)} %constant_dynamic-slice_fusion), channel_id=1, source_target_pairs={{0,1},{1,0},{2,3},{3,2},{4,5},{5,4},{6,7},{7,6},{8,9},{9,8},{10,11... | collective-permute-start | bytes 786440 | tf_op jit(solution)/shard_map/ppermute | solution.py:157

commit v20 on v18

--- a/solution.py
+++ b/solution.py
@@ -97,9 +97,13 @@
 
     trace_float = traces.astype(jnp.float32)
     source_float = sources.astype(jnp.float32)
+    lane_sums = jnp.sum(
+        (trace_float * trace_float).reshape(station_count, 2, group_bins // 128, 128), axis=(1, 2)
+    )
+    lane_sums = lax.optimization_barrier(lane_sums)
     trace_power, source_power = lax.psum(
         (
-            jnp.sum(trace_float * trace_float, axis=(1, 2)),
+            jnp.sum(lane_sums, axis=1),
             jnp.sum(source_float * source_float, axis=(1, 2)),
         ),
         "band",

time: 55.9 us -> 55.3 us (0.989)
  waiting for transfers between devices: 20.4 us -> 21.7 us
  starting transfers between devices: 14.3 us -> 13.1 us
  local copies, waits for them, and re-layouts: 4.73 us -> 4.13 us
    reduce_sum x1 -> x3, other arithmetic: 2.82 us -> 4.22 us  [the longest x2 4.12 us: per_device(): jnp.sum((trace_float * trace_float).reshape(station_count, 2, group_bins...]
    all_to_all x1, starting transfers between devices: 5.1 us -> 3.9 us  [per_device(): lax.all_to_all(partial, 'blk', split_axis=0, concat_axis=0, tiled=True)]
    ppermute x6, waiting for transfers between devices: 5.76 us -> 6.96 us  [per_device(): got = lax.ppermute(held, 'blk', route)]
    dynamic_update_slice x1, other arithmetic: 0.88 us -> 0.12 us  [per_device(): lax.dynamic_update_slice_in_dim(widened, got[None], jnp.bitwise_xor(posit...]
    reduce_sum x1, other arithmetic: 0.89 us -> 0.14 us  [per_device(): jnp.sum(source_float * source_float, axis=(1, 2))]
    unnamed x3 -> x8, local copies, waits for them, and re-layouts: 1.81 us -> 1.21 us
  transfers between devices with their start and end apart: 8 -> 8, of which waited for: 6 -> 6; matrix products, arithmetic and copies ran while one was open for 10% -> 7% of each run, Pallas kernels for 0% -> 0%
where the time goes in v20:
time: 55.3 us; the launch traced here: 55 us
  waiting for transfers between devices  21.7 us (39%)
  starting transfers between devices  13.1 us (24%)
  Pallas kernels  6.11 us (11%)
  other arithmetic  5.02 us (9%)
  local copies, waits for them, and re-layouts  4.13 us (7%)
  blocking collectives  2.59 us (5%)
  matrix products  2.18 us (4%)
    all_to_all x1, waiting for transfers between devices, per_device(): lax.all_to_all(partial, 'blk', split_axis=0, concat_axis=0, tiled=True)  13.3 us
    ppermute x6, starting transfers between devices, per_device(): got = lax.ppermute(held, 'blk', route)  9.11 us
    ppermute x6, waiting for transfers between devices, per_device(): got = lax.ppermute(held, 'blk', route)  6.96 us
    pallas_call x1, Pallas kernels, correlate(): pl.pallas_call(body, grid=(blocks // group,), in_specs=[pl.BlockSpec(plac...  6.11 us
    reduce_sum x2, other arithmetic, per_device(): jnp.sum((trace_float * trace_float).reshape(station_count, 2, group_bins...  4.12 us
    all_to_all x1, starting transfers between devices, per_device(): lax.all_to_all(partial, 'blk', split_axis=0, concat_axis=0, tiled=True)  3.9 us
    psum x1, blocking collectives, per_device(): lax.psum((jnp.sum(lane_sums, axis=1), jnp.sum(source_float * source_float...  2.59 us
    dot_general x1, matrix products, per_device(): jnp.dot(chosen.astype(jnp.bfloat16), traces.reshape(station_count, 2 * gr...  2.18 us
  transfers between devices with their start and end apart: 8, of which 6 were waited for; matrix products, arithmetic and copies ran while one was open for 7% of the time, Pallas kernels for 0%

profile of v20, /device:TPU:0, one launch (start us, length us, event | category | flops | bytes accessed | tf_op | source)
XLA Modules:
  0.0 55.0 jit_solution(9401382115706751756)
XLA Ops:
  0.0 4.0 %multiply_reduce_fusion = f32[64,4096]{1,0:T(8,128)S(1)} fusion(bf16[64,2,4096]{2,1,0:T(2,128)(2,1)} %param.4), kind=kLoop, calls=%fused_computation.2 | loop fusion | flops 1310720 | bytes 2097152 | tf_op jit(solution)/shard_map/reduce_sum | solution.py:100
  4.0 0.2 copy.22
  4.3 0.1 bitcast_reduce_fusion
  4.4 0.4 copy-done.1
  4.8 0.1 fusion.1
  4.9 0.1 reduce_sum.56
  5.0 2.6 %all-reduce = (f32[64]{0:T(128)S(1)}, f32[2]{0:T(128)S(1)}) all-reduce(f32[64]{0:T(128)S(1)} %reduce_sum.56, f32[2]{0:T(128)S(1)} %fusion.1), channel_id=1, replica_groups=mesh['blk'=16,'band'=2] {'band'}, use_global_device_ids=true, to_apply=%region_5.0 | all-reduce | flops 66 | bytes 528 | tf_op jit(solution)/shard_map/psum | solution.py:104
  7.7 0.1 bitcast_dynamic-update-slice_fusion.7
  7.8 3.0 %collective-permute-start = (bf16[1,2,2,4096]{3,2,1,0:T(2,128)(2,1)S(1)}, bf16[1,2,2,4096]{3,2,1,0:T(2,128)(2,1)S(1)}, u32[]{:S(2)}, u32[]{:S(2)}) collective-permute-start(bf16[1,2,2,4096]{3,2,1,0:T(2,128)(2,1)S(1)} %bitcast.57), channel_id=1, source_target_pairs={{0,8},{2,10},{4,12},{6,14},{8,0},{10,2},{12,4},{14,6},{16,24},{18,... | collective-permute-start | bytes 98312 | tf_op jit(solution)/shard_map/ppermute | solution.py:129
  10.8 2.6 %collective-permute-start.1 = (bf16[1,2,2,4096]{3,2,1,0:T(2,128)(2,1)S(1)}, bf16[1,2,2,4096]{3,2,1,0:T(2,128)(2,1)S(1)}, u32[]{:S(2)}, u32[]{:S(2)}) collective-permute-start(bf16[1,2,2,4096]{3,2,1,0:T(2,128)(2,1)S(1)} %bitcast.58), channel_id=1, source_target_pairs={{0,16},{2,18},{4,20},{6,22},{8,24},{10,26},{12,28},{14,30},{16,0},... | collective-permute-start | bytes 98312 | tf_op jit(solution)/shard_map/ppermute | solution.py:129
  13.4 0.6 %copy.21 = bf16[8,8,2,4096]{3,1,2,0:T(8,128)(2,1)S(1)} copy(bf16[8,8,2,4096]{3,2,1,0:T(2,128)(2,1)S(1)} %bitcast.52) | data formatting | bytes 2097152
  14.2 0.2 select_reduce_fusion.1
  14.4 0.1 select_reduce_fusion
  14.5 2.2 %fusion = bf16[128,8192]{1,0:T(8,128)(2,1)} fusion(bf16[64,8192]{1,0:T(8,128)(2,1)S(1)} %bitcast.53, f32[128]{0:T(128)S(1)} %select_reduce_fusion, s32[64]{0:T(128)S(1)} %multiply_add_fusion), kind=kOutput, calls=%fused_computation.1 | convolution fusion | flops 136323072 | bytes 3146496 | tf_op jit(solution)/shard_map/dot_general | solution.py:142
  16.7 2.4 %collective-permute-done.2 = bf16[1,2,2,4096]{3,2,1,0:T(2,128)(2,1)S(1)} collective-permute-done((bf16[1,2,2,4096]{3,2,1,0:T(2,128)(2,1)S(1)}, bf16[1,2,2,4096]{3,2,1,0:T(2,128)(2,1)S(1)}, u32[]{:S(2)}, u32[]{:S(2)}) %collective-permute-start.2) | collective-permute-done | bytes 32800 | tf_op jit(solution)/shard_map/ppermute | solution.py:129
  19.1 1.6 %collective-permute-start.3 = (bf16[4,1,2,2,4096]{4,3,2,0,1:T(2,128)(2,1)S(1)}, bf16[4,1,2,2,4096]{4,3,2,0,1:T(2,128)(2,1)S(1)}, u32[]{:S(2)}, u32[]{:S(2)}) collective-permute-start(bf16[4,1,2,2,4096]{4,3,2,0,1:T(2,128)(2,1)S(1)} %bitcast_dynamic-update-slice_fusion.4), channel_id=1, source_target_pairs={{0,2},{2,0},{4,6},{6,4},{8,10},{10,8},{12,14},{14,12},{16,18},{18,... | collective-permute-start | bytes 393224 | tf_op jit(solution)/shard_map/ppermute | solution.py:129
  20.7 1.5 %collective-permute-start.4 = (bf16[4,1,2,2,4096]{4,3,2,0,1:T(2,128)(2,1)S(1)}, bf16[4,1,2,2,4096]{4,3,2,0,1:T(2,128)(2,1)S(1)}, u32[]{:S(2)}, u32[]{:S(2)}) collective-permute-start(bf16[4,1,2,2,4096]{4,3,2,0,1:T(2,128)(2,1)S(1)} %bitcast_dynamic-update-slice_fusion.4), channel_id=1, source_target_pairs={{0,4},{2,6},{4,0},{6,2},{8,12},{10,14},{12,8},{14,10},{16,20},{18,... | collective-permute-start | bytes 393224 | tf_op jit(solution)/shard_map/ppermute | solution.py:129
  22.2 0.5 collective-permute-start.5
  22.7 0.5 broadcast_in_dim.50
  23.2 0.1 bitcast_dynamic-update-slice_fusion.2
  23.3 2.2 %collective-permute-done.3 = bf16[4,1,2,2,4096]{4,3,2,0,1:T(2,128)(2,1)S(1)} collective-permute-done((bf16[4,1,2,2,4096]{4,3,2,0,1:T(2,128)(2,1)S(1)}, bf16[4,1,2,2,4096]{4,3,2,0,1:T(2,128)(2,1)S(1)}, u32[]{:S(2)}, u32[]{:S(2)}) %collective-permute-start.3) | collective-permute-done | bytes 131104 | tf_op jit(solution)/shard_map/ppermute | solution.py:129
  25.5 0.1 bitcast_dynamic-update-slice_fusion.1
  25.6 1.1 %collective-permute-done.4 = bf16[4,1,2,2,4096]{4,3,2,0,1:T(2,128)(2,1)S(1)} collective-permute-done((bf16[4,1,2,2,4096]{4,3,2,0,1:T(2,128)(2,1)S(1)}, bf16[4,1,2,2,4096]{4,3,2,0,1:T(2,128)(2,1)S(1)}, u32[]{:S(2)}, u32[]{:S(2)}) %collective-permute-start.4) | collective-permute-done | bytes 131104 | tf_op jit(solution)/shard_map/ppermute | solution.py:129
  26.7 0.1 bitcast_dynamic-update-slice_fusion
  26.8 1.3 %collective-permute-done.5 = bf16[4,1,2,2,4096]{4,3,2,0,1:T(2,128)(2,1)S(1)} collective-permute-done((bf16[4,1,2,2,4096]{4,3,2,0,1:T(2,128)(2,1)S(1)}, bf16[4,1,2,2,4096]{4,3,2,0,1:T(2,128)(2,1)S(1)}, u32[]{:S(2)}, u32[]{:S(2)}) %collective-permute-start.5) | collective-permute-done | bytes 131104 | tf_op jit(solution)/shard_map/ppermute | solution.py:129
  28.1 0.1 bitcast_dynamic-update-slice_fusion.3
  28.2 1.0 %reshape.34.source_ref = bf16[16,4,4096]{2,1,0:T(4,128)(2,1)} reshape(bf16[1,4,4,2,2,4096]{5,4,3,2,1,0:T(2,128)(2,1)S(1)} %bitcast.56) | data formatting | bytes 1048576 | tf_op jit(solution)/shard_map/reshape | solution.py:154
  29.2 6.1 %shard_map.46 = bf16[16,64,256]{2,1,0:T(8,128)(2,1)} custom-call(bf16[16,16,4096]{2,1,0:T(8,128)(2,1)} %bitcast.51, bf16[16,4,4096]{2,1,0:T(4,128)(2,1)} %reshape.34.source_ref, bf16[2048,256]{1,0:T(8,128)(2,1)} %constant.42.clone.table_ref), custom_call_target="tpu_custom_call" | custom-call | flops 1107296256 | bytes 4194304 | tf_op jit(solution)/shard_map/pallas_call | solution.py:59
  35.3 3.9 %all-to-all-start = ((bf16[16,64,256]{2,1,0:T(8,128)(2,1)}), bf16[16,64,256]{2,1,0:T(8,128)(2,1)S(1)}, u32[]{:S(2)}, u32[]{:S(2)}) async-start(bf16[16,64,256]{2,1,0:T(8,128)(2,1)} %shard_map.46), calls=%async_computation | async-start | bytes 1048576 | tf_op jit(solution)/shard_map/all_to_all | solution.py:157
  39.2 13.3 %all-to-all-done = bf16[16,64,256]{2,1,0:T(8,128)(2,1)S(1)} async-done(((bf16[16,64,256]{2,1,0:T(8,128)(2,1)}), bf16[16,64,256]{2,1,0:T(8,128)(2,1)S(1)}, u32[]{:S(2)}, u32[]{:S(2)}) %all-to-all-start) | async-done | bytes 524320 | tf_op jit(solution)/shard_map/all_to_all | solution.py:157
  52.6 1.5 %collective-permute-done.6 = bf16[8,64,256]{2,1,0:T(8,128)(2,1)S(1)} collective-permute-done((bf16[8,64,256]{2,1,0:T(8,128)(2,1)S(1)}, bf16[8,64,256]{2,1,0:T(8,128)(2,1)S(1)}, u32[]{:S(2)}, u32[]{:S(2)}) %collective-permute-start.6) | collective-permute-done | bytes 262176 | tf_op jit(solution)/shard_map/ppermute | solution.py:161
  54.2 0.8 %copy.24 = f32[2,4,8,8,256]{4,3,2,1,0:T(8,128)} copy(f32[2,4,8,8,256]{4,3,1,0,2:T(8,128)S(1)} %bitcast.55) | data formatting | bytes 1048576 | tf_op jit(solution)/shard_map/transpose | solution.py:164
  (20 shorter events, 0.5 us)
Async XLA Ops:
  4.0 0.8 %copy-start.1 = (bf16[2,2,4096]{2,1,0:T(2,128)(2,1)S(1)}, bf16[2,2,4096]{2,1,0:T(2,128)(2,1)}, u32[]{:S(2)}) copy-start(bf16[2,2,4096]{2,1,0:T(2,128)(2,1)} %param.5) | copy-start | bytes 98308
  4.0 9.4 %copy-start = (bf16[64,2,4096]{2,1,0:T(2,128)(2,1)S(1)}, bf16[64,2,4096]{2,1,0:T(2,128)(2,1)}, u32[]{:S(2)}) copy-start(bf16[64,2,4096]{2,1,0:T(2,128)(2,1)} %param.4) | copy-start | bytes 3145732
  4.2 9.8 %copy-start.2 = (s32[64,1]{0,1:T(1,128)S(1)}, s32[64,1]{0,1:T(1,128)}, u32[]{:S(2)}) copy-start(s32[64,1]{0,1:T(1,128)} %param.6) | copy-start | bytes 772
  7.8 8.8 %collective-permute-start = (bf16[1,2,2,4096]{3,2,1,0:T(2,128)(2,1)S(1)}, bf16[1,2,2,4096]{3,2,1,0:T(2,128)(2,1)S(1)}, u32[]{:S(2)}, u32[]{:S(2)}) collective-permute-start(bf16[1,2,2,4096]{3,2,1,0:T(2,128)(2,1)S(1)} %bitcast.57), channel_id=1, source_target_pairs={{0,8},{2,10},{4,12},{6,14},{8,0},{10,2},{12,4},{14,6},{16,24},{18,... | collective-permute-start | bytes 98312 | tf_op jit(solution)/shard_map/ppermute | solution.py:129
  10.8 5.9 %collective-permute-start.1 = (bf16[1,2,2,4096]{3,2,1,0:T(2,128)(2,1)S(1)}, bf16[1,2,2,4096]{3,2,1,0:T(2,128)(2,1)S(1)}, u32[]{:S(2)}, u32[]{:S(2)}) collective-permute-start(bf16[1,2,2,4096]{3,2,1,0:T(2,128)(2,1)S(1)} %bitcast.58), channel_id=1, source_target_pairs={{0,16},{2,18},{4,20},{6,22},{8,24},{10,26},{12,28},{14,30},{16,0},... | collective-permute-start | bytes 98312 | tf_op jit(solution)/shard_map/ppermute | solution.py:129
  13.4 5.7 %collective-permute-start.2 = (bf16[1,2,2,4096]{3,2,1,0:T(2,128)(2,1)S(1)}, bf16[1,2,2,4096]{3,2,1,0:T(2,128)(2,1)S(1)}, u32[]{:S(2)}, u32[]{:S(2)}) collective-permute-start(bf16[1,2,2,4096]{3,2,1,0:T(2,128)(2,1)S(1)} %bitcast.59), channel_id=1, source_target_pairs={{0,24},{2,26},{4,28},{6,30},{8,16},{10,18},{12,20},{14,22},{16,8},... | collective-permute-start | bytes 98312 | tf_op jit(solution)/shard_map/ppermute | solution.py:129
  19.1 6.3 %collective-permute-start.3 = (bf16[4,1,2,2,4096]{4,3,2,0,1:T(2,128)(2,1)S(1)}, bf16[4,1,2,2,4096]{4,3,2,0,1:T(2,128)(2,1)S(1)}, u32[]{:S(2)}, u32[]{:S(2)}) collective-permute-start(bf16[4,1,2,2,4096]{4,3,2,0,1:T(2,128)(2,1)S(1)} %bitcast_dynamic-update-slice_fusion.4), channel_id=1, source_target_pairs={{0,2},{2,0},{4,6},{6,4},{8,10},{10,8},{12,14},{14,12},{16,18},{18,... | collective-permute-start | bytes 393224 | tf_op jit(solution)/shard_map/ppermute | solution.py:129
  20.7 6.0 %collective-permute-start.4 = (bf16[4,1,2,2,4096]{4,3,2,0,1:T(2,128)(2,1)S(1)}, bf16[4,1,2,2,4096]{4,3,2,0,1:T(2,128)(2,1)S(1)}, u32[]{:S(2)}, u32[]{:S(2)}) collective-permute-start(bf16[4,1,2,2,4096]{4,3,2,0,1:T(2,128)(2,1)S(1)} %bitcast_dynamic-update-slice_fusion.4), channel_id=1, source_target_pairs={{0,4},{2,6},{4,0},{6,2},{8,12},{10,14},{12,8},{14,10},{16,20},{18,... | collective-permute-start | bytes 393224 | tf_op jit(solution)/shard_map/ppermute | solution.py:129
  22.2 5.9 %collective-permute-start.5 = (bf16[4,1,2,2,4096]{4,3,2,0,1:T(2,128)(2,1)S(1)}, bf16[4,1,2,2,4096]{4,3,2,0,1:T(2,128)(2,1)S(1)}, u32[]{:S(2)}, u32[]{:S(2)}) collective-permute-start(bf16[4,1,2,2,4096]{4,3,2,0,1:T(2,128)(2,1)S(1)} %bitcast_dynamic-update-slice_fusion.4), channel_id=1, source_target_pairs={{0,6},{2,4},{4,2},{6,0},{8,14},{10,12},{12,10},{14,8},{16,22},{18,... | collective-permute-start | bytes 393224 | tf_op jit(solution)/shard_map/ppermute | solution.py:129
  35.3 17.2 %all-to-all-start = ((bf16[16,64,256]{2,1,0:T(8,128)(2,1)}), bf16[16,64,256]{2,1,0:T(8,128)(2,1)S(1)}, u32[]{:S(2)}, u32[]{:S(2)}) async-start(bf16[16,64,256]{2,1,0:T(8,128)(2,1)} %shard_map.46), calls=%async_computation | async-start | bytes 1048576 | tf_op jit(solution)/shard_map/all_to_all | solution.py:157
  52.5 1.6 %collective-permute-start.6 = (bf16[8,64,256]{2,1,0:T(8,128)(2,1)S(1)}, bf16[8,64,256]{2,1,0:T(8,128)(2,1)S(1)}, u32[]{:S(2)}, u32[]{:S(2)}) collective-permute-start(bf16[8,64,256]{2,1,0:T(8,128)(2,1)S(1)} %constant_dynamic-slice_fusion), channel_id=1, source_target_pairs={{0,1},{1,0},{2,3},{3,2},{4,5},{5,4},{6,7},{7,6},{8,9},{9,8},{10,11... | collective-permute-start | bytes 786440 | tf_op jit(solution)/shard_map/ppermute | solution.py:161

commit v21 on v18

--- a/solution.py
+++ b/solution.py
@@ -30,8 +30,8 @@
             real_t = owned[:capacity]
             imag_t = owned[capacity:]
             for source in range(2):
-                real_s = source_ref[member, 2 * source : 2 * source + 1]
-                imag_s = source_ref[member, 2 * source + 1 : 2 * source + 2]
+                real_s = source_ref[member, source, 0:1]
+                imag_s = source_ref[member, source, 1:2]
                 even = real_t * real_s + imag_t * imag_s
                 odd = real_t * imag_s - imag_t * real_s
                 even_fold = even[:, :PERIOD]
@@ -61,7 +61,7 @@
         grid=(blocks // group,),
         in_specs=[
             pl.BlockSpec(placed.shape, lambda a: (0, 0, 0)),
-            pl.BlockSpec((group,) + white_sources.shape[1:], lambda a: (a, 0, 0)),
+            pl.BlockSpec((group,) + white_sources.shape[1:], lambda a: (a, 0, 0, 0)),
             pl.BlockSpec(table.shape, lambda a: (0, 0)),
         ],
         out_specs=pl.BlockSpec((group, rows, lags_out), lambda a: (a, 0, 0)),
@@ -111,24 +111,25 @@
     held = white_sources[None]
     bits = blocks.bit_length() - 1
     shift = bits
+    grouped = 1
     while shift > 0:
         width = 2 if shift >= 2 else 1
         shift -= width
         radix = 1 << width
         position = jnp.bitwise_and(me >> shift, radix - 1)
-        widened = jnp.zeros((radix,) + held.shape, held.dtype)
+        widened = jnp.zeros(held.shape[:grouped] + (radix,) + held.shape[grouped:], held.dtype)
+        rest = (0,) * (held.ndim - grouped)
         for partner in range(radix):
             if partner == 0:
                 got = held
             else:
                 route = [(i, i ^ (partner << shift)) for i in range(blocks)]
                 got = lax.ppermute(held, "blk", route)
-            widened = lax.dynamic_update_slice_in_dim(
-                widened, got[None], jnp.bitwise_xor(position, partner), axis=0
-            )
+            start = (0,) * grouped + (jnp.bitwise_xor(position, partner),) + rest
+            widened = lax.dynamic_update_slice(widened, jnp.expand_dims(got, grouped), start)
         held = widened
-    groups = held.ndim - white_sources.ndim
-    held = held.transpose(tuple(reversed(range(groups))) + tuple(range(groups, held.ndim)))
+        grouped += 1
+    held = held.reshape((blocks,) + white_sources.shape)
     owners = owner[:, 0]
     owner_hits = (owners[:, None] == jnp.arange(blocks, dtype=jnp.int32)[None, :]).astype(jnp.int32)
     earlier = jnp.cumsum(owner_hits, axis=0) - owner_hits
@@ -147,7 +148,7 @@
 
     table = jnp.asarray(twiddle_table(lags_out))
 
-    white_sources = held.reshape(blocks, source_count * 2, group_bins)
+    white_sources = held
 
     partial = correlate(placed, white_sources, table, offsets, capacity)
     arrived = lax.all_to_all(partial, "blk", split_axis=0, concat_axis=0, tiled=True)

time: 55.9 us -> 55.8 us (level)
    reshape x1 -> x0, local copies, waits for them, and re-layouts: 0.99 us -> none  [per_device(): white_sources = held.reshape(blocks, source_count * 2, group_bins)]
    unnamed x3 -> x5, local copies, waits for them, and re-layouts: 1.81 us -> 2.6 us
where the time goes in v21:
time: 55.8 us; the launch traced here: 55.4 us
  waiting for transfers between devices  20.3 us (36%)
  starting transfers between devices  14.3 us (26%)
  Pallas kernels  6.21 us (11%)
  other arithmetic  5.13 us (9%)
  local copies, waits for them, and re-layouts  4.52 us (8%)
  blocking collectives  2.56 us (5%)
  matrix products  2.18 us (4%)
    all_to_all x1, waiting for transfers between devices, per_device(): lax.all_to_all(partial, 'blk', split_axis=0, concat_axis=0, tiled=True)  13.1 us
    ppermute x6, starting transfers between devices, per_device(): got = lax.ppermute(held, 'blk', route)  9.11 us
    pallas_call x1, Pallas kernels, correlate(): pl.pallas_call(body, grid=(blocks // group,), in_specs=[pl.BlockSpec(plac...  6.21 us
    ppermute x6, waiting for transfers between devices, per_device(): got = lax.ppermute(held, 'blk', route)  5.76 us
    all_to_all x1, starting transfers between devices, per_device(): lax.all_to_all(partial, 'blk', split_axis=0, concat_axis=0, tiled=True)  5.1 us
    reduce_sum x1, other arithmetic, per_device(): jnp.sum(trace_float * trace_float, axis=(1, 2))  2.82 us
    unnamed x5, local copies, waits for them, and re-layouts  2.6 us
    psum x1, blocking collectives, per_device(): lax.psum((jnp.sum(trace_float * trace_float, axis=(1, 2)), jnp.sum(source...  2.56 us
  transfers between devices with their start and end apart: 8, of which 6 were waited for; matrix products, arithmetic and copies ran while one was open for 10% of the time, Pallas kernels for 0%

profile of v21, /device:TPU:0, one launch (start us, length us, event | category | flops | bytes accessed | tf_op | source)
XLA Modules:
  0.0 55.4 jit_solution(8254262393622547242)
XLA Ops:
  0.0 2.8 %multiply_reduce_fusion = f32[64]{0:T(128)S(1)} fusion(bf16[64,2,4096]{2,1,0:T(2,128)(2,1)} %param.4), kind=kLoop, calls=%fused_computation.2 | loop fusion | flops 1572800 | bytes 1048832 | tf_op jit(solution)/shard_map/reduce_sum | solution.py:102
  2.8 0.9 %fusion.1 = f32[2]{0:T(128)S(1)} fusion(bf16[2,2,4096]{2,1,0:T(2,128)(2,1)} %param.5), kind=kLoop, calls=%fused_computation.11 | loop fusion | flops 49150 | bytes 32776 | tf_op jit(solution)/shard_map/reduce_sum | solution.py:103
  3.7 2.6 %all-reduce = (f32[64]{0:T(128)S(1)}, f32[2]{0:T(128)S(1)}) all-reduce(f32[64]{0:T(128)S(1)} %multiply_reduce_fusion, f32[2]{0:T(128)S(1)} %fusion.1), channel_id=1, replica_groups=mesh['blk'=16,'band'=2] {'band'}, use_global_device_ids=true, to_apply=%region_3.0 | all-reduce | flops 66 | bytes 528 | tf_op jit(solution)/shard_map/psum | solution.py:100
  6.3 0.1 broadcast_in_dim.51
  6.4 0.9 %bitcast_dynamic-update-slice_fusion.7 = (bf16[1,4,2,2,4096]{4,3,2,1,0:T(2,128)(2,1)S(1)}, bf16[2,2,4096]{2,1,0:T(2,128)(2,1)S(1)}) fusion(bf16[1,4,2,2,4096]{4,3,2,1,0:T(2,128)(2,1)S(1)} %broadcast_in_dim.51, s32[]{:T(128)S(6)} %select_n.35, f32[2]{0:T(128)S(1)} %add_rsqrt_fusion, bf16[2,2,4096]{2,1,0:T(2,128)(2,1)} %param.5), kind=kLoop, calls=%fused_computation.16 | loop fusion | flops 49152 | bytes 98820 | tf_op jit(solution)/shard_map/dynamic_update_slice | solution.py:129
  7.2 3.0 %collective-permute-start = (bf16[1,2,2,4096]{3,2,1,0:T(2,128)(2,1)S(1)}, bf16[1,2,2,4096]{3,2,1,0:T(2,128)(2,1)S(1)}, u32[]{:S(2)}, u32[]{:S(2)}) collective-permute-start(bf16[1,2,2,4096]{3,2,1,0:T(2,128)(2,1)S(1)} %bitcast.45), channel_id=1, source_target_pairs={{0,8},{2,10},{4,12},{6,14},{8,0},{10,2},{12,4},{14,6},{16,24},{18,... | collective-permute-start | bytes 98312 | tf_op jit(solution)/shard_map/ppermute | solution.py:127
  10.2 2.6 %collective-permute-start.1 = (bf16[1,2,2,4096]{3,2,1,0:T(2,128)(2,1)S(1)}, bf16[1,2,2,4096]{3,2,1,0:T(2,128)(2,1)S(1)}, u32[]{:S(2)}, u32[]{:S(2)}) collective-permute-start(bf16[1,2,2,4096]{3,2,1,0:T(2,128)(2,1)S(1)} %bitcast.46), channel_id=1, source_target_pairs={{0,16},{2,18},{4,20},{6,22},{8,24},{10,26},{12,28},{14,30},{16,0},... | collective-permute-start | bytes 98312 | tf_op jit(solution)/shard_map/ppermute | solution.py:127
  12.8 1.8 %copy.13 = bf16[8,8,2,4096]{3,1,2,0:T(8,128)(2,1)S(1)} copy(bf16[8,8,2,4096]{3,2,1,0:T(2,128)(2,1)} %bitcast.41) | data formatting | bytes 2097152
  14.6 0.1 fusion.3
  14.7 0.1 reduce_window_sum.11
  14.8 0.2 select_reduce_fusion.1
  15.0 0.1 select_reduce_fusion
  15.1 2.2 %fusion = bf16[128,8192]{1,0:T(8,128)(2,1)} fusion(bf16[64,8192]{1,0:T(8,128)(2,1)S(1)} %bitcast.42, f32[128]{0:T(128)S(1)} %select_reduce_fusion, s32[64]{0:T(128)S(1)} %multiply_add_fusion), kind=kOutput, calls=%fused_computation.1 | convolution fusion | flops 136323072 | bytes 3146496 | tf_op jit(solution)/shard_map/dot_general | solution.py:139
  17.4 1.1 %collective-permute-done.2 = bf16[1,2,2,4096]{3,2,1,0:T(2,128)(2,1)S(1)} collective-permute-done((bf16[1,2,2,4096]{3,2,1,0:T(2,128)(2,1)S(1)}, bf16[1,2,2,4096]{3,2,1,0:T(2,128)(2,1)S(1)}, u32[]{:S(2)}, u32[]{:S(2)}) %collective-permute-start.2) | collective-permute-done | bytes 32800 | tf_op jit(solution)/shard_map/ppermute | solution.py:127
  18.6 1.6 %collective-permute-start.3 = (bf16[1,4,2,2,4096]{4,3,2,1,0:T(2,128)(2,1)S(1)}, bf16[1,4,2,2,4096]{4,3,2,1,0:T(2,128)(2,1)S(1)}, u32[]{:S(2)}, u32[]{:S(2)}) collective-permute-start(bf16[1,4,2,2,4096]{4,3,2,1,0:T(2,128)(2,1)S(1)} %bitcast_dynamic-update-slice_fusion.4), channel_id=1, source_target_pairs={{0,2},{2,0},{4,6},{6,4},{8,10},{10,8},{12,14},{14,12},{16,18},{18,... | collective-permute-start | bytes 393224 | tf_op jit(solution)/shard_map/ppermute | solution.py:127
  20.1 1.5 %collective-permute-start.4 = (bf16[1,4,2,2,4096]{4,3,2,1,0:T(2,128)(2,1)S(1)}, bf16[1,4,2,2,4096]{4,3,2,1,0:T(2,128)(2,1)S(1)}, u32[]{:S(2)}, u32[]{:S(2)}) collective-permute-start(bf16[1,4,2,2,4096]{4,3,2,1,0:T(2,128)(2,1)S(1)} %bitcast_dynamic-update-slice_fusion.4), channel_id=1, source_target_pairs={{0,4},{2,6},{4,0},{6,2},{8,12},{10,14},{12,8},{14,10},{16,20},{18,... | collective-permute-start | bytes 393224 | tf_op jit(solution)/shard_map/ppermute | solution.py:127
  21.6 0.5 collective-permute-start.5
  22.1 0.5 broadcast_in_dim.50
  22.6 0.1 bitcast_dynamic-update-slice_fusion.2
  22.7 2.2 %collective-permute-done.3 = bf16[1,4,2,2,4096]{4,3,2,1,0:T(2,128)(2,1)S(1)} collective-permute-done((bf16[1,4,2,2,4096]{4,3,2,1,0:T(2,128)(2,1)S(1)}, bf16[1,4,2,2,4096]{4,3,2,1,0:T(2,128)(2,1)S(1)}, u32[]{:S(2)}, u32[]{:S(2)}) %collective-permute-start.3) | collective-permute-done | bytes 131104 | tf_op jit(solution)/shard_map/ppermute | solution.py:127
  24.9 0.1 bitcast_dynamic-update-slice_fusion.1
  25.0 1.1 %collective-permute-done.4 = bf16[1,4,2,2,4096]{4,3,2,1,0:T(2,128)(2,1)S(1)} collective-permute-done((bf16[1,4,2,2,4096]{4,3,2,1,0:T(2,128)(2,1)S(1)}, bf16[1,4,2,2,4096]{4,3,2,1,0:T(2,128)(2,1)S(1)}, u32[]{:S(2)}, u32[]{:S(2)}) %collective-permute-start.4) | collective-permute-done | bytes 131104 | tf_op jit(solution)/shard_map/ppermute | solution.py:127
  26.1 0.1 bitcast_dynamic-update-slice_fusion
  26.2 1.3 %collective-permute-done.5 = bf16[1,4,2,2,4096]{4,3,2,1,0:T(2,128)(2,1)S(1)} collective-permute-done((bf16[1,4,2,2,4096]{4,3,2,1,0:T(2,128)(2,1)S(1)}, bf16[1,4,2,2,4096]{4,3,2,1,0:T(2,128)(2,1)S(1)}, u32[]{:S(2)}, u32[]{:S(2)}) %collective-permute-start.5) | collective-permute-done | bytes 131104 | tf_op jit(solution)/shard_map/ppermute | solution.py:127
  27.5 0.1 bitcast_dynamic-update-slice_fusion.3
  27.6 0.8 %copy-done = bf16[1,4,4,2,2,4096]{5,4,3,2,1,0:T(2,128)(2,1)} copy-done((bf16[1,4,4,2,2,4096]{5,4,3,2,1,0:T(2,128)(2,1)}, bf16[1,4,4,2,2,4096]{5,4,3,2,1,0:T(2,128)(2,1)S(1)}, u32[]{:S(2)}) %copy-start) | copy-done | bytes 524312
  28.4 6.2 %shard_map.46 = bf16[16,64,256]{2,1,0:T(8,128)(2,1)} custom-call(bf16[16,16,4096]{2,1,0:T(8,128)(2,1)} %bitcast.40, bf16[16,2,2,4096]{3,2,1,0:T(2,128)(2,1)} %bitcast.44, bf16[2048,256]{1,0:T(8,128)(2,1)} %constant.42.clone.table_ref), custom_call_target="tpu_custom_call" | custom-call | flops 1107296256 | bytes 4194304 | tf_op jit(solution)/shard_map/pallas_call | solution.py:59
  34.6 5.1 %all-to-all-start = ((bf16[16,64,256]{2,1,0:T(8,128)(2,1)}), bf16[16,64,256]{2,1,0:T(8,128)(2,1)S(1)}, u32[]{:S(2)}, u32[]{:S(2)}) async-start(bf16[16,64,256]{2,1,0:T(8,128)(2,1)} %shard_map.46), calls=%async_computation | async-start | bytes 1048576 | tf_op jit(solution)/shard_map/all_to_all | solution.py:154
  39.8 13.1 %all-to-all-done = bf16[16,64,256]{2,1,0:T(8,128)(2,1)S(1)} async-done(((bf16[16,64,256]{2,1,0:T(8,128)(2,1)}), bf16[16,64,256]{2,1,0:T(8,128)(2,1)S(1)}, u32[]{:S(2)}, u32[]{:S(2)}) %all-to-all-start) | async-done | bytes 524320 | tf_op jit(solution)/shard_map/all_to_all | solution.py:154
  52.8 0.1 collective-permute-start.6
  52.9 1.5 %collective-permute-done.6 = bf16[8,64,256]{2,1,0:T(8,128)(2,1)S(1)} collective-permute-done((bf16[8,64,256]{2,1,0:T(8,128)(2,1)S(1)}, bf16[8,64,256]{2,1,0:T(8,128)(2,1)S(1)}, u32[]{:S(2)}, u32[]{:S(2)}) %collective-permute-start.6) | collective-permute-done | bytes 262176 | tf_op jit(solution)/shard_map/ppermute | solution.py:158
  54.5 0.8 %copy.15 = f32[2,4,8,8,256]{4,3,2,1,0:T(8,128)} copy(f32[2,4,8,8,256]{4,3,1,0,2:T(8,128)S(1)} %bitcast.43) | data formatting | bytes 1048576 | tf_op jit(solution)/shard_map/transpose | solution.py:161
  (14 shorter events, 0.2 us)
Async XLA Ops:
  0.0 14.6 %copy-start.1 = (s32[64,1]{0,1:T(1,128)S(1)}, s32[64,1]{0,1:T(1,128)}, u32[]{:S(2)}) copy-start(s32[64,1]{0,1:T(1,128)} %param.6) | copy-start | bytes 772
  7.2 10.0 %collective-permute-start = (bf16[1,2,2,4096]{3,2,1,0:T(2,128)(2,1)S(1)}, bf16[1,2,2,4096]{3,2,1,0:T(2,128)(2,1)S(1)}, u32[]{:S(2)}, u32[]{:S(2)}) collective-permute-start(bf16[1,2,2,4096]{3,2,1,0:T(2,128)(2,1)S(1)} %bitcast.45), channel_id=1, source_target_pairs={{0,8},{2,10},{4,12},{6,14},{8,0},{10,2},{12,4},{14,6},{16,24},{18,... | collective-permute-start | bytes 98312 | tf_op jit(solution)/shard_map/ppermute | solution.py:127
  10.2 7.1 %collective-permute-start.1 = (bf16[1,2,2,4096]{3,2,1,0:T(2,128)(2,1)S(1)}, bf16[1,2,2,4096]{3,2,1,0:T(2,128)(2,1)S(1)}, u32[]{:S(2)}, u32[]{:S(2)}) collective-permute-start(bf16[1,2,2,4096]{3,2,1,0:T(2,128)(2,1)S(1)} %bitcast.46), channel_id=1, source_target_pairs={{0,16},{2,18},{4,20},{6,22},{8,24},{10,26},{12,28},{14,30},{16,0},... | collective-permute-start | bytes 98312 | tf_op jit(solution)/shard_map/ppermute | solution.py:127
  12.8 5.7 %collective-permute-start.2 = (bf16[1,2,2,4096]{3,2,1,0:T(2,128)(2,1)S(1)}, bf16[1,2,2,4096]{3,2,1,0:T(2,128)(2,1)S(1)}, u32[]{:S(2)}, u32[]{:S(2)}) collective-permute-start(bf16[1,2,2,4096]{3,2,1,0:T(2,128)(2,1)S(1)} %bitcast.47), channel_id=1, source_target_pairs={{0,24},{2,26},{4,28},{6,30},{8,16},{10,18},{12,20},{14,22},{16,8},... | collective-permute-start | bytes 98312 | tf_op jit(solution)/shard_map/ppermute | solution.py:127
  18.6 6.3 %collective-permute-start.3 = (bf16[1,4,2,2,4096]{4,3,2,1,0:T(2,128)(2,1)S(1)}, bf16[1,4,2,2,4096]{4,3,2,1,0:T(2,128)(2,1)S(1)}, u32[]{:S(2)}, u32[]{:S(2)}) collective-permute-start(bf16[1,4,2,2,4096]{4,3,2,1,0:T(2,128)(2,1)S(1)} %bitcast_dynamic-update-slice_fusion.4), channel_id=1, source_target_pairs={{0,2},{2,0},{4,6},{6,4},{8,10},{10,8},{12,14},{14,12},{16,18},{18,... | collective-permute-start | bytes 393224 | tf_op jit(solution)/shard_map/ppermute | solution.py:127
  20.1 6.0 %collective-permute-start.4 = (bf16[1,4,2,2,4096]{4,3,2,1,0:T(2,128)(2,1)S(1)}, bf16[1,4,2,2,4096]{4,3,2,1,0:T(2,128)(2,1)S(1)}, u32[]{:S(2)}, u32[]{:S(2)}) collective-permute-start(bf16[1,4,2,2,4096]{4,3,2,1,0:T(2,128)(2,1)S(1)} %bitcast_dynamic-update-slice_fusion.4), channel_id=1, source_target_pairs={{0,4},{2,6},{4,0},{6,2},{8,12},{10,14},{12,8},{14,10},{16,20},{18,... | collective-permute-start | bytes 393224 | tf_op jit(solution)/shard_map/ppermute | solution.py:127
  21.6 5.9 %collective-permute-start.5 = (bf16[1,4,2,2,4096]{4,3,2,1,0:T(2,128)(2,1)S(1)}, bf16[1,4,2,2,4096]{4,3,2,1,0:T(2,128)(2,1)S(1)}, u32[]{:S(2)}, u32[]{:S(2)}) collective-permute-start(bf16[1,4,2,2,4096]{4,3,2,1,0:T(2,128)(2,1)S(1)} %bitcast_dynamic-update-slice_fusion.4), channel_id=1, source_target_pairs={{0,6},{2,4},{4,2},{6,0},{8,14},{10,12},{12,10},{14,8},{16,22},{18,... | collective-permute-start | bytes 393224 | tf_op jit(solution)/shard_map/ppermute | solution.py:127
  27.6 0.8 %copy-start = (bf16[1,4,4,2,2,4096]{5,4,3,2,1,0:T(2,128)(2,1)}, bf16[1,4,4,2,2,4096]{5,4,3,2,1,0:T(2,128)(2,1)S(1)}, u32[]{:S(2)}) copy-start(bf16[1,4,4,2,2,4096]{5,4,3,2,1,0:T(2,128)(2,1)S(1)} %bitcast_dynamic-update-slice_fusion.3) | copy-start | bytes 1572868
  34.6 18.2 %all-to-all-start = ((bf16[16,64,256]{2,1,0:T(8,128)(2,1)}), bf16[16,64,256]{2,1,0:T(8,128)(2,1)S(1)}, u32[]{:S(2)}, u32[]{:S(2)}) async-start(bf16[16,64,256]{2,1,0:T(8,128)(2,1)} %shard_map.46), calls=%async_computation | async-start | bytes 1048576 | tf_op jit(solution)/shard_map/all_to_all | solution.py:154
  52.8 1.6 %collective-permute-start.6 = (bf16[8,64,256]{2,1,0:T(8,128)(2,1)S(1)}, bf16[8,64,256]{2,1,0:T(8,128)(2,1)S(1)}, u32[]{:S(2)}, u32[]{:S(2)}) collective-permute-start(bf16[8,64,256]{2,1,0:T(8,128)(2,1)S(1)} %constant_dynamic-slice_fusion), channel_id=1, source_target_pairs={{0,1},{1,0},{2,3},{3,2},{4,5},{5,4},{6,7},{7,6},{8,9},{9,8},{10,11... | collective-permute-start | bytes 786440 | tf_op jit(solution)/shard_map/ppermute | solution.py:158

commit v22 on v13

--- a/solution.py
+++ b/solution.py
@@ -54,7 +54,7 @@
     blocks, _, group_bins = placed.shape
     rows = 2 * offsets * capacity
     lags_out = table.shape[1]
-    group = 4
+    group = 8
     body = functools.partial(correlate_kernel, blocks, offsets, capacity, group, BINS ** (-0.5))
     return pl.pallas_call(
         body,
@@ -98,12 +98,11 @@
     source_float = sources.astype(jnp.float32)
     source_sums = jnp.sum(source_float * source_float, axis=(1, 2))
     source_power = source_sums + lax.ppermute(source_sums, "band", [(0, 1), (1, 0)])
+    trace_float = traces.astype(jnp.float32)
+    trace_power = lax.psum(jnp.sum(trace_float * trace_float, axis=(1, 2)), "band")
     white_sources = (
         source_float * lax.rsqrt(source_power / (2 * BINS) + EPS)[:, None, None]
     ).astype(jnp.bfloat16)
-    traces, white_sources = lax.optimization_barrier((traces, white_sources))
-    trace_float = traces.astype(jnp.float32)
-    trace_power = lax.psum(jnp.sum(trace_float * trace_float, axis=(1, 2)), "band")
     me = lax.axis_index("blk")
     held = white_sources[None]
     bits = blocks.bit_length() - 1

time: 60.3 us -> 59.1 us (0.980)
  waiting for transfers between devices: 21.5 us -> 25.7 us
  other arithmetic: 7.06 us -> 4.43 us
  starting transfers between devices: 15.3 us -> 13 us
    ppermute x6, waiting for transfers between devices: 5.63 us -> 10.5 us  [per_device(): got = lax.ppermute(held, 'blk', route)]
    all_to_all x1, starting transfers between devices: 5.94 us -> 3.57 us  [per_device(): lax.all_to_all(partial, 'blk', split_axis=0, concat_axis=0, tiled=True)]
    convert_element_type x1 -> x0, other arithmetic: 0.85 us -> none  [per_device(): white_sources = (source_float * lax.rsqrt(source_power / (2 * BINS) + EPS...]
    all_to_all x1, waiting for transfers between devices: 14.4 us -> 13.7 us  [per_device(): lax.all_to_all(partial, 'blk', split_axis=0, concat_axis=0, tiled=True)]
    add x1, other arithmetic: 0.67 us -> 0.01 us  [per_device(): slot_index = owners * capacity + arrival]
    reduce_sum x1, other arithmetic: 0.84 us -> 0.18 us  [per_device(): arrival = jnp.sum(owner_hits * earlier, axis=1)]
    convert_element_type x1, other arithmetic: 0.73 us -> 0.07 us  [per_device(): (owners[:, None] == jnp.arange(blocks, dtype=jnp.int32)[None, :]).astype(...]
    unnamed x1 -> x5, local copies, waits for them, and re-layouts: 1.81 us -> 1.81 us
  transfers between devices with their start and end apart: 9 -> 9, of which waited for: 4 -> 6; matrix products, arithmetic and copies ran while one was open for 17% -> 14% of each run, Pallas kernels for 0% -> 0%
where the time goes in v22:
time: 59.1 us; the launch traced here: 58.8 us
  waiting for transfers between devices  25.7 us (43%)
  starting transfers between devices  13 us (22%)
  Pallas kernels  6.11 us (10%)
  local copies, waits for them, and re-layouts  4.73 us (8%)
  other arithmetic  4.43 us (7%)
  blocking collectives  2.47 us (4%)
  matrix products  2.17 us (4%)
    all_to_all x1, waiting for transfers between devices, per_device(): lax.all_to_all(partial, 'blk', split_axis=0, concat_axis=0, tiled=True)  13.7 us
    ppermute x6, waiting for transfers between devices, per_device(): got = lax.ppermute(held, 'blk', route)  10.5 us
    ppermute x6, starting transfers between devices, per_device(): got = lax.ppermute(held, 'blk', route)  8.95 us
    pallas_call x1, Pallas kernels, correlate(): pl.pallas_call(body, grid=(blocks // group,), in_specs=[pl.BlockSpec(plac...  6.11 us
    all_to_all x1, starting transfers between devices, per_device(): lax.all_to_all(partial, 'blk', split_axis=0, concat_axis=0, tiled=True)  3.57 us
    reduce_sum x1, other arithmetic, per_device(): jnp.sum(trace_float * trace_float, axis=(1, 2))  2.81 us
    psum x1, blocking collectives, per_device(): lax.psum(jnp.sum(trace_float * trace_float, axis=(1, 2)), 'band')  2.47 us
    dot_general x1, matrix products, per_device(): jnp.dot(chosen.astype(jnp.bfloat16), traces.reshape(station_count, 2 * gr...  2.17 us
  transfers between devices with their start and end apart: 9, of which 6 were waited for; matrix products, arithmetic and copies ran while one was open for 14% of the time, Pallas kernels for 0%

profile of v22, /device:TPU:0, one launch (start us, length us, event | category | flops | bytes accessed | tf_op | source)
XLA Modules:
  0.0 58.8 jit_solution(3621827275947044013)
XLA Ops:
  0.0 1.0 %fusion.1 = f32[2]{0:T(128)S(1)} fusion(bf16[2,2,4096]{2,1,0:T(2,128)(2,1)} %param.5), kind=kLoop, calls=%fused_computation.11 | loop fusion | flops 49150 | bytes 32776 | tf_op jit(solution)/shard_map/reduce_sum | solution.py:99
  1.0 0.5 collective-permute-start
  1.4 2.8 %multiply_reduce_fusion = f32[64]{0:T(128)S(1)} fusion(bf16[64,2,4096]{2,1,0:T(2,128)(2,1)} %param.4), kind=kLoop, calls=%fused_computation.2 | loop fusion | flops 1572800 | bytes 1048832 | tf_op jit(solution)/shard_map/reduce_sum | solution.py:102
  4.2 1.8 %copy.21 = bf16[8,8,2,4096]{3,1,2,0:T(8,128)(2,1)S(1)} copy(bf16[8,8,2,4096]{3,2,1,0:T(2,128)(2,1)} %bitcast.49) | data formatting | bytes 2097152
  6.0 2.5 %psum.7 = f32[64]{0:T(128)S(1)} all-reduce(f32[64]{0:T(128)S(1)} %multiply_reduce_fusion), channel_id=1, replica_groups=mesh['blk'=16,'band'=2] {'band'}, use_global_device_ids=true, to_apply=%region_3.0 | all-reduce | flops 64 | bytes 512 | tf_op jit(solution)/shard_map/psum | solution.py:102
  8.5 0.1 fusion.3
  8.6 0.1 reduce_window_sum.11
  8.7 0.2 select_reduce_fusion.1
  8.9 0.1 select_reduce_fusion
  9.1 0.1 bitcast_dynamic-update-slice_fusion.7
  9.2 2.8 %collective-permute-start.1 = (bf16[1,2,2,4096]{3,2,1,0:T(2,128)(2,1)S(1)}, bf16[1,2,2,4096]{3,2,1,0:T(2,128)(2,1)S(1)}, u32[]{:S(2)}, u32[]{:S(2)}) collective-permute-start(bf16[1,2,2,4096]{3,2,1,0:T(2,128)(2,1)S(1)} %bitcast.53), channel_id=1, source_target_pairs={{0,8},{2,10},{4,12},{6,14},{8,0},{10,2},{12,4},{14,6},{16,24},{18,... | collective-permute-start | bytes 98312 | tf_op jit(solution)/shard_map/ppermute | solution.py:121
  12.0 2.2 %fusion = bf16[128,8192]{1,0:T(8,128)(2,1)} fusion(bf16[64,8192]{1,0:T(8,128)(2,1)S(1)} %bitcast.50, f32[128]{0:T(128)S(1)} %select_reduce_fusion, s32[64]{0:T(128)S(1)} %multiply_add_fusion), kind=kOutput, calls=%fused_computation.1 | convolution fusion | flops 136323072 | bytes 3146496 | tf_op jit(solution)/shard_map/dot_general | solution.py:134
  14.2 2.6 %collective-permute-start.2 = (bf16[1,2,2,4096]{3,2,1,0:T(2,128)(2,1)S(1)}, bf16[1,2,2,4096]{3,2,1,0:T(2,128)(2,1)S(1)}, u32[]{:S(2)}, u32[]{:S(2)}) collective-permute-start(bf16[1,2,2,4096]{3,2,1,0:T(2,128)(2,1)S(1)} %bitcast.54), channel_id=1, source_target_pairs={{0,16},{2,18},{4,20},{6,22},{8,24},{10,26},{12,28},{14,30},{16,0},... | collective-permute-start | bytes 98312 | tf_op jit(solution)/shard_map/ppermute | solution.py:121
  16.8 2.2 %collective-permute-done.2 = bf16[1,2,2,4096]{3,2,1,0:T(2,128)(2,1)S(1)} collective-permute-done((bf16[1,2,2,4096]{3,2,1,0:T(2,128)(2,1)S(1)}, bf16[1,2,2,4096]{3,2,1,0:T(2,128)(2,1)S(1)}, u32[]{:S(2)}, u32[]{:S(2)}) %collective-permute-start.2) | collective-permute-done | bytes 32800 | tf_op jit(solution)/shard_map/ppermute | solution.py:121
  19.1 3.5 %collective-permute-done.3 = bf16[1,2,2,4096]{3,2,1,0:T(2,128)(2,1)S(1)} collective-permute-done((bf16[1,2,2,4096]{3,2,1,0:T(2,128)(2,1)S(1)}, bf16[1,2,2,4096]{3,2,1,0:T(2,128)(2,1)S(1)}, u32[]{:S(2)}, u32[]{:S(2)}) %collective-permute-start.3) | collective-permute-done | bytes 32800 | tf_op jit(solution)/shard_map/ppermute | solution.py:121
  22.6 1.6 %collective-permute-start.4 = (bf16[4,1,2,2,4096]{4,3,2,0,1:T(2,128)(2,1)S(1)}, bf16[4,1,2,2,4096]{4,3,2,0,1:T(2,128)(2,1)S(1)}, u32[]{:S(2)}, u32[]{:S(2)}) collective-permute-start(bf16[4,1,2,2,4096]{4,3,2,0,1:T(2,128)(2,1)S(1)} %bitcast_dynamic-update-slice_fusion.4), channel_id=1, source_target_pairs={{0,2},{2,0},{4,6},{6,4},{8,10},{10,8},{12,14},{14,12},{16,18},{18,... | collective-permute-start | bytes 393224 | tf_op jit(solution)/shard_map/ppermute | solution.py:121
  24.1 1.5 %collective-permute-start.5 = (bf16[4,1,2,2,4096]{4,3,2,0,1:T(2,128)(2,1)S(1)}, bf16[4,1,2,2,4096]{4,3,2,0,1:T(2,128)(2,1)S(1)}, u32[]{:S(2)}, u32[]{:S(2)}) collective-permute-start(bf16[4,1,2,2,4096]{4,3,2,0,1:T(2,128)(2,1)S(1)} %bitcast_dynamic-update-slice_fusion.4), channel_id=1, source_target_pairs={{0,4},{2,6},{4,0},{6,2},{8,12},{10,14},{12,8},{14,10},{16,20},{18,... | collective-permute-start | bytes 393224 | tf_op jit(solution)/shard_map/ppermute | solution.py:121
  25.6 0.5 collective-permute-start.6
  26.1 0.5 broadcast_in_dim.50
  26.6 0.1 bitcast_dynamic-update-slice_fusion.2
  26.7 2.2 %collective-permute-done.4 = bf16[4,1,2,2,4096]{4,3,2,0,1:T(2,128)(2,1)S(1)} collective-permute-done((bf16[4,1,2,2,4096]{4,3,2,0,1:T(2,128)(2,1)S(1)}, bf16[4,1,2,2,4096]{4,3,2,0,1:T(2,128)(2,1)S(1)}, u32[]{:S(2)}, u32[]{:S(2)}) %collective-permute-start.4) | collective-permute-done | bytes 131104 | tf_op jit(solution)/shard_map/ppermute | solution.py:121
  28.9 0.1 bitcast_dynamic-update-slice_fusion.1
  29.0 2.6 %collective-permute-done.5 = bf16[4,1,2,2,4096]{4,3,2,0,1:T(2,128)(2,1)S(1)} collective-permute-done((bf16[4,1,2,2,4096]{4,3,2,0,1:T(2,128)(2,1)S(1)}, bf16[4,1,2,2,4096]{4,3,2,0,1:T(2,128)(2,1)S(1)}, u32[]{:S(2)}, u32[]{:S(2)}) %collective-permute-start.5) | collective-permute-done | bytes 131104 | tf_op jit(solution)/shard_map/ppermute | solution.py:121
  31.6 0.1 bitcast_dynamic-update-slice_fusion
  31.8 0.1 bitcast_dynamic-update-slice_fusion.3
  31.9 1.0 %reshape.32.source_ref = bf16[16,4,4096]{2,1,0:T(4,128)(2,1)} reshape(bf16[1,4,4,2,2,4096]{5,4,3,2,1,0:T(2,128)(2,1)S(1)} %bitcast.52) | data formatting | bytes 1048576 | tf_op jit(solution)/shard_map/reshape | solution.py:146
  32.9 6.1 %shard_map.46 = bf16[16,64,256]{2,1,0:T(8,128)(2,1)} custom-call(bf16[16,16,4096]{2,1,0:T(8,128)(2,1)} %bitcast.48, bf16[16,4,4096]{2,1,0:T(4,128)(2,1)} %reshape.32.source_ref, bf16[2048,256]{1,0:T(8,128)(2,1)} %constant.42.clone.table_ref), custom_call_target="tpu_custom_call" | custom-call | flops 1107296256 | bytes 4194304 | tf_op jit(solution)/shard_map/pallas_call | solution.py:59
  39.0 3.6 %all-to-all-start = ((bf16[16,64,256]{2,1,0:T(8,128)(2,1)}), bf16[16,64,256]{2,1,0:T(8,128)(2,1)S(1)}, u32[]{:S(2)}, u32[]{:S(2)}) async-start(bf16[16,64,256]{2,1,0:T(8,128)(2,1)} %shard_map.46), calls=%async_computation | async-start | bytes 1048576 | tf_op jit(solution)/shard_map/all_to_all | solution.py:149
  42.6 13.7 %all-to-all-done = bf16[16,64,256]{2,1,0:T(8,128)(2,1)S(1)} async-done(((bf16[16,64,256]{2,1,0:T(8,128)(2,1)}), bf16[16,64,256]{2,1,0:T(8,128)(2,1)S(1)}, u32[]{:S(2)}, u32[]{:S(2)}) %all-to-all-start) | async-done | bytes 524320 | tf_op jit(solution)/shard_map/all_to_all | solution.py:149
  56.2 0.1 collective-permute-start.7
  56.3 1.5 %collective-permute-done.7 = bf16[8,64,256]{2,1,0:T(8,128)(2,1)S(1)} collective-permute-done((bf16[8,64,256]{2,1,0:T(8,128)(2,1)S(1)}, bf16[8,64,256]{2,1,0:T(8,128)(2,1)S(1)}, u32[]{:S(2)}, u32[]{:S(2)}) %collective-permute-start.7) | collective-permute-done | bytes 262176 | tf_op jit(solution)/shard_map/ppermute | solution.py:153
  57.9 0.8 %copy.23 = f32[2,4,8,8,256]{4,3,2,1,0:T(8,128)} copy(f32[2,4,8,8,256]{4,3,1,0,2:T(8,128)S(1)} %bitcast.51) | data formatting | bytes 1048576 | tf_op jit(solution)/shard_map/transpose | solution.py:156
  (17 shorter events, 0.3 us)
Async XLA Ops:
  0.0 9.1 %copy-start = (bf16[2,2,4096]{2,1,0:T(2,128)(2,1)S(1)}, bf16[2,2,4096]{2,1,0:T(2,128)(2,1)}, u32[]{:S(2)}) copy-start(bf16[2,2,4096]{2,1,0:T(2,128)(2,1)} %param.5) | copy-start | bytes 98308
  0.0 8.5 %copy-start.1 = (s32[64,1]{0,1:T(1,128)S(1)}, s32[64,1]{0,1:T(1,128)}, u32[]{:S(2)}) copy-start(s32[64,1]{0,1:T(1,128)} %param.6) | copy-start | bytes 772
  1.0 8.0 %collective-permute-start = (f32[2]{0:T(128)S(1)}, f32[2]{0:T(128)S(1)}, u32[]{:S(2)}, u32[]{:S(2)}) collective-permute-start(f32[2]{0:T(128)S(1)} %fusion.1), channel_id=1, source_target_pairs={{0,1},{1,0},{2,3},{3,2},{4,5},{5,4},{6,7},{7,6},{8,9},{9,8},{10,11... | collective-permute-start | bytes 32 | tf_op jit(solution)/shard_map/ppermute | solution.py:100
  9.2 7.6 %collective-permute-start.1 = (bf16[1,2,2,4096]{3,2,1,0:T(2,128)(2,1)S(1)}, bf16[1,2,2,4096]{3,2,1,0:T(2,128)(2,1)S(1)}, u32[]{:S(2)}, u32[]{:S(2)}) collective-permute-start(bf16[1,2,2,4096]{3,2,1,0:T(2,128)(2,1)S(1)} %bitcast.53), channel_id=1, source_target_pairs={{0,8},{2,10},{4,12},{6,14},{8,0},{10,2},{12,4},{14,6},{16,24},{18,... | collective-permute-start | bytes 98312 | tf_op jit(solution)/shard_map/ppermute | solution.py:121
  14.2 4.8 %collective-permute-start.2 = (bf16[1,2,2,4096]{3,2,1,0:T(2,128)(2,1)S(1)}, bf16[1,2,2,4096]{3,2,1,0:T(2,128)(2,1)S(1)}, u32[]{:S(2)}, u32[]{:S(2)}) collective-permute-start(bf16[1,2,2,4096]{3,2,1,0:T(2,128)(2,1)S(1)} %bitcast.54), channel_id=1, source_target_pairs={{0,16},{2,18},{4,20},{6,22},{8,24},{10,26},{12,28},{14,30},{16,0},... | collective-permute-start | bytes 98312 | tf_op jit(solution)/shard_map/ppermute | solution.py:121
  16.8 5.7 %collective-permute-start.3 = (bf16[1,2,2,4096]{3,2,1,0:T(2,128)(2,1)S(1)}, bf16[1,2,2,4096]{3,2,1,0:T(2,128)(2,1)S(1)}, u32[]{:S(2)}, u32[]{:S(2)}) collective-permute-start(bf16[1,2,2,4096]{3,2,1,0:T(2,128)(2,1)S(1)} %bitcast.55), channel_id=1, source_target_pairs={{0,24},{2,26},{4,28},{6,30},{8,16},{10,18},{12,20},{14,22},{16,8},... | collective-permute-start | bytes 98312 | tf_op jit(solution)/shard_map/ppermute | solution.py:121
  22.6 6.4 %collective-permute-start.4 = (bf16[4,1,2,2,4096]{4,3,2,0,1:T(2,128)(2,1)S(1)}, bf16[4,1,2,2,4096]{4,3,2,0,1:T(2,128)(2,1)S(1)}, u32[]{:S(2)}, u32[]{:S(2)}) collective-permute-start(bf16[4,1,2,2,4096]{4,3,2,0,1:T(2,128)(2,1)S(1)} %bitcast_dynamic-update-slice_fusion.4), channel_id=1, source_target_pairs={{0,2},{2,0},{4,6},{6,4},{8,10},{10,8},{12,14},{14,12},{16,18},{18,... | collective-permute-start | bytes 393224 | tf_op jit(solution)/shard_map/ppermute | solution.py:121
  24.1 7.5 %collective-permute-start.5 = (bf16[4,1,2,2,4096]{4,3,2,0,1:T(2,128)(2,1)S(1)}, bf16[4,1,2,2,4096]{4,3,2,0,1:T(2,128)(2,1)S(1)}, u32[]{:S(2)}, u32[]{:S(2)}) collective-permute-start(bf16[4,1,2,2,4096]{4,3,2,0,1:T(2,128)(2,1)S(1)} %bitcast_dynamic-update-slice_fusion.4), channel_id=1, source_target_pairs={{0,4},{2,6},{4,0},{6,2},{8,12},{10,14},{12,8},{14,10},{16,20},{18,... | collective-permute-start | bytes 393224 | tf_op jit(solution)/shard_map/ppermute | solution.py:121
  25.6 6.1 %collective-permute-start.6 = (bf16[4,1,2,2,4096]{4,3,2,0,1:T(2,128)(2,1)S(1)}, bf16[4,1,2,2,4096]{4,3,2,0,1:T(2,128)(2,1)S(1)}, u32[]{:S(2)}, u32[]{:S(2)}) collective-permute-start(bf16[4,1,2,2,4096]{4,3,2,0,1:T(2,128)(2,1)S(1)} %bitcast_dynamic-update-slice_fusion.4), channel_id=1, source_target_pairs={{0,6},{2,4},{4,2},{6,0},{8,14},{10,12},{12,10},{14,8},{16,22},{18,... | collective-permute-start | bytes 393224 | tf_op jit(solution)/shard_map/ppermute | solution.py:121
  39.0 17.2 %all-to-all-start = ((bf16[16,64,256]{2,1,0:T(8,128)(2,1)}), bf16[16,64,256]{2,1,0:T(8,128)(2,1)S(1)}, u32[]{:S(2)}, u32[]{:S(2)}) async-start(bf16[16,64,256]{2,1,0:T(8,128)(2,1)} %shard_map.46), calls=%async_computation | async-start | bytes 1048576 | tf_op jit(solution)/shard_map/all_to_all | solution.py:149
  56.2 1.6 %collective-permute-start.7 = (bf16[8,64,256]{2,1,0:T(8,128)(2,1)S(1)}, bf16[8,64,256]{2,1,0:T(8,128)(2,1)S(1)}, u32[]{:S(2)}, u32[]{:S(2)}) collective-permute-start(bf16[8,64,256]{2,1,0:T(8,128)(2,1)S(1)} %constant_dynamic-slice_fusion), channel_id=1, source_target_pairs={{0,1},{1,0},{2,3},{3,2},{4,5},{5,4},{6,7},{7,6},{8,9},{9,8},{10,11... | collective-permute-start | bytes 786440 | tf_op jit(solution)/shard_map/ppermute | solution.py:153

commit v23 on v18

--- a/solution.py
+++ b/solution.py
@@ -45,7 +45,7 @@
     product = jnp.dot(
         cross_ref[...].astype(jnp.bfloat16), table_ref[...], preferred_element_type=jnp.float32
     )
-    product = (product * norm_scale).astype(out_ref.dtype)
+    product = product.astype(out_ref.dtype)
     for member in range(group):
         out_ref[member] = product[member * rows : (member + 1) * rows]
 
@@ -80,7 +80,7 @@
     lag_value = (np.arange(lags_out, dtype=np.int64) - lags_out // 2) * DEC
     phase = np.mod(bin_index[:, None] * lag_value[None, :], BINS).astype(np.float32)
     phase = (phase * np.float32(2.0 * math.pi / BINS)).astype(np.float64)
-    table = np.concatenate([np.cos(phase), np.sin(phase)], axis=0)
+    table = np.concatenate([np.cos(phase), np.sin(phase)], axis=0) * BINS ** (-0.5)
     return table.astype(ml_dtypes.bfloat16)
 
 

time: 55.9 us -> 55.9 us (level)
  no operation moved by 1% of the time
where the time goes in v23:
time: 55.9 us; the launch traced here: 55.4 us
  waiting for transfers between devices  20.4 us (36%)
  starting transfers between devices  14.3 us (26%)
  Pallas kernels  6.1 us (11%)
  other arithmetic  5.13 us (9%)
  local copies, waits for them, and re-layouts  4.73 us (8%)
  blocking collectives  2.56 us (5%)
  matrix products  2.18 us (4%)
    all_to_all x1, waiting for transfers between devices, per_device(): lax.all_to_all(partial, 'blk', split_axis=0, concat_axis=0, tiled=True)  13.1 us
    ppermute x6, starting transfers between devices, per_device(): got = lax.ppermute(held, 'blk', route)  9.11 us
    pallas_call x1, Pallas kernels, correlate(): pl.pallas_call(body, grid=(blocks // group,), in_specs=[pl.BlockSpec(plac...  6.1 us
    ppermute x6, waiting for transfers between devices, per_device(): got = lax.ppermute(held, 'blk', route)  5.76 us
    all_to_all x1, starting transfers between devices, per_device(): lax.all_to_all(partial, 'blk', split_axis=0, concat_axis=0, tiled=True)  5.1 us
    reduce_sum x1, other arithmetic, per_device(): jnp.sum(trace_float * trace_float, axis=(1, 2))  2.82 us
    psum x1, blocking collectives, per_device(): lax.psum((jnp.sum(trace_float * trace_float, axis=(1, 2)), jnp.sum(source...  2.56 us
    dot_general x1, matrix products, per_device(): jnp.dot(chosen.astype(jnp.bfloat16), traces.reshape(station_count, 2 * gr...  2.18 us
  transfers between devices with their start and end apart: 8, of which 6 were waited for; matrix products, arithmetic and copies ran while one was open for 10% of the time, Pallas kernels for 0%

profile of v23, /device:TPU:0, one launch (start us, length us, event | category | flops | bytes accessed | tf_op | source)
XLA Modules:
  0.0 55.4 jit_solution(17490724873747465366)
XLA Ops:
  0.0 2.8 %multiply_reduce_fusion = f32[64]{0:T(128)S(1)} fusion(bf16[64,2,4096]{2,1,0:T(2,128)(2,1)} %param.4), kind=kLoop, calls=%fused_computation.2 | loop fusion | flops 1572800 | bytes 1048832 | tf_op jit(solution)/shard_map/reduce_sum | solution.py:102
  2.8 0.9 %fusion.1 = f32[2]{0:T(128)S(1)} fusion(bf16[2,2,4096]{2,1,0:T(2,128)(2,1)} %param.5), kind=kLoop, calls=%fused_computation.11 | loop fusion | flops 49150 | bytes 32776 | tf_op jit(solution)/shard_map/reduce_sum | solution.py:103
  3.7 2.6 %all-reduce = (f32[64]{0:T(128)S(1)}, f32[2]{0:T(128)S(1)}) all-reduce(f32[64]{0:T(128)S(1)} %multiply_reduce_fusion, f32[2]{0:T(128)S(1)} %fusion.1), channel_id=1, replica_groups=mesh['blk'=16,'band'=2] {'band'}, use_global_device_ids=true, to_apply=%region_3.0 | all-reduce | flops 66 | bytes 528 | tf_op jit(solution)/shard_map/psum | solution.py:100
  6.3 0.1 broadcast_in_dim.51
  6.4 0.9 %bitcast_dynamic-update-slice_fusion.7 = (bf16[4,1,2,2,4096]{4,3,2,0,1:T(2,128)(2,1)S(1)}, bf16[2,2,4096]{2,1,0:T(2,128)(2,1)S(1)}) fusion(bf16[4,1,2,2,4096]{4,3,2,0,1:T(2,128)(2,1)S(1)} %broadcast_in_dim.51, s32[]{:T(128)S(6)} %select_n.35, f32[2]{0:T(128)S(1)} %add_rsqrt_fusion, bf16[2,2,4096]{2,1,0:T(2,128)(2,1)} %param.5), kind=kLoop, calls=%fused_computation.16 | loop fusion | flops 49152 | bytes 98820 | tf_op jit(solution)/shard_map/dynamic_update_slice | solution.py:126
  7.2 3.0 %collective-permute-start = (bf16[1,2,2,4096]{3,2,1,0:T(2,128)(2,1)S(1)}, bf16[1,2,2,4096]{3,2,1,0:T(2,128)(2,1)S(1)}, u32[]{:S(2)}, u32[]{:S(2)}) collective-permute-start(bf16[1,2,2,4096]{3,2,1,0:T(2,128)(2,1)S(1)} %bitcast.53), channel_id=1, source_target_pairs={{0,8},{2,10},{4,12},{6,14},{8,0},{10,2},{12,4},{14,6},{16,24},{18,... | collective-permute-start | bytes 98312 | tf_op jit(solution)/shard_map/ppermute | solution.py:125
  10.2 2.6 %collective-permute-start.1 = (bf16[1,2,2,4096]{3,2,1,0:T(2,128)(2,1)S(1)}, bf16[1,2,2,4096]{3,2,1,0:T(2,128)(2,1)S(1)}, u32[]{:S(2)}, u32[]{:S(2)}) collective-permute-start(bf16[1,2,2,4096]{3,2,1,0:T(2,128)(2,1)S(1)} %bitcast.54), channel_id=1, source_target_pairs={{0,16},{2,18},{4,20},{6,22},{8,24},{10,26},{12,28},{14,30},{16,0},... | collective-permute-start | bytes 98312 | tf_op jit(solution)/shard_map/ppermute | solution.py:125
  12.8 1.8 %copy.21 = bf16[8,8,2,4096]{3,1,2,0:T(8,128)(2,1)S(1)} copy(bf16[8,8,2,4096]{3,2,1,0:T(2,128)(2,1)} %bitcast.49) | data formatting | bytes 2097152
  14.6 0.1 fusion.3
  14.7 0.1 reduce_window_sum.11
  14.8 0.2 select_reduce_fusion.1
  15.0 0.1 select_reduce_fusion
  15.1 2.2 %fusion = bf16[128,8192]{1,0:T(8,128)(2,1)} fusion(bf16[64,8192]{1,0:T(8,128)(2,1)S(1)} %bitcast.50, f32[128]{0:T(128)S(1)} %select_reduce_fusion, s32[64]{0:T(128)S(1)} %multiply_add_fusion), kind=kOutput, calls=%fused_computation.1 | convolution fusion | flops 136323072 | bytes 3146496 | tf_op jit(solution)/shard_map/dot_general | solution.py:138
  17.4 1.1 %collective-permute-done.2 = bf16[1,2,2,4096]{3,2,1,0:T(2,128)(2,1)S(1)} collective-permute-done((bf16[1,2,2,4096]{3,2,1,0:T(2,128)(2,1)S(1)}, bf16[1,2,2,4096]{3,2,1,0:T(2,128)(2,1)S(1)}, u32[]{:S(2)}, u32[]{:S(2)}) %collective-permute-start.2) | collective-permute-done | bytes 32800 | tf_op jit(solution)/shard_map/ppermute | solution.py:125
  18.6 1.6 %collective-permute-start.3 = (bf16[4,1,2,2,4096]{4,3,2,0,1:T(2,128)(2,1)S(1)}, bf16[4,1,2,2,4096]{4,3,2,0,1:T(2,128)(2,1)S(1)}, u32[]{:S(2)}, u32[]{:S(2)}) collective-permute-start(bf16[4,1,2,2,4096]{4,3,2,0,1:T(2,128)(2,1)S(1)} %bitcast_dynamic-update-slice_fusion.4), channel_id=1, source_target_pairs={{0,2},{2,0},{4,6},{6,4},{8,10},{10,8},{12,14},{14,12},{16,18},{18,... | collective-permute-start | bytes 393224 | tf_op jit(solution)/shard_map/ppermute | solution.py:125
  20.1 1.5 %collective-permute-start.4 = (bf16[4,1,2,2,4096]{4,3,2,0,1:T(2,128)(2,1)S(1)}, bf16[4,1,2,2,4096]{4,3,2,0,1:T(2,128)(2,1)S(1)}, u32[]{:S(2)}, u32[]{:S(2)}) collective-permute-start(bf16[4,1,2,2,4096]{4,3,2,0,1:T(2,128)(2,1)S(1)} %bitcast_dynamic-update-slice_fusion.4), channel_id=1, source_target_pairs={{0,4},{2,6},{4,0},{6,2},{8,12},{10,14},{12,8},{14,10},{16,20},{18,... | collective-permute-start | bytes 393224 | tf_op jit(solution)/shard_map/ppermute | solution.py:125
  21.6 0.5 collective-permute-start.5
  22.1 0.5 broadcast_in_dim.50
  22.6 0.1 bitcast_dynamic-update-slice_fusion.2
  22.7 2.2 %collective-permute-done.3 = bf16[4,1,2,2,4096]{4,3,2,0,1:T(2,128)(2,1)S(1)} collective-permute-done((bf16[4,1,2,2,4096]{4,3,2,0,1:T(2,128)(2,1)S(1)}, bf16[4,1,2,2,4096]{4,3,2,0,1:T(2,128)(2,1)S(1)}, u32[]{:S(2)}, u32[]{:S(2)}) %collective-permute-start.3) | collective-permute-done | bytes 131104 | tf_op jit(solution)/shard_map/ppermute | solution.py:125
  24.9 0.1 bitcast_dynamic-update-slice_fusion.1
  25.0 1.1 %collective-permute-done.4 = bf16[4,1,2,2,4096]{4,3,2,0,1:T(2,128)(2,1)S(1)} collective-permute-done((bf16[4,1,2,2,4096]{4,3,2,0,1:T(2,128)(2,1)S(1)}, bf16[4,1,2,2,4096]{4,3,2,0,1:T(2,128)(2,1)S(1)}, u32[]{:S(2)}, u32[]{:S(2)}) %collective-permute-start.4) | collective-permute-done | bytes 131104 | tf_op jit(solution)/shard_map/ppermute | solution.py:125
  26.1 0.1 bitcast_dynamic-update-slice_fusion
  26.2 1.3 %collective-permute-done.5 = bf16[4,1,2,2,4096]{4,3,2,0,1:T(2,128)(2,1)S(1)} collective-permute-done((bf16[4,1,2,2,4096]{4,3,2,0,1:T(2,128)(2,1)S(1)}, bf16[4,1,2,2,4096]{4,3,2,0,1:T(2,128)(2,1)S(1)}, u32[]{:S(2)}, u32[]{:S(2)}) %collective-permute-start.5) | collective-permute-done | bytes 131104 | tf_op jit(solution)/shard_map/ppermute | solution.py:125
  27.5 0.1 bitcast_dynamic-update-slice_fusion.3
  27.6 1.0 %reshape.32.source_ref = bf16[16,4,4096]{2,1,0:T(4,128)(2,1)} reshape(bf16[1,4,4,2,2,4096]{5,4,3,2,1,0:T(2,128)(2,1)S(1)} %bitcast.52) | data formatting | bytes 1048576 | tf_op jit(solution)/shard_map/reshape | solution.py:150
  28.6 6.1 %shard_map.46 = bf16[16,64,256]{2,1,0:T(8,128)(2,1)} custom-call(bf16[16,16,4096]{2,1,0:T(8,128)(2,1)} %bitcast.48, bf16[16,4,4096]{2,1,0:T(4,128)(2,1)} %reshape.32.source_ref, bf16[2048,256]{1,0:T(8,128)(2,1)} %constant.42.clone.table_ref), custom_call_target="tpu_custom_call" | custom-call | flops 1107296256 | bytes 4194304 | tf_op jit(solution)/shard_map/pallas_call | solution.py:59
  34.7 5.1 %all-to-all-start = ((bf16[16,64,256]{2,1,0:T(8,128)(2,1)}), bf16[16,64,256]{2,1,0:T(8,128)(2,1)S(1)}, u32[]{:S(2)}, u32[]{:S(2)}) async-start(bf16[16,64,256]{2,1,0:T(8,128)(2,1)} %shard_map.46), calls=%async_computation | async-start | bytes 1048576 | tf_op jit(solution)/shard_map/all_to_all | solution.py:153
  39.8 13.1 %all-to-all-done = bf16[16,64,256]{2,1,0:T(8,128)(2,1)S(1)} async-done(((bf16[16,64,256]{2,1,0:T(8,128)(2,1)}), bf16[16,64,256]{2,1,0:T(8,128)(2,1)S(1)}, u32[]{:S(2)}, u32[]{:S(2)}) %all-to-all-start) | async-done | bytes 524320 | tf_op jit(solution)/shard_map/all_to_all | solution.py:153
  52.9 0.1 collective-permute-start.6
  53.0 1.5 %collective-permute-done.6 = bf16[8,64,256]{2,1,0:T(8,128)(2,1)S(1)} collective-permute-done((bf16[8,64,256]{2,1,0:T(8,128)(2,1)S(1)}, bf16[8,64,256]{2,1,0:T(8,128)(2,1)S(1)}, u32[]{:S(2)}, u32[]{:S(2)}) %collective-permute-start.6) | collective-permute-done | bytes 262176 | tf_op jit(solution)/shard_map/ppermute | solution.py:157
  54.6 0.8 %copy.23 = f32[2,4,8,8,256]{4,3,2,1,0:T(8,128)} copy(f32[2,4,8,8,256]{4,3,1,0,2:T(8,128)S(1)} %bitcast.51) | data formatting | bytes 1048576 | tf_op jit(solution)/shard_map/transpose | solution.py:160
  (13 shorter events, 0.2 us)
Async XLA Ops:
  0.0 14.6 %copy-start = (s32[64,1]{0,1:T(1,128)S(1)}, s32[64,1]{0,1:T(1,128)}, u32[]{:S(2)}) copy-start(s32[64,1]{0,1:T(1,128)} %param.6) | copy-start | bytes 772
  7.2 10.0 %collective-permute-start = (bf16[1,2,2,4096]{3,2,1,0:T(2,128)(2,1)S(1)}, bf16[1,2,2,4096]{3,2,1,0:T(2,128)(2,1)S(1)}, u32[]{:S(2)}, u32[]{:S(2)}) collective-permute-start(bf16[1,2,2,4096]{3,2,1,0:T(2,128)(2,1)S(1)} %bitcast.53), channel_id=1, source_target_pairs={{0,8},{2,10},{4,12},{6,14},{8,0},{10,2},{12,4},{14,6},{16,24},{18,... | collective-permute-start | bytes 98312 | tf_op jit(solution)/shard_map/ppermute | solution.py:125
  10.2 7.1 %collective-permute-start.1 = (bf16[1,2,2,4096]{3,2,1,0:T(2,128)(2,1)S(1)}, bf16[1,2,2,4096]{3,2,1,0:T(2,128)(2,1)S(1)}, u32[]{:S(2)}, u32[]{:S(2)}) collective-permute-start(bf16[1,2,2,4096]{3,2,1,0:T(2,128)(2,1)S(1)} %bitcast.54), channel_id=1, source_target_pairs={{0,16},{2,18},{4,20},{6,22},{8,24},{10,26},{12,28},{14,30},{16,0},... | collective-permute-start | bytes 98312 | tf_op jit(solution)/shard_map/ppermute | solution.py:125
  12.8 5.7 %collective-permute-start.2 = (bf16[1,2,2,4096]{3,2,1,0:T(2,128)(2,1)S(1)}, bf16[1,2,2,4096]{3,2,1,0:T(2,128)(2,1)S(1)}, u32[]{:S(2)}, u32[]{:S(2)}) collective-permute-start(bf16[1,2,2,4096]{3,2,1,0:T(2,128)(2,1)S(1)} %bitcast.55), channel_id=1, source_target_pairs={{0,24},{2,26},{4,28},{6,30},{8,16},{10,18},{12,20},{14,22},{16,8},... | collective-permute-start | bytes 98312 | tf_op jit(solution)/shard_map/ppermute | solution.py:125
  18.6 6.3 %collective-permute-start.3 = (bf16[4,1,2,2,4096]{4,3,2,0,1:T(2,128)(2,1)S(1)}, bf16[4,1,2,2,4096]{4,3,2,0,1:T(2,128)(2,1)S(1)}, u32[]{:S(2)}, u32[]{:S(2)}) collective-permute-start(bf16[4,1,2,2,4096]{4,3,2,0,1:T(2,128)(2,1)S(1)} %bitcast_dynamic-update-slice_fusion.4), channel_id=1, source_target_pairs={{0,2},{2,0},{4,6},{6,4},{8,10},{10,8},{12,14},{14,12},{16,18},{18,... | collective-permute-start | bytes 393224 | tf_op jit(solution)/shard_map/ppermute | solution.py:125
  20.1 6.0 %collective-permute-start.4 = (bf16[4,1,2,2,4096]{4,3,2,0,1:T(2,128)(2,1)S(1)}, bf16[4,1,2,2,4096]{4,3,2,0,1:T(2,128)(2,1)S(1)}, u32[]{:S(2)}, u32[]{:S(2)}) collective-permute-start(bf16[4,1,2,2,4096]{4,3,2,0,1:T(2,128)(2,1)S(1)} %bitcast_dynamic-update-slice_fusion.4), channel_id=1, source_target_pairs={{0,4},{2,6},{4,0},{6,2},{8,12},{10,14},{12,8},{14,10},{16,20},{18,... | collective-permute-start | bytes 393224 | tf_op jit(solution)/shard_map/ppermute | solution.py:125
  21.6 5.9 %collective-permute-start.5 = (bf16[4,1,2,2,4096]{4,3,2,0,1:T(2,128)(2,1)S(1)}, bf16[4,1,2,2,4096]{4,3,2,0,1:T(2,128)(2,1)S(1)}, u32[]{:S(2)}, u32[]{:S(2)}) collective-permute-start(bf16[4,1,2,2,4096]{4,3,2,0,1:T(2,128)(2,1)S(1)} %bitcast_dynamic-update-slice_fusion.4), channel_id=1, source_target_pairs={{0,6},{2,4},{4,2},{6,0},{8,14},{10,12},{12,10},{14,8},{16,22},{18,... | collective-permute-start | bytes 393224 | tf_op jit(solution)/shard_map/ppermute | solution.py:125
  34.7 18.2 %all-to-all-start = ((bf16[16,64,256]{2,1,0:T(8,128)(2,1)}), bf16[16,64,256]{2,1,0:T(8,128)(2,1)S(1)}, u32[]{:S(2)}, u32[]{:S(2)}) async-start(bf16[16,64,256]{2,1,0:T(8,128)(2,1)} %shard_map.46), calls=%async_computation | async-start | bytes 1048576 | tf_op jit(solution)/shard_map/all_to_all | solution.py:153
  52.9 1.6 %collective-permute-start.6 = (bf16[8,64,256]{2,1,0:T(8,128)(2,1)S(1)}, bf16[8,64,256]{2,1,0:T(8,128)(2,1)S(1)}, u32[]{:S(2)}, u32[]{:S(2)}) collective-permute-start(bf16[8,64,256]{2,1,0:T(8,128)(2,1)S(1)} %constant_dynamic-slice_fusion), channel_id=1, source_target_pairs={{0,1},{1,0},{2,3},{3,2},{4,5},{5,4},{6,7},{7,6},{8,9},{9,8},{10,11... | collective-permute-start | bytes 786440 | tf_op jit(solution)/shard_map/ppermute | solution.py:157

commit v24 on v18

--- a/solution.py
+++ b/solution.py
@@ -40,10 +40,10 @@
                     even_fold = even_fold + even[:, fold * PERIOD : (fold + 1) * PERIOD]
                     odd_fold = odd_fold + odd[:, fold * PERIOD : (fold + 1) * PERIOD]
                 row = member * rows + (source * offsets + offset) * capacity
-                cross_ref[row : row + capacity, :PERIOD] = even_fold.astype(jnp.float32)
-                cross_ref[row : row + capacity, PERIOD:] = odd_fold.astype(jnp.float32)
+                cross_ref[row : row + capacity, :PERIOD] = even_fold
+                cross_ref[row : row + capacity, PERIOD:] = odd_fold
     product = jnp.dot(
-        cross_ref[...].astype(jnp.bfloat16), table_ref[...], preferred_element_type=jnp.float32
+        cross_ref[...], table_ref[...], preferred_element_type=jnp.float32
     )
     product = (product * norm_scale).astype(out_ref.dtype)
     for member in range(group):
@@ -66,7 +66,7 @@
         ],
         out_specs=pl.BlockSpec((group, rows, lags_out), lambda a: (a, 0, 0)),
         out_shape=jax.ShapeDtypeStruct((blocks, rows, lags_out), jnp.bfloat16),
-        scratch_shapes=[pltpu.VMEM((group * rows, 2 * PERIOD), jnp.float32)],
+        scratch_shapes=[pltpu.VMEM((group * rows, 2 * PERIOD), jnp.bfloat16)],
         cost_estimate=pl.CostEstimate(
             flops=blocks * rows * 2 * PERIOD * lags_out * 2 + blocks * offsets * 16 * capacity * group_bins,
             bytes_accessed=placed.size * 2 + white_sources.size * 2 + table.size * 2 + blocks * rows * lags_out * 2,

time: 55.9 us -> 55.9 us (level)
  no operation moved by 1% of the time
where the time goes in v24:
time: 55.9 us; the launch traced here: 55.5 us
  waiting for transfers between devices  20.4 us (36%)
  starting transfers between devices  14.3 us (26%)
  Pallas kernels  6.11 us (11%)
  other arithmetic  5.13 us (9%)
  local copies, waits for them, and re-layouts  4.73 us (8%)
  blocking collectives  2.56 us (5%)
  matrix products  2.18 us (4%)
    all_to_all x1, waiting for transfers between devices, per_device(): lax.all_to_all(partial, 'blk', split_axis=0, concat_axis=0, tiled=True)  13.1 us
    ppermute x6, starting transfers between devices, per_device(): got = lax.ppermute(held, 'blk', route)  9.11 us
    pallas_call x1, Pallas kernels, correlate(): pl.pallas_call(body, grid=(blocks // group,), in_specs=[pl.BlockSpec(plac...  6.11 us
    ppermute x6, waiting for transfers between devices, per_device(): got = lax.ppermute(held, 'blk', route)  5.76 us
    all_to_all x1, starting transfers between devices, per_device(): lax.all_to_all(partial, 'blk', split_axis=0, concat_axis=0, tiled=True)  5.1 us
    reduce_sum x1, other arithmetic, per_device(): jnp.sum(trace_float * trace_float, axis=(1, 2))  2.82 us
    psum x1, blocking collectives, per_device(): lax.psum((jnp.sum(trace_float * trace_float, axis=(1, 2)), jnp.sum(source...  2.56 us
    dot_general x1, matrix products, per_device(): jnp.dot(chosen.astype(jnp.bfloat16), traces.reshape(station_count, 2 * gr...  2.18 us
  transfers between devices with their start and end apart: 8, of which 6 were waited for; matrix products, arithmetic and copies ran while one was open for 10% of the time, Pallas kernels for 0%

profile of v24, /device:TPU:0, one launch (start us, length us, event | category | flops | bytes accessed | tf_op | source)
XLA Modules:
  0.0 55.5 jit_solution(2639720969234603746)
XLA Ops:
  0.0 2.8 %multiply_reduce_fusion = f32[64]{0:T(128)S(1)} fusion(bf16[64,2,4096]{2,1,0:T(2,128)(2,1)} %param.4), kind=kLoop, calls=%fused_computation.2 | loop fusion | flops 1572800 | bytes 1048832 | tf_op jit(solution)/shard_map/reduce_sum | solution.py:102
  2.8 0.9 %fusion.1 = f32[2]{0:T(128)S(1)} fusion(bf16[2,2,4096]{2,1,0:T(2,128)(2,1)} %param.5), kind=kLoop, calls=%fused_computation.11 | loop fusion | flops 49150 | bytes 32776 | tf_op jit(solution)/shard_map/reduce_sum | solution.py:103
  3.7 2.6 %all-reduce = (f32[64]{0:T(128)S(1)}, f32[2]{0:T(128)S(1)}) all-reduce(f32[64]{0:T(128)S(1)} %multiply_reduce_fusion, f32[2]{0:T(128)S(1)} %fusion.1), channel_id=1, replica_groups=mesh['blk'=16,'band'=2] {'band'}, use_global_device_ids=true, to_apply=%region_3.0 | all-reduce | flops 66 | bytes 528 | tf_op jit(solution)/shard_map/psum | solution.py:100
  6.3 0.1 broadcast_in_dim.51
  6.4 0.9 %bitcast_dynamic-update-slice_fusion.7 = (bf16[4,1,2,2,4096]{4,3,2,0,1:T(2,128)(2,1)S(1)}, bf16[2,2,4096]{2,1,0:T(2,128)(2,1)S(1)}) fusion(bf16[4,1,2,2,4096]{4,3,2,0,1:T(2,128)(2,1)S(1)} %broadcast_in_dim.51, s32[]{:T(128)S(6)} %select_n.35, f32[2]{0:T(128)S(1)} %add_rsqrt_fusion, bf16[2,2,4096]{2,1,0:T(2,128)(2,1)} %param.5), kind=kLoop, calls=%fused_computation.16 | loop fusion | flops 49152 | bytes 98820 | tf_op jit(solution)/shard_map/dynamic_update_slice | solution.py:126
  7.2 3.0 %collective-permute-start = (bf16[1,2,2,4096]{3,2,1,0:T(2,128)(2,1)S(1)}, bf16[1,2,2,4096]{3,2,1,0:T(2,128)(2,1)S(1)}, u32[]{:S(2)}, u32[]{:S(2)}) collective-permute-start(bf16[1,2,2,4096]{3,2,1,0:T(2,128)(2,1)S(1)} %bitcast.53), channel_id=1, source_target_pairs={{0,8},{2,10},{4,12},{6,14},{8,0},{10,2},{12,4},{14,6},{16,24},{18,... | collective-permute-start | bytes 98312 | tf_op jit(solution)/shard_map/ppermute | solution.py:125
  10.2 2.6 %collective-permute-start.1 = (bf16[1,2,2,4096]{3,2,1,0:T(2,128)(2,1)S(1)}, bf16[1,2,2,4096]{3,2,1,0:T(2,128)(2,1)S(1)}, u32[]{:S(2)}, u32[]{:S(2)}) collective-permute-start(bf16[1,2,2,4096]{3,2,1,0:T(2,128)(2,1)S(1)} %bitcast.54), channel_id=1, source_target_pairs={{0,16},{2,18},{4,20},{6,22},{8,24},{10,26},{12,28},{14,30},{16,0},... | collective-permute-start | bytes 98312 | tf_op jit(solution)/shard_map/ppermute | solution.py:125
  12.8 1.8 %copy.21 = bf16[8,8,2,4096]{3,1,2,0:T(8,128)(2,1)S(1)} copy(bf16[8,8,2,4096]{3,2,1,0:T(2,128)(2,1)} %bitcast.49) | data formatting | bytes 2097152
  14.6 0.1 fusion.3
  14.7 0.1 reduce_window_sum.11
  14.8 0.2 select_reduce_fusion.1
  15.0 0.1 select_reduce_fusion
  15.1 2.2 %fusion = bf16[128,8192]{1,0:T(8,128)(2,1)} fusion(bf16[64,8192]{1,0:T(8,128)(2,1)S(1)} %bitcast.50, f32[128]{0:T(128)S(1)} %select_reduce_fusion, s32[64]{0:T(128)S(1)} %multiply_add_fusion), kind=kOutput, calls=%fused_computation.1 | convolution fusion | flops 136323072 | bytes 3146496 | tf_op jit(solution)/shard_map/dot_general | solution.py:138
  17.4 1.1 %collective-permute-done.2 = bf16[1,2,2,4096]{3,2,1,0:T(2,128)(2,1)S(1)} collective-permute-done((bf16[1,2,2,4096]{3,2,1,0:T(2,128)(2,1)S(1)}, bf16[1,2,2,4096]{3,2,1,0:T(2,128)(2,1)S(1)}, u32[]{:S(2)}, u32[]{:S(2)}) %collective-permute-start.2) | collective-permute-done | bytes 32800 | tf_op jit(solution)/shard_map/ppermute | solution.py:125
  18.6 1.6 %collective-permute-start.3 = (bf16[4,1,2,2,4096]{4,3,2,0,1:T(2,128)(2,1)S(1)}, bf16[4,1,2,2,4096]{4,3,2,0,1:T(2,128)(2,1)S(1)}, u32[]{:S(2)}, u32[]{:S(2)}) collective-permute-start(bf16[4,1,2,2,4096]{4,3,2,0,1:T(2,128)(2,1)S(1)} %bitcast_dynamic-update-slice_fusion.4), channel_id=1, source_target_pairs={{0,2},{2,0},{4,6},{6,4},{8,10},{10,8},{12,14},{14,12},{16,18},{18,... | collective-permute-start | bytes 393224 | tf_op jit(solution)/shard_map/ppermute | solution.py:125
  20.1 1.5 %collective-permute-start.4 = (bf16[4,1,2,2,4096]{4,3,2,0,1:T(2,128)(2,1)S(1)}, bf16[4,1,2,2,4096]{4,3,2,0,1:T(2,128)(2,1)S(1)}, u32[]{:S(2)}, u32[]{:S(2)}) collective-permute-start(bf16[4,1,2,2,4096]{4,3,2,0,1:T(2,128)(2,1)S(1)} %bitcast_dynamic-update-slice_fusion.4), channel_id=1, source_target_pairs={{0,4},{2,6},{4,0},{6,2},{8,12},{10,14},{12,8},{14,10},{16,20},{18,... | collective-permute-start | bytes 393224 | tf_op jit(solution)/shard_map/ppermute | solution.py:125
  21.6 0.5 collective-permute-start.5
  22.1 0.5 broadcast_in_dim.50
  22.6 0.1 bitcast_dynamic-update-slice_fusion.2
  22.7 2.2 %collective-permute-done.3 = bf16[4,1,2,2,4096]{4,3,2,0,1:T(2,128)(2,1)S(1)} collective-permute-done((bf16[4,1,2,2,4096]{4,3,2,0,1:T(2,128)(2,1)S(1)}, bf16[4,1,2,2,4096]{4,3,2,0,1:T(2,128)(2,1)S(1)}, u32[]{:S(2)}, u32[]{:S(2)}) %collective-permute-start.3) | collective-permute-done | bytes 131104 | tf_op jit(solution)/shard_map/ppermute | solution.py:125
  24.9 0.1 bitcast_dynamic-update-slice_fusion.1
  25.0 1.1 %collective-permute-done.4 = bf16[4,1,2,2,4096]{4,3,2,0,1:T(2,128)(2,1)S(1)} collective-permute-done((bf16[4,1,2,2,4096]{4,3,2,0,1:T(2,128)(2,1)S(1)}, bf16[4,1,2,2,4096]{4,3,2,0,1:T(2,128)(2,1)S(1)}, u32[]{:S(2)}, u32[]{:S(2)}) %collective-permute-start.4) | collective-permute-done | bytes 131104 | tf_op jit(solution)/shard_map/ppermute | solution.py:125
  26.1 0.1 bitcast_dynamic-update-slice_fusion
  26.2 1.3 %collective-permute-done.5 = bf16[4,1,2,2,4096]{4,3,2,0,1:T(2,128)(2,1)S(1)} collective-permute-done((bf16[4,1,2,2,4096]{4,3,2,0,1:T(2,128)(2,1)S(1)}, bf16[4,1,2,2,4096]{4,3,2,0,1:T(2,128)(2,1)S(1)}, u32[]{:S(2)}, u32[]{:S(2)}) %collective-permute-start.5) | collective-permute-done | bytes 131104 | tf_op jit(solution)/shard_map/ppermute | solution.py:125
  27.5 0.1 bitcast_dynamic-update-slice_fusion.3
  27.6 1.0 %reshape.32.source_ref = bf16[16,4,4096]{2,1,0:T(4,128)(2,1)} reshape(bf16[1,4,4,2,2,4096]{5,4,3,2,1,0:T(2,128)(2,1)S(1)} %bitcast.52) | data formatting | bytes 1048576 | tf_op jit(solution)/shard_map/reshape | solution.py:150
  28.6 6.1 %shard_map.46 = bf16[16,64,256]{2,1,0:T(8,128)(2,1)} custom-call(bf16[16,16,4096]{2,1,0:T(8,128)(2,1)} %bitcast.48, bf16[16,4,4096]{2,1,0:T(4,128)(2,1)} %reshape.32.source_ref, bf16[2048,256]{1,0:T(8,128)(2,1)} %constant.42.clone.table_ref), custom_call_target="tpu_custom_call" | custom-call | flops 1107296256 | bytes 4194304 | tf_op jit(solution)/shard_map/pallas_call | solution.py:59
  34.7 5.1 %all-to-all-start = ((bf16[16,64,256]{2,1,0:T(8,128)(2,1)}), bf16[16,64,256]{2,1,0:T(8,128)(2,1)S(1)}, u32[]{:S(2)}, u32[]{:S(2)}) async-start(bf16[16,64,256]{2,1,0:T(8,128)(2,1)} %shard_map.46), calls=%async_computation | async-start | bytes 1048576 | tf_op jit(solution)/shard_map/all_to_all | solution.py:153
  39.9 13.1 %all-to-all-done = bf16[16,64,256]{2,1,0:T(8,128)(2,1)S(1)} async-done(((bf16[16,64,256]{2,1,0:T(8,128)(2,1)}), bf16[16,64,256]{2,1,0:T(8,128)(2,1)S(1)}, u32[]{:S(2)}, u32[]{:S(2)}) %all-to-all-start) | async-done | bytes 524320 | tf_op jit(solution)/shard_map/all_to_all | solution.py:153
  52.9 0.1 collective-permute-start.6
  53.0 1.5 %collective-permute-done.6 = bf16[8,64,256]{2,1,0:T(8,128)(2,1)S(1)} collective-permute-done((bf16[8,64,256]{2,1,0:T(8,128)(2,1)S(1)}, bf16[8,64,256]{2,1,0:T(8,128)(2,1)S(1)}, u32[]{:S(2)}, u32[]{:S(2)}) %collective-permute-start.6) | collective-permute-done | bytes 262176 | tf_op jit(solution)/shard_map/ppermute | solution.py:157
  54.6 0.8 %copy.23 = f32[2,4,8,8,256]{4,3,2,1,0:T(8,128)} copy(f32[2,4,8,8,256]{4,3,1,0,2:T(8,128)S(1)} %bitcast.51) | data formatting | bytes 1048576 | tf_op jit(solution)/shard_map/transpose | solution.py:160
  (13 shorter events, 0.2 us)
Async XLA Ops:
  0.0 14.6 %copy-start = (s32[64,1]{0,1:T(1,128)S(1)}, s32[64,1]{0,1:T(1,128)}, u32[]{:S(2)}) copy-start(s32[64,1]{0,1:T(1,128)} %param.6) | copy-start | bytes 772
  7.2 10.0 %collective-permute-start = (bf16[1,2,2,4096]{3,2,1,0:T(2,128)(2,1)S(1)}, bf16[1,2,2,4096]{3,2,1,0:T(2,128)(2,1)S(1)}, u32[]{:S(2)}, u32[]{:S(2)}) collective-permute-start(bf16[1,2,2,4096]{3,2,1,0:T(2,128)(2,1)S(1)} %bitcast.53), channel_id=1, source_target_pairs={{0,8},{2,10},{4,12},{6,14},{8,0},{10,2},{12,4},{14,6},{16,24},{18,... | collective-permute-start | bytes 98312 | tf_op jit(solution)/shard_map/ppermute | solution.py:125
  10.2 7.1 %collective-permute-start.1 = (bf16[1,2,2,4096]{3,2,1,0:T(2,128)(2,1)S(1)}, bf16[1,2,2,4096]{3,2,1,0:T(2,128)(2,1)S(1)}, u32[]{:S(2)}, u32[]{:S(2)}) collective-permute-start(bf16[1,2,2,4096]{3,2,1,0:T(2,128)(2,1)S(1)} %bitcast.54), channel_id=1, source_target_pairs={{0,16},{2,18},{4,20},{6,22},{8,24},{10,26},{12,28},{14,30},{16,0},... | collective-permute-start | bytes 98312 | tf_op jit(solution)/shard_map/ppermute | solution.py:125
  12.8 5.7 %collective-permute-start.2 = (bf16[1,2,2,4096]{3,2,1,0:T(2,128)(2,1)S(1)}, bf16[1,2,2,4096]{3,2,1,0:T(2,128)(2,1)S(1)}, u32[]{:S(2)}, u32[]{:S(2)}) collective-permute-start(bf16[1,2,2,4096]{3,2,1,0:T(2,128)(2,1)S(1)} %bitcast.55), channel_id=1, source_target_pairs={{0,24},{2,26},{4,28},{6,30},{8,16},{10,18},{12,20},{14,22},{16,8},... | collective-permute-start | bytes 98312 | tf_op jit(solution)/shard_map/ppermute | solution.py:125
  18.6 6.3 %collective-permute-start.3 = (bf16[4,1,2,2,4096]{4,3,2,0,1:T(2,128)(2,1)S(1)}, bf16[4,1,2,2,4096]{4,3,2,0,1:T(2,128)(2,1)S(1)}, u32[]{:S(2)}, u32[]{:S(2)}) collective-permute-start(bf16[4,1,2,2,4096]{4,3,2,0,1:T(2,128)(2,1)S(1)} %bitcast_dynamic-update-slice_fusion.4), channel_id=1, source_target_pairs={{0,2},{2,0},{4,6},{6,4},{8,10},{10,8},{12,14},{14,12},{16,18},{18,... | collective-permute-start | bytes 393224 | tf_op jit(solution)/shard_map/ppermute | solution.py:125
  20.1 6.0 %collective-permute-start.4 = (bf16[4,1,2,2,4096]{4,3,2,0,1:T(2,128)(2,1)S(1)}, bf16[4,1,2,2,4096]{4,3,2,0,1:T(2,128)(2,1)S(1)}, u32[]{:S(2)}, u32[]{:S(2)}) collective-permute-start(bf16[4,1,2,2,4096]{4,3,2,0,1:T(2,128)(2,1)S(1)} %bitcast_dynamic-update-slice_fusion.4), channel_id=1, source_target_pairs={{0,4},{2,6},{4,0},{6,2},{8,12},{10,14},{12,8},{14,10},{16,20},{18,... | collective-permute-start | bytes 393224 | tf_op jit(solution)/shard_map/ppermute | solution.py:125
  21.6 5.9 %collective-permute-start.5 = (bf16[4,1,2,2,4096]{4,3,2,0,1:T(2,128)(2,1)S(1)}, bf16[4,1,2,2,4096]{4,3,2,0,1:T(2,128)(2,1)S(1)}, u32[]{:S(2)}, u32[]{:S(2)}) collective-permute-start(bf16[4,1,2,2,4096]{4,3,2,0,1:T(2,128)(2,1)S(1)} %bitcast_dynamic-update-slice_fusion.4), channel_id=1, source_target_pairs={{0,6},{2,4},{4,2},{6,0},{8,14},{10,12},{12,10},{14,8},{16,22},{18,... | collective-permute-start | bytes 393224 | tf_op jit(solution)/shard_map/ppermute | solution.py:125
  34.7 18.2 %all-to-all-start = ((bf16[16,64,256]{2,1,0:T(8,128)(2,1)}), bf16[16,64,256]{2,1,0:T(8,128)(2,1)S(1)}, u32[]{:S(2)}, u32[]{:S(2)}) async-start(bf16[16,64,256]{2,1,0:T(8,128)(2,1)} %shard_map.46), calls=%async_computation | async-start | bytes 1048576 | tf_op jit(solution)/shard_map/all_to_all | solution.py:153
  52.9 1.6 %collective-permute-start.6 = (bf16[8,64,256]{2,1,0:T(8,128)(2,1)S(1)}, bf16[8,64,256]{2,1,0:T(8,128)(2,1)S(1)}, u32[]{:S(2)}, u32[]{:S(2)}) collective-permute-start(bf16[8,64,256]{2,1,0:T(8,128)(2,1)S(1)} %constant_dynamic-slice_fusion), channel_id=1, source_target_pairs={{0,1},{1,0},{2,3},{3,2},{4,5},{5,4},{6,7},{7,6},{8,9},{9,8},{10,11... | collective-permute-start | bytes 786440 | tf_op jit(solution)/shard_map/ppermute | solution.py:157
